TPU v7x, 128 devices: a whole 4x4x4 slice. The times are simulated.
128 devices in a mesh: area: 128 (over x, z, y, core).
Axes of the slice: x: 4, y: 4, z: 4, core: 2. Of those that a mesh axis runs over, the one named last changes fastest.
Arguments:
- population: float32 [2048, 96, 1024], P('area'), may hold values from 0.1 to 10
- area_target: float32 [2048, 96], P('area'), may hold values from 500 to 5000
- national_target: float32 [96, 32], replicated, may hold values from 50000 to 500000
- zone_target: float32 [1024, 1536], P('area'), may hold values from 500 to 10000
- area_zone: int32 [2048], P('area'), may hold values from 0 to 1023, never falling along the last dimension, each value on 1 to 6 neighbouring positions
- zone_order: int32 [1024], replicated, may hold values from 0 to 1023, each once
Outputs:
- fitted: float32 [2048, 96, 1024], P('area')
Inputs may be any that keep to these rules, and one draw needn't show every extreme that they name: area_zone never falls along the areas; every zone holds 1 to 6 areas, and some zone exactly 6. `zone_order`: every zone appears once.
All inputs are finite; a program needn't handle non-finite values.
Results may differ from a plain program's by a relative error of at most 0.0001.
Values sent between devices are 32-bit elements; how exact they have to be, the bound alone decides.
No kernel may reach another device: no remote copies, remote signals or barrier semaphores. Data moves between devices by JAX's collectives and lax.ppermute only.
A program may use at most 128 MiB of HBM per device.

v0:
```python
import jax
import jax.numpy as jnp
from jax import lax
from jax.sharding import PartitionSpec as P

AGE = 48
SEX = 2
INC = 32
HH = 8
TU = 4


def body(population, area_target, national_target, zone_target, area_zone, zone_order):
    count = population.shape[0]
    zones = zone_order.shape[0]
    area_sum = jnp.sum(population, axis=2)
    first = population * (area_target / area_sum)[:, :, None]
    view = first.reshape(count, AGE * SEX, INC, HH * TU)
    national = lax.psum(jnp.sum(view, axis=(0, 2)), "area")
    second = view * (national_target / national)[None, :, None, :]
    split = second.reshape(count, AGE, SEX, INC, HH * TU)
    area_margin = jnp.sum(split, axis=(2, 4)).reshape(count, AGE * INC)
    labels = jnp.arange(zones, dtype=jnp.int32)
    slot_of = jnp.zeros((zones,), jnp.int32).at[zone_order].set(labels)
    area_slot = jnp.take(slot_of, area_zone, axis=0)
    partial_value = jax.ops.segment_sum(area_margin, area_zone, num_segments=zones)
    owned = jnp.take(partial_value, zone_order, axis=0)
    totals = lax.psum_scatter(owned, "area", scatter_dimension=0, tiled=True)
    local_ratio = zone_target / totals
    slot_ratio = lax.all_gather(local_ratio, "area", axis=0, tiled=True)
    area_ratio = jnp.take(slot_ratio, area_slot, axis=0)
    factor = area_ratio.reshape(count, AGE, 1, INC, 1)
    return (split * factor).reshape(count, AGE * SEX, INC * HH * TU)


def solution(mesh):
    placed = (P("area", None, None), P("area", None), P(), P("area", None), P("area"), P())
    return jax.shard_map(
        body, mesh=mesh, in_specs=placed, out_specs=P("area", None, None), check_vma=False
    )
```

profile of v0, /device:TPU:6, one launch (start us, length us, event | category | flops | bytes accessed | tf_op | source)
XLA Modules:
  0.0 459.7 jit_solution(10945307009008888673)
XLA Ops:
  6.5 0.7 compare_select_fusion
  7.2 0.7 compare_and_fusion
  7.9 3.1 reduce_sum.34
  11.1 6.1 %fusion.4 = (f32[96,1024]{1,0:T(8,128)S(1)}, f32[16,96,1024]{2,1,0:T(8,128)}) fusion(f32[16,96,1024]{2,1,0:T(8,128)} %param.6, f32[16,96]{1,0:T(8,128)S(1)} %div.9), kind=kLoop, calls=%fused_computation.23 | loop fusion | flops 3047424 | bytes 12982272 | tf_op jit(solution)/shard_map/reduce_sum | solution.py:19
  17.2 16.8 %reshape.45 = f32[16,48,2,32,32]{4,3,2,1,0:T(8,128)} reshape(f32[16,96,1024]{2,1,0:T(8,128)} %get-tuple-element.8) | data formatting | bytes 12582912 | tf_op jit(solution)/shard_map/reshape | solution.py:18
  34.0 0.2 copy.10
  34.2 0.1 reduce_sum.37
  34.3 66.0 %psum.7 = f32[96,32]{0,1:T(8,128)S(1)} all-reduce(f32[96,32]{0,1:T(8,128)S(1)} %reduce_sum.37), channel_id=1, replica_groups=mesh['area'=128] {'area'}, use_global_device_ids=true, to_apply=%region_3.0 | all-reduce | flops 3072 | bytes 24576 | tf_op jit(solution)/shard_map/psum | solution.py:19
  100.3 0.1 copy.11
  100.4 0.0 copy-start.3
  100.4 10.6 %multiply_reduce_fusion = f32[16,48,32]{2,1,0:T(8,128)S(1)} fusion(f32[16,48,2,32,32]{4,3,2,1,0:T(8,128)} %reshape.45, f32[48,2,32]{2,1,0:T(2,128)S(1)} %bitcast.7), kind=kLoop, calls=%fused_computation.5 | loop fusion | flops 3121152 | bytes 6402048 | tf_op jit(solution)/shard_map/reduce_sum | solution.py:22
  111.0 0.2 reshape.83
  111.2 0.0 copy-done.3
  111.2 3.8 scatter_custom_fusion.1
  114.9 10.6 %gather_fusion.1 = f32[1024,1536]{1,0:T(8,128)} fusion(f32[1024,1536]{1,0:T(8,128)} %scatter_custom_fusion.1, s32[1024]{0:T(1024)S(1)} %get-tuple-element.10), kind=kCustom, calls=%fused_computation.1 | custom fusion | bytes 12587008 | tf_op jit(solution)/shard_map/jit(_take)/gather | solution.py:27
  125.5 5.9 %broadcast_select_fusion = f32[1024,1536]{1,0:T(8,128)} fusion(f32[1024,1536]{1,0:T(8,128)} %gather_fusion.1, pred[1024]{0:T(1024)(128)(4,1)S(1)} %compare_and_fusion), kind=kLoop, calls=%fused_computation.7 | loop fusion | flops 1572864 | bytes 12583936 | tf_op jit(solution)/shard_map/jit(_take)/select_n | solution.py:27
  131.5 0.0 reduce-scatter.2.cloned.1.call-update
  131.5 0.0 all-gather.2.cloned.1.call-start
  131.5 210.1 %reduce-scatter.2.cloned.1.call-done = f32[8,1536]{1,0:T(8,128)} async-done(((f32[1024,1536]{1,0:T(8,128)}), f32[8,1536]{1,0:T(8,128)}) %reduce-scatter.2.cloned.1.call-update) | async-done | bytes 49168 | tf_op jit(solution)/shard_map/reduce_scatter | solution.py:28
  341.6 1.4 div.11
  343.1 0.0 all-gather.2.cloned.1.call-update
  343.1 0.1 mul.42
  343.2 0.7 mul.43
  343.9 4.5 scatter_custom_fusion
  348.4 0.6 gather_fusion
  349.1 61.2 %all-gather.2.cloned.1.call-done = f32[1024,1536]{1,0:T(8,128)} async-done(((f32[8,1536]{1,0:T(8,128)}), f32[1024,1536]{1,0:T(8,128)}) %all-gather.2.cloned.1.call-update) | async-done | bytes 6291472 | tf_op jit(solution)/shard_map/all_gather | solution.py:30
  410.3 3.4 gather_fusion.2
  413.8 0.1 gather.17
  413.9 0.1 broadcast_select_fusion.1
  414.0 9.4 %mul.48 = f32[16,48,2,32,32]{4,3,2,1,0:T(8,128)} broadcast(f32[16,48,32]{2,1,0:T(8,128)S(1)} %broadcast_select_fusion.1), dimensions={0,1,3} | broadcast | bytes 6389760 | tf_op jit(solution)/shard_map/mul | solution.py:33
  423.4 19.9 %mul.49 = f32[16,96,1024]{2,1,0:T(8,128)} reshape(f32[16,48,2,32,32]{4,3,2,1,0:T(8,128)} %mul.48) | data formatting | bytes 12582912 | tf_op jit(solution)/shard_map/mul | solution.py:33
  443.3 9.5 %multiply_multiply_fusion = f32[16,96,1024]{2,1,0:T(8,128)} fusion(f32[16,96,1024]{2,1,0:T(8,128)} %mul.49, f32[16,96,1024]{2,1,0:T(8,128)} %get-tuple-element.8, f32[96,1024]{1,0:T(8,128)S(1)} %mul.43), kind=kLoop, calls=%fused_computation.6 | loop fusion | flops 3145728 | bytes 19267584 | tf_op jit(solution)/shard_map/mul | solution.py:33
  (14 shorter events, 0.1 us)
Async XLA Ops:
  6.5 4.5 copy-start.2
  6.5 335.1 %reduce-scatter.2.cloned.1.call-start = ((), (), s32[]{:S(2)}) async-start(), calls=%async_computation.1 | async-start | bytes 6340608 | tf_op jit(solution)/shard_map/reduce_scatter | solution.py:28
  17.2 83.1 %copy-start.1 = (f32[96,32]{0,1:T(8,128)S(1)}, f32[96,32]{0,1:T(8,128)}, u32[]{:S(2)}) copy-start(f32[96,32]{0,1:T(8,128)} %param.8) | copy-start | bytes 36868
  100.4 10.8 %copy-start.3 = (s32[16]{0:T(128)S(1)}, s32[16]{0:T(128)}, u32[]{:S(2)}) copy-start(s32[16]{0:T(128)} %param.10) | copy-start | bytes 196
  131.5 210.2 %copy-start = (f32[8,1536]{1,0:T(8,128)S(1)}, f32[8,1536]{1,0:T(8,128)}, u32[]{:S(2)}) copy-start(f32[8,1536]{1,0:T(8,128)} %param.9) | copy-start | bytes 147460
  131.5 278.9 %all-gather.2.cloned.1.call-start = ((), (), s32[]{:S(2)}) async-start(), calls=%async_computation.2 | async-start | bytes 6340608 | tf_op jit(solution)/shard_map/all_gather | solution.py:30
Sparse Core Ops, SparseCore 0:
  131.6 209.9 reduce-scatter.1
  344.7 65.5 all-gather.1
where the time goes:
time: 464 us; the launch traced here: 460 us
  waiting for transfers between devices  271 us (58%)
  local copies, waits for them, and re-layouts  66.7 us (14%)
  blocking collectives  66 us (14%)
  other arithmetic  42.1 us (9%)
  between operations  13.5 us (3%)
    reduce_scatter x1, waiting for transfers between devices, body(): totals = lax.psum_scatter(owned, 'area', scatter_dimension=0, tiled=True)  210 us
    psum x1, blocking collectives, body(): national = lax.psum(jnp.sum(view, axis=(0, 2)), 'area')  66 us
    all_gather x1, waiting for transfers between devices, body(): slot_ratio = lax.all_gather(local_ratio, 'area', axis=0, tiled=True)  61.2 us
    mul x2, local copies, waits for them, and re-layouts, body(): return (split * factor).reshape(count, AGE * SEX, INC * HH * TU)  29.3 us
    reshape x1, local copies, waits for them, and re-layouts, body(): view = first.reshape(count, AGE * SEX, INC, HH * TU)  16.8 us
    gather x1, local copies, waits for them, and re-layouts, body(): owned = jnp.take(partial_value, zone_order, axis=0)  10.6 us
    reduce_sum x1, other arithmetic, body(): area_margin = jnp.sum(split, axis=(2, 4)).reshape(count, AGE * INC)  10.6 us
    mul x1, other arithmetic, body(): return (split * factor).reshape(count, AGE * SEX, INC * HH * TU)  9.55 us
  transfers between devices with their start and end apart: 2, of which 2 were waited for; matrix products, arithmetic and copies ran while one was open for 1% of the time, Pallas kernels for 0%

commit v1 on v0

v1 whole, which is shorter than its diff:
```python
import jax
import jax.numpy as jnp
from jax import lax
from jax.sharding import PartitionSpec as P

AGE = 48
SEX = 2
INC = 32
HH = 8
TU = 4
ZONE_MOST = 6
GROUP = 16


def _shift(x, n, group, k):
    perm = [(i, (i // group) * group + (i % group + k) % group) for i in range(n)]
    return lax.ppermute(x, "area", perm)


def _across(x, n, group, j):
    groups = n // group
    perm = [(i, ((i // group + j) % groups) * group + i % group) for i in range(n)]
    return lax.ppermute(x, "area", perm)


def make_body(n):
    groups = n // GROUP

    def body(population, area_target, national_target, zone_target, area_zone, zone_order):
        count = population.shape[0]
        rows = zone_target.shape[0]
        zones = zone_order.shape[0]
        cols = zone_target.shape[1]
        most = count
        assert ZONE_MOST < count
        idx = lax.axis_index("area")
        grp, pos = idx // GROUP, idx % GROUP
        f32 = jnp.float32

        labels = jnp.arange(zones, dtype=jnp.int32)
        slot_of = jnp.zeros((zones,), jnp.int32).at[zone_order].set(labels)
        zlo = area_zone[0]
        zhi = area_zone[count - 1]
        ks = jnp.arange(most, dtype=jnp.int32)
        kz = zlo + ks
        valid = kz <= zhi
        slot = slot_of[jnp.minimum(kz, zones - 1)]
        owner_grp = slot // (rows * GROUP)
        j_k = (owner_grp - grp) % groups
        member = (slot // rows) % GROUP
        pidx = ((pos - member) % GROUP) * rows + slot % rows
        same = (j_k[:, None] == j_k[None, :]) & valid[None, :] & (ks[None, :] < ks[:, None])
        q_k = jnp.sum(same.astype(jnp.int32), axis=1)
        req = jnp.zeros((groups, most), jnp.int32).at[jnp.where(valid, j_k, groups), q_k].set(pidx, mode="drop")

        pool = [zone_target]
        for k in range(1, GROUP):
            pool.append(_shift(zone_target, n, GROUP, k))
        pool = jnp.concatenate(pool, axis=0)
        asked = [req[0]]
        for j in range(1, groups):
            asked.append(_across(req[j], n, GROUP, j))
        replies = [jnp.take(pool, req[0], axis=0)]
        for j in range(1, groups):
            replies.append(_across(jnp.take(pool, asked[j], axis=0), n, GROUP, -j))
        reply = jnp.stack(replies)
        target = reply[j_k, q_k]

        right = [(i, i + 1) for i in range(n - 1)]
        left = [(i, i - 1) for i in range(1, n)]
        zhi_left = lax.ppermute(zhi[None], "area", right)[0]
        zlo_right = lax.ppermute(zlo[None], "area", left)[0]

        view = population.reshape(count, AGE * SEX, INC, HH * TU)
        t1 = jnp.sum(view, axis=2)
        area_sum = jnp.sum(t1, axis=2)
        s1 = area_target / area_sum
        part = jnp.sum(t1 * s1[:, :, None], axis=0)
        acc = part
        for k in range(1, GROUP):
            acc = acc + _shift(part, n, GROUP, k)
        national = acc
        for j in range(1, groups):
            national = national + _across(acc, n, GROUP, j)
        s2 = national_target / national

        w = s1[:, :, None] * s2[None, :, :]
        am = jnp.sum(view * w[:, :, None, :], axis=3)
        am = jnp.sum(am.reshape(count, AGE, SEX, INC), axis=2).reshape(count, AGE * INC)
        k_a = area_zone - zlo
        onehot = (k_a[:, None] == ks[None, :]).astype(f32)
        zp = jnp.sum(onehot[:, :, None] * am[:, None, :], axis=0)
        nk = zhi - zlo
        from_left = lax.ppermute(zp[nk], "area", right)
        from_right = lax.ppermute(zp[0], "area", left)
        zp = zp.at[0].add(jnp.where(zhi_left == zlo, from_left, 0.0))
        zp = zp.at[nk].add(jnp.where(zlo_right == zhi, from_right, 0.0))
        ratio = target / zp
        ratio_a = jnp.take(ratio, k_a, axis=0)

        fac = (w.reshape(count, AGE, SEX, 1, HH * TU)
               * ratio_a.reshape(count, AGE, 1, INC, 1))
        out = population.reshape(count, AGE, SEX, INC, HH * TU) * fac
        return out.reshape(count, AGE * SEX, INC * HH * TU)

    return body


def solution(mesh):
    n = mesh.shape["area"]
    placed = (P("area", None, None), P("area", None), P(), P("area", None), P("area"), P())
    return jax.shard_map(
        make_body(n), mesh=mesh, in_specs=placed, out_specs=P("area", None, None), check_vma=False
    )
```

time: 464 us -> 246 us (0.53)
  waiting for transfers between devices: 271 us -> 74.5 us
  starting transfers between devices: 0.04 us -> 80.3 us
  blocking collectives: 66 us -> 0 us
  local copies, waits for them, and re-layouts: 66.7 us -> 43 us
  between operations: 13.5 us -> 4.4 us
    reduce_scatter x1 -> x0, waiting for transfers between devices: 210 us -> none  [body(): totals = lax.psum_scatter(owned, 'area', scatter_dimension=0, tiled=True)]
    ppermute x0 -> x55, starting transfers between devices: none -> 80.3 us  [the longest x21 44.3 us: _across(): return lax.ppermute(x, 'area', perm)]
    ppermute x0 -> x55, waiting for transfers between devices: none -> 74.5 us  [the longest x30 56.7 us: _shift(): return lax.ppermute(x, 'area', perm)]
    psum x1 -> x0, blocking collectives: 66 us -> none  [body(): national = lax.psum(jnp.sum(view, axis=(0, 2)), 'area')]
    all_gather x1 -> x0, waiting for transfers between devices: 61.2 us -> none  [body(): slot_ratio = lax.all_gather(local_ratio, 'area', axis=0, tiled=True)]
    reshape x2 -> x0, local copies, waits for them, and re-layouts: 17 us -> none  [the longest x1 16.8 us: body(): view = first.reshape(count, AGE * SEX, INC, HH * TU)]
    mul x1 -> x4, other arithmetic: 9.55 us -> 20 us  [the longest x1 9.55 us: body(): w.reshape(count, AGE, SEX, 1, HH * TU)]
    mul x4 -> x3, local copies, waits for them, and re-layouts: 30.1 us -> 20.5 us  [the longest x1 19.9 us: body(): w.reshape(count, AGE, SEX, 1, HH * TU)]
  transfers between devices with their start and end apart: 2 -> 55, of which waited for: 2 -> 24; matrix products, arithmetic and copies ran while one was open for 1% -> 9% of each run, Pallas kernels for 0% -> 0%
where the time goes in v1:
time: 246 us; the launch traced here: 242 us
  starting transfers between devices  80.3 us (33%)
  waiting for transfers between devices  74.5 us (30%)
  local copies, waits for them, and re-layouts  43 us (17%)
  other arithmetic  39.8 us (16%)
  between operations  4.4 us (2%)
    ppermute x30, waiting for transfers between devices, _shift(): return lax.ppermute(x, 'area', perm)  56.7 us
    ppermute x21, starting transfers between devices, _across(): return lax.ppermute(x, 'area', perm)  44.3 us
    ppermute x30, starting transfers between devices, _shift(): return lax.ppermute(x, 'area', perm)  23.5 us
    mul x1, local copies, waits for them, and re-layouts, body(): w.reshape(count, AGE, SEX, 1, HH * TU)  19.9 us
    ppermute x21, waiting for transfers between devices, _across(): return lax.ppermute(x, 'area', perm)  12.4 us
    mul x1, other arithmetic, body(): w.reshape(count, AGE, SEX, 1, HH * TU)  9.55 us
    mul x1, other arithmetic, body(): out = population.reshape(count, AGE, SEX, INC, HH * TU) * fac  9.49 us
    unnamed x34, local copies, waits for them, and re-layouts  8.57 us
  transfers between devices with their start and end apart: 55, of which 24 were waited for; matrix products, arithmetic and copies ran while one was open for 9% of the time, Pallas kernels for 0%

profile of v1, /device:TPU:6, one launch (start us, length us, event | category | flops | bytes accessed | tf_op | source)
XLA Modules:
  0.0 242.1 jit_solution(9198240422745281121)
XLA Ops:
  0.0 8.4 %copy.30 = f32[16,96,1024]{1,2,0:T(8,128)} copy(f32[16,96,1024]{2,1,0:T(8,128)} %param.12) | data formatting | bytes 12582912 | tf_op args[0]
  8.5 3.2 %reduce_sum.65 = f32[16,96]{1,0:T(8,128)S(1)} reduce(f32[16,96,1024]{2,1,0:T(8,128)} %param.12, f32[]{:T(128)} %constant.150.clone.1), dimensions={2}, to_apply=%region_0.1 | reduce | flops 1571328 | bytes 6297604 | tf_op jit(solution)/shard_map/reduce_sum | solution.py:76
  11.7 4.5 %reduce_sum.66 = f32[16,96,32]{1,2,0:T(8,128)S(1)} reduce(f32[16,96,32,32]{1,3,2,0:T(8,128)} %bitcast.73, f32[]{:T(128)} %constant.150.clone.1), dimensions={2}, to_apply=%region_1.2 | reduce | flops 1523712 | bytes 6488068 | tf_op jit(solution)/shard_map/reduce_sum | solution.py:75
  16.2 3.9 %collective-permute-start.14 = (f32[96,32]{0,1:T(8,128)S(1)}, f32[96,32]{0,1:T(8,128)S(1)}, u32[]{:S(2)}, u32[]{:S(2)}) collective-permute-start(f32[96,32]{0,1:T(8,128)S(1)} %multiply_reduce_fusion.2), channel_id=1, source_target_pairs={{0,15},{1,0},{2,1},{3,2},{4,3},{5,4},{6,5},{7,6},{8,7},{9,8},{10,9... | collective-permute-start | bytes 36872 | tf_op jit(solution)/shard_map/ppermute | solution.py:17
  21.6 4.8 %collective-permute-start.53 = (s32[1]{0:T(128)}, s32[1]{0:T(128)}, u32[]{:S(2)}, u32[]{:S(2)}) collective-permute-start(s32[1]{0:T(128)} %get-tuple-element.47), channel_id=1, source_target_pairs={{1,0},{2,1},{3,2},{4,3},{5,4},{6,5},{7,6},{8,7},{9,8},{10,9},{11,1... | collective-permute-start | bytes 20 | tf_op jit(solution)/shard_map/ppermute | solution.py:72
  32.2 4.3 %scatter_custom_fusion = s32[1024]{0:T(1024)S(1)} fusion(s32[1024]{0:T(1024)S(1)} %compare_select_fusion, s32[1024]{0:T(1024)S(1)} %iota.23, s32[]{:T(128)} %constant.151.clone.1), kind=kCustom, calls=%fused_computation.96 | custom fusion | bytes 4100 | tf_op jit(solution)/shard_map/scatter | solution.py:41
  46.4 2.9 %collective-permute-start.45 = (s32[16]{0:T(128)S(1)}, s32[16]{0:T(128)S(1)}, u32[]{:S(2)}, u32[]{:S(2)}) collective-permute-start(s32[16]{0:T(128)S(1)} %get-tuple-element.38), channel_id=1, source_target_pairs={{0,80},{1,81},{2,82},{3,83},{4,84},{5,85},{6,86},{7,87},{8,88},{9,... | collective-permute-start | bytes 200 | tf_op jit(solution)/shard_map/ppermute | solution.py:23
  49.3 3.3 %collective-permute-start.43 = (s32[16]{0:T(128)S(1)}, s32[16]{0:T(128)S(1)}, u32[]{:S(2)}, u32[]{:S(2)}) collective-permute-start(s32[16]{0:T(128)S(1)} %get-tuple-element.39), channel_id=1, source_target_pairs={{0,64},{1,65},{2,66},{3,67},{4,68},{5,69},{6,70},{7,71},{8,72},{9,... | collective-permute-start | bytes 200 | tf_op jit(solution)/shard_map/ppermute | solution.py:23
  53.6 4.0 %collective-permute-start.41 = (s32[16]{0:T(128)S(1)}, s32[16]{0:T(128)S(1)}, u32[]{:S(2)}, u32[]{:S(2)}) collective-permute-start(s32[16]{0:T(128)S(1)} %get-tuple-element.40), channel_id=1, source_target_pairs={{0,48},{1,49},{2,50},{3,51},{4,52},{5,53},{6,54},{7,55},{8,56},{9,... | collective-permute-start | bytes 200 | tf_op jit(solution)/shard_map/ppermute | solution.py:23
  57.6 3.4 %collective-permute-done.41 = s32[16]{0:T(128)S(1)} collective-permute-done((s32[16]{0:T(128)S(1)}, s32[16]{0:T(128)S(1)}, u32[]{:S(2)}, u32[]{:S(2)}) %collective-permute-start.41) | collective-permute-done | bytes 96 | tf_op jit(solution)/shard_map/ppermute | solution.py:23
  62.8 3.2 %collective-permute-start.37 = (s32[16]{0:T(128)S(1)}, s32[16]{0:T(128)S(1)}, u32[]{:S(2)}, u32[]{:S(2)}) collective-permute-start(s32[16]{0:T(128)S(1)} %get-tuple-element.42), channel_id=1, source_target_pairs={{0,16},{1,17},{2,18},{3,19},{4,20},{5,21},{6,22},{7,23},{8,24},{9,... | collective-permute-start | bytes 200 | tf_op jit(solution)/shard_map/ppermute | solution.py:23
  88.5 5.6 %collective-permute-start.19 = (f32[96,32]{0,1:T(8,128)S(1)}, f32[96,32]{0,1:T(8,128)S(1)}, u32[]{:S(2)}, u32[]{:S(2)}) collective-permute-start(f32[96,32]{0,1:T(8,128)S(1)} %add_add_fusion), channel_id=1, source_target_pairs={{0,80},{1,81},{2,82},{3,83},{4,84},{5,85},{6,86},{7,87},{8,88},{9,... | collective-permute-start | bytes 36872 | tf_op jit(solution)/shard_map/ppermute | solution.py:23
  94.1 4.0 %collective-permute-start.17 = (f32[96,32]{0,1:T(8,128)S(1)}, f32[96,32]{0,1:T(8,128)S(1)}, u32[]{:S(2)}, u32[]{:S(2)}) collective-permute-start(f32[96,32]{0,1:T(8,128)S(1)} %add_add_fusion), channel_id=1, source_target_pairs={{0,48},{1,49},{2,50},{3,51},{4,52},{5,53},{6,54},{7,55},{8,56},{9,... | collective-permute-start | bytes 36872 | tf_op jit(solution)/shard_map/ppermute | solution.py:23
  98.1 3.1 %collective-permute-start.15 = (f32[96,32]{0,1:T(8,128)S(1)}, f32[96,32]{0,1:T(8,128)S(1)}, u32[]{:S(2)}, u32[]{:S(2)}) collective-permute-start(f32[96,32]{0,1:T(8,128)S(1)} %add_add_fusion), channel_id=1, source_target_pairs={{0,16},{1,17},{2,18},{3,19},{4,20},{5,21},{6,22},{7,23},{8,24},{9,... | collective-permute-start | bytes 36872 | tf_op jit(solution)/shard_map/ppermute | solution.py:23
  104.9 5.4 %multiply_reduce_fusion = f32[16,96,32]{1,2,0:T(8,128)S(1)} fusion(f32[16,96,32]{1,2,0:T(8,128)S(1)} %broadcast_multiply_fusion.2, f32[16,96,1024]{1,2,0:T(8,128)} %copy.30), kind=kLoop, calls=%fused_computation.14 | loop fusion | flops 3096576 | bytes 6684672 | tf_op jit(solution)/shard_map/reduce_sum | solution.py:88
  111.3 3.9 %collective-permute-start.52 = (f32[1536]{0:T(1024)S(1)}, f32[1536]{0:T(1024)S(1)}, u32[]{:S(2)}, u32[]{:S(2)}) collective-permute-start(f32[1536]{0:T(1024)S(1)} %get-tuple-element.31), channel_id=1, source_target_pairs={{0,1},{1,2},{2,3},{3,4},{4,5},{5,6},{6,7},{7,8},{8,9},{9,10},{10,1... | collective-permute-start | bytes 18440 | tf_op jit(solution)/shard_map/ppermute | solution.py:94
  116.2 4.3 %collective-permute-done.52 = f32[1536]{0:T(1024)S(1)} collective-permute-done((f32[1536]{0:T(1024)S(1)}, f32[1536]{0:T(1024)S(1)}, u32[]{:S(2)}, u32[]{:S(2)}) %collective-permute-start.52) | collective-permute-done | bytes 6176 | tf_op jit(solution)/shard_map/ppermute | solution.py:94
  124.7 4.8 %collective-permute-done.22 = f32[8,1536]{1,0:T(8,128)S(1)} collective-permute-done((f32[8,1536]{1,0:T(8,128)S(1)}, f32[8,1536]{1,0:T(8,128)S(1)}, u32[]{:S(2)}, u32[]{:S(2)}) %collective-permute-start.22) | collective-permute-done | bytes 49184 | tf_op jit(solution)/shard_map/ppermute | solution.py:17
  129.4 6.2 %collective-permute-done.23 = f32[8,1536]{1,0:T(8,128)S(1)} collective-permute-done((f32[8,1536]{1,0:T(8,128)S(1)}, f32[8,1536]{1,0:T(8,128)S(1)}, u32[]{:S(2)}, u32[]{:S(2)}) %collective-permute-start.23) | collective-permute-done | bytes 49184 | tf_op jit(solution)/shard_map/ppermute | solution.py:17
  135.6 5.9 %collective-permute-done.24 = f32[8,1536]{1,0:T(8,128)S(1)} collective-permute-done((f32[8,1536]{1,0:T(8,128)S(1)}, f32[8,1536]{1,0:T(8,128)S(1)}, u32[]{:S(2)}, u32[]{:S(2)}) %collective-permute-start.24) | collective-permute-done | bytes 49184 | tf_op jit(solution)/shard_map/ppermute | solution.py:17
  141.5 6.5 %collective-permute-done.25 = f32[8,1536]{1,0:T(8,128)S(1)} collective-permute-done((f32[8,1536]{1,0:T(8,128)S(1)}, f32[8,1536]{1,0:T(8,128)S(1)}, u32[]{:S(2)}, u32[]{:S(2)}) %collective-permute-start.25) | collective-permute-done | bytes 49184 | tf_op jit(solution)/shard_map/ppermute | solution.py:17
  148.0 4.4 %collective-permute-done.26 = f32[8,1536]{1,0:T(8,128)S(1)} collective-permute-done((f32[8,1536]{1,0:T(8,128)S(1)}, f32[8,1536]{1,0:T(8,128)S(1)}, u32[]{:S(2)}, u32[]{:S(2)}) %collective-permute-start.26) | collective-permute-done | bytes 49184 | tf_op jit(solution)/shard_map/ppermute | solution.py:17
  152.5 5.0 %collective-permute-done.27 = f32[8,1536]{1,0:T(8,128)S(1)} collective-permute-done((f32[8,1536]{1,0:T(8,128)S(1)}, f32[8,1536]{1,0:T(8,128)S(1)}, u32[]{:S(2)}, u32[]{:S(2)}) %collective-permute-start.27) | collective-permute-done | bytes 49184 | tf_op jit(solution)/shard_map/ppermute | solution.py:17
  157.4 3.5 %collective-permute-done.28 = f32[8,1536]{1,0:T(8,128)S(1)} collective-permute-done((f32[8,1536]{1,0:T(8,128)S(1)}, f32[8,1536]{1,0:T(8,128)S(1)}, u32[]{:S(2)}, u32[]{:S(2)}) %collective-permute-start.28) | collective-permute-done | bytes 49184 | tf_op jit(solution)/shard_map/ppermute | solution.py:17
  161.0 4.1 %collective-permute-done.29 = f32[8,1536]{1,0:T(8,128)S(1)} collective-permute-done((f32[8,1536]{1,0:T(8,128)S(1)}, f32[8,1536]{1,0:T(8,128)S(1)}, u32[]{:S(2)}, u32[]{:S(2)}) %collective-permute-start.29) | collective-permute-done | bytes 49184 | tf_op jit(solution)/shard_map/ppermute | solution.py:17
  165.0 4.7 %collective-permute-done.30 = f32[8,1536]{1,0:T(8,128)S(1)} collective-permute-done((f32[8,1536]{1,0:T(8,128)S(1)}, f32[8,1536]{1,0:T(8,128)S(1)}, u32[]{:S(2)}, u32[]{:S(2)}) %collective-permute-start.30) | collective-permute-done | bytes 49184 | tf_op jit(solution)/shard_map/ppermute | solution.py:17
  169.8 5.3 %collective-permute-done.31 = f32[8,1536]{1,0:T(8,128)S(1)} collective-permute-done((f32[8,1536]{1,0:T(8,128)S(1)}, f32[8,1536]{1,0:T(8,128)S(1)}, u32[]{:S(2)}, u32[]{:S(2)}) %collective-permute-start.31) | collective-permute-done | bytes 49184 | tf_op jit(solution)/shard_map/ppermute | solution.py:17
  181.7 3.6 %collective-permute-start.38 = (f32[16,1536]{1,0:T(8,128)S(1)}, f32[16,1536]{1,0:T(8,128)S(1)}, u32[]{:S(2)}, u32[]{:S(2)}) collective-permute-start(f32[16,1536]{1,0:T(8,128)S(1)} %broadcast_select_fusion.7), channel_id=1, source_target_pairs={{0,112},{1,113},{2,114},{3,115},{4,116},{5,117},{6,118},{7,119},{8... | collective-permute-start | bytes 294920 | tf_op jit(solution)/shard_map/ppermute | solution.py:23
  187.1 2.9 %collective-permute-start.44 = (f32[16,1536]{1,0:T(8,128)S(1)}, f32[16,1536]{1,0:T(8,128)S(1)}, u32[]{:S(2)}, u32[]{:S(2)}) collective-permute-start(f32[16,1536]{1,0:T(8,128)S(1)} %broadcast_select_fusion.4), channel_id=1, source_target_pairs={{0,64},{1,65},{2,66},{3,67},{4,68},{5,69},{6,70},{7,71},{8,72},{9,... | collective-permute-start | bytes 294920 | tf_op jit(solution)/shard_map/ppermute | solution.py:23
  203.1 9.5 %broadcast_multiply_fusion = f32[16,48,2,32,32]{4,3,2,1,0:T(8,128)} fusion(f32[16,48,32]{2,1,0:T(8,128)S(1)} %broadcast_select_fusion, f32[16,48,2,32]{3,2,1,0:T(2,128)S(1)} %broadcast_multiply_fusion.1), kind=kLoop, calls=%fused_computation.13 | loop fusion | flops 1572864 | bytes 6586368 | tf_op jit(solution)/shard_map/mul | solution.py:101
  212.7 19.9 %mul.103 = f32[16,96,1024]{2,1,0:T(8,128)} reshape(f32[16,48,2,32,32]{4,3,2,1,0:T(8,128)} %broadcast_multiply_fusion) | data formatting | bytes 12582912 | tf_op jit(solution)/shard_map/mul | solution.py:101
  232.6 9.5 %mul.104 = f32[16,96,1024]{2,1,0:T(8,128)} multiply(f32[16,96,1024]{2,1,0:T(8,128)} %param.12, f32[16,96,1024]{2,1,0:T(8,128)} %mul.103) | non-fusion elementwise | flops 1572864 | bytes 18874368 | tf_op jit(solution)/shard_map/mul | solution.py:103
  (198 shorter events, 69.8 us)
Async XLA Ops:
  16.2 52.6 %collective-permute-start.14 = (f32[96,32]{0,1:T(8,128)S(1)}, f32[96,32]{0,1:T(8,128)S(1)}, u32[]{:S(2)}, u32[]{:S(2)}) collective-permute-start(f32[96,32]{0,1:T(8,128)S(1)} %multiply_reduce_fusion.2), channel_id=1, source_target_pairs={{0,15},{1,0},{2,1},{3,2},{4,3},{5,4},{6,5},{7,6},{8,7},{9,8},{10,9... | collective-permute-start | bytes 36872 | tf_op jit(solution)/shard_map/ppermute | solution.py:17
  20.1 51.2 %collective-permute-start.13 = (f32[96,32]{0,1:T(8,128)S(1)}, f32[96,32]{0,1:T(8,128)S(1)}, u32[]{:S(2)}, u32[]{:S(2)}) collective-permute-start(f32[96,32]{0,1:T(8,128)S(1)} %multiply_reduce_fusion.2), channel_id=1, source_target_pairs={{0,14},{1,15},{2,0},{3,1},{4,2},{5,3},{6,4},{7,5},{8,6},{9,7},{10,... | collective-permute-start | bytes 36872 | tf_op jit(solution)/shard_map/ppermute | solution.py:17
  20.8 51.1 %collective-permute-start.12 = (f32[96,32]{0,1:T(8,128)S(1)}, f32[96,32]{0,1:T(8,128)S(1)}, u32[]{:S(2)}, u32[]{:S(2)}) collective-permute-start(f32[96,32]{0,1:T(8,128)S(1)} %multiply_reduce_fusion.2), channel_id=1, source_target_pairs={{0,13},{1,14},{2,15},{3,0},{4,1},{5,2},{6,3},{7,4},{8,5},{9,6},{10... | collective-permute-start | bytes 36872 | tf_op jit(solution)/shard_map/ppermute | solution.py:17
  21.6 19.7 %collective-permute-start.53 = (s32[1]{0:T(128)}, s32[1]{0:T(128)}, u32[]{:S(2)}, u32[]{:S(2)}) collective-permute-start(s32[1]{0:T(128)} %get-tuple-element.47), channel_id=1, source_target_pairs={{1,0},{2,1},{3,2},{4,3},{5,4},{6,5},{7,6},{8,7},{9,8},{10,9},{11,1... | collective-permute-start | bytes 20 | tf_op jit(solution)/shard_map/ppermute | solution.py:72
  26.5 17.4 %collective-permute-start.51 = (s32[1]{0:T(128)}, s32[1]{0:T(128)}, u32[]{:S(2)}, u32[]{:S(2)}) collective-permute-start(s32[1]{0:T(128)} %get-tuple-element.48), channel_id=1, source_target_pairs={{0,1},{1,2},{2,3},{3,4},{4,5},{5,6},{6,7},{7,8},{8,9},{9,10},{10,1... | collective-permute-start | bytes 20 | tf_op jit(solution)/shard_map/ppermute | solution.py:71
  46.4 7.2 %collective-permute-start.45 = (s32[16]{0:T(128)S(1)}, s32[16]{0:T(128)S(1)}, u32[]{:S(2)}, u32[]{:S(2)}) collective-permute-start(s32[16]{0:T(128)S(1)} %get-tuple-element.38), channel_id=1, source_target_pairs={{0,80},{1,81},{2,82},{3,83},{4,84},{5,85},{6,86},{7,87},{8,88},{9,... | collective-permute-start | bytes 200 | tf_op jit(solution)/shard_map/ppermute | solution.py:23
  49.3 8.3 %collective-permute-start.43 = (s32[16]{0:T(128)S(1)}, s32[16]{0:T(128)S(1)}, u32[]{:S(2)}, u32[]{:S(2)}) collective-permute-start(s32[16]{0:T(128)S(1)} %get-tuple-element.39), channel_id=1, source_target_pairs={{0,64},{1,65},{2,66},{3,67},{4,68},{5,69},{6,70},{7,71},{8,72},{9,... | collective-permute-start | bytes 200 | tf_op jit(solution)/shard_map/ppermute | solution.py:23
  53.6 7.5 %collective-permute-start.41 = (s32[16]{0:T(128)S(1)}, s32[16]{0:T(128)S(1)}, u32[]{:S(2)}, u32[]{:S(2)}) collective-permute-start(s32[16]{0:T(128)S(1)} %get-tuple-element.40), channel_id=1, source_target_pairs={{0,48},{1,49},{2,50},{3,51},{4,52},{5,53},{6,54},{7,55},{8,56},{9,... | collective-permute-start | bytes 200 | tf_op jit(solution)/shard_map/ppermute | solution.py:23
  61.0 13.1 %collective-permute-start.11 = (f32[96,32]{0,1:T(8,128)S(1)}, f32[96,32]{0,1:T(8,128)S(1)}, u32[]{:S(2)}, u32[]{:S(2)}) collective-permute-start(f32[96,32]{0,1:T(8,128)S(1)} %multiply_reduce_fusion.2), channel_id=1, source_target_pairs={{0,12},{1,13},{2,14},{3,15},{4,0},{5,1},{6,2},{7,3},{8,4},{9,5},{1... | collective-permute-start | bytes 36872 | tf_op jit(solution)/shard_map/ppermute | solution.py:17
  68.8 7.9 %collective-permute-start.9 = (f32[96,32]{0,1:T(8,128)S(1)}, f32[96,32]{0,1:T(8,128)S(1)}, u32[]{:S(2)}, u32[]{:S(2)}) collective-permute-start(f32[96,32]{0,1:T(8,128)S(1)} %multiply_reduce_fusion.2), channel_id=1, source_target_pairs={{0,10},{1,11},{2,12},{3,13},{4,14},{5,15},{6,0},{7,1},{8,2},{9,3},... | collective-permute-start | bytes 36872 | tf_op jit(solution)/shard_map/ppermute | solution.py:17
  71.2 7.3 %collective-permute-start.8 = (f32[96,32]{0,1:T(8,128)S(1)}, f32[96,32]{0,1:T(8,128)S(1)}, u32[]{:S(2)}, u32[]{:S(2)}) collective-permute-start(f32[96,32]{0,1:T(8,128)S(1)} %multiply_reduce_fusion.2), channel_id=1, source_target_pairs={{0,9},{1,10},{2,11},{3,12},{4,13},{5,14},{6,15},{7,0},{8,1},{9,2},... | collective-permute-start | bytes 36872 | tf_op jit(solution)/shard_map/ppermute | solution.py:17
  71.9 7.5 %collective-permute-start.7 = (f32[96,32]{0,1:T(8,128)S(1)}, f32[96,32]{0,1:T(8,128)S(1)}, u32[]{:S(2)}, u32[]{:S(2)}) collective-permute-start(f32[96,32]{0,1:T(8,128)S(1)} %multiply_reduce_fusion.2), channel_id=1, source_target_pairs={{0,8},{1,9},{2,10},{3,11},{4,12},{5,13},{6,14},{7,15},{8,0},{9,1},... | collective-permute-start | bytes 36872 | tf_op jit(solution)/shard_map/ppermute | solution.py:17
  74.6 6.8 %collective-permute-start.5 = (f32[96,32]{0,1:T(8,128)S(1)}, f32[96,32]{0,1:T(8,128)S(1)}, u32[]{:S(2)}, u32[]{:S(2)}) collective-permute-start(f32[96,32]{0,1:T(8,128)S(1)} %multiply_reduce_fusion.2), channel_id=1, source_target_pairs={{0,6},{1,7},{2,8},{3,9},{4,10},{5,11},{6,12},{7,13},{8,14},{9,15},... | collective-permute-start | bytes 36872 | tf_op jit(solution)/shard_map/ppermute | solution.py:17
  86.9 11.2 %collective-permute-start.21 = (f32[96,32]{0,1:T(8,128)S(1)}, f32[96,32]{0,1:T(8,128)S(1)}, u32[]{:S(2)}, u32[]{:S(2)}) collective-permute-start(f32[96,32]{0,1:T(8,128)S(1)} %add_add_fusion), channel_id=1, source_target_pairs={{0,112},{1,113},{2,114},{3,115},{4,116},{5,117},{6,118},{7,119},{8... | collective-permute-start | bytes 36872 | tf_op jit(solution)/shard_map/ppermute | solution.py:23
  87.9 10.1 %collective-permute-start.20 = (f32[96,32]{0,1:T(8,128)S(1)}, f32[96,32]{0,1:T(8,128)S(1)}, u32[]{:S(2)}, u32[]{:S(2)}) collective-permute-start(f32[96,32]{0,1:T(8,128)S(1)} %add_add_fusion), channel_id=1, source_target_pairs={{0,96},{1,97},{2,98},{3,99},{4,100},{5,101},{6,102},{7,103},{8,104... | collective-permute-start | bytes 36872 | tf_op jit(solution)/shard_map/ppermute | solution.py:23
  88.5 12.7 %collective-permute-start.19 = (f32[96,32]{0,1:T(8,128)S(1)}, f32[96,32]{0,1:T(8,128)S(1)}, u32[]{:S(2)}, u32[]{:S(2)}) collective-permute-start(f32[96,32]{0,1:T(8,128)S(1)} %add_add_fusion), channel_id=1, source_target_pairs={{0,80},{1,81},{2,82},{3,83},{4,84},{5,85},{6,86},{7,87},{8,88},{9,... | collective-permute-start | bytes 36872 | tf_op jit(solution)/shard_map/ppermute | solution.py:23
  94.1 7.9 %collective-permute-start.18 = (f32[96,32]{0,1:T(8,128)S(1)}, f32[96,32]{0,1:T(8,128)S(1)}, u32[]{:S(2)}, u32[]{:S(2)}) collective-permute-start(f32[96,32]{0,1:T(8,128)S(1)} %add_add_fusion), channel_id=1, source_target_pairs={{0,64},{1,65},{2,66},{3,67},{4,68},{5,69},{6,70},{7,71},{8,72},{9,... | collective-permute-start | bytes 36872 | tf_op jit(solution)/shard_map/ppermute | solution.py:23
  94.1 7.9 %collective-permute-start.17 = (f32[96,32]{0,1:T(8,128)S(1)}, f32[96,32]{0,1:T(8,128)S(1)}, u32[]{:S(2)}, u32[]{:S(2)}) collective-permute-start(f32[96,32]{0,1:T(8,128)S(1)} %add_add_fusion), channel_id=1, source_target_pairs={{0,48},{1,49},{2,50},{3,51},{4,52},{5,53},{6,54},{7,55},{8,56},{9,... | collective-permute-start | bytes 36872 | tf_op jit(solution)/shard_map/ppermute | solution.py:23
  98.1 6.6 %collective-permute-start.15 = (f32[96,32]{0,1:T(8,128)S(1)}, f32[96,32]{0,1:T(8,128)S(1)}, u32[]{:S(2)}, u32[]{:S(2)}) collective-permute-start(f32[96,32]{0,1:T(8,128)S(1)} %add_add_fusion), channel_id=1, source_target_pairs={{0,16},{1,17},{2,18},{3,19},{4,20},{5,21},{6,22},{7,23},{8,24},{9,... | collective-permute-start | bytes 36872 | tf_op jit(solution)/shard_map/ppermute | solution.py:23
  101.2 74.0 %collective-permute-start.35 = (f32[8,1536]{1,0:T(8,128)S(1)}, f32[8,1536]{1,0:T(8,128)S(1)}, u32[]{:S(2)}, u32[]{:S(2)}) collective-permute-start(f32[8,1536]{1,0:T(8,128)S(1)} %copy-done), channel_id=1, source_target_pairs={{0,14},{1,15},{2,0},{3,1},{4,2},{5,3},{6,4},{7,5},{8,6},{9,7},{10,... | collective-permute-start | bytes 147464 | tf_op jit(solution)/shard_map/ppermute | solution.py:17
  101.9 73.2 %collective-permute-start.34 = (f32[8,1536]{1,0:T(8,128)S(1)}, f32[8,1536]{1,0:T(8,128)S(1)}, u32[]{:S(2)}, u32[]{:S(2)}) collective-permute-start(f32[8,1536]{1,0:T(8,128)S(1)} %copy-done), channel_id=1, source_target_pairs={{0,13},{1,14},{2,15},{3,0},{4,1},{5,2},{6,3},{7,4},{8,5},{9,6},{10... | collective-permute-start | bytes 147464 | tf_op jit(solution)/shard_map/ppermute | solution.py:17
  101.9 73.2 %collective-permute-start.33 = (f32[8,1536]{1,0:T(8,128)S(1)}, f32[8,1536]{1,0:T(8,128)S(1)}, u32[]{:S(2)}, u32[]{:S(2)}) collective-permute-start(f32[8,1536]{1,0:T(8,128)S(1)} %copy-done), channel_id=1, source_target_pairs={{0,12},{1,13},{2,14},{3,15},{4,0},{5,1},{6,2},{7,3},{8,4},{9,5},{1... | collective-permute-start | bytes 147464 | tf_op jit(solution)/shard_map/ppermute | solution.py:17
  103.7 71.4 %collective-permute-start.32 = (f32[8,1536]{1,0:T(8,128)S(1)}, f32[8,1536]{1,0:T(8,128)S(1)}, u32[]{:S(2)}, u32[]{:S(2)}) collective-permute-start(f32[8,1536]{1,0:T(8,128)S(1)} %copy-done), channel_id=1, source_target_pairs={{0,11},{1,12},{2,13},{3,14},{4,15},{5,0},{6,1},{7,2},{8,3},{9,4},{... | collective-permute-start | bytes 147464 | tf_op jit(solution)/shard_map/ppermute | solution.py:17
  111.3 9.2 %collective-permute-start.52 = (f32[1536]{0:T(1024)S(1)}, f32[1536]{0:T(1024)S(1)}, u32[]{:S(2)}, u32[]{:S(2)}) collective-permute-start(f32[1536]{0:T(1024)S(1)} %get-tuple-element.31), channel_id=1, source_target_pairs={{0,1},{1,2},{2,3},{3,4},{4,5},{5,6},{6,7},{7,8},{8,9},{9,10},{10,1... | collective-permute-start | bytes 18440 | tf_op jit(solution)/shard_map/ppermute | solution.py:94
  129.4 6.2 %collective-permute-start.23 = (f32[8,1536]{1,0:T(8,128)S(1)}, f32[8,1536]{1,0:T(8,128)S(1)}, u32[]{:S(2)}, u32[]{:S(2)}) collective-permute-start(f32[8,1536]{1,0:T(8,128)S(1)} %copy-done), channel_id=1, source_target_pairs={{0,2},{1,3},{2,4},{3,5},{4,6},{5,7},{6,8},{7,9},{8,10},{9,11},{10,... | collective-permute-start | bytes 147464 | tf_op jit(solution)/shard_map/ppermute | solution.py:17
  141.5 6.5 %collective-permute-start.25 = (f32[8,1536]{1,0:T(8,128)S(1)}, f32[8,1536]{1,0:T(8,128)S(1)}, u32[]{:S(2)}, u32[]{:S(2)}) collective-permute-start(f32[8,1536]{1,0:T(8,128)S(1)} %copy-done), channel_id=1, source_target_pairs={{0,4},{1,5},{2,6},{3,7},{4,8},{5,9},{6,10},{7,11},{8,12},{9,13},{1... | collective-permute-start | bytes 147464 | tf_op jit(solution)/shard_map/ppermute | solution.py:17
  181.7 11.4 %collective-permute-start.38 = (f32[16,1536]{1,0:T(8,128)S(1)}, f32[16,1536]{1,0:T(8,128)S(1)}, u32[]{:S(2)}, u32[]{:S(2)}) collective-permute-start(f32[16,1536]{1,0:T(8,128)S(1)} %broadcast_select_fusion.7), channel_id=1, source_target_pairs={{0,112},{1,113},{2,114},{3,115},{4,116},{5,117},{6,118},{7,119},{8... | collective-permute-start | bytes 294920 | tf_op jit(solution)/shard_map/ppermute | solution.py:23
  185.3 8.7 %collective-permute-start.40 = (f32[16,1536]{1,0:T(8,128)S(1)}, f32[16,1536]{1,0:T(8,128)S(1)}, u32[]{:S(2)}, u32[]{:S(2)}) collective-permute-start(f32[16,1536]{1,0:T(8,128)S(1)} %broadcast_select_fusion.6), channel_id=1, source_target_pairs={{0,96},{1,97},{2,98},{3,99},{4,100},{5,101},{6,102},{7,103},{8,104... | collective-permute-start | bytes 294920 | tf_op jit(solution)/shard_map/ppermute | solution.py:23
  186.9 10.6 %collective-permute-start.42 = (f32[16,1536]{1,0:T(8,128)S(1)}, f32[16,1536]{1,0:T(8,128)S(1)}, u32[]{:S(2)}, u32[]{:S(2)}) collective-permute-start(f32[16,1536]{1,0:T(8,128)S(1)} %broadcast_select_fusion.5), channel_id=1, source_target_pairs={{0,80},{1,81},{2,82},{3,83},{4,84},{5,85},{6,86},{7,87},{8,88},{9,... | collective-permute-start | bytes 294920 | tf_op jit(solution)/shard_map/ppermute | solution.py:23
  187.1 10.4 %collective-permute-start.44 = (f32[16,1536]{1,0:T(8,128)S(1)}, f32[16,1536]{1,0:T(8,128)S(1)}, u32[]{:S(2)}, u32[]{:S(2)}) collective-permute-start(f32[16,1536]{1,0:T(8,128)S(1)} %broadcast_select_fusion.4), channel_id=1, source_target_pairs={{0,64},{1,65},{2,66},{3,67},{4,68},{5,69},{6,70},{7,71},{8,72},{9,... | collective-permute-start | bytes 294920 | tf_op jit(solution)/shard_map/ppermute | solution.py:23
  190.1 9.1 %collective-permute-start.46 = (f32[16,1536]{1,0:T(8,128)S(1)}, f32[16,1536]{1,0:T(8,128)S(1)}, u32[]{:S(2)}, u32[]{:S(2)}) collective-permute-start(f32[16,1536]{1,0:T(8,128)S(1)} %broadcast_select_fusion.3), channel_id=1, source_target_pairs={{0,48},{1,49},{2,50},{3,51},{4,52},{5,53},{6,54},{7,55},{8,56},{9,... | collective-permute-start | bytes 294920 | tf_op jit(solution)/shard_map/ppermute | solution.py:23
  194.0 7.5 %collective-permute-start.50 = (f32[16,1536]{1,0:T(8,128)S(1)}, f32[16,1536]{1,0:T(8,128)S(1)}, u32[]{:S(2)}, u32[]{:S(2)}) collective-permute-start(f32[16,1536]{1,0:T(8,128)S(1)} %broadcast_select_fusion.1), channel_id=1, source_target_pairs={{0,16},{1,17},{2,18},{3,19},{4,20},{5,21},{6,22},{7,23},{8,24},{9,... | collective-permute-start | bytes 294920 | tf_op jit(solution)/shard_map/ppermute | solution.py:23
  (29 other events, 321.5 us)

commit v2 on v1

v2 whole, which is shorter than its diff:
```python
import jax
import jax.numpy as jnp
import numpy as np
from jax import lax
from jax.sharding import Mesh, PartitionSpec as P

AGE = 48
SEX = 2
INC = 32
HH = 8
TU = 4
ZONE_MOST = 6
MEMBERS = 8
ROOMY = 5
AXES = ("col", "mem")


def _xor(x, n, bit):
    return lax.ppermute(x, AXES, [(i, i ^ bit) for i in range(n)])


def make_body(n):
    cols = n // MEMBERS

    def body(population, area_target, national_target, zone_target, area_zone, zone_order):
        count = population.shape[0]
        rows = zone_target.shape[0]
        zones = zone_order.shape[0]
        width = zone_target.shape[1]
        most = count
        pool_rows = rows * MEMBERS
        assert ZONE_MOST < count and (AGE * SEX * HH * TU) % width == 0 and 2 * cols <= width
        f32 = jnp.float32
        idx = lax.axis_index(AXES)
        col, mem = idx // MEMBERS, idx % MEMBERS

        labels = jnp.arange(zones, dtype=jnp.int32)
        slot_of = jnp.zeros((zones,), jnp.int32).at[zone_order].set(labels)
        zlo = area_zone[0]
        zhi = area_zone[count - 1]
        ks = jnp.arange(most, dtype=jnp.int32)
        lanes = jnp.arange(width, dtype=jnp.int32)

        view = population.reshape(count, AGE * SEX, INC, HH * TU)
        t1 = jnp.sum(view, axis=2)
        area_sum = jnp.sum(t1, axis=2)
        s1 = area_target / area_sum
        part = jnp.sum(t1 * s1[:, :, None], axis=0)
        nat_rows = (AGE * SEX * HH * TU) // width

        zrow = jnp.where(lanes == 2 * col, zlo.astype(f32), 0.0) + jnp.where(lanes == 2 * col + 1, zhi.astype(f32), 0.0)
        msg = jnp.concatenate([part.reshape(nat_rows, width), zrow[None]], axis=0)
        bit = MEMBERS
        while bit < n:
            msg = msg + _xor(msg, n, bit)
            bit *= 2
        nat = msg[:nat_rows]
        zinfo = msg[nat_rows, : 2 * cols].reshape(cols, 2).astype(jnp.int32)

        c_kz = zinfo[:, 0:1] + ks[None, :]
        c_valid = c_kz <= zinfo[:, 1:2]
        c_slot = slot_of[jnp.minimum(c_kz, zones - 1)]
        c_grp = c_slot // pool_rows
        earlier = (c_grp[:, :, None] == c_grp[:, None, :]) & c_valid[:, None, :] & (ks[None, None, :] < ks[None, :, None])
        c_rank = jnp.sum(earlier.astype(jnp.int32), axis=2)
        over = jnp.any(c_valid & (c_rank >= ROOMY)).astype(f32)

        pool = zone_target
        flag = jnp.where(lanes == 0, over, 0.0)[None]
        bit = 1
        while bit < MEMBERS:
            msg = jnp.concatenate([nat, flag, pool], axis=0)
            got = _xor(msg, n, bit)
            nat = nat + got[:nat_rows]
            flag = flag + got[nat_rows:nat_rows + 1]
            theirs = got[nat_rows + 1:]
            pool = jnp.where((mem & bit) == 0, jnp.concatenate([pool, theirs], 0), jnp.concatenate([theirs, pool], 0))
            bit *= 2
        s2 = national_target / nat.reshape(AGE * SEX, HH * TU)

        m_kz = zlo + ks
        m_valid = m_kz <= zhi
        m_slot = slot_of[jnp.minimum(m_kz, zones - 1)]
        m_grp = m_slot // pool_rows
        m_rank = jnp.sum(((m_grp[:, None] == m_grp[None, :]) & m_valid[None, :] & (ks[None, :] < ks[:, None])).astype(jnp.int32), axis=1)
        mine = c_valid & (c_grp == col)
        dest = jnp.broadcast_to(jnp.arange(cols, dtype=jnp.int32)[:, None], (cols, most))

        def route(room):
            keep = mine & (c_rank < room)
            at = jnp.zeros((cols, room), jnp.int32).at[jnp.where(keep, dest, cols), c_rank].set(c_slot % pool_rows, mode="drop")
            sent = jnp.take(pool, at.reshape(-1), axis=0).reshape(cols, room, width)
            came = lax.all_to_all(sent, "col", 0, 0, tiled=True)
            return came[m_grp, jnp.minimum(m_rank, room - 1)]

        target = lax.cond(flag[0, 0] > 0, lambda: route(most), lambda: route(ROOMY))

        w = s1[:, :, None] * s2[None, :, :]
        am = jnp.sum(view * w[:, :, None, :], axis=3)
        am = jnp.sum(am.reshape(count, AGE, SEX, INC), axis=2).reshape(count, AGE * INC)
        k_a = area_zone - zlo
        onehot = (k_a[:, None] == ks[None, :]).astype(f32)
        zp = jnp.sum(onehot[:, :, None] * am[:, None, :], axis=0)
        nk = zhi - zlo
        right = [(i, i + 1) for i in range(n - 1)]
        left = [(i, i - 1) for i in range(1, n)]
        to_right = jnp.stack([zp[nk], jnp.where(lanes == 0, zhi.astype(f32), -1.0)])
        to_left = jnp.stack([zp[0], jnp.where(lanes == 0, zlo.astype(f32), -1.0)])
        from_left = lax.ppermute(to_right, AXES, right)
        from_right = lax.ppermute(to_left, AXES, left)
        zp = zp.at[0].add(jnp.where((from_left[1, 0] == zlo.astype(f32)) & (idx > 0), from_left[0], 0.0))
        zp = zp.at[nk].add(jnp.where((from_right[1, 0] == zhi.astype(f32)) & (idx < n - 1), from_right[0], 0.0))
        ratio = target / zp
        ratio_a = jnp.take(ratio, k_a, axis=0)

        fac = w.reshape(count, AGE, SEX, 1, HH * TU) * ratio_a.reshape(count, AGE, 1, INC, 1)
        out = population.reshape(count, AGE, SEX, INC, HH * TU) * fac
        return out.reshape(count, AGE * SEX, INC * HH * TU)

    return body


def solution(mesh):
    n = mesh.shape["area"]
    grid = Mesh(np.asarray(mesh.devices).reshape(n // MEMBERS, MEMBERS), AXES)
    placed = (P(AXES, None, None), P(AXES, None), P(), P(AXES, None), P(AXES), P())
    return jax.shard_map(
        make_body(n), mesh=grid, in_specs=placed, out_specs=P(AXES, None, None), check_vma=False
    )
```

time: 246 us -> 160 us (0.65)
  starting transfers between devices: 80.3 us -> 22 us
  waiting for transfers between devices: 74.5 us -> 33.4 us
  local copies, waits for them, and re-layouts: 43 us -> 54.8 us
    ppermute x55 -> x9, starting transfers between devices: 80.3 us -> 17.2 us  [the longest x7 13.4 us: _xor(): return lax.ppermute(x, AXES, [(i, i ^ bit) for i in range(n)])]
    ppermute x55 -> x9, waiting for transfers between devices: 74.5 us -> 20.3 us  [the longest x7 14 us: _xor(): return lax.ppermute(x, AXES, [(i, i ^ bit) for i in range(n)])]
    all_to_all x0 -> x1, waiting for transfers between devices: none -> 13.1 us  [route(): came = lax.all_to_all(sent, 'col', 0, 0, tiled=True)]
    scatter x1 -> x2, local copies, waits for them, and re-layouts: 1.27 us -> 11.4 us  [route(): jnp.zeros((cols, room), jnp.int32).at[jnp.where(keep, dest, cols), c_rank]]
    all_to_all x0 -> x1, starting transfers between devices: none -> 4.8 us  [route(): came = lax.all_to_all(sent, 'col', 0, 0, tiled=True)]
    gather x10 -> x6, local copies, waits for them, and re-layouts: 6.05 us -> 3.6 us  [the longest x2 1.44 us: body(): c_slot = slot_of[jnp.minimum(c_kz, zones - 1)]]
    unnamed x34 -> x14, local copies, waits for them, and re-layouts: 8.57 us -> 8.49 us
  transfers between devices with their start and end apart: 55 -> 10, of which waited for: 24 -> 8; matrix products, arithmetic and copies ran while one was open for 9% -> 17% of each run, Pallas kernels for 0% -> 0%
where the time goes in v2:
time: 160 us; the launch traced here: 157 us
  local copies, waits for them, and re-layouts  54.8 us (34%)
  other arithmetic  40.5 us (25%)
  waiting for transfers between devices  33.4 us (21%)
  starting transfers between devices  22 us (14%)
  between operations  6.32 us (4%)
    mul x1, local copies, waits for them, and re-layouts, body(): w.reshape(count, AGE, SEX, 1, HH * TU)  19.9 us
    ppermute x7, waiting for transfers between devices, _xor(): return lax.ppermute(x, AXES, [(i, i ^ bit) for i in range(n)])  14 us
    ppermute x7, starting transfers between devices, _xor(): return lax.ppermute(x, AXES, [(i, i ^ bit) for i in range(n)])  13.4 us
    all_to_all x1, waiting for transfers between devices, route(): came = lax.all_to_all(sent, 'col', 0, 0, tiled=True)  13.1 us
    scatter x2, local copies, waits for them, and re-layouts, route(): jnp.zeros((cols, room), jnp.int32).at[jnp.where(keep, dest, cols), c_rank]  11.4 us
    mul x1, other arithmetic, body(): w.reshape(count, AGE, SEX, 1, HH * TU)  9.64 us
    mul x1, other arithmetic, body(): out = population.reshape(count, AGE, SEX, INC, HH * TU) * fac  9.49 us
    unnamed x14, local copies, waits for them, and re-layouts  8.49 us
  transfers between devices with their start and end apart: 10, of which 8 were waited for; matrix products, arithmetic and copies ran while one was open for 17% of the time, Pallas kernels for 0%

profile of v2, /device:TPU:6, one launch (start us, length us, event | category | flops | bytes accessed | tf_op | source)
XLA Modules:
  0.0 157.3 jit_solution(2729899943669500739)
XLA Ops:
  0.0 1.3 fusion.37
  2.5 8.4 %copy.54 = f32[16,96,1024]{1,2,0:T(8,128)} copy(f32[16,96,1024]{2,1,0:T(8,128)} %param.12) | data formatting | bytes 12582912 | tf_op args[0]
  10.9 3.1 %reduce_sum.72 = f32[16,96]{1,0:T(8,128)S(1)} reduce(f32[16,96,1024]{2,1,0:T(8,128)} %param.12, f32[]{:T(128)} %constant.198.clone.1), dimensions={2}, to_apply=%region_0.1 | reduce | flops 1571328 | bytes 6297604 | tf_op jit(solution)/shard_map/reduce_sum | solution.py:46
  14.1 4.5 %reduce_sum.73 = f32[16,96,32]{1,2,0:T(8,128)S(1)} reduce(f32[16,96,32,32]{1,3,2,0:T(8,128)} %bitcast.44, f32[]{:T(128)} %constant.198.clone.1), dimensions={2}, to_apply=%region_1.2 | reduce | flops 1523712 | bytes 6488068 | tf_op jit(solution)/shard_map/reduce_sum | solution.py:45
  18.9 2.0 %collective-permute-start = (f32[3,1536]{1,0:T(4,128)S(1)}, f32[3,1536]{1,0:T(4,128)S(1)}, u32[]{:S(2)}, u32[]{:S(2)}) collective-permute-start(f32[3,1536]{1,0:T(4,128)S(1)} %pad_maximum_fusion.3), channel_id=1, source_target_pairs={{0,8},{1,9},{2,10},{3,11},{4,12},{5,13},{6,14},{7,15},{8,0},{9,1},... | collective-permute-start | bytes 55304 | tf_op jit(solution)/shard_map/ppermute | solution.py:19
  22.8 4.0 %collective-permute-start.1 = (f32[3,1536]{1,0:T(4,128)S(1)}, f32[3,1536]{1,0:T(4,128)S(1)}, u32[]{:S(2)}, u32[]{:S(2)}) collective-permute-start(f32[3,1536]{1,0:T(4,128)S(1)} %fusion.35), channel_id=1, source_target_pairs={{0,16},{1,17},{2,18},{3,19},{4,20},{5,21},{6,22},{7,23},{8,24},{9,... | collective-permute-start | bytes 55304 | tf_op jit(solution)/shard_map/ppermute | solution.py:19
  26.8 4.3 %scatter_custom_fusion.2 = s32[1024]{0:T(1024)S(1)} fusion(s32[1024]{0:T(1024)S(1)} %compare_select_fusion.15, s32[1024]{0:T(1024)S(1)} %iota.62, s32[]{:T(128)} %constant.204.clone.1), kind=kCustom, calls=%fused_computation.121 | custom fusion | bytes 4100 | tf_op jit(solution)/shard_map/scatter | solution.py:38
  31.7 0.9 collective-permute-start.2
  33.9 1.8 %collective-permute-done.2 = f32[3,1536]{1,0:T(4,128)S(1)} collective-permute-done((f32[3,1536]{1,0:T(4,128)S(1)}, f32[3,1536]{1,0:T(4,128)S(1)}, u32[]{:S(2)}, u32[]{:S(2)}) %collective-permute-start.2) | collective-permute-done | bytes 18464 | tf_op jit(solution)/shard_map/ppermute | solution.py:19
  35.7 1.5 collective-permute-start.3
  37.9 3.2 %collective-permute-done.3 = f32[3,1536]{1,0:T(4,128)S(1)} collective-permute-done((f32[3,1536]{1,0:T(4,128)S(1)}, f32[3,1536]{1,0:T(4,128)S(1)}, u32[]{:S(2)}, u32[]{:S(2)}) %collective-permute-start.3) | collective-permute-done | bytes 18464 | tf_op jit(solution)/shard_map/ppermute | solution.py:19
  41.6 1.4 gather_fusion.4
  45.1 1.3 collective-permute-done.4
  46.4 1.7 %collective-permute-start.5 = (f32[19,1536]{1,0:T(8,128)S(1)}, f32[19,1536]{1,0:T(8,128)S(1)}, u32[]{:S(2)}, u32[]{:S(2)}) collective-permute-start(f32[19,1536]{1,0:T(8,128)S(1)} %pad_maximum_fusion.1), channel_id=1, source_target_pairs={{0,2},{1,3},{2,0},{3,1},{4,6},{5,7},{6,4},{7,5},{8,10},{9,11},{10,... | collective-permute-start | bytes 350216 | tf_op jit(solution)/shard_map/ppermute | solution.py:19
  48.1 1.2 add_compare_fusion.1
  50.1 2.3 %collective-permute-done.5 = f32[19,1536]{1,0:T(8,128)S(1)} collective-permute-done((f32[19,1536]{1,0:T(8,128)S(1)}, f32[19,1536]{1,0:T(8,128)S(1)}, u32[]{:S(2)}, u32[]{:S(2)}) %collective-permute-start.5) | collective-permute-done | bytes 116768 | tf_op jit(solution)/shard_map/ppermute | solution.py:19
  52.6 3.3 %collective-permute-start.6 = (f32[35,1536]{1,0:T(8,128)S(1)}, f32[35,1536]{1,0:T(8,128)S(1)}, u32[]{:S(2)}, u32[]{:S(2)}) collective-permute-start(f32[35,1536]{1,0:T(8,128)S(1)} %pad_maximum_fusion), channel_id=1, source_target_pairs={{0,4},{1,5},{2,6},{3,7},{4,0},{5,1},{6,2},{7,3},{8,12},{9,13},{10,... | collective-permute-start | bytes 645128 | tf_op jit(solution)/shard_map/ppermute | solution.py:19
  56.3 4.9 %collective-permute-done.6 = f32[35,1536]{1,0:T(8,128)S(1)} collective-permute-done((f32[35,1536]{1,0:T(8,128)S(1)}, f32[35,1536]{1,0:T(8,128)S(1)}, u32[]{:S(2)}, u32[]{:S(2)}) %collective-permute-start.6) | collective-permute-done | bytes 215072 | tf_op jit(solution)/shard_map/ppermute | solution.py:19
  61.5 5.4 %multiply_reduce_fusion = f32[16,96,32]{1,2,0:T(8,128)S(1)} fusion(f32[16,96,32]{1,2,0:T(8,128)S(1)} %broadcast_multiply_fusion.2, f32[16,96,1024]{1,2,0:T(8,128)} %copy.54), kind=kLoop, calls=%fused_computation.66 | loop fusion | flops 3096576 | bytes 6684672 | tf_op jit(solution)/shard_map/reduce_sum | solution.py:99
  68.0 1.9 %collective-permute-start.7 = (f32[2,1536]{1,0:T(2,128)S(1)}, f32[2,1536]{1,0:T(2,128)S(1)}, u32[]{:S(2)}, u32[]{:S(2)}) collective-permute-start(f32[2,1536]{1,0:T(2,128)S(1)} %pad_maximum_fusion.4), channel_id=1, source_target_pairs={{0,1},{1,2},{2,3},{3,4},{4,5},{5,6},{6,7},{7,8},{8,9},{9,10},{10,1... | collective-permute-start | bytes 36872 | tf_op jit(solution)/shard_map/ppermute | solution.py:109
  69.9 1.0 broadcast_multiply_fusion.1
  70.9 6.3 %collective-permute-done.7 = f32[2,1536]{1,0:T(2,128)S(1)} collective-permute-done((f32[2,1536]{1,0:T(2,128)S(1)}, f32[2,1536]{1,0:T(2,128)S(1)}, u32[]{:S(2)}, u32[]{:S(2)}) %collective-permute-start.7) | collective-permute-done | bytes 12320 | tf_op jit(solution)/shard_map/ppermute | solution.py:109
  78.5 1.9 %collective-permute-start.8 = (f32[2,1536]{1,0:T(2,128)S(1)}, f32[2,1536]{1,0:T(2,128)S(1)}, u32[]{:S(2)}, u32[]{:S(2)}) collective-permute-start(f32[2,1536]{1,0:T(2,128)S(1)} %pad_maximum_fusion.5), channel_id=1, source_target_pairs={{1,0},{2,1},{3,2},{4,3},{5,4},{6,5},{7,6},{8,7},{9,8},{10,9},{11,1... | collective-permute-start | bytes 36872 | tf_op jit(solution)/shard_map/ppermute | solution.py:110
  82.5 32.8 %conditional.1 = (f32[16,1536]{1,0:T(8,128)S(1)}) conditional(s32[]{:T(128)} %bitcast.12, (s32[16,16]{1,0:T(8,128)S(1)}, pred[16,16]{1,0:T(8,128)(4,1)S(1)}, s32[16,16]{1,0:T(8,128)S(1)}, s32[16,16]{1,0:T(8,128)S(1)}, f32[64,1536]{1,0:T(8,128)S(1)}, /*index=5*/s32[16]{0:T(128)S(1)}, s32[16]{0:T(128)S(1)}) %tuple.19, (s32[16,16]{1,0:T(8,128)S(1)}, ...), branch_computations={%region_7.9_spmd, %region_9.11_spmd} | conditional | flops 404160 | bytes 11234412 | solution.py:96
  82.7 11.3 %scatter_fusion = s32[16,5]{0,1:T(8,128)S(1)} fusion(s32[16,5]{0,1:T(8,128)S(1)} %broadcast.512, s32[256]{0:T(256)S(1)} %reshape.485, s32[256]{0:T(256)S(1)} %reshape.487), kind=kCustom, calls=%fused_computation.7 | custom fusion | bytes 5120 | tf_op jit(solution)/shard_map/cond/branch_0_fun/scatter | solution.py:91
  94.3 0.8 gather_fusion
  95.2 1.0 broadcast_select_fusion
  96.2 4.8 %all-to-all-start = ((f32[16,5,1536]{2,1,0:T(8,128)}), f32[16,5,1536]{2,1,0:T(8,128)S(1)}, u32[]{:S(2)}, u32[]{:S(2)}) async-start(f32[16,5,1536]{2,1,0:T(8,128)} %broadcast_select_fusion), calls=%async_computation | async-start | bytes 1572864 | tf_op jit(solution)/shard_map/cond/branch_0_fun/all_to_all | solution.py:93
  101.0 13.1 %all-to-all-done = f32[16,5,1536]{2,1,0:T(8,128)S(1)} async-done(((f32[16,5,1536]{2,1,0:T(8,128)}), f32[16,5,1536]{2,1,0:T(8,128)S(1)}, u32[]{:S(2)}, u32[]{:S(2)}) %all-to-all-start) | async-done | bytes 491552 | tf_op jit(solution)/shard_map/cond/branch_0_fun/all_to_all | solution.py:93
  118.3 9.6 %broadcast_multiply_fusion = f32[16,48,2,32,32]{4,3,2,1,0:T(8,128)} fusion(f32[16,48,32]{2,1,0:T(8,128)S(1)} %broadcast_select_fusion.2, f32[16,48,2,32]{3,2,1,0:T(2,128)S(1)} %broadcast_multiply_fusion.1), kind=kLoop, calls=%fused_computation.65 | loop fusion | flops 1572864 | bytes 6586368 | tf_op jit(solution)/shard_map/mul | solution.py:116
  127.9 19.9 %mul.108 = f32[16,96,1024]{2,1,0:T(8,128)} reshape(f32[16,48,2,32,32]{4,3,2,1,0:T(8,128)} %broadcast_multiply_fusion) | data formatting | bytes 12582912 | tf_op jit(solution)/shard_map/mul | solution.py:116
  147.8 9.5 %mul.109 = f32[16,96,1024]{2,1,0:T(8,128)} multiply(f32[16,96,1024]{2,1,0:T(8,128)} %param.12, f32[16,96,1024]{2,1,0:T(8,128)} %mul.108) | non-fusion elementwise | flops 1572864 | bytes 18874368 | tf_op jit(solution)/shard_map/mul | solution.py:117
  (109 shorter events, 13.2 us)
Async XLA Ops:
  14.1 4.5 %copy-start.2 = (f32[16,96]{1,0:T(8,128)S(1)}, f32[16,96]{1,0:T(8,128)}, u32[]{:S(2)}) copy-start(f32[16,96]{1,0:T(8,128)} %param.13) | copy-start | bytes 18436
  14.1 6.8 %copy-start.3 = (s32[16]{0:T(128)S(1)}, s32[16]{0:T(128)}, u32[]{:S(2)}) copy-start(s32[16]{0:T(128)} %param.16) | copy-start | bytes 196
  14.1 7.5 %copy-start.4 = (s32[1024]{0:T(1024)S(1)}, s32[1024]{0:T(1024)}, u32[]{:S(2)}) copy-start(s32[1024]{0:T(1024)} %param.17) | copy-start | bytes 12292
  14.1 23.1 %copy-start.5 = (s32[2]{0:T(128)S(1)}, s32[2]{0:T(128)}, u32[]{:S(2)}) copy-start(s32[2]{0:T(128)} %constant.221.clone.1) | copy-start | bytes 28
  18.9 3.9 %collective-permute-start = (f32[3,1536]{1,0:T(4,128)S(1)}, f32[3,1536]{1,0:T(4,128)S(1)}, u32[]{:S(2)}, u32[]{:S(2)}) collective-permute-start(f32[3,1536]{1,0:T(4,128)S(1)} %pad_maximum_fusion.3), channel_id=1, source_target_pairs={{0,8},{1,9},{2,10},{3,11},{4,12},{5,13},{6,14},{7,15},{8,0},{9,1},... | collective-permute-start | bytes 55304 | tf_op jit(solution)/shard_map/ppermute | solution.py:19
  22.8 8.9 %collective-permute-start.1 = (f32[3,1536]{1,0:T(4,128)S(1)}, f32[3,1536]{1,0:T(4,128)S(1)}, u32[]{:S(2)}, u32[]{:S(2)}) collective-permute-start(f32[3,1536]{1,0:T(4,128)S(1)} %fusion.35), channel_id=1, source_target_pairs={{0,16},{1,17},{2,18},{3,19},{4,20},{5,21},{6,22},{7,23},{8,24},{9,... | collective-permute-start | bytes 55304 | tf_op jit(solution)/shard_map/ppermute | solution.py:19
  31.7 3.9 %collective-permute-start.2 = (f32[3,1536]{1,0:T(4,128)S(1)}, f32[3,1536]{1,0:T(4,128)S(1)}, u32[]{:S(2)}, u32[]{:S(2)}) collective-permute-start(f32[3,1536]{1,0:T(4,128)S(1)} %add.251), channel_id=1, source_target_pairs={{0,32},{1,33},{2,34},{3,35},{4,36},{5,37},{6,38},{7,39},{8,40},{9,... | collective-permute-start | bytes 55304 | tf_op jit(solution)/shard_map/ppermute | solution.py:19
  35.7 5.4 %collective-permute-start.3 = (f32[3,1536]{1,0:T(4,128)S(1)}, f32[3,1536]{1,0:T(4,128)S(1)}, u32[]{:S(2)}, u32[]{:S(2)}) collective-permute-start(f32[3,1536]{1,0:T(4,128)S(1)} %add.252), channel_id=1, source_target_pairs={{0,64},{1,65},{2,66},{3,67},{4,68},{5,69},{6,70},{7,71},{8,72},{9,... | collective-permute-start | bytes 55304 | tf_op jit(solution)/shard_map/ppermute | solution.py:19
  41.6 3.4 %copy-start = (f32[8,1536]{1,0:T(8,128)S(1)}, f32[8,1536]{1,0:T(8,128)}, u32[]{:S(2)}) copy-start(f32[8,1536]{1,0:T(8,128)} %param.15) | copy-start | bytes 147460
  41.6 7.9 %copy-start.1 = (f32[96,32]{0,1:T(8,128)S(1)}, f32[96,32]{0,1:T(8,128)}, u32[]{:S(2)}) copy-start(f32[96,32]{0,1:T(8,128)} %param.14) | copy-start | bytes 36868
  45.0 1.4 collective-permute-start.4
  46.4 6.0 %collective-permute-start.5 = (f32[19,1536]{1,0:T(8,128)S(1)}, f32[19,1536]{1,0:T(8,128)S(1)}, u32[]{:S(2)}, u32[]{:S(2)}) collective-permute-start(f32[19,1536]{1,0:T(8,128)S(1)} %pad_maximum_fusion.1), channel_id=1, source_target_pairs={{0,2},{1,3},{2,0},{3,1},{4,6},{5,7},{6,4},{7,5},{8,10},{9,11},{10,... | collective-permute-start | bytes 350216 | tf_op jit(solution)/shard_map/ppermute | solution.py:19
  52.6 8.7 %collective-permute-start.6 = (f32[35,1536]{1,0:T(8,128)S(1)}, f32[35,1536]{1,0:T(8,128)S(1)}, u32[]{:S(2)}, u32[]{:S(2)}) collective-permute-start(f32[35,1536]{1,0:T(8,128)S(1)} %pad_maximum_fusion), channel_id=1, source_target_pairs={{0,4},{1,5},{2,6},{3,7},{4,0},{5,1},{6,2},{7,3},{8,12},{9,13},{10,... | collective-permute-start | bytes 645128 | tf_op jit(solution)/shard_map/ppermute | solution.py:19
  68.0 9.2 %collective-permute-start.7 = (f32[2,1536]{1,0:T(2,128)S(1)}, f32[2,1536]{1,0:T(2,128)S(1)}, u32[]{:S(2)}, u32[]{:S(2)}) collective-permute-start(f32[2,1536]{1,0:T(2,128)S(1)} %pad_maximum_fusion.4), channel_id=1, source_target_pairs={{0,1},{1,2},{2,3},{3,4},{4,5},{5,6},{6,7},{7,8},{8,9},{9,10},{10,1... | collective-permute-start | bytes 36872 | tf_op jit(solution)/shard_map/ppermute | solution.py:109
  78.5 36.9 %collective-permute-start.8 = (f32[2,1536]{1,0:T(2,128)S(1)}, f32[2,1536]{1,0:T(2,128)S(1)}, u32[]{:S(2)}, u32[]{:S(2)}) collective-permute-start(f32[2,1536]{1,0:T(2,128)S(1)} %pad_maximum_fusion.5), channel_id=1, source_target_pairs={{1,0},{2,1},{3,2},{4,3},{5,4},{6,5},{7,6},{8,7},{9,8},{10,9},{11,1... | collective-permute-start | bytes 36872 | tf_op jit(solution)/shard_map/ppermute | solution.py:110
  96.2 17.9 %all-to-all-start = ((f32[16,5,1536]{2,1,0:T(8,128)}), f32[16,5,1536]{2,1,0:T(8,128)S(1)}, u32[]{:S(2)}, u32[]{:S(2)}) async-start(f32[16,5,1536]{2,1,0:T(8,128)} %broadcast_select_fusion), calls=%async_computation | async-start | bytes 1572864 | tf_op jit(solution)/shard_map/cond/branch_0_fun/all_to_all | solution.py:93

commit v3 on v2

--- a/solution.py
+++ b/solution.py
@@ -2,6 +2,7 @@
 import jax.numpy as jnp
 import numpy as np
 from jax import lax
+from jax.experimental import pallas as pl
 from jax.sharding import Mesh, PartitionSpec as P
 
 AGE = 48
@@ -13,6 +14,44 @@
 MEMBERS = 8
 ROOMY = 5
 AXES = ("col", "mem")
+
+
+HI = lax.Precision.HIGHEST
+BLOCK = 2
+LANES = (((1,), (1,)), ((), ()))
+
+
+def _sum_kernel(pop_ref, e1_ref, o_ref):
+    for b in range(pop_ref.shape[0]):
+        o_ref[b] = lax.dot_general(pop_ref[b], e1_ref[...], LANES, precision=HI, preferred_element_type=jnp.float32)
+
+
+def _margin_kernel(pop_ref, w_ref, e1_ref, e2_ref, o_ref):
+    for b in range(pop_ref.shape[0]):
+        wide = jnp.dot(w_ref[b], e1_ref[...], precision=HI, preferred_element_type=jnp.float32)
+        o_ref[b] = lax.dot_general(pop_ref[b] * wide, e2_ref[...], LANES, precision=HI, preferred_element_type=jnp.float32)
+
+
+def _fit_kernel(pop_ref, w_ref, r_ref, e1_ref, e2_ref, o_ref):
+    for b in range(pop_ref.shape[0]):
+        wide = jnp.dot(w_ref[b], e1_ref[...], precision=HI, preferred_element_type=jnp.float32)
+        rep = jnp.dot(r_ref[b], e2_ref[...], precision=HI, preferred_element_type=jnp.float32)
+        o_ref[b] = pop_ref[b] * wide * rep
+
+
+def _table_call(kernel, table, smalls, consts, out_last):
+    count, rows, width = table.shape
+    grid = (count // BLOCK,)
+    specs = [pl.BlockSpec((BLOCK, rows, width), lambda i: (i, 0, 0))]
+    specs += [pl.BlockSpec((BLOCK,) + x.shape[1:], lambda i: (i, 0, 0)) for x in smalls]
+    specs += [pl.BlockSpec(c.shape, lambda i: (0, 0)) for c in consts]
+    return pl.pallas_call(
+        kernel,
+        grid=grid,
+        in_specs=specs,
+        out_specs=pl.BlockSpec((BLOCK, rows, out_last), lambda i: (i, 0, 0)),
+        out_shape=jax.ShapeDtypeStruct((count, rows, out_last), jnp.float32),
+    )(table, *smalls, *consts)
 
 
 def _xor(x, n, bit):
@@ -41,8 +80,10 @@
         ks = jnp.arange(most, dtype=jnp.int32)
         lanes = jnp.arange(width, dtype=jnp.int32)
 
-        view = population.reshape(count, AGE * SEX, INC, HH * TU)
-        t1 = jnp.sum(view, axis=2)
+        lane = jnp.arange(INC * HH * TU, dtype=jnp.int32)
+        e1 = (lane[None, :] % (HH * TU) == jnp.arange(HH * TU, dtype=jnp.int32)[:, None]).astype(f32)
+        e2 = (lane[None, :] // (HH * TU) == jnp.arange(INC, dtype=jnp.int32)[:, None]).astype(f32)
+        t1 = _table_call(_sum_kernel, population, [], [e1], HH * TU)
         area_sum = jnp.sum(t1, axis=2)
         s1 = area_target / area_sum
         part = jnp.sum(t1 * s1[:, :, None], axis=0)
@@ -84,11 +125,11 @@
         m_grp = m_slot // pool_rows
         m_rank = jnp.sum(((m_grp[:, None] == m_grp[None, :]) & m_valid[None, :] & (ks[None, :] < ks[:, None])).astype(jnp.int32), axis=1)
         mine = c_valid & (c_grp == col)
-        dest = jnp.broadcast_to(jnp.arange(cols, dtype=jnp.int32)[:, None], (cols, most))
 
         def route(room):
             keep = mine & (c_rank < room)
-            at = jnp.zeros((cols, room), jnp.int32).at[jnp.where(keep, dest, cols), c_rank].set(c_slot % pool_rows, mode="drop")
+            hit = keep[:, :, None] & (c_rank[:, :, None] == jnp.arange(room, dtype=jnp.int32)[None, None, :])
+            at = jnp.sum(jnp.where(hit, (c_slot % pool_rows)[:, :, None], 0), axis=1)
             sent = jnp.take(pool, at.reshape(-1), axis=0).reshape(cols, room, width)
             came = lax.all_to_all(sent, "col", 0, 0, tiled=True)
             return came[m_grp, jnp.minimum(m_rank, room - 1)]
@@ -96,7 +137,7 @@
         target = lax.cond(flag[0, 0] > 0, lambda: route(most), lambda: route(ROOMY))
 
         w = s1[:, :, None] * s2[None, :, :]
-        am = jnp.sum(view * w[:, :, None, :], axis=3)
+        am = _table_call(_margin_kernel, population, [w], [e1, e2], INC)
         am = jnp.sum(am.reshape(count, AGE, SEX, INC), axis=2).reshape(count, AGE * INC)
         k_a = area_zone - zlo
         onehot = (k_a[:, None] == ks[None, :]).astype(f32)
@@ -113,9 +154,8 @@
         ratio = target / zp
         ratio_a = jnp.take(ratio, k_a, axis=0)
 
-        fac = w.reshape(count, AGE, SEX, 1, HH * TU) * ratio_a.reshape(count, AGE, 1, INC, 1)
-        out = population.reshape(count, AGE, SEX, INC, HH * TU) * fac
-        return out.reshape(count, AGE * SEX, INC * HH * TU)
+        r96 = jnp.repeat(ratio_a.reshape(count, AGE, INC), SEX, axis=1)
+        return _table_call(_fit_kernel, population, [w, r96], [e1, e2], INC * HH * TU)
 
     return body
 

time: 160 us -> 133 us (0.83)
  the two profiles are of different devices: /device:TPU:6 before, /device:TPU:0 now
where the time goes in v3:
time: 133 us; the launch traced here: 132 us
  Pallas kernels  37.5 us (28%)
  starting transfers between devices  31 us (23%)
  waiting for transfers between devices  27.2 us (20%)
  local copies, waits for them, and re-layouts  15.2 us (11%)
  other arithmetic  14.8 us (11%)
  between operations  6.26 us (5%)
    pallas_call x3, Pallas kernels, _table_call(): pl.pallas_call(kernel, grid=grid, in_specs=specs, out_specs=pl.BlockSpec(...  37.5 us
    ppermute x7, starting transfers between devices, _xor(): return lax.ppermute(x, AXES, [(i, i ^ bit) for i in range(n)])  15.6 us
    all_to_all x1, waiting for transfers between devices, route(): came = lax.all_to_all(sent, 'col', 0, 0, tiled=True)  15.3 us
    all_to_all x1, starting transfers between devices, route(): came = lax.all_to_all(sent, 'col', 0, 0, tiled=True)  12.9 us
    ppermute x7, waiting for transfers between devices, _xor(): return lax.ppermute(x, AXES, [(i, i ^ bit) for i in range(n)])  11.7 us
    scatter x1, local copies, waits for them, and re-layouts, body(): slot_of = jnp.zeros((zones,), jnp.int32).at[zone_order].set(labels)  4.31 us
  transfers between devices with their start and end apart: 10, of which 8 were waited for; matrix products, arithmetic and copies ran while one was open for 10% of the time, Pallas kernels for 0%

profile of v3, /device:TPU:0, one launch (start us, length us, event | category | flops | bytes accessed | tf_op | source)
XLA Modules:
  0.0 132.0 jit_solution(3616862480062336458)
XLA Ops:
  0.0 1.4 %fusion.36 = (s32[1]{0:T(128)}, s32[1]{0:T(128)}) fusion(s32[16]{0:T(128)} %param.16), kind=kLoop, calls=%fused_computation.132 | loop fusion | bytes 16 | tf_op jit(solution)/shard_map/slice | solution.py:78
  3.3 9.3 %shard_map.64 = f32[16,96,32]{2,1,0:T(8,128)} custom-call(f32[16,96,1024]{2,1,0:T(8,128)} %pop_ref.5, f32[32,1024]{1,0:T(8,128)} %fusion.15.e1_ref), custom_call_target="tpu_custom_call" | custom-call | tf_op jit(solution)/shard_map/pallas_call | solution.py:48
  12.6 1.5 %reduce_sum.72 = f32[16,96]{1,0:T(8,128)S(1)} reduce(f32[16,96,32]{2,1,0:T(8,128)} %shard_map.64, f32[]{:T(128)} %constant.222.clone.1), dimensions={2}, to_apply=%region_0.1 | reduce | flops 47616 | bytes 202756 | tf_op jit(solution)/shard_map/reduce_sum | solution.py:87
  14.1 1.4 %multiply_reduce_fusion.1 = f32[96,32]{1,0:T(8,128)S(1)} fusion(f32[16,96,32]{2,1,0:T(8,128)} %shard_map.64, f32[16,96]{1,0:T(8,128)S(1)} %div.51), kind=kLoop, calls=%fused_computation.50 | loop fusion | flops 95232 | bytes 215040 | tf_op jit(solution)/shard_map/reduce_sum | solution.py:89
  15.7 2.1 %collective-permute-start = (f32[3,1536]{1,0:T(4,128)S(1)}, f32[3,1536]{1,0:T(4,128)S(1)}, u32[]{:S(2)}, u32[]{:S(2)}) collective-permute-start(f32[3,1536]{1,0:T(4,128)S(1)} %pad_maximum_fusion.3), channel_id=1, source_target_pairs={{0,8},{1,9},{2,10},{3,11},{4,12},{5,13},{6,14},{7,15},{8,0},{9,1},... | collective-permute-start | bytes 55304 | tf_op jit(solution)/shard_map/ppermute | solution.py:58
  19.6 4.1 %collective-permute-start.1 = (f32[3,1536]{1,0:T(4,128)S(1)}, f32[3,1536]{1,0:T(4,128)S(1)}, u32[]{:S(2)}, u32[]{:S(2)}) collective-permute-start(f32[3,1536]{1,0:T(4,128)S(1)} %fusion.34), channel_id=1, source_target_pairs={{0,16},{1,17},{2,18},{3,19},{4,20},{5,21},{6,22},{7,23},{8,24},{9,... | collective-permute-start | bytes 55304 | tf_op jit(solution)/shard_map/ppermute | solution.py:58
  24.3 1.2 collective-permute-done.1
  25.5 1.6 %collective-permute-start.2 = (f32[3,1536]{1,0:T(4,128)S(1)}, f32[3,1536]{1,0:T(4,128)S(1)}, u32[]{:S(2)}, u32[]{:S(2)}) collective-permute-start(f32[3,1536]{1,0:T(4,128)S(1)} %add.261), channel_id=1, source_target_pairs={{0,32},{1,33},{2,34},{3,35},{4,36},{5,37},{6,38},{7,39},{8,40},{9,... | collective-permute-start | bytes 55304 | tf_op jit(solution)/shard_map/ppermute | solution.py:58
  27.1 4.3 %scatter_custom_fusion = s32[1024]{0:T(1024)S(1)} fusion(s32[1024]{0:T(1024)S(1)} %compare_select_fusion.11, s32[1024]{0:T(1024)S(1)} %iota.93, s32[]{:T(128)} %constant.220.clone.1), kind=kCustom, calls=%fused_computation.116 | custom fusion | bytes 4100 | tf_op jit(solution)/shard_map/scatter | solution.py:77
  32.1 2.8 %collective-permute-start.3 = (f32[3,1536]{1,0:T(4,128)S(1)}, f32[3,1536]{1,0:T(4,128)S(1)}, u32[]{:S(2)}, u32[]{:S(2)}) collective-permute-start(f32[3,1536]{1,0:T(4,128)S(1)} %add.262), channel_id=1, source_target_pairs={{0,64},{1,65},{2,66},{3,67},{4,68},{5,69},{6,70},{7,71},{8,72},{9,... | collective-permute-start | bytes 55304 | tf_op jit(solution)/shard_map/ppermute | solution.py:58
  36.2 1.3 collective-permute-done.3
  38.0 1.4 %gather_fusion.4 = s32[256]{0:T(256)S(1)} fusion(s32[1024]{0:T(1024)S(1)} %scatter_custom_fusion, s32[1024]{0:T(1024)S(1)} %pad_clamp_fusion.4), kind=kCustom, calls=%fused_computation.4 | custom fusion | bytes 3072 | tf_op jit(solution)/shard_map/gather | solution.py:103
  40.0 0.7 and_reduce_fusion
  41.5 0.7 and_reduce_fusion.1
  42.9 1.7 %collective-permute-start.5 = (f32[19,1536]{1,0:T(8,128)S(1)}, f32[19,1536]{1,0:T(8,128)S(1)}, u32[]{:S(2)}, u32[]{:S(2)}) collective-permute-start(f32[19,1536]{1,0:T(8,128)S(1)} %pad_maximum_fusion.1), channel_id=1, source_target_pairs={{0,2},{1,3},{2,0},{3,1},{4,6},{5,7},{6,4},{7,5},{8,10},{9,11},{10,... | collective-permute-start | bytes 350216 | tf_op jit(solution)/shard_map/ppermute | solution.py:58
  44.5 1.3 add_compare_fusion.1
  46.1 2.8 %collective-permute-done.5 = f32[19,1536]{1,0:T(8,128)S(1)} collective-permute-done((f32[19,1536]{1,0:T(8,128)S(1)}, f32[19,1536]{1,0:T(8,128)S(1)}, u32[]{:S(2)}, u32[]{:S(2)}) %collective-permute-start.5) | collective-permute-done | bytes 116768 | tf_op jit(solution)/shard_map/ppermute | solution.py:58
  49.0 3.3 %collective-permute-start.6 = (f32[35,1536]{1,0:T(8,128)S(1)}, f32[35,1536]{1,0:T(8,128)S(1)}, u32[]{:S(2)}, u32[]{:S(2)}) collective-permute-start(f32[35,1536]{1,0:T(8,128)S(1)} %pad_maximum_fusion), channel_id=1, source_target_pairs={{0,4},{1,5},{2,6},{3,7},{4,0},{5,1},{6,2},{7,3},{8,12},{9,13},{10,... | collective-permute-start | bytes 645128 | tf_op jit(solution)/shard_map/ppermute | solution.py:58
  52.3 5.5 %collective-permute-done.6 = f32[35,1536]{1,0:T(8,128)S(1)} collective-permute-done((f32[35,1536]{1,0:T(8,128)S(1)}, f32[35,1536]{1,0:T(8,128)S(1)}, u32[]{:S(2)}, u32[]{:S(2)}) %collective-permute-start.6) | collective-permute-done | bytes 215072 | tf_op jit(solution)/shard_map/ppermute | solution.py:58
  57.8 1.1 broadcast_multiply_fusion.w_ref
  59.0 14.7 %shard_map.65 = f32[16,96,32]{2,1,0:T(8,128)} custom-call(f32[16,96,1024]{2,1,0:T(8,128)} %pop_ref.5, f32[16,96,32]{2,1,0:T(8,128)} %broadcast_multiply_fusion.w_ref, f32[32,1024]{1,0:T(8,128)} %fusion.15.e1_ref, f32[32,1024]{1,0:T(8,128)} %fusion.16.e2_ref), custom_call_target="tpu_custom_call" | custom-call | tf_op jit(solution)/shard_map/pallas_call | solution.py:48
  73.7 2.1 %reduce_sum.76 = f32[16,48,32]{2,1,0:T(8,128)S(1)} reduce(f32[16,48,2,32]{3,2,1,0:T(2,128)} %bitcast.19, f32[]{:T(128)} %constant.222.clone.1), dimensions={2}, to_apply=%region_10.11 | reduce | flops 24576 | bytes 294916 | tf_op jit(solution)/shard_map/reduce_sum | solution.py:141
  76.2 1.3 collective-permute-start.7
  79.5 1.3 collective-permute-start.8
  82.7 31.5 %conditional.1 = (f32[16,1536]{1,0:T(8,128)S(1)}) conditional(s32[]{:T(128)} %bitcast.5, (s32[16,16]{1,0:T(8,128)S(1)}, pred[16,16]{1,0:T(8,128)(4,1)S(1)}, s32[16,16]{1,0:T(8,128)S(1)}, f32[64,1536]{1,0:T(8,128)S(1)}, s32[16]{0:T(128)S(1)}, /*index=5*/s32[16]{0:T(128)S(1)}) %tuple.19, (s32[16,16]{1,0:T(8,128)S(1)}, pred[16,16]{1,0:T(8,128)(4,1)S(1)}, ...), branch_computations={%region_6.8_spmd, %region_8.10_spmd} | conditional | flops 416192 | bytes 11225704 | solution.py:137
  83.2 0.8 gather_fusion
  84.1 1.0 broadcast_select_fusion
  85.1 12.9 %all-to-all-start = ((f32[16,5,1536]{2,1,0:T(8,128)}), f32[16,5,1536]{2,1,0:T(8,128)S(1)}, u32[]{:S(2)}, u32[]{:S(2)}) async-start(f32[16,5,1536]{2,1,0:T(8,128)} %broadcast_select_fusion), calls=%async_computation | async-start | bytes 1572864 | tf_op jit(solution)/shard_map/cond/branch_0_fun/all_to_all | solution.py:134
  98.0 15.3 %all-to-all-done = f32[16,5,1536]{2,1,0:T(8,128)S(1)} async-done(((f32[16,5,1536]{2,1,0:T(8,128)}), f32[16,5,1536]{2,1,0:T(8,128)S(1)}, u32[]{:S(2)}, u32[]{:S(2)}) %all-to-all-start) | async-done | bytes 491552 | tf_op jit(solution)/shard_map/cond/branch_0_fun/all_to_all | solution.py:134
  113.5 0.7 gather_fusion.1
  117.2 1.3 broadcast_in_dim.142
  118.5 13.5 %shard_map.66 = f32[16,96,1024]{2,1,0:T(8,128)} custom-call(f32[16,96,1024]{2,1,0:T(8,128)} %pop_ref.5, f32[16,96,32]{2,1,0:T(8,128)} %broadcast_multiply_fusion.w_ref, f32[16,96,32]{2,1,0:T(8,128)} %bitcast.18, f32[32,1024]{1,0:T(8,128)} %fusion.15.e1_ref, f32[32,1024]{1,0:T(8,128)} %fusion.16.e2_ref), custom_call_target="tpu_custom_call" | custom-call | tf_op jit(solution)/shard_map/pallas_call | solution.py:48
  (100 shorter events, 11.7 us)
Async XLA Ops:
  3.3 10.8 %copy-start.2 = (f32[16,96]{1,0:T(8,128)S(1)}, f32[16,96]{1,0:T(8,128)}, u32[]{:S(2)}) copy-start(f32[16,96]{1,0:T(8,128)} %param.13) | copy-start | bytes 18436
  12.6 5.2 %copy-start.3 = (s32[16]{0:T(128)S(1)}, s32[16]{0:T(128)}, u32[]{:S(2)}) copy-start(s32[16]{0:T(128)} %param.16) | copy-start | bytes 196
  12.6 6.6 %copy-start.4 = (s32[1024]{0:T(1024)S(1)}, s32[1024]{0:T(1024)}, u32[]{:S(2)}) copy-start(s32[1024]{0:T(1024)} %param.17) | copy-start | bytes 12292
  15.7 3.9 %collective-permute-start = (f32[3,1536]{1,0:T(4,128)S(1)}, f32[3,1536]{1,0:T(4,128)S(1)}, u32[]{:S(2)}, u32[]{:S(2)}) collective-permute-start(f32[3,1536]{1,0:T(4,128)S(1)} %pad_maximum_fusion.3), channel_id=1, source_target_pairs={{0,8},{1,9},{2,10},{3,11},{4,12},{5,13},{6,14},{7,15},{8,0},{9,1},... | collective-permute-start | bytes 55304 | tf_op jit(solution)/shard_map/ppermute | solution.py:58
  19.6 5.9 %collective-permute-start.1 = (f32[3,1536]{1,0:T(4,128)S(1)}, f32[3,1536]{1,0:T(4,128)S(1)}, u32[]{:S(2)}, u32[]{:S(2)}) collective-permute-start(f32[3,1536]{1,0:T(4,128)S(1)} %fusion.34), channel_id=1, source_target_pairs={{0,16},{1,17},{2,18},{3,19},{4,20},{5,21},{6,22},{7,23},{8,24},{9,... | collective-permute-start | bytes 55304 | tf_op jit(solution)/shard_map/ppermute | solution.py:58
  25.5 6.5 %collective-permute-start.2 = (f32[3,1536]{1,0:T(4,128)S(1)}, f32[3,1536]{1,0:T(4,128)S(1)}, u32[]{:S(2)}, u32[]{:S(2)}) collective-permute-start(f32[3,1536]{1,0:T(4,128)S(1)} %add.261), channel_id=1, source_target_pairs={{0,32},{1,33},{2,34},{3,35},{4,36},{5,37},{6,38},{7,39},{8,40},{9,... | collective-permute-start | bytes 55304 | tf_op jit(solution)/shard_map/ppermute | solution.py:58
  32.1 5.4 %collective-permute-start.3 = (f32[3,1536]{1,0:T(4,128)S(1)}, f32[3,1536]{1,0:T(4,128)S(1)}, u32[]{:S(2)}, u32[]{:S(2)}) collective-permute-start(f32[3,1536]{1,0:T(4,128)S(1)} %add.262), channel_id=1, source_target_pairs={{0,64},{1,65},{2,66},{3,67},{4,68},{5,69},{6,70},{7,71},{8,72},{9,... | collective-permute-start | bytes 55304 | tf_op jit(solution)/shard_map/ppermute | solution.py:58
  38.0 3.4 %copy-start = (f32[8,1536]{1,0:T(8,128)S(1)}, f32[8,1536]{1,0:T(8,128)}, u32[]{:S(2)}) copy-start(f32[8,1536]{1,0:T(8,128)} %param.15) | copy-start | bytes 147460
  38.0 3.5 %copy-start.5 = (s32[2]{0:T(128)S(1)}, s32[2]{0:T(128)}, u32[]{:S(2)}) copy-start(s32[2]{0:T(128)} %constant.244.clone.1) | copy-start | bytes 28
  38.0 7.8 %copy-start.1 = (f32[96,32]{0,1:T(8,128)S(1)}, f32[96,32]{0,1:T(8,128)}, u32[]{:S(2)}) copy-start(f32[96,32]{0,1:T(8,128)} %param.14) | copy-start | bytes 36868
  41.4 1.4 %collective-permute-start.4 = (f32[11,1536]{1,0:T(8,128)S(1)}, f32[11,1536]{1,0:T(8,128)S(1)}, u32[]{:S(2)}, u32[]{:S(2)}) collective-permute-start(f32[11,1536]{1,0:T(8,128)S(1)} %pad_maximum_fusion.2), channel_id=1, source_target_pairs={{0,1},{1,0},{2,3},{3,2},{4,5},{5,4},{6,7},{7,6},{8,9},{9,8},{10,11... | collective-permute-start | bytes 202760 | tf_op jit(solution)/shard_map/ppermute | solution.py:58
  42.9 6.0 %collective-permute-start.5 = (f32[19,1536]{1,0:T(8,128)S(1)}, f32[19,1536]{1,0:T(8,128)S(1)}, u32[]{:S(2)}, u32[]{:S(2)}) collective-permute-start(f32[19,1536]{1,0:T(8,128)S(1)} %pad_maximum_fusion.1), channel_id=1, source_target_pairs={{0,2},{1,3},{2,0},{3,1},{4,6},{5,7},{6,4},{7,5},{8,10},{9,11},{10,... | collective-permute-start | bytes 350216 | tf_op jit(solution)/shard_map/ppermute | solution.py:58
  49.0 8.7 %collective-permute-start.6 = (f32[35,1536]{1,0:T(8,128)S(1)}, f32[35,1536]{1,0:T(8,128)S(1)}, u32[]{:S(2)}, u32[]{:S(2)}) collective-permute-start(f32[35,1536]{1,0:T(8,128)S(1)} %pad_maximum_fusion), channel_id=1, source_target_pairs={{0,4},{1,5},{2,6},{3,7},{4,0},{5,1},{6,2},{7,3},{8,12},{9,13},{10,... | collective-permute-start | bytes 645128 | tf_op jit(solution)/shard_map/ppermute | solution.py:58
  76.2 2.1 %collective-permute-start.7 = (f32[2,1536]{1,0:T(2,128)S(1)}, f32[2,1536]{1,0:T(2,128)S(1)}, u32[]{:S(2)}, u32[]{:S(2)}) collective-permute-start(f32[2,1536]{1,0:T(2,128)S(1)} %pad_maximum_fusion.4), channel_id=1, source_target_pairs={{0,1},{1,2},{2,3},{3,4},{4,5},{5,6},{6,7},{7,8},{8,9},{9,10},{10,1... | collective-permute-start | bytes 36872 | tf_op jit(solution)/shard_map/ppermute | solution.py:150
  79.5 34.9 %collective-permute-start.8 = (f32[2,1536]{1,0:T(2,128)S(1)}, f32[2,1536]{1,0:T(2,128)S(1)}, u32[]{:S(2)}, u32[]{:S(2)}) collective-permute-start(f32[2,1536]{1,0:T(2,128)S(1)} %pad_maximum_fusion.5), channel_id=1, source_target_pairs={{1,0},{2,1},{3,2},{4,3},{5,4},{6,5},{7,6},{8,7},{9,8},{10,9},{11,1... | collective-permute-start | bytes 36872 | tf_op jit(solution)/shard_map/ppermute | solution.py:151
  85.1 28.2 %all-to-all-start = ((f32[16,5,1536]{2,1,0:T(8,128)}), f32[16,5,1536]{2,1,0:T(8,128)S(1)}, u32[]{:S(2)}, u32[]{:S(2)}) async-start(f32[16,5,1536]{2,1,0:T(8,128)} %broadcast_select_fusion), calls=%async_computation | async-start | bytes 1572864 | tf_op jit(solution)/shard_map/cond/branch_0_fun/all_to_all | solution.py:134

commit v4 on v3

--- a/solution.py
+++ b/solution.py
@@ -21,22 +21,44 @@
 LANES = (((1,), (1,)), ((), ()))
 
 
-def _sum_kernel(pop_ref, e1_ref, o_ref):
-    for b in range(pop_ref.shape[0]):
-        o_ref[b] = lax.dot_general(pop_ref[b], e1_ref[...], LANES, precision=HI, preferred_element_type=jnp.float32)
+def _split3(x):
+    bf = jnp.bfloat16
+    x1 = x.astype(bf)
+    r1 = x - x1.astype(jnp.float32)
+    x2 = r1.astype(bf)
+    x3 = (r1 - x2.astype(jnp.float32)).astype(bf)
+    return x1, x2, x3
 
 
-def _margin_kernel(pop_ref, w_ref, e1_ref, e2_ref, o_ref):
-    for b in range(pop_ref.shape[0]):
-        wide = jnp.dot(w_ref[b], e1_ref[...], precision=HI, preferred_element_type=jnp.float32)
-        o_ref[b] = lax.dot_general(pop_ref[b] * wide, e2_ref[...], LANES, precision=HI, preferred_element_type=jnp.float32)
+def _dot3(x, e, dims):
+    out = None
+    for part in _split3(x):
+        term = lax.dot_general(part, e, dims, preferred_element_type=jnp.float32)
+        out = term if out is None else out + term
+    return out
 
 
-def _fit_kernel(pop_ref, w_ref, r_ref, e1_ref, e2_ref, o_ref):
+ROWS = (((1,), (0,)), ((), ()))
+
+
+def _sum_kernel(pop_ref, g1_ref, o_ref):
     for b in range(pop_ref.shape[0]):
-        wide = jnp.dot(w_ref[b], e1_ref[...], precision=HI, preferred_element_type=jnp.float32)
-        rep = jnp.dot(r_ref[b], e2_ref[...], precision=HI, preferred_element_type=jnp.float32)
-        o_ref[b] = pop_ref[b] * wide * rep
+        x = pop_ref[b]
+        folded = x[:, 0:128]
+        for j in range(1, x.shape[1] // 128):
+            folded = folded + x[:, j * 128:(j + 1) * 128]
+        o_ref[b] = _dot3(folded, g1_ref[...], ROWS)
+
+
+def _margin_kernel(pop_ref, s2t_ref, e2t_ref, o_ref):
+    for b in range(pop_ref.shape[0]):
+        o_ref[b] = _dot3(pop_ref[b] * s2t_ref[...], e2t_ref[...], ROWS)
+
+
+def _fit_kernel(pop_ref, s1_ref, r_ref, s2t_ref, e2_ref, o_ref):
+    for b in range(pop_ref.shape[0]):
+        rep = _dot3(r_ref[b], e2_ref[...], ROWS)
+        o_ref[b] = pop_ref[b] * (s1_ref[b] * s2t_ref[...]) * rep
 
 
 def _table_call(kernel, table, smalls, consts, out_last):
@@ -81,9 +103,11 @@
         lanes = jnp.arange(width, dtype=jnp.int32)
 
         lane = jnp.arange(INC * HH * TU, dtype=jnp.int32)
-        e1 = (lane[None, :] % (HH * TU) == jnp.arange(HH * TU, dtype=jnp.int32)[:, None]).astype(f32)
-        e2 = (lane[None, :] // (HH * TU) == jnp.arange(INC, dtype=jnp.int32)[:, None]).astype(f32)
-        t1 = _table_call(_sum_kernel, population, [], [e1], HH * TU)
+        bf = jnp.bfloat16
+        g1 = (jnp.arange(128, dtype=jnp.int32)[:, None] % (HH * TU) == jnp.arange(HH * TU, dtype=jnp.int32)[None, :]).astype(bf)
+        e2 = (lane[None, :] // (HH * TU) == jnp.arange(INC, dtype=jnp.int32)[:, None]).astype(bf)
+        e2t = e2.T
+        t1 = _table_call(_sum_kernel, population, [], [g1], HH * TU)
         area_sum = jnp.sum(t1, axis=2)
         s1 = area_target / area_sum
         part = jnp.sum(t1 * s1[:, :, None], axis=0)
@@ -136,8 +160,8 @@
 
         target = lax.cond(flag[0, 0] > 0, lambda: route(most), lambda: route(ROOMY))
 
-        w = s1[:, :, None] * s2[None, :, :]
-        am = _table_call(_margin_kernel, population, [w], [e1, e2], INC)
+        s2t = jnp.tile(s2, (1, INC))
+        am = _table_call(_margin_kernel, population, [], [s2t, e2t], INC) * s1[:, :, None]
         am = jnp.sum(am.reshape(count, AGE, SEX, INC), axis=2).reshape(count, AGE * INC)
         k_a = area_zone - zlo
         onehot = (k_a[:, None] == ks[None, :]).astype(f32)
@@ -155,7 +179,7 @@
         ratio_a = jnp.take(ratio, k_a, axis=0)
 
         r96 = jnp.repeat(ratio_a.reshape(count, AGE, INC), SEX, axis=1)
-        return _table_call(_fit_kernel, population, [w, r96], [e1, e2], INC * HH * TU)
+        return _table_call(_fit_kernel, population, [s1[:, :, None], r96], [s2t, e2], INC * HH * TU)
 
     return body
 

time: 133 us -> 120 us (0.902)
  Pallas kernels: 37.5 us -> 24.8 us
  local copies, waits for them, and re-layouts: 15.2 us -> 17.3 us
    pallas_call x3, Pallas kernels: 37.5 us -> 24.8 us  [_table_call(): pl.pallas_call(kernel, grid=grid, in_specs=specs, out_specs=pl.BlockSpec(...]
  transfers between devices with their start and end apart: 10 -> 10, of which waited for: 8 -> 6; matrix products, arithmetic and copies ran while one was open for 10% -> 13% of each run, Pallas kernels for 0% -> 0%
where the time goes in v4:
time: 120 us; the launch traced here: 119 us
  starting transfers between devices  30 us (25%)
  waiting for transfers between devices  26.2 us (22%)
  Pallas kernels  24.8 us (21%)
  local copies, waits for them, and re-layouts  17.3 us (14%)
  other arithmetic  14.8 us (12%)
  between operations  6.28 us (5%)
    pallas_call x3, Pallas kernels, _table_call(): pl.pallas_call(kernel, grid=grid, in_specs=specs, out_specs=pl.BlockSpec(...  24.8 us
    ppermute x7, starting transfers between devices, _xor(): return lax.ppermute(x, AXES, [(i, i ^ bit) for i in range(n)])  15.2 us
    all_to_all x1, waiting for transfers between devices, route(): came = lax.all_to_all(sent, 'col', 0, 0, tiled=True)  14.8 us
    all_to_all x1, starting transfers between devices, route(): came = lax.all_to_all(sent, 'col', 0, 0, tiled=True)  12.2 us
    ppermute x7, waiting for transfers between devices, _xor(): return lax.ppermute(x, AXES, [(i, i ^ bit) for i in range(n)])  11.4 us
    scatter x1, local copies, waits for them, and re-layouts, body(): slot_of = jnp.zeros((zones,), jnp.int32).at[zone_order].set(labels)  4.31 us
  transfers between devices with their start and end apart: 10, of which 6 were waited for; matrix products, arithmetic and copies ran while one was open for 13% of the time, Pallas kernels for 0%

profile of v4, /device:TPU:0, one launch (start us, length us, event | category | flops | bytes accessed | tf_op | source)
XLA Modules:
  0.0 119.5 jit_solution(6706056732414363098)
XLA Ops:
  0.0 1.3 %fusion.35 = (s32[1]{0:T(128)}, s32[1]{0:T(128)}) fusion(s32[16]{0:T(128)} %param.16), kind=kLoop, calls=%fused_computation.132 | loop fusion | bytes 16 | tf_op jit(solution)/shard_map/slice | solution.py:100
  3.3 6.9 %shard_map.64 = f32[16,96,32]{2,1,0:T(8,128)} custom-call(f32[16,96,1024]{2,1,0:T(8,128)} %pop_ref.5, bf16[128,32]{1,0:T(8,128)(2,1)} %fusion.17.g1_ref), custom_call_target="tpu_custom_call" | custom-call | tf_op jit(solution)/shard_map/pallas_call | solution.py:70
  10.2 1.5 %reduce_sum.72 = f32[16,96]{1,0:T(8,128)S(1)} reduce(f32[16,96,32]{2,1,0:T(8,128)} %shard_map.64, f32[]{:T(128)} %constant.222.clone.1), dimensions={2}, to_apply=%region_0.1 | reduce | flops 47616 | bytes 202756 | tf_op jit(solution)/shard_map/reduce_sum | solution.py:111
  11.7 1.4 %multiply_reduce_fusion.1 = f32[96,32]{1,0:T(8,128)S(1)} fusion(f32[16,96,32]{2,1,0:T(8,128)} %shard_map.64, f32[16,96]{1,0:T(8,128)S(1)} %div.51), kind=kLoop, calls=%fused_computation.50 | loop fusion | flops 95232 | bytes 215040 | tf_op jit(solution)/shard_map/reduce_sum | solution.py:113
  13.3 2.1 %collective-permute-start = (f32[3,1536]{1,0:T(4,128)S(1)}, f32[3,1536]{1,0:T(4,128)S(1)}, u32[]{:S(2)}, u32[]{:S(2)}) collective-permute-start(f32[3,1536]{1,0:T(4,128)S(1)} %pad_maximum_fusion.3), channel_id=1, source_target_pairs={{0,8},{1,9},{2,10},{3,11},{4,12},{5,13},{6,14},{7,15},{8,0},{9,1},... | collective-permute-start | bytes 55304 | tf_op jit(solution)/shard_map/ppermute | solution.py:80
  16.7 0.9 fusion.15.e2t_ref
  17.7 3.7 %collective-permute-start.1 = (f32[3,1536]{1,0:T(4,128)S(1)}, f32[3,1536]{1,0:T(4,128)S(1)}, u32[]{:S(2)}, u32[]{:S(2)}) collective-permute-start(f32[3,1536]{1,0:T(4,128)S(1)} %fusion.33), channel_id=1, source_target_pairs={{0,16},{1,17},{2,18},{3,19},{4,20},{5,21},{6,22},{7,23},{8,24},{9,... | collective-permute-start | bytes 55304 | tf_op jit(solution)/shard_map/ppermute | solution.py:80
  22.0 1.2 collective-permute-done.1
  23.2 1.6 %collective-permute-start.2 = (f32[3,1536]{1,0:T(4,128)S(1)}, f32[3,1536]{1,0:T(4,128)S(1)}, u32[]{:S(2)}, u32[]{:S(2)}) collective-permute-start(f32[3,1536]{1,0:T(4,128)S(1)} %add.258), channel_id=1, source_target_pairs={{0,32},{1,33},{2,34},{3,35},{4,36},{5,37},{6,38},{7,39},{8,40},{9,... | collective-permute-start | bytes 55304 | tf_op jit(solution)/shard_map/ppermute | solution.py:80
  24.8 4.3 %scatter_custom_fusion = s32[1024]{0:T(1024)S(1)} fusion(s32[1024]{0:T(1024)S(1)} %compare_select_fusion.11, s32[1024]{0:T(1024)S(1)} %iota.91, s32[]{:T(128)} %constant.220.clone.1), kind=kCustom, calls=%fused_computation.115 | custom fusion | bytes 4100 | tf_op jit(solution)/shard_map/scatter | solution.py:99
  29.7 2.8 %collective-permute-start.3 = (f32[3,1536]{1,0:T(4,128)S(1)}, f32[3,1536]{1,0:T(4,128)S(1)}, u32[]{:S(2)}, u32[]{:S(2)}) collective-permute-start(f32[3,1536]{1,0:T(4,128)S(1)} %add.259), channel_id=1, source_target_pairs={{0,64},{1,65},{2,66},{3,67},{4,68},{5,69},{6,70},{7,71},{8,72},{9,... | collective-permute-start | bytes 55304 | tf_op jit(solution)/shard_map/ppermute | solution.py:80
  33.8 1.3 %collective-permute-done.3 = f32[3,1536]{1,0:T(4,128)S(1)} collective-permute-done((f32[3,1536]{1,0:T(4,128)S(1)}, f32[3,1536]{1,0:T(4,128)S(1)}, u32[]{:S(2)}, u32[]{:S(2)}) %collective-permute-start.3) | collective-permute-done | bytes 18464 | tf_op jit(solution)/shard_map/ppermute | solution.py:80
  35.7 1.4 %gather_fusion.4 = s32[256]{0:T(256)S(1)} fusion(s32[1024]{0:T(1024)S(1)} %scatter_custom_fusion, s32[1024]{0:T(1024)S(1)} %pad_clamp_fusion.4), kind=kCustom, calls=%fused_computation.4 | custom fusion | bytes 3072 | tf_op jit(solution)/shard_map/gather | solution.py:127
  40.5 1.7 %collective-permute-start.5 = (f32[19,1536]{1,0:T(8,128)S(1)}, f32[19,1536]{1,0:T(8,128)S(1)}, u32[]{:S(2)}, u32[]{:S(2)}) collective-permute-start(f32[19,1536]{1,0:T(8,128)S(1)} %pad_maximum_fusion.1), channel_id=1, source_target_pairs={{0,2},{1,3},{2,0},{3,1},{4,6},{5,7},{6,4},{7,5},{8,10},{9,11},{10,... | collective-permute-start | bytes 350216 | tf_op jit(solution)/shard_map/ppermute | solution.py:80
  42.2 1.3 %add_compare_fusion.1 = pred[16]{0:T(512)(128)(4,1)S(1)} fusion(s32[]{:T(128)} %bitcast.5, s32[]{:T(128)} %bitcast.4), kind=kLoop, calls=%fused_computation.127 | loop fusion | flops 32 | bytes 24 | tf_op jit(solution)/shard_map/le | solution.py:147
  43.7 2.9 %collective-permute-done.5 = f32[19,1536]{1,0:T(8,128)S(1)} collective-permute-done((f32[19,1536]{1,0:T(8,128)S(1)}, f32[19,1536]{1,0:T(8,128)S(1)}, u32[]{:S(2)}, u32[]{:S(2)}) %collective-permute-start.5) | collective-permute-done | bytes 116768 | tf_op jit(solution)/shard_map/ppermute | solution.py:80
  46.7 3.3 %collective-permute-start.6 = (f32[35,1536]{1,0:T(8,128)S(1)}, f32[35,1536]{1,0:T(8,128)S(1)}, u32[]{:S(2)}, u32[]{:S(2)}) collective-permute-start(f32[35,1536]{1,0:T(8,128)S(1)} %pad_maximum_fusion), channel_id=1, source_target_pairs={{0,4},{1,5},{2,6},{3,7},{4,0},{5,1},{6,2},{7,3},{8,12},{9,13},{10,... | collective-permute-start | bytes 645128 | tf_op jit(solution)/shard_map/ppermute | solution.py:80
  49.9 5.5 %collective-permute-done.6 = f32[35,1536]{1,0:T(8,128)S(1)} collective-permute-done((f32[35,1536]{1,0:T(8,128)S(1)}, f32[35,1536]{1,0:T(8,128)S(1)}, u32[]{:S(2)}, u32[]{:S(2)}) %collective-permute-start.6) | collective-permute-done | bytes 215072 | tf_op jit(solution)/shard_map/ppermute | solution.py:80
  55.6 0.9 copy.36.s2t_ref
  56.6 8.2 %shard_map.65 = f32[16,96,32]{2,1,0:T(8,128)} custom-call(f32[16,96,1024]{2,1,0:T(8,128)} %pop_ref.5, f32[96,1024]{1,0:T(8,128)} %copy.36.s2t_ref, bf16[1024,32]{1,0:T(8,128)(2,1)} %fusion.15.e2t_ref), custom_call_target="tpu_custom_call" | custom-call | tf_op jit(solution)/shard_map/pallas_call | solution.py:70
  64.8 1.4 %broadcast_multiply_fusion = f32[16,96,32]{2,1,0:T(8,128)S(1)} fusion(f32[16,96,32]{2,1,0:T(8,128)} %shard_map.65, f32[16,96]{1,0:T(8,128)S(1)} %div.51), kind=kLoop, calls=%fused_computation.54 | loop fusion | flops 49152 | bytes 399360 | tf_op jit(solution)/shard_map/mul | solution.py:164
  66.2 1.0 reduce_sum.76
  67.6 1.3 %collective-permute-start.7 = (f32[2,1536]{1,0:T(2,128)S(1)}, f32[2,1536]{1,0:T(2,128)S(1)}, u32[]{:S(2)}, u32[]{:S(2)}) collective-permute-start(f32[2,1536]{1,0:T(2,128)S(1)} %pad_maximum_fusion.4), channel_id=1, source_target_pairs={{0,1},{1,2},{2,3},{3,4},{4,5},{5,6},{6,7},{7,8},{8,9},{9,10},{10,1... | collective-permute-start | bytes 36872 | tf_op jit(solution)/shard_map/ppermute | solution.py:174
  68.9 1.2 copy.37.s1_ref
  71.8 1.3 %collective-permute-start.8 = (f32[2,1536]{1,0:T(2,128)S(1)}, f32[2,1536]{1,0:T(2,128)S(1)}, u32[]{:S(2)}, u32[]{:S(2)}) collective-permute-start(f32[2,1536]{1,0:T(2,128)S(1)} %pad_maximum_fusion.5), channel_id=1, source_target_pairs={{1,0},{2,1},{3,2},{4,3},{5,4},{6,5},{7,6},{8,7},{9,8},{10,9},{11,1... | collective-permute-start | bytes 36872 | tf_op jit(solution)/shard_map/ppermute | solution.py:175
  75.0 30.4 %conditional.1 = (f32[16,1536]{1,0:T(8,128)S(1)}) conditional(s32[]{:T(128)} %bitcast.6, (s32[16,16]{1,0:T(8,128)S(1)}, pred[16,16]{1,0:T(8,128)(4,1)S(1)}, s32[16,16]{1,0:T(8,128)S(1)}, f32[64,1536]{1,0:T(8,128)S(1)}, s32[16]{0:T(128)S(1)}, /*index=5*/s32[16]{0:T(128)S(1)}) %tuple.19, (s32[16,16]{1,0:T(8,128)S(1)}, pred[16,16]{1,0:T(8,128)(4,1)S(1)}, ...), branch_computations={%region_6.8_spmd, %region_8.10_spmd} | conditional | flops 416192 | bytes 11225704 | solution.py:161
  75.5 0.8 gather_fusion
  76.4 1.0 broadcast_select_fusion
  77.4 12.2 %all-to-all-start = ((f32[16,5,1536]{2,1,0:T(8,128)}), f32[16,5,1536]{2,1,0:T(8,128)S(1)}, u32[]{:S(2)}, u32[]{:S(2)}) async-start(f32[16,5,1536]{2,1,0:T(8,128)} %broadcast_select_fusion), calls=%async_computation | async-start | bytes 1572864 | tf_op jit(solution)/shard_map/cond/branch_0_fun/all_to_all | solution.py:158
  89.6 14.8 %all-to-all-done = f32[16,5,1536]{2,1,0:T(8,128)S(1)} async-done(((f32[16,5,1536]{2,1,0:T(8,128)}), f32[16,5,1536]{2,1,0:T(8,128)S(1)}, u32[]{:S(2)}, u32[]{:S(2)}) %all-to-all-start) | async-done | bytes 491552 | tf_op jit(solution)/shard_map/cond/branch_0_fun/all_to_all | solution.py:158
  108.4 1.3 %broadcast_in_dim.145 = f32[16,48,2,32]{3,2,1,0:T(2,128)} broadcast(f32[16,48,32]{2,1,0:T(8,128)S(1)} %broadcast_select_fusion.2), dimensions={0,1,3} | broadcast | bytes 294912 | tf_op jit(solution)/shard_map/broadcast_in_dim | solution.py:181
  109.7 9.8 %shard_map.66 = f32[16,96,1024]{2,1,0:T(8,128)} custom-call(f32[16,96,1024]{2,1,0:T(8,128)} %pop_ref.5, f32[16,96,1]{2,1,0:T(8,128)} %copy.37.s1_ref, f32[16,96,32]{2,1,0:T(8,128)} %bitcast.20, f32[96,1024]{1,0:T(8,128)} %copy.36.s2t_ref, bf16[32,1024]{1,0:T(8,128)(2,1)} %fusion.16.e2_ref), custom_call_target="tpu_custom_call" | custom-call | tf_op jit(solution)/shard_map/pallas_call | solution.py:70
  (104 shorter events, 13.1 us)
Async XLA Ops:
  3.3 8.4 %copy-start.2 = (f32[16,96]{1,0:T(8,128)S(1)}, f32[16,96]{1,0:T(8,128)}, u32[]{:S(2)}) copy-start(f32[16,96]{1,0:T(8,128)} %param.13) | copy-start | bytes 18436
  10.2 5.2 %copy-start.3 = (s32[16]{0:T(128)S(1)}, s32[16]{0:T(128)}, u32[]{:S(2)}) copy-start(s32[16]{0:T(128)} %param.16) | copy-start | bytes 196
  10.2 7.5 %copy-start.4 = (s32[1024]{0:T(1024)S(1)}, s32[1024]{0:T(1024)}, u32[]{:S(2)}) copy-start(s32[1024]{0:T(1024)} %param.17) | copy-start | bytes 12292
  13.3 4.4 %collective-permute-start = (f32[3,1536]{1,0:T(4,128)S(1)}, f32[3,1536]{1,0:T(4,128)S(1)}, u32[]{:S(2)}, u32[]{:S(2)}) collective-permute-start(f32[3,1536]{1,0:T(4,128)S(1)} %pad_maximum_fusion.3), channel_id=1, source_target_pairs={{0,8},{1,9},{2,10},{3,11},{4,12},{5,13},{6,14},{7,15},{8,0},{9,1},... | collective-permute-start | bytes 55304 | tf_op jit(solution)/shard_map/ppermute | solution.py:80
  17.7 5.5 %collective-permute-start.1 = (f32[3,1536]{1,0:T(4,128)S(1)}, f32[3,1536]{1,0:T(4,128)S(1)}, u32[]{:S(2)}, u32[]{:S(2)}) collective-permute-start(f32[3,1536]{1,0:T(4,128)S(1)} %fusion.33), channel_id=1, source_target_pairs={{0,16},{1,17},{2,18},{3,19},{4,20},{5,21},{6,22},{7,23},{8,24},{9,... | collective-permute-start | bytes 55304 | tf_op jit(solution)/shard_map/ppermute | solution.py:80
  23.2 6.5 %collective-permute-start.2 = (f32[3,1536]{1,0:T(4,128)S(1)}, f32[3,1536]{1,0:T(4,128)S(1)}, u32[]{:S(2)}, u32[]{:S(2)}) collective-permute-start(f32[3,1536]{1,0:T(4,128)S(1)} %add.258), channel_id=1, source_target_pairs={{0,32},{1,33},{2,34},{3,35},{4,36},{5,37},{6,38},{7,39},{8,40},{9,... | collective-permute-start | bytes 55304 | tf_op jit(solution)/shard_map/ppermute | solution.py:80
  29.7 5.4 %collective-permute-start.3 = (f32[3,1536]{1,0:T(4,128)S(1)}, f32[3,1536]{1,0:T(4,128)S(1)}, u32[]{:S(2)}, u32[]{:S(2)}) collective-permute-start(f32[3,1536]{1,0:T(4,128)S(1)} %add.259), channel_id=1, source_target_pairs={{0,64},{1,65},{2,66},{3,67},{4,68},{5,69},{6,70},{7,71},{8,72},{9,... | collective-permute-start | bytes 55304 | tf_op jit(solution)/shard_map/ppermute | solution.py:80
  35.6 3.4 %copy-start = (f32[8,1536]{1,0:T(8,128)S(1)}, f32[8,1536]{1,0:T(8,128)}, u32[]{:S(2)}) copy-start(f32[8,1536]{1,0:T(8,128)} %param.15) | copy-start | bytes 147460
  35.6 3.5 %copy-start.5 = (s32[2]{0:T(128)S(1)}, s32[2]{0:T(128)}, u32[]{:S(2)}) copy-start(s32[2]{0:T(128)} %constant.244.clone.1) | copy-start | bytes 28
  37.0 18.5 %copy-start.1 = (f32[96,32]{0,1:T(8,128)S(1)}, f32[96,32]{0,1:T(8,128)}, u32[]{:S(2)}) copy-start(f32[96,32]{0,1:T(8,128)} %param.14) | copy-start | bytes 36868
  39.1 1.4 %collective-permute-start.4 = (f32[11,1536]{1,0:T(8,128)S(1)}, f32[11,1536]{1,0:T(8,128)S(1)}, u32[]{:S(2)}, u32[]{:S(2)}) collective-permute-start(f32[11,1536]{1,0:T(8,128)S(1)} %pad_maximum_fusion.2), channel_id=1, source_target_pairs={{0,1},{1,0},{2,3},{3,2},{4,5},{5,4},{6,7},{7,6},{8,9},{9,8},{10,11... | collective-permute-start | bytes 202760 | tf_op jit(solution)/shard_map/ppermute | solution.py:80
  40.5 6.0 %collective-permute-start.5 = (f32[19,1536]{1,0:T(8,128)S(1)}, f32[19,1536]{1,0:T(8,128)S(1)}, u32[]{:S(2)}, u32[]{:S(2)}) collective-permute-start(f32[19,1536]{1,0:T(8,128)S(1)} %pad_maximum_fusion.1), channel_id=1, source_target_pairs={{0,2},{1,3},{2,0},{3,1},{4,6},{5,7},{6,4},{7,5},{8,10},{9,11},{10,... | collective-permute-start | bytes 350216 | tf_op jit(solution)/shard_map/ppermute | solution.py:80
  46.7 8.7 %collective-permute-start.6 = (f32[35,1536]{1,0:T(8,128)S(1)}, f32[35,1536]{1,0:T(8,128)S(1)}, u32[]{:S(2)}, u32[]{:S(2)}) collective-permute-start(f32[35,1536]{1,0:T(8,128)S(1)} %pad_maximum_fusion), channel_id=1, source_target_pairs={{0,4},{1,5},{2,6},{3,7},{4,0},{5,1},{6,2},{7,3},{8,12},{9,13},{10,... | collective-permute-start | bytes 645128 | tf_op jit(solution)/shard_map/ppermute | solution.py:80
  67.6 3.1 %collective-permute-start.7 = (f32[2,1536]{1,0:T(2,128)S(1)}, f32[2,1536]{1,0:T(2,128)S(1)}, u32[]{:S(2)}, u32[]{:S(2)}) collective-permute-start(f32[2,1536]{1,0:T(2,128)S(1)} %pad_maximum_fusion.4), channel_id=1, source_target_pairs={{0,1},{1,2},{2,3},{3,4},{4,5},{5,6},{6,7},{7,8},{8,9},{9,10},{10,1... | collective-permute-start | bytes 36872 | tf_op jit(solution)/shard_map/ppermute | solution.py:174
  71.8 33.8 %collective-permute-start.8 = (f32[2,1536]{1,0:T(2,128)S(1)}, f32[2,1536]{1,0:T(2,128)S(1)}, u32[]{:S(2)}, u32[]{:S(2)}) collective-permute-start(f32[2,1536]{1,0:T(2,128)S(1)} %pad_maximum_fusion.5), channel_id=1, source_target_pairs={{1,0},{2,1},{3,2},{4,3},{5,4},{6,5},{7,6},{8,7},{9,8},{10,9},{11,1... | collective-permute-start | bytes 36872 | tf_op jit(solution)/shard_map/ppermute | solution.py:175
  77.4 27.0 %all-to-all-start = ((f32[16,5,1536]{2,1,0:T(8,128)}), f32[16,5,1536]{2,1,0:T(8,128)S(1)}, u32[]{:S(2)}, u32[]{:S(2)}) async-start(f32[16,5,1536]{2,1,0:T(8,128)} %broadcast_select_fusion), calls=%async_computation | async-start | bytes 1572864 | tf_op jit(solution)/shard_map/cond/branch_0_fun/all_to_all | solution.py:158

commit v5 on v4

--- a/solution.py
+++ b/solution.py
@@ -12,7 +12,7 @@
 TU = 4
 ZONE_MOST = 6
 MEMBERS = 8
-ROOMY = 5
+ROOMY = 6
 AXES = ("col", "mem")
 
 
@@ -96,11 +96,21 @@
         col, mem = idx // MEMBERS, idx % MEMBERS
 
         labels = jnp.arange(zones, dtype=jnp.int32)
-        slot_of = jnp.zeros((zones,), jnp.int32).at[zone_order].set(labels)
+
+        def slot_of(z):
+            return jnp.sum(jnp.where(zone_order[None, :] == z.reshape(-1)[:, None], labels[None, :], 0), axis=1).reshape(z.shape)
+
         zlo = area_zone[0]
         zhi = area_zone[count - 1]
         ks = jnp.arange(most, dtype=jnp.int32)
         lanes = jnp.arange(width, dtype=jnp.int32)
+
+        m_kz = zlo + ks
+        m_valid = m_kz <= zhi
+        m_slot = slot_of(jnp.minimum(m_kz, zones - 1))
+        m_mem = (m_slot // rows) % MEMBERS
+        m_rank = jnp.sum(((m_mem[:, None] == m_mem[None, :]) & m_valid[None, :] & (ks[None, :] < ks[:, None])).astype(jnp.int32), axis=1)
+        over = jnp.any(m_valid & (m_rank >= ROOMY)).astype(f32)
 
         lane = jnp.arange(INC * HH * TU, dtype=jnp.int32)
         bf = jnp.bfloat16
@@ -113,52 +123,46 @@
         part = jnp.sum(t1 * s1[:, :, None], axis=0)
         nat_rows = (AGE * SEX * HH * TU) // width
 
-        zrow = jnp.where(lanes == 2 * col, zlo.astype(f32), 0.0) + jnp.where(lanes == 2 * col + 1, zhi.astype(f32), 0.0)
-        msg = jnp.concatenate([part.reshape(nat_rows, width), zrow[None]], axis=0)
+        nat = part.reshape(nat_rows, width)
+        flag = jnp.where(lanes == 0, over, 0.0)[None]
+        pool = zone_target
         bit = MEMBERS
         while bit < n:
+            got = _xor(jnp.concatenate([nat, flag, pool], axis=0), n, bit)
+            nat = nat + got[:nat_rows]
+            flag = flag + got[nat_rows:nat_rows + 1]
+            theirs = got[nat_rows + 1:]
+            pool = jnp.where((idx & bit) == 0, jnp.concatenate([pool, theirs], 0), jnp.concatenate([theirs, pool], 0))
+            bit *= 2
+
+        zrow = jnp.where(lanes == 2 * mem, zlo.astype(f32), 0.0) + jnp.where(lanes == 2 * mem + 1, zhi.astype(f32), 0.0)
+        msg = jnp.concatenate([nat, flag, zrow[None]], axis=0)
+        bit = 1
+        while bit < MEMBERS:
             msg = msg + _xor(msg, n, bit)
             bit *= 2
         nat = msg[:nat_rows]
-        zinfo = msg[nat_rows, : 2 * cols].reshape(cols, 2).astype(jnp.int32)
+        total_over = msg[nat_rows, 0]
+        zinfo = msg[nat_rows + 1, : 2 * MEMBERS].reshape(MEMBERS, 2).astype(jnp.int32)
+        s2 = national_target / nat.reshape(AGE * SEX, HH * TU)
 
         c_kz = zinfo[:, 0:1] + ks[None, :]
         c_valid = c_kz <= zinfo[:, 1:2]
-        c_slot = slot_of[jnp.minimum(c_kz, zones - 1)]
-        c_grp = c_slot // pool_rows
-        earlier = (c_grp[:, :, None] == c_grp[:, None, :]) & c_valid[:, None, :] & (ks[None, None, :] < ks[None, :, None])
+        c_slot = slot_of(jnp.minimum(c_kz, zones - 1))
+        c_mem = (c_slot // rows) % MEMBERS
+        earlier = (c_mem[:, :, None] == c_mem[:, None, :]) & c_valid[:, None, :] & (ks[None, None, :] < ks[None, :, None])
         c_rank = jnp.sum(earlier.astype(jnp.int32), axis=2)
-        over = jnp.any(c_valid & (c_rank >= ROOMY)).astype(f32)
-
-        pool = zone_target
-        flag = jnp.where(lanes == 0, over, 0.0)[None]
-        bit = 1
-        while bit < MEMBERS:
-            msg = jnp.concatenate([nat, flag, pool], axis=0)
-            got = _xor(msg, n, bit)
-            nat = nat + got[:nat_rows]
-            flag = flag + got[nat_rows:nat_rows + 1]
-            theirs = got[nat_rows + 1:]
-            pool = jnp.where((mem & bit) == 0, jnp.concatenate([pool, theirs], 0), jnp.concatenate([theirs, pool], 0))
-            bit *= 2
-        s2 = national_target / nat.reshape(AGE * SEX, HH * TU)
-
-        m_kz = zlo + ks
-        m_valid = m_kz <= zhi
-        m_slot = slot_of[jnp.minimum(m_kz, zones - 1)]
-        m_grp = m_slot // pool_rows
-        m_rank = jnp.sum(((m_grp[:, None] == m_grp[None, :]) & m_valid[None, :] & (ks[None, :] < ks[:, None])).astype(jnp.int32), axis=1)
-        mine = c_valid & (c_grp == col)
+        mine = c_valid & (c_mem == mem)
+        c_at = (c_slot // (rows * MEMBERS)) * rows + c_slot % rows
 
         def route(room):
-            keep = mine & (c_rank < room)
-            hit = keep[:, :, None] & (c_rank[:, :, None] == jnp.arange(room, dtype=jnp.int32)[None, None, :])
-            at = jnp.sum(jnp.where(hit, (c_slot % pool_rows)[:, :, None], 0), axis=1)
-            sent = jnp.take(pool, at.reshape(-1), axis=0).reshape(cols, room, width)
-            came = lax.all_to_all(sent, "col", 0, 0, tiled=True)
-            return came[m_grp, jnp.minimum(m_rank, room - 1)]
+            hit = (mine & (c_rank < room))[:, :, None] & (c_rank[:, :, None] == jnp.arange(room, dtype=jnp.int32)[None, None, :])
+            at = jnp.sum(jnp.where(hit, c_at[:, :, None], 0), axis=1)
+            sent = jnp.take(pool, at.reshape(-1), axis=0).reshape(MEMBERS, room, width)
+            came = lax.all_to_all(sent, "mem", 0, 0, tiled=True)
+            return came[m_mem, jnp.minimum(m_rank, room - 1)]
 
-        target = lax.cond(flag[0, 0] > 0, lambda: route(most), lambda: route(ROOMY))
+        target = lax.cond(total_over > 0, lambda: route(most), lambda: route(ROOMY))
 
         s2t = jnp.tile(s2, (1, INC))
         am = _table_call(_margin_kernel, population, [], [s2t, e2t], INC) * s1[:, :, None]

time: 120 us -> 114 us (0.950)
  the two profiles are of different devices: /device:TPU:0 before, /device:TPU:6 now
where the time goes in v5:
time: 114 us; the launch traced here: 113 us
  waiting for transfers between devices  37.2 us (33%)
  Pallas kernels  24.8 us (22%)
  starting transfers between devices  19.5 us (17%)
  other arithmetic  15.7 us (14%)
  local copies, waits for them, and re-layouts  10.2 us (9%)
  between operations  5.61 us (5%)
    pallas_call x3, Pallas kernels, _table_call(): pl.pallas_call(kernel, grid=grid, in_specs=specs, out_specs=pl.BlockSpec(...  24.8 us
    ppermute x7, waiting for transfers between devices, _xor(): return lax.ppermute(x, AXES, [(i, i ^ bit) for i in range(n)])  21.2 us
    ppermute x7, starting transfers between devices, _xor(): return lax.ppermute(x, AXES, [(i, i ^ bit) for i in range(n)])  12.2 us
    all_to_all x1, waiting for transfers between devices, route(): came = lax.all_to_all(sent, 'mem', 0, 0, tiled=True)  8.82 us
    ppermute x1, waiting for transfers between devices, body(): from_left = lax.ppermute(to_right, AXES, right)  7.21 us
    all_to_all x1, starting transfers between devices, route(): came = lax.all_to_all(sent, 'mem', 0, 0, tiled=True)  3.45 us
  transfers between devices with their start and end apart: 10, of which 9 were waited for; matrix products, arithmetic and copies ran while one was open for 7% of the time, Pallas kernels for 0%

profile of v5, /device:TPU:6, one launch (start us, length us, event | category | flops | bytes accessed | tf_op | source)
XLA Modules:
  0.0 113.1 jit_solution(5434382974930750212)
XLA Ops:
  0.0 1.4 %fusion.42 = (s32[1]{0:T(128)}, s32[1]{0:T(128)}) fusion(s32[16]{0:T(128)} %param.16), kind=kLoop, calls=%fused_computation.142 | loop fusion | bytes 16 | tf_op jit(solution)/shard_map/slice | solution.py:103
  2.0 0.9 select_reduce_fusion.3
  2.9 1.9 %compare_and_fusion.5 = (pred[16]{0:T(512)(128)(4,1)S(1)}, s32[16]{0:T(128)S(1)}, pred[16]{0:T(512)(128)(4,1)S(1)}) fusion(s32[16]{0:T(128)} %param.16, s32[]{:T(128)} %bitcast.4, s32[]{:T(128)} %bitcast.5), kind=kLoop, calls=%fused_computation.127 | loop fusion | flops 144 | bytes 168 | tf_op jit(solution)/shard_map/jit(_take)/and | solution.py:183
  7.0 6.9 %shard_map.64 = f32[16,96,32]{2,1,0:T(8,128)} custom-call(f32[16,96,1024]{2,1,0:T(8,128)} %pop_ref.5, bf16[128,32]{1,0:T(8,128)(2,1)} %fusion.16.g1_ref), custom_call_target="tpu_custom_call" | custom-call | tf_op jit(solution)/shard_map/pallas_call | solution.py:70
  13.9 1.5 %reduce_sum.90 = f32[16,96]{1,0:T(8,128)S(1)} reduce(f32[16,96,32]{2,1,0:T(8,128)} %shard_map.64, f32[]{:T(128)} %constant.224.clone.1), dimensions={2}, to_apply=%region_0.1 | reduce | flops 47616 | bytes 202756 | tf_op jit(solution)/shard_map/reduce_sum | solution.py:121
  15.4 1.4 %multiply_reduce_fusion.1 = f32[96,32]{1,0:T(8,128)S(1)} fusion(f32[16,96,32]{2,1,0:T(8,128)} %shard_map.64, f32[16,96]{1,0:T(8,128)S(1)} %div.53), kind=kLoop, calls=%fused_computation.41 | loop fusion | flops 95232 | bytes 215040 | tf_op jit(solution)/shard_map/reduce_sum | solution.py:123
  17.0 2.0 %collective-permute-start = (f32[11,1536]{1,0:T(8,128)S(1)}, f32[11,1536]{1,0:T(8,128)S(1)}, u32[]{:S(2)}, u32[]{:S(2)}) collective-permute-start(f32[11,1536]{1,0:T(8,128)S(1)} %pad_maximum_fusion.3), channel_id=1, source_target_pairs={{0,8},{1,9},{2,10},{3,11},{4,12},{5,13},{6,14},{7,15},{8,0},{9,1},... | collective-permute-start | bytes 202760 | tf_op jit(solution)/shard_map/ppermute | solution.py:80
  21.9 3.9 %collective-permute-start.1 = (f32[19,1536]{1,0:T(8,128)S(1)}, f32[19,1536]{1,0:T(8,128)S(1)}, u32[]{:S(2)}, u32[]{:S(2)}) collective-permute-start(f32[19,1536]{1,0:T(8,128)S(1)} %pad_maximum_fusion.2), channel_id=1, source_target_pairs={{0,16},{1,17},{2,18},{3,19},{4,20},{5,21},{6,22},{7,23},{8,24},{9,... | collective-permute-start | bytes 350216 | tf_op jit(solution)/shard_map/ppermute | solution.py:80
  27.8 1.1 collective-permute-done.1
  29.0 0.9 collective-permute-start.2
  29.9 6.5 %collective-permute-done.2 = f32[35,1536]{1,0:T(8,128)S(1)} collective-permute-done((f32[35,1536]{1,0:T(8,128)S(1)}, f32[35,1536]{1,0:T(8,128)S(1)}, u32[]{:S(2)}, u32[]{:S(2)}) %collective-permute-start.2) | collective-permute-done | bytes 215072 | tf_op jit(solution)/shard_map/ppermute | solution.py:80
  36.9 0.9 fusion.14.e2t_ref
  37.8 8.6 %collective-permute-done.3 = f32[67,1536]{1,0:T(8,128)S(1)} collective-permute-done((f32[67,1536]{1,0:T(8,128)S(1)}, f32[67,1536]{1,0:T(8,128)S(1)}, u32[]{:S(2)}, u32[]{:S(2)}) %collective-permute-start.3) | collective-permute-done | bytes 411680 | tf_op jit(solution)/shard_map/ppermute | solution.py:80
  46.6 1.2 %collective-permute-done.4 = f32[4,1536]{1,0:T(4,128)S(1)} collective-permute-done((f32[4,1536]{1,0:T(4,128)S(1)}, f32[4,1536]{1,0:T(4,128)S(1)}, u32[]{:S(2)}, u32[]{:S(2)}) %collective-permute-start.4) | collective-permute-done | bytes 24608 | tf_op jit(solution)/shard_map/ppermute | solution.py:80
  47.8 1.7 %collective-permute-start.5 = (f32[4,1536]{1,0:T(4,128)S(1)}, f32[4,1536]{1,0:T(4,128)S(1)}, u32[]{:S(2)}, u32[]{:S(2)}) collective-permute-start(f32[4,1536]{1,0:T(4,128)S(1)} %fusion.40), channel_id=1, source_target_pairs={{0,2},{1,3},{2,0},{3,1},{4,6},{5,7},{6,4},{7,5},{8,10},{9,11},{10,... | collective-permute-start | bytes 73736 | tf_op jit(solution)/shard_map/ppermute | solution.py:80
  49.5 1.2 %copy.37.s1_ref = f32[16,96,1]{2,1,0:T(8,128)} copy(f32[16,96,1]{1,0,2:T(8,128)S(1)} %bitcast.19) | data formatting | bytes 12288 | tf_op jit(solution)/shard_map/broadcast_in_dim | solution.py:186
  50.8 1.0 collective-permute-done.5
  51.7 3.3 %collective-permute-start.6 = (f32[4,1536]{1,0:T(4,128)S(1)}, f32[4,1536]{1,0:T(4,128)S(1)}, u32[]{:S(2)}, u32[]{:S(2)}) collective-permute-start(f32[4,1536]{1,0:T(4,128)S(1)} %add.255), channel_id=1, source_target_pairs={{0,4},{1,5},{2,6},{3,7},{4,0},{5,1},{6,2},{7,3},{8,12},{9,13},{10,... | collective-permute-start | bytes 73736 | tf_op jit(solution)/shard_map/ppermute | solution.py:80
  55.1 2.0 %collective-permute-done.6 = f32[4,1536]{1,0:T(4,128)S(1)} collective-permute-done((f32[4,1536]{1,0:T(4,128)S(1)}, f32[4,1536]{1,0:T(4,128)S(1)}, u32[]{:S(2)}, u32[]{:S(2)}) %collective-permute-start.6) | collective-permute-done | bytes 24608 | tf_op jit(solution)/shard_map/ppermute | solution.py:80
  58.2 0.9 copy.36.s2t_ref
  59.1 8.2 %shard_map.65 = f32[16,96,32]{2,1,0:T(8,128)} custom-call(f32[16,96,1024]{2,1,0:T(8,128)} %pop_ref.5, f32[96,1024]{1,0:T(8,128)} %copy.36.s2t_ref, bf16[1024,32]{1,0:T(8,128)(2,1)} %fusion.14.e2t_ref), custom_call_target="tpu_custom_call" | custom-call | tf_op jit(solution)/shard_map/pallas_call | solution.py:70
  67.3 1.4 %broadcast_multiply_fusion = f32[16,96,32]{2,1,0:T(8,128)S(1)} fusion(f32[16,96,32]{2,1,0:T(8,128)} %shard_map.65, f32[16,96]{1,0:T(8,128)S(1)} %div.53), kind=kLoop, calls=%fused_computation.47 | loop fusion | flops 49152 | bytes 399360 | tf_op jit(solution)/shard_map/mul | solution.py:168
  68.7 1.0 reduce_sum.96
  70.1 1.9 %collective-permute-start.7 = (f32[2,1536]{1,0:T(2,128)S(1)}, f32[2,1536]{1,0:T(2,128)S(1)}, u32[]{:S(2)}, u32[]{:S(2)}) collective-permute-start(f32[2,1536]{1,0:T(2,128)S(1)} %pad_maximum_fusion.5), channel_id=1, source_target_pairs={{0,1},{1,2},{2,3},{3,4},{4,5},{5,6},{6,7},{7,8},{8,9},{9,10},{10,1... | collective-permute-start | bytes 36872 | tf_op jit(solution)/shard_map/ppermute | solution.py:178
  72.1 7.2 %collective-permute-done.7 = f32[2,1536]{1,0:T(2,128)S(1)} collective-permute-done((f32[2,1536]{1,0:T(2,128)S(1)}, f32[2,1536]{1,0:T(2,128)S(1)}, u32[]{:S(2)}, u32[]{:S(2)}) %collective-permute-start.7) | collective-permute-done | bytes 12320 | tf_op jit(solution)/shard_map/ppermute | solution.py:178
  80.5 1.9 %collective-permute-start.8 = (f32[2,1536]{1,0:T(2,128)S(1)}, f32[2,1536]{1,0:T(2,128)S(1)}, u32[]{:S(2)}, u32[]{:S(2)}) collective-permute-start(f32[2,1536]{1,0:T(2,128)S(1)} %pad_maximum_fusion.6), channel_id=1, source_target_pairs={{1,0},{2,1},{3,2},{4,3},{5,4},{6,5},{7,6},{8,7},{9,8},{10,9},{11,1... | collective-permute-start | bytes 36872 | tf_op jit(solution)/shard_map/ppermute | solution.py:179
  83.9 15.2 %conditional.1 = (f32[16,1536]{1,0:T(8,128)S(1)}) conditional(s32[]{:T(128)} %bitcast.6, (s32[8,16]{1,0:T(8,128)S(1)}, pred[8,16]{1,0:T(8,128)(4,1)S(1)}, s32[8,16]{1,0:T(8,128)S(1)}, f32[128,1536]{1,0:T(8,128)S(1)}, s32[16]{0:T(128)S(1)}, /*index=5*/s32[16]{0:T(128)S(1)}) %tuple.19, (s32[8,16]{1,0:T(8,128)S(1)}, pred[8,16]{1,0:T(8,128)(4,1)S(1)}, ...), branch_computations={%region_7.9_spmd, %region_9.11_spmd} | conditional | flops 207296 | bytes 5712360 | solution.py:165
  85.1 0.8 broadcast_select_fusion
  86.0 3.5 %all-to-all-start = ((f32[8,6,1536]{2,1,0:T(8,128)}), f32[8,6,1536]{2,1,0:T(8,128)S(1)}, u32[]{:S(2)}, u32[]{:S(2)}) async-start(f32[8,6,1536]{2,1,0:T(8,128)} %broadcast_select_fusion), calls=%async_computation | async-start | bytes 786432 | tf_op jit(solution)/shard_map/cond/branch_0_fun/all_to_all | solution.py:162
  89.5 8.8 %all-to-all-done = f32[8,6,1536]{2,1,0:T(8,128)S(1)} async-done(((f32[8,6,1536]{2,1,0:T(8,128)}), f32[8,6,1536]{2,1,0:T(8,128)S(1)}, u32[]{:S(2)}, u32[]{:S(2)}) %all-to-all-start) | async-done | bytes 294944 | tf_op jit(solution)/shard_map/cond/branch_0_fun/all_to_all | solution.py:162
  102.1 1.3 %broadcast_in_dim.172 = f32[16,48,2,32]{3,2,1,0:T(2,128)} broadcast(f32[16,48,32]{2,1,0:T(8,128)S(1)} %broadcast_select_fusion.2), dimensions={0,1,3} | broadcast | bytes 294912 | tf_op jit(solution)/shard_map/broadcast_in_dim | solution.py:185
  103.4 9.7 %shard_map.66 = f32[16,96,1024]{2,1,0:T(8,128)} custom-call(f32[16,96,1024]{2,1,0:T(8,128)} %pop_ref.5, f32[16,96,1]{2,1,0:T(8,128)} %copy.37.s1_ref, f32[16,96,32]{2,1,0:T(8,128)} %bitcast.15, f32[96,1024]{1,0:T(8,128)} %copy.36.s2t_ref, bf16[32,1024]{1,0:T(8,128)(2,1)} %fusion.15.e2_ref), custom_call_target="tpu_custom_call" | custom-call | tf_op jit(solution)/shard_map/pallas_call | solution.py:70
  (101 shorter events, 12.5 us)
Async XLA Ops:
  7.0 8.4 %copy-start.3 = (f32[16,96]{1,0:T(8,128)S(1)}, f32[16,96]{1,0:T(8,128)}, u32[]{:S(2)}) copy-start(f32[16,96]{1,0:T(8,128)} %param.13) | copy-start | bytes 18436
  13.9 3.0 %copy-start = (f32[8,1536]{1,0:T(8,128)S(1)}, f32[8,1536]{1,0:T(8,128)}, u32[]{:S(2)}) copy-start(f32[8,1536]{1,0:T(8,128)} %param.15) | copy-start | bytes 147460
  13.9 13.1 %copy-start.4 = (s32[2]{0:T(128)S(1)}, s32[2]{0:T(128)}, u32[]{:S(2)}) copy-start(s32[2]{0:T(128)} %constant.245.clone.1) | copy-start | bytes 28
  17.0 4.8 %collective-permute-start = (f32[11,1536]{1,0:T(8,128)S(1)}, f32[11,1536]{1,0:T(8,128)S(1)}, u32[]{:S(2)}, u32[]{:S(2)}) collective-permute-start(f32[11,1536]{1,0:T(8,128)S(1)} %pad_maximum_fusion.3), channel_id=1, source_target_pairs={{0,8},{1,9},{2,10},{3,11},{4,12},{5,13},{6,14},{7,15},{8,0},{9,1},... | collective-permute-start | bytes 202760 | tf_op jit(solution)/shard_map/ppermute | solution.py:80
  21.9 7.0 %collective-permute-start.1 = (f32[19,1536]{1,0:T(8,128)S(1)}, f32[19,1536]{1,0:T(8,128)S(1)}, u32[]{:S(2)}, u32[]{:S(2)}) collective-permute-start(f32[19,1536]{1,0:T(8,128)S(1)} %pad_maximum_fusion.2), channel_id=1, source_target_pairs={{0,16},{1,17},{2,18},{3,19},{4,20},{5,21},{6,22},{7,23},{8,24},{9,... | collective-permute-start | bytes 350216 | tf_op jit(solution)/shard_map/ppermute | solution.py:80
  29.0 7.4 %collective-permute-start.2 = (f32[35,1536]{1,0:T(8,128)S(1)}, f32[35,1536]{1,0:T(8,128)S(1)}, u32[]{:S(2)}, u32[]{:S(2)}) collective-permute-start(f32[35,1536]{1,0:T(8,128)S(1)} %pad_maximum_fusion.1), channel_id=1, source_target_pairs={{0,32},{1,33},{2,34},{3,35},{4,36},{5,37},{6,38},{7,39},{8,40},{9,... | collective-permute-start | bytes 645128 | tf_op jit(solution)/shard_map/ppermute | solution.py:80
  36.6 9.9 %collective-permute-start.3 = (f32[67,1536]{1,0:T(8,128)S(1)}, f32[67,1536]{1,0:T(8,128)S(1)}, u32[]{:S(2)}, u32[]{:S(2)}) collective-permute-start(f32[67,1536]{1,0:T(8,128)S(1)} %pad_maximum_fusion), channel_id=1, source_target_pairs={{0,64},{1,65},{2,66},{3,67},{4,68},{5,69},{6,70},{7,71},{8,72},{9,... | collective-permute-start | bytes 1234952 | tf_op jit(solution)/shard_map/ppermute | solution.py:80
  46.5 1.3 %collective-permute-start.4 = (f32[4,1536]{1,0:T(4,128)S(1)}, f32[4,1536]{1,0:T(4,128)S(1)}, u32[]{:S(2)}, u32[]{:S(2)}) collective-permute-start(f32[4,1536]{1,0:T(4,128)S(1)} %pad_maximum_fusion.4), channel_id=1, source_target_pairs={{0,1},{1,0},{2,3},{3,2},{4,5},{5,4},{6,7},{7,6},{8,9},{9,8},{10,11... | collective-permute-start | bytes 73736 | tf_op jit(solution)/shard_map/ppermute | solution.py:80
  47.8 3.9 %collective-permute-start.5 = (f32[4,1536]{1,0:T(4,128)S(1)}, f32[4,1536]{1,0:T(4,128)S(1)}, u32[]{:S(2)}, u32[]{:S(2)}) collective-permute-start(f32[4,1536]{1,0:T(4,128)S(1)} %fusion.40), channel_id=1, source_target_pairs={{0,2},{1,3},{2,0},{3,1},{4,6},{5,7},{6,4},{7,5},{8,10},{9,11},{10,... | collective-permute-start | bytes 73736 | tf_op jit(solution)/shard_map/ppermute | solution.py:80
  49.5 8.1 %copy-start.2 = (s32[1024]{0:T(1024)S(1)}, s32[1024]{0:T(1024)}, u32[]{:S(2)}) copy-start(s32[1024]{0:T(1024)} %param.17) | copy-start | bytes 12292
  49.5 8.5 %copy-start.1 = (f32[96,32]{0,1:T(8,128)S(1)}, f32[96,32]{0,1:T(8,128)}, u32[]{:S(2)}) copy-start(f32[96,32]{0,1:T(8,128)} %param.14) | copy-start | bytes 36868
  51.7 5.4 %collective-permute-start.6 = (f32[4,1536]{1,0:T(4,128)S(1)}, f32[4,1536]{1,0:T(4,128)S(1)}, u32[]{:S(2)}, u32[]{:S(2)}) collective-permute-start(f32[4,1536]{1,0:T(4,128)S(1)} %add.255), channel_id=1, source_target_pairs={{0,4},{1,5},{2,6},{3,7},{4,0},{5,1},{6,2},{7,3},{8,12},{9,13},{10,... | collective-permute-start | bytes 73736 | tf_op jit(solution)/shard_map/ppermute | solution.py:80
  70.1 9.2 %collective-permute-start.7 = (f32[2,1536]{1,0:T(2,128)S(1)}, f32[2,1536]{1,0:T(2,128)S(1)}, u32[]{:S(2)}, u32[]{:S(2)}) collective-permute-start(f32[2,1536]{1,0:T(2,128)S(1)} %pad_maximum_fusion.5), channel_id=1, source_target_pairs={{0,1},{1,2},{2,3},{3,4},{4,5},{5,6},{6,7},{7,8},{8,9},{9,10},{10,1... | collective-permute-start | bytes 36872 | tf_op jit(solution)/shard_map/ppermute | solution.py:178
  80.5 18.8 %collective-permute-start.8 = (f32[2,1536]{1,0:T(2,128)S(1)}, f32[2,1536]{1,0:T(2,128)S(1)}, u32[]{:S(2)}, u32[]{:S(2)}) collective-permute-start(f32[2,1536]{1,0:T(2,128)S(1)} %pad_maximum_fusion.6), channel_id=1, source_target_pairs={{1,0},{2,1},{3,2},{4,3},{5,4},{6,5},{7,6},{8,7},{9,8},{10,9},{11,1... | collective-permute-start | bytes 36872 | tf_op jit(solution)/shard_map/ppermute | solution.py:179
  86.0 12.3 %all-to-all-start = ((f32[8,6,1536]{2,1,0:T(8,128)}), f32[8,6,1536]{2,1,0:T(8,128)S(1)}, u32[]{:S(2)}, u32[]{:S(2)}) async-start(f32[8,6,1536]{2,1,0:T(8,128)} %broadcast_select_fusion), calls=%async_computation | async-start | bytes 786432 | tf_op jit(solution)/shard_map/cond/branch_0_fun/all_to_all | solution.py:162

commit v6 on v5

--- a/solution.py
+++ b/solution.py
@@ -17,7 +17,7 @@
 
 
 HI = lax.Precision.HIGHEST
-BLOCK = 2
+BLOCK = 4
 LANES = (((1,), (1,)), ((), ()))
 
 
@@ -155,14 +155,18 @@
         mine = c_valid & (c_mem == mem)
         c_at = (c_slot // (rows * MEMBERS)) * rows + c_slot % rows
 
-        def route(room):
-            hit = (mine & (c_rank < room))[:, :, None] & (c_rank[:, :, None] == jnp.arange(room, dtype=jnp.int32)[None, None, :])
+        def exchange(room, low):
+            rank = c_rank - low
+            hit = (mine & (rank >= 0) & (rank < room))[:, :, None] & (rank[:, :, None] == jnp.arange(room, dtype=jnp.int32)[None, None, :])
             at = jnp.sum(jnp.where(hit, c_at[:, :, None], 0), axis=1)
             sent = jnp.take(pool, at.reshape(-1), axis=0).reshape(MEMBERS, room, width)
-            came = lax.all_to_all(sent, "mem", 0, 0, tiled=True)
-            return came[m_mem, jnp.minimum(m_rank, room - 1)]
-
-        target = lax.cond(total_over > 0, lambda: route(most), lambda: route(ROOMY))
+            return lax.all_to_all(sent, "mem", 0, 0, tiled=True)
+
+        fast = exchange(ROOMY, 0)
+        spare = most - ROOMY
+        slow = lax.cond(total_over > 0, lambda: exchange(spare, ROOMY), lambda: jnp.zeros((MEMBERS, spare, width), f32))
+        target = jnp.where((m_rank < ROOMY)[:, None], fast[m_mem, jnp.minimum(m_rank, ROOMY - 1)],
+                           slow[m_mem, jnp.clip(m_rank - ROOMY, 0, spare - 1)])
 
         s2t = jnp.tile(s2, (1, INC))
         am = _table_call(_margin_kernel, population, [], [s2t, e2t], INC) * s1[:, :, None]

time: 114 us -> 105 us (0.921)
  Pallas kernels: 24.8 us -> 18.9 us
  waiting for transfers between devices: 37.2 us -> 33.7 us
    pallas_call x3, Pallas kernels: 24.8 us -> 18.9 us  [_table_call(): pl.pallas_call(kernel, grid=grid, in_specs=specs, out_specs=pl.BlockSpec(...]
    all_to_all x1, waiting for transfers between devices: 8.82 us -> 6.1 us  [exchange(): return lax.all_to_all(sent, 'mem', 0, 0, tiled=True)]
where the time goes in v6:
time: 105 us
  waiting for transfers between devices  33.7 us (32%)
  starting transfers between devices  19.5 us (19%)
  Pallas kernels  18.9 us (18%)
  other arithmetic  15.9 us (15%)
  local copies, waits for them, and re-layouts  11.1 us (11%)
  between operations  5.55 us (5%)
    ppermute x7, waiting for transfers between devices, _xor(): return lax.ppermute(x, AXES, [(i, i ^ bit) for i in range(n)])  21.2 us
    pallas_call x3, Pallas kernels, _table_call(): pl.pallas_call(kernel, grid=grid, in_specs=specs, out_specs=pl.BlockSpec(...  18.9 us
    ppermute x7, starting transfers between devices, _xor(): return lax.ppermute(x, AXES, [(i, i ^ bit) for i in range(n)])  12.2 us
    ppermute x1, waiting for transfers between devices, body(): from_left = lax.ppermute(to_right, AXES, right)  6.46 us
    all_to_all x1, waiting for transfers between devices, exchange(): return lax.all_to_all(sent, 'mem', 0, 0, tiled=True)  6.1 us
    all_to_all x1, starting transfers between devices, exchange(): return lax.all_to_all(sent, 'mem', 0, 0, tiled=True)  3.47 us
  transfers between devices with their start and end apart: 10, of which 9 were waited for; matrix products, arithmetic and copies ran while one was open for 7% of the time, Pallas kernels for 0%

profile of v6, /device:TPU:6, one launch (start us, length us, event | category | flops | bytes accessed | tf_op | source)
XLA Modules:
  0.0 104.7 jit_solution(7242410005536939793)
XLA Ops:
  0.0 1.4 %fusion.48 = (s32[1]{0:T(128)}, s32[1]{0:T(128)}) fusion(s32[16]{0:T(128)} %param.16), kind=kLoop, calls=%fused_computation.164 | loop fusion | bytes 16 | tf_op jit(solution)/shard_map/slice | solution.py:103
  2.0 0.9 select_reduce_fusion.2
  2.9 1.9 %compare_and_fusion.3 = (pred[16]{0:T(512)(128)(4,1)S(1)}, s32[16]{0:T(128)S(1)}, pred[16]{0:T(512)(128)(4,1)S(1)}) fusion(s32[16]{0:T(128)} %param.16, s32[]{:T(128)} %bitcast.2, s32[]{:T(128)} %bitcast.3), kind=kLoop, calls=%fused_computation.132 | loop fusion | flops 144 | bytes 168 | tf_op jit(solution)/shard_map/jit(_take)/and | solution.py:187
  7.0 4.8 %shard_map.64 = f32[16,96,32]{2,1,0:T(8,128)} custom-call(f32[16,96,1024]{2,1,0:T(8,128)} %pop_ref.5, bf16[128,32]{1,0:T(8,128)(2,1)} %fusion.12.g1_ref), custom_call_target="tpu_custom_call" | custom-call | tf_op jit(solution)/shard_map/pallas_call | solution.py:70
  11.8 1.5 %reduce_sum.92 = f32[16,96]{1,0:T(8,128)S(1)} reduce(f32[16,96,32]{2,1,0:T(8,128)} %shard_map.64, f32[]{:T(128)} %constant.220.clone.1), dimensions={2}, to_apply=%region_0.1 | reduce | flops 47616 | bytes 202756 | tf_op jit(solution)/shard_map/reduce_sum | solution.py:121
  13.3 1.4 %multiply_reduce_fusion.1 = f32[96,32]{1,0:T(8,128)S(1)} fusion(f32[16,96,32]{2,1,0:T(8,128)} %shard_map.64, f32[16,96]{1,0:T(8,128)S(1)} %div.59), kind=kLoop, calls=%fused_computation.30 | loop fusion | flops 95232 | bytes 215040 | tf_op jit(solution)/shard_map/reduce_sum | solution.py:123
  14.9 2.0 %collective-permute-start = (f32[11,1536]{1,0:T(8,128)S(1)}, f32[11,1536]{1,0:T(8,128)S(1)}, u32[]{:S(2)}, u32[]{:S(2)}) collective-permute-start(f32[11,1536]{1,0:T(8,128)S(1)} %pad_maximum_fusion.3), channel_id=1, source_target_pairs={{0,8},{1,9},{2,10},{3,11},{4,12},{5,13},{6,14},{7,15},{8,0},{9,1},... | collective-permute-start | bytes 202760 | tf_op jit(solution)/shard_map/ppermute | solution.py:80
  18.9 0.8 collective-permute-done
  19.8 3.9 %collective-permute-start.1 = (f32[19,1536]{1,0:T(8,128)S(1)}, f32[19,1536]{1,0:T(8,128)S(1)}, u32[]{:S(2)}, u32[]{:S(2)}) collective-permute-start(f32[19,1536]{1,0:T(8,128)S(1)} %pad_maximum_fusion.2), channel_id=1, source_target_pairs={{0,16},{1,17},{2,18},{3,19},{4,20},{5,21},{6,22},{7,23},{8,24},{9,... | collective-permute-start | bytes 350216 | tf_op jit(solution)/shard_map/ppermute | solution.py:80
  25.7 1.1 %collective-permute-done.1 = f32[19,1536]{1,0:T(8,128)S(1)} collective-permute-done((f32[19,1536]{1,0:T(8,128)S(1)}, f32[19,1536]{1,0:T(8,128)S(1)}, u32[]{:S(2)}, u32[]{:S(2)}) %collective-permute-start.1) | collective-permute-done | bytes 116768 | tf_op jit(solution)/shard_map/ppermute | solution.py:80
  26.9 0.9 collective-permute-start.2
  27.8 6.5 %collective-permute-done.2 = f32[35,1536]{1,0:T(8,128)S(1)} collective-permute-done((f32[35,1536]{1,0:T(8,128)S(1)}, f32[35,1536]{1,0:T(8,128)S(1)}, u32[]{:S(2)}, u32[]{:S(2)}) %collective-permute-start.2) | collective-permute-done | bytes 215072 | tf_op jit(solution)/shard_map/ppermute | solution.py:80
  34.8 0.9 fusion.10.e2t_ref
  35.7 8.6 %collective-permute-done.3 = f32[67,1536]{1,0:T(8,128)S(1)} collective-permute-done((f32[67,1536]{1,0:T(8,128)S(1)}, f32[67,1536]{1,0:T(8,128)S(1)}, u32[]{:S(2)}, u32[]{:S(2)}) %collective-permute-start.3) | collective-permute-done | bytes 411680 | tf_op jit(solution)/shard_map/ppermute | solution.py:80
  44.5 1.2 %collective-permute-done.4 = f32[4,1536]{1,0:T(4,128)S(1)} collective-permute-done((f32[4,1536]{1,0:T(4,128)S(1)}, f32[4,1536]{1,0:T(4,128)S(1)}, u32[]{:S(2)}, u32[]{:S(2)}) %collective-permute-start.4) | collective-permute-done | bytes 24608 | tf_op jit(solution)/shard_map/ppermute | solution.py:80
  45.7 1.7 %collective-permute-start.5 = (f32[4,1536]{1,0:T(4,128)S(1)}, f32[4,1536]{1,0:T(4,128)S(1)}, u32[]{:S(2)}, u32[]{:S(2)}) collective-permute-start(f32[4,1536]{1,0:T(4,128)S(1)} %fusion.46), channel_id=1, source_target_pairs={{0,2},{1,3},{2,0},{3,1},{4,6},{5,7},{6,4},{7,5},{8,10},{9,11},{10,... | collective-permute-start | bytes 73736 | tf_op jit(solution)/shard_map/ppermute | solution.py:80
  47.4 1.2 %copy.46.s1_ref = f32[16,96,1]{2,1,0:T(8,128)} copy(f32[16,96,1]{1,0,2:T(8,128)S(1)} %bitcast.43) | data formatting | bytes 12288 | tf_op jit(solution)/shard_map/broadcast_in_dim | solution.py:190
  48.7 1.0 collective-permute-done.5
  49.6 3.3 %collective-permute-start.6 = (f32[4,1536]{1,0:T(4,128)S(1)}, f32[4,1536]{1,0:T(4,128)S(1)}, u32[]{:S(2)}, u32[]{:S(2)}) collective-permute-start(f32[4,1536]{1,0:T(4,128)S(1)} %add.333), channel_id=1, source_target_pairs={{0,4},{1,5},{2,6},{3,7},{4,0},{5,1},{6,2},{7,3},{8,12},{9,13},{10,... | collective-permute-start | bytes 73736 | tf_op jit(solution)/shard_map/ppermute | solution.py:80
  53.0 2.0 %collective-permute-done.6 = f32[4,1536]{1,0:T(4,128)S(1)} collective-permute-done((f32[4,1536]{1,0:T(4,128)S(1)}, f32[4,1536]{1,0:T(4,128)S(1)}, u32[]{:S(2)}, u32[]{:S(2)}) %collective-permute-start.6) | collective-permute-done | bytes 24608 | tf_op jit(solution)/shard_map/ppermute | solution.py:80
  57.7 0.9 copy.45.s2t_ref
  58.7 6.3 %shard_map.65 = f32[16,96,32]{2,1,0:T(8,128)} custom-call(f32[16,96,1024]{2,1,0:T(8,128)} %pop_ref.5, f32[96,1024]{1,0:T(8,128)} %copy.45.s2t_ref, bf16[1024,32]{1,0:T(8,128)(2,1)} %fusion.10.e2t_ref), custom_call_target="tpu_custom_call" | custom-call | tf_op jit(solution)/shard_map/pallas_call | solution.py:70
  65.0 1.4 %broadcast_multiply_fusion = f32[16,96,32]{2,1,0:T(8,128)S(1)} fusion(f32[16,96,32]{2,1,0:T(8,128)} %shard_map.65, f32[16,96]{1,0:T(8,128)S(1)} %div.59), kind=kLoop, calls=%fused_computation.36 | loop fusion | flops 49152 | bytes 399360 | tf_op jit(solution)/shard_map/mul | solution.py:172
  66.4 1.0 reduce_sum.100
  67.8 1.9 %collective-permute-start.7 = (f32[2,1536]{1,0:T(2,128)S(1)}, f32[2,1536]{1,0:T(2,128)S(1)}, u32[]{:S(2)}, u32[]{:S(2)}) collective-permute-start(f32[2,1536]{1,0:T(2,128)S(1)} %pad_maximum_fusion.5), channel_id=1, source_target_pairs={{0,1},{1,2},{2,3},{3,4},{4,5},{5,6},{6,7},{7,8},{8,9},{9,10},{10,1... | collective-permute-start | bytes 36872 | tf_op jit(solution)/shard_map/ppermute | solution.py:182
  69.7 0.8 broadcast_select_fusion.2
  70.5 6.5 %collective-permute-done.7 = f32[2,1536]{1,0:T(2,128)S(1)} collective-permute-done((f32[2,1536]{1,0:T(2,128)S(1)}, f32[2,1536]{1,0:T(2,128)S(1)}, u32[]{:S(2)}, u32[]{:S(2)}) %collective-permute-start.7) | collective-permute-done | bytes 12320 | tf_op jit(solution)/shard_map/ppermute | solution.py:182
  78.2 1.9 %collective-permute-start.8 = (f32[2,1536]{1,0:T(2,128)S(1)}, f32[2,1536]{1,0:T(2,128)S(1)}, u32[]{:S(2)}, u32[]{:S(2)}) collective-permute-start(f32[2,1536]{1,0:T(2,128)S(1)} %pad_maximum_fusion.6), channel_id=1, source_target_pairs={{1,0},{2,1},{3,2},{4,3},{5,4},{6,5},{7,6},{8,7},{9,8},{10,9},{11,1... | collective-permute-start | bytes 36872 | tf_op jit(solution)/shard_map/ppermute | solution.py:183
  81.5 3.5 %all-to-all-start.1 = ((f32[8,6,1536]{2,1,0:T(8,128)}), f32[8,6,1536]{2,1,0:T(8,128)S(1)}, u32[]{:S(2)}, u32[]{:S(2)}) async-start(f32[8,6,1536]{2,1,0:T(8,128)} %broadcast_select_fusion.2), calls=%async_computation.1 | async-start | bytes 786432 | tf_op jit(solution)/shard_map/all_to_all | solution.py:163
  87.8 6.1 %all-to-all-done.1 = f32[8,6,1536]{2,1,0:T(8,128)S(1)} async-done(((f32[8,6,1536]{2,1,0:T(8,128)}), f32[8,6,1536]{2,1,0:T(8,128)S(1)}, u32[]{:S(2)}, u32[]{:S(2)}) %all-to-all-start.1) | async-done | bytes 294944 | tf_op jit(solution)/shard_map/all_to_all | solution.py:163
  95.6 1.3 %broadcast_in_dim.178 = f32[16,48,2,32]{3,2,1,0:T(2,128)} broadcast(f32[16,48,32]{2,1,0:T(8,128)S(1)} %broadcast_select_fusion.1), dimensions={0,1,3} | broadcast | bytes 294912 | tf_op jit(solution)/shard_map/broadcast_in_dim | solution.py:189
  96.9 7.8 %shard_map.66 = f32[16,96,1024]{2,1,0:T(8,128)} custom-call(f32[16,96,1024]{2,1,0:T(8,128)} %pop_ref.5, f32[16,96,1]{2,1,0:T(8,128)} %copy.46.s1_ref, f32[16,96,32]{2,1,0:T(8,128)} %bitcast.40, f32[96,1024]{1,0:T(8,128)} %copy.45.s2t_ref, bf16[32,1024]{1,0:T(8,128)(2,1)} %fusion.11.e2_ref), custom_call_target="tpu_custom_call" | custom-call | tf_op jit(solution)/shard_map/pallas_call | solution.py:70
  (108 shorter events, 12.9 us)
Async XLA Ops:
  7.0 6.3 %copy-start.3 = (f32[16,96]{1,0:T(8,128)S(1)}, f32[16,96]{1,0:T(8,128)}, u32[]{:S(2)}) copy-start(f32[16,96]{1,0:T(8,128)} %param.13) | copy-start | bytes 18436
  11.8 3.0 %copy-start = (f32[8,1536]{1,0:T(8,128)S(1)}, f32[8,1536]{1,0:T(8,128)}, u32[]{:S(2)}) copy-start(f32[8,1536]{1,0:T(8,128)} %param.15) | copy-start | bytes 147460
  11.8 13.1 %copy-start.4 = (s32[2]{0:T(128)S(1)}, s32[2]{0:T(128)}, u32[]{:S(2)}) copy-start(s32[2]{0:T(128)} %constant.247.clone.1) | copy-start | bytes 28
  14.9 4.8 %collective-permute-start = (f32[11,1536]{1,0:T(8,128)S(1)}, f32[11,1536]{1,0:T(8,128)S(1)}, u32[]{:S(2)}, u32[]{:S(2)}) collective-permute-start(f32[11,1536]{1,0:T(8,128)S(1)} %pad_maximum_fusion.3), channel_id=1, source_target_pairs={{0,8},{1,9},{2,10},{3,11},{4,12},{5,13},{6,14},{7,15},{8,0},{9,1},... | collective-permute-start | bytes 202760 | tf_op jit(solution)/shard_map/ppermute | solution.py:80
  19.8 7.0 %collective-permute-start.1 = (f32[19,1536]{1,0:T(8,128)S(1)}, f32[19,1536]{1,0:T(8,128)S(1)}, u32[]{:S(2)}, u32[]{:S(2)}) collective-permute-start(f32[19,1536]{1,0:T(8,128)S(1)} %pad_maximum_fusion.2), channel_id=1, source_target_pairs={{0,16},{1,17},{2,18},{3,19},{4,20},{5,21},{6,22},{7,23},{8,24},{9,... | collective-permute-start | bytes 350216 | tf_op jit(solution)/shard_map/ppermute | solution.py:80
  26.9 7.4 %collective-permute-start.2 = (f32[35,1536]{1,0:T(8,128)S(1)}, f32[35,1536]{1,0:T(8,128)S(1)}, u32[]{:S(2)}, u32[]{:S(2)}) collective-permute-start(f32[35,1536]{1,0:T(8,128)S(1)} %pad_maximum_fusion.1), channel_id=1, source_target_pairs={{0,32},{1,33},{2,34},{3,35},{4,36},{5,37},{6,38},{7,39},{8,40},{9,... | collective-permute-start | bytes 645128 | tf_op jit(solution)/shard_map/ppermute | solution.py:80
  34.5 9.9 %collective-permute-start.3 = (f32[67,1536]{1,0:T(8,128)S(1)}, f32[67,1536]{1,0:T(8,128)S(1)}, u32[]{:S(2)}, u32[]{:S(2)}) collective-permute-start(f32[67,1536]{1,0:T(8,128)S(1)} %pad_maximum_fusion), channel_id=1, source_target_pairs={{0,64},{1,65},{2,66},{3,67},{4,68},{5,69},{6,70},{7,71},{8,72},{9,... | collective-permute-start | bytes 1234952 | tf_op jit(solution)/shard_map/ppermute | solution.py:80
  44.4 1.3 %collective-permute-start.4 = (f32[4,1536]{1,0:T(4,128)S(1)}, f32[4,1536]{1,0:T(4,128)S(1)}, u32[]{:S(2)}, u32[]{:S(2)}) collective-permute-start(f32[4,1536]{1,0:T(4,128)S(1)} %pad_maximum_fusion.4), channel_id=1, source_target_pairs={{0,1},{1,0},{2,3},{3,2},{4,5},{5,4},{6,7},{7,6},{8,9},{9,8},{10,11... | collective-permute-start | bytes 73736 | tf_op jit(solution)/shard_map/ppermute | solution.py:80
  45.7 3.9 %collective-permute-start.5 = (f32[4,1536]{1,0:T(4,128)S(1)}, f32[4,1536]{1,0:T(4,128)S(1)}, u32[]{:S(2)}, u32[]{:S(2)}) collective-permute-start(f32[4,1536]{1,0:T(4,128)S(1)} %fusion.46), channel_id=1, source_target_pairs={{0,2},{1,3},{2,0},{3,1},{4,6},{5,7},{6,4},{7,5},{8,10},{9,11},{10,... | collective-permute-start | bytes 73736 | tf_op jit(solution)/shard_map/ppermute | solution.py:80
  47.4 8.2 %copy-start.2 = (s32[1024]{0:T(1024)S(1)}, s32[1024]{0:T(1024)}, u32[]{:S(2)}) copy-start(s32[1024]{0:T(1024)} %param.17) | copy-start | bytes 12292
  49.6 5.4 %collective-permute-start.6 = (f32[4,1536]{1,0:T(4,128)S(1)}, f32[4,1536]{1,0:T(4,128)S(1)}, u32[]{:S(2)}, u32[]{:S(2)}) collective-permute-start(f32[4,1536]{1,0:T(4,128)S(1)} %add.333), channel_id=1, source_target_pairs={{0,4},{1,5},{2,6},{3,7},{4,0},{5,1},{6,2},{7,3},{8,12},{9,13},{10,... | collective-permute-start | bytes 73736 | tf_op jit(solution)/shard_map/ppermute | solution.py:80
  56.9 0.8 copy-start.1
  67.8 9.2 %collective-permute-start.7 = (f32[2,1536]{1,0:T(2,128)S(1)}, f32[2,1536]{1,0:T(2,128)S(1)}, u32[]{:S(2)}, u32[]{:S(2)}) collective-permute-start(f32[2,1536]{1,0:T(2,128)S(1)} %pad_maximum_fusion.5), channel_id=1, source_target_pairs={{0,1},{1,2},{2,3},{3,4},{4,5},{5,6},{6,7},{7,8},{8,9},{9,10},{10,1... | collective-permute-start | bytes 36872 | tf_op jit(solution)/shard_map/ppermute | solution.py:182
  78.2 7.6 %collective-permute-start.8 = (f32[2,1536]{1,0:T(2,128)S(1)}, f32[2,1536]{1,0:T(2,128)S(1)}, u32[]{:S(2)}, u32[]{:S(2)}) collective-permute-start(f32[2,1536]{1,0:T(2,128)S(1)} %pad_maximum_fusion.6), channel_id=1, source_target_pairs={{1,0},{2,1},{3,2},{4,3},{5,4},{6,5},{7,6},{8,7},{9,8},{10,9},{11,1... | collective-permute-start | bytes 36872 | tf_op jit(solution)/shard_map/ppermute | solution.py:183
  81.5 12.3 %all-to-all-start.1 = ((f32[8,6,1536]{2,1,0:T(8,128)}), f32[8,6,1536]{2,1,0:T(8,128)S(1)}, u32[]{:S(2)}, u32[]{:S(2)}) async-start(f32[8,6,1536]{2,1,0:T(8,128)} %broadcast_select_fusion.2), calls=%async_computation.1 | async-start | bytes 786432 | tf_op jit(solution)/shard_map/all_to_all | solution.py:163

commit v7 on v6

--- a/solution.py
+++ b/solution.py
@@ -55,10 +55,10 @@
         o_ref[b] = _dot3(pop_ref[b] * s2t_ref[...], e2t_ref[...], ROWS)
 
 
-def _fit_kernel(pop_ref, s1_ref, r_ref, s2t_ref, e2_ref, o_ref):
+def _fit_kernel(pop_ref, r_ref, s2t_ref, e2_ref, o_ref):
     for b in range(pop_ref.shape[0]):
         rep = _dot3(r_ref[b], e2_ref[...], ROWS)
-        o_ref[b] = pop_ref[b] * (s1_ref[b] * s2t_ref[...]) * rep
+        o_ref[b] = pop_ref[b] * s2t_ref[...] * rep
 
 
 def _table_call(kernel, table, smalls, consts, out_last):
@@ -112,11 +112,11 @@
         m_rank = jnp.sum(((m_mem[:, None] == m_mem[None, :]) & m_valid[None, :] & (ks[None, :] < ks[:, None])).astype(jnp.int32), axis=1)
         over = jnp.any(m_valid & (m_rank >= ROOMY)).astype(f32)
 
-        lane = jnp.arange(INC * HH * TU, dtype=jnp.int32)
         bf = jnp.bfloat16
-        g1 = (jnp.arange(128, dtype=jnp.int32)[:, None] % (HH * TU) == jnp.arange(HH * TU, dtype=jnp.int32)[None, :]).astype(bf)
-        e2 = (lane[None, :] // (HH * TU) == jnp.arange(INC, dtype=jnp.int32)[:, None]).astype(bf)
-        e2t = e2.T
+        g1 = jnp.asarray(np.arange(128)[:, None] % (HH * TU) == np.arange(HH * TU)[None, :], bf)
+        e2_np = np.arange(INC * HH * TU)[None, :] // (HH * TU) == np.arange(INC)[:, None]
+        e2 = jnp.asarray(e2_np, bf)
+        e2t = jnp.asarray(e2_np.T, bf)
         t1 = _table_call(_sum_kernel, population, [], [g1], HH * TU)
         area_sum = jnp.sum(t1, axis=2)
         s1 = area_target / area_sum
@@ -186,8 +186,8 @@
         ratio = target / zp
         ratio_a = jnp.take(ratio, k_a, axis=0)
 
-        r96 = jnp.repeat(ratio_a.reshape(count, AGE, INC), SEX, axis=1)
-        return _table_call(_fit_kernel, population, [s1[:, :, None], r96], [s2t, e2], INC * HH * TU)
+        r96 = jnp.repeat(ratio_a.reshape(count, AGE, INC), SEX, axis=1) * s1[:, :, None]
+        return _table_call(_fit_kernel, population, [r96], [s2t, e2], INC * HH * TU)
 
     return body
 

time: 105 us -> 105 us (level)
  waiting for transfers between devices: 33.7 us -> 36.3 us
  local copies, waits for them, and re-layouts: 11.1 us -> 8.97 us
    ppermute x7, waiting for transfers between devices: 21.2 us -> 23.8 us  [_xor(): return lax.ppermute(x, AXES, [(i, i ^ bit) for i in range(n)])]
    convert_element_type x3 -> x0, other arithmetic: 2.24 us -> none  [the longest x2 1.55 us: body(): (lane[None, :] // (HH * TU) == jnp.arange(INC, dtype=jnp.int32)[:, None])...]
    broadcast_in_dim x2 -> x1, local copies, waits for them, and re-layouts: 2.5 us -> 0.4 us  [body(): jnp.repeat(ratio_a.reshape(count, AGE, INC), SEX, axis=1) * s1[:, :, None]]
    mul x0 -> x1, other arithmetic: none -> 1.15 us  [body(): jnp.repeat(ratio_a.reshape(count, AGE, INC), SEX, axis=1) * s1[:, :, None]]
  transfers between devices with their start and end apart: 10 -> 10, of which waited for: 9 -> 9; matrix products, arithmetic and copies ran while one was open for 7% -> 4% of each run, Pallas kernels for 0% -> 0%
where the time goes in v7:
time: 105 us; the launch traced here: 104 us
  waiting for transfers between devices  36.3 us (35%)
  starting transfers between devices  19.5 us (19%)
  Pallas kernels  18.6 us (18%)
  other arithmetic  15 us (14%)
  local copies, waits for them, and re-layouts  8.97 us (9%)
  between operations  5.71 us (5%)
    ppermute x7, waiting for transfers between devices, _xor(): return lax.ppermute(x, AXES, [(i, i ^ bit) for i in range(n)])  23.8 us
    pallas_call x3, Pallas kernels, _table_call(): pl.pallas_call(kernel, grid=grid, in_specs=specs, out_specs=pl.BlockSpec(...  18.6 us
    ppermute x7, starting transfers between devices, _xor(): return lax.ppermute(x, AXES, [(i, i ^ bit) for i in range(n)])  12.2 us
    ppermute x1, waiting for transfers between devices, body(): from_left = lax.ppermute(to_right, AXES, right)  6.46 us
    all_to_all x1, waiting for transfers between devices, exchange(): return lax.all_to_all(sent, 'mem', 0, 0, tiled=True)  6.1 us
    all_to_all x1, starting transfers between devices, exchange(): return lax.all_to_all(sent, 'mem', 0, 0, tiled=True)  3.47 us
  transfers between devices with their start and end apart: 10, of which 9 were waited for; matrix products, arithmetic and copies ran while one was open for 4% of the time, Pallas kernels for 0%

profile of v7, /device:TPU:6, one launch (start us, length us, event | category | flops | bytes accessed | tf_op | source)
XLA Modules:
  0.0 104.1 jit_solution(1796891987875189172)
XLA Ops:
  0.0 1.3 %fusion.42 = (s32[1]{0:T(128)}, s32[1]{0:T(128)}) fusion(s32[16]{0:T(128)} %param.19), kind=kLoop, calls=%fused_computation.151 | loop fusion | bytes 16 | tf_op jit(solution)/shard_map/slice | solution.py:103
  2.0 0.9 select_reduce_fusion.2
  2.9 2.0 %compare_and_fusion.3 = (pred[16]{0:T(512)(128)(4,1)S(1)}, s32[16]{0:T(128)S(1)}, pred[16]{0:T(512)(128)(4,1)S(1)}) fusion(s32[16]{0:T(128)} %param.19, s32[]{:T(128)} %bitcast.1, s32[]{:T(128)} %bitcast.2), kind=kLoop, calls=%fused_computation.120 | loop fusion | flops 144 | bytes 168 | tf_op jit(solution)/shard_map/jit(_take)/and | solution.py:187
  6.4 4.8 %shard_map.91 = f32[16,96,32]{2,1,0:T(8,128)} custom-call(f32[16,96,1024]{2,1,0:T(8,128)} %pop_ref.5, bf16[128,32]{1,0:T(8,128)(2,1)} %constant.230.clone.g1_ref), custom_call_target="tpu_custom_call" | custom-call | tf_op jit(solution)/shard_map/pallas_call | solution.py:70
  11.2 1.5 %reduce_sum.94 = f32[16,96]{1,0:T(8,128)S(1)} reduce(f32[16,96,32]{2,1,0:T(8,128)} %shard_map.91, f32[]{:T(128)} %constant.209.clone.1), dimensions={2}, to_apply=%region_2.3 | reduce | flops 47616 | bytes 202756 | tf_op jit(solution)/shard_map/reduce_sum | solution.py:121
  12.7 1.4 %multiply_reduce_fusion.1 = f32[96,32]{1,0:T(8,128)S(1)} fusion(f32[16,96,32]{2,1,0:T(8,128)} %shard_map.91, f32[16,96]{1,0:T(8,128)S(1)} %div.53), kind=kLoop, calls=%fused_computation.30 | loop fusion | flops 95232 | bytes 215040 | tf_op jit(solution)/shard_map/reduce_sum | solution.py:123
  14.3 2.0 %collective-permute-start = (f32[11,1536]{1,0:T(8,128)S(1)}, f32[11,1536]{1,0:T(8,128)S(1)}, u32[]{:S(2)}, u32[]{:S(2)}) collective-permute-start(f32[11,1536]{1,0:T(8,128)S(1)} %pad_maximum_fusion.3), channel_id=1, source_target_pairs={{0,8},{1,9},{2,10},{3,11},{4,12},{5,13},{6,14},{7,15},{8,0},{9,1},... | collective-permute-start | bytes 202760 | tf_op jit(solution)/shard_map/ppermute | solution.py:80
  17.7 1.4 %collective-permute-done = f32[11,1536]{1,0:T(8,128)S(1)} collective-permute-done((f32[11,1536]{1,0:T(8,128)S(1)}, f32[11,1536]{1,0:T(8,128)S(1)}, u32[]{:S(2)}, u32[]{:S(2)}) %collective-permute-start) | collective-permute-done | bytes 67616 | tf_op jit(solution)/shard_map/ppermute | solution.py:80
  19.2 3.9 %collective-permute-start.1 = (f32[19,1536]{1,0:T(8,128)S(1)}, f32[19,1536]{1,0:T(8,128)S(1)}, u32[]{:S(2)}, u32[]{:S(2)}) collective-permute-start(f32[19,1536]{1,0:T(8,128)S(1)} %pad_maximum_fusion.2), channel_id=1, source_target_pairs={{0,16},{1,17},{2,18},{3,19},{4,20},{5,21},{6,22},{7,23},{8,24},{9,... | collective-permute-start | bytes 350216 | tf_op jit(solution)/shard_map/ppermute | solution.py:80
  24.4 0.7 and_reduce_fusion
  25.2 1.0 collective-permute-done.1
  26.3 0.9 collective-permute-start.2
  27.2 6.5 %collective-permute-done.2 = f32[35,1536]{1,0:T(8,128)S(1)} collective-permute-done((f32[35,1536]{1,0:T(8,128)S(1)}, f32[35,1536]{1,0:T(8,128)S(1)}, u32[]{:S(2)}, u32[]{:S(2)}) %collective-permute-start.2) | collective-permute-done | bytes 215072 | tf_op jit(solution)/shard_map/ppermute | solution.py:80
  34.3 9.5 %collective-permute-done.3 = f32[67,1536]{1,0:T(8,128)S(1)} collective-permute-done((f32[67,1536]{1,0:T(8,128)S(1)}, f32[67,1536]{1,0:T(8,128)S(1)}, u32[]{:S(2)}, u32[]{:S(2)}) %collective-permute-start.3) | collective-permute-done | bytes 411680 | tf_op jit(solution)/shard_map/ppermute | solution.py:80
  43.9 1.2 %collective-permute-done.4 = f32[4,1536]{1,0:T(4,128)S(1)} collective-permute-done((f32[4,1536]{1,0:T(4,128)S(1)}, f32[4,1536]{1,0:T(4,128)S(1)}, u32[]{:S(2)}, u32[]{:S(2)}) %collective-permute-start.4) | collective-permute-done | bytes 24608 | tf_op jit(solution)/shard_map/ppermute | solution.py:80
  45.1 1.7 %collective-permute-start.5 = (f32[4,1536]{1,0:T(4,128)S(1)}, f32[4,1536]{1,0:T(4,128)S(1)}, u32[]{:S(2)}, u32[]{:S(2)}) collective-permute-start(f32[4,1536]{1,0:T(4,128)S(1)} %fusion.40), channel_id=1, source_target_pairs={{0,2},{1,3},{2,0},{3,1},{4,6},{5,7},{6,4},{7,5},{8,10},{9,11},{10,... | collective-permute-start | bytes 73736 | tf_op jit(solution)/shard_map/ppermute | solution.py:80
  46.9 2.2 %collective-permute-done.5 = f32[4,1536]{1,0:T(4,128)S(1)} collective-permute-done((f32[4,1536]{1,0:T(4,128)S(1)}, f32[4,1536]{1,0:T(4,128)S(1)}, u32[]{:S(2)}, u32[]{:S(2)}) %collective-permute-start.5) | collective-permute-done | bytes 24608 | tf_op jit(solution)/shard_map/ppermute | solution.py:80
  49.1 3.3 %collective-permute-start.6 = (f32[4,1536]{1,0:T(4,128)S(1)}, f32[4,1536]{1,0:T(4,128)S(1)}, u32[]{:S(2)}, u32[]{:S(2)}) collective-permute-start(f32[4,1536]{1,0:T(4,128)S(1)} %add.315), channel_id=1, source_target_pairs={{0,4},{1,5},{2,6},{3,7},{4,0},{5,1},{6,2},{7,3},{8,12},{9,13},{10,... | collective-permute-start | bytes 73736 | tf_op jit(solution)/shard_map/ppermute | solution.py:80
  52.4 2.0 %collective-permute-done.6 = f32[4,1536]{1,0:T(4,128)S(1)} collective-permute-done((f32[4,1536]{1,0:T(4,128)S(1)}, f32[4,1536]{1,0:T(4,128)S(1)}, u32[]{:S(2)}, u32[]{:S(2)}) %collective-permute-start.6) | collective-permute-done | bytes 24608 | tf_op jit(solution)/shard_map/ppermute | solution.py:80
  56.3 0.7 gather_fusion.1
  57.1 0.9 copy.45.s2t_ref
  58.1 6.3 %shard_map.92 = f32[16,96,32]{2,1,0:T(8,128)} custom-call(f32[16,96,1024]{2,1,0:T(8,128)} %pop_ref.5, f32[96,1024]{1,0:T(8,128)} %copy.45.s2t_ref, bf16[1024,32]{1,0:T(8,128)(2,1)} %constant.232.clone.e2t_ref), custom_call_target="tpu_custom_call" | custom-call | tf_op jit(solution)/shard_map/pallas_call | solution.py:70
  64.4 1.4 %broadcast_multiply_fusion.1 = f32[16,96,32]{2,1,0:T(8,128)S(1)} fusion(f32[16,96,32]{2,1,0:T(8,128)} %shard_map.92, f32[16,96]{1,0:T(8,128)S(1)} %div.53), kind=kLoop, calls=%fused_computation.35 | loop fusion | flops 49152 | bytes 399360 | tf_op jit(solution)/shard_map/mul | solution.py:172
  65.8 1.0 reduce_sum.100
  67.2 1.9 %collective-permute-start.7 = (f32[2,1536]{1,0:T(2,128)S(1)}, f32[2,1536]{1,0:T(2,128)S(1)}, u32[]{:S(2)}, u32[]{:S(2)}) collective-permute-start(f32[2,1536]{1,0:T(2,128)S(1)} %pad_maximum_fusion.5), channel_id=1, source_target_pairs={{0,1},{1,2},{2,3},{3,4},{4,5},{5,6},{6,7},{7,8},{8,9},{9,10},{10,1... | collective-permute-start | bytes 36872 | tf_op jit(solution)/shard_map/ppermute | solution.py:182
  69.1 0.8 broadcast_select_fusion.2
  69.9 6.5 %collective-permute-done.7 = f32[2,1536]{1,0:T(2,128)S(1)} collective-permute-done((f32[2,1536]{1,0:T(2,128)S(1)}, f32[2,1536]{1,0:T(2,128)S(1)}, u32[]{:S(2)}, u32[]{:S(2)}) %collective-permute-start.7) | collective-permute-done | bytes 12320 | tf_op jit(solution)/shard_map/ppermute | solution.py:182
  77.7 1.9 %collective-permute-start.8 = (f32[2,1536]{1,0:T(2,128)S(1)}, f32[2,1536]{1,0:T(2,128)S(1)}, u32[]{:S(2)}, u32[]{:S(2)}) collective-permute-start(f32[2,1536]{1,0:T(2,128)S(1)} %pad_maximum_fusion.6), channel_id=1, source_target_pairs={{1,0},{2,1},{3,2},{4,3},{5,4},{6,5},{7,6},{8,7},{9,8},{10,9},{11,1... | collective-permute-start | bytes 36872 | tf_op jit(solution)/shard_map/ppermute | solution.py:183
  81.0 3.5 %all-to-all-start.1 = ((f32[8,6,1536]{2,1,0:T(8,128)}), f32[8,6,1536]{2,1,0:T(8,128)S(1)}, u32[]{:S(2)}, u32[]{:S(2)}) async-start(f32[8,6,1536]{2,1,0:T(8,128)} %broadcast_select_fusion.2), calls=%async_computation.1 | async-start | bytes 786432 | tf_op jit(solution)/shard_map/all_to_all | solution.py:163
  87.2 6.1 %all-to-all-done.1 = f32[8,6,1536]{2,1,0:T(8,128)S(1)} async-done(((f32[8,6,1536]{2,1,0:T(8,128)}), f32[8,6,1536]{2,1,0:T(8,128)S(1)}, u32[]{:S(2)}, u32[]{:S(2)}) %all-to-all-start.1) | async-done | bytes 294944 | tf_op jit(solution)/shard_map/all_to_all | solution.py:163
  95.4 1.2 %broadcast_multiply_fusion.r_ref = f32[16,96,32]{2,1,0:T(8,128)} fusion(f32[16,96,32]{2,1,0:T(8,128)S(1)} %bitcast.40, f32[16,96]{1,0:T(8,128)S(1)} %div.53), kind=kLoop, calls=%fused_computation.34 | loop fusion | flops 49152 | bytes 399360 | tf_op jit(solution)/shard_map/mul | solution.py:189
  96.6 7.5 %shard_map.93 = f32[16,96,1024]{2,1,0:T(8,128)} custom-call(f32[16,96,1024]{2,1,0:T(8,128)} %pop_ref.5, f32[16,96,32]{2,1,0:T(8,128)} %broadcast_multiply_fusion.r_ref, f32[96,1024]{1,0:T(8,128)} %copy.45.s2t_ref, bf16[32,1024]{1,0:T(8,128)(2,1)} %constant.231.clone.e2_ref), custom_call_target="tpu_custom_call" | custom-call | tf_op jit(solution)/shard_map/pallas_call | solution.py:70
  (103 shorter events, 10.6 us)
Async XLA Ops:
  6.4 6.3 %copy-start.3 = (f32[16,96]{1,0:T(8,128)S(1)}, f32[16,96]{1,0:T(8,128)}, u32[]{:S(2)}) copy-start(f32[16,96]{1,0:T(8,128)} %param.16) | copy-start | bytes 18436
  11.2 3.0 %copy-start = (f32[8,1536]{1,0:T(8,128)S(1)}, f32[8,1536]{1,0:T(8,128)}, u32[]{:S(2)}) copy-start(f32[8,1536]{1,0:T(8,128)} %param.18) | copy-start | bytes 147460
  11.2 13.2 %copy-start.4 = (s32[2]{0:T(128)S(1)}, s32[2]{0:T(128)}, u32[]{:S(2)}) copy-start(s32[2]{0:T(128)} %constant.228.clone.1) | copy-start | bytes 28
  14.3 4.8 %collective-permute-start = (f32[11,1536]{1,0:T(8,128)S(1)}, f32[11,1536]{1,0:T(8,128)S(1)}, u32[]{:S(2)}, u32[]{:S(2)}) collective-permute-start(f32[11,1536]{1,0:T(8,128)S(1)} %pad_maximum_fusion.3), channel_id=1, source_target_pairs={{0,8},{1,9},{2,10},{3,11},{4,12},{5,13},{6,14},{7,15},{8,0},{9,1},... | collective-permute-start | bytes 202760 | tf_op jit(solution)/shard_map/ppermute | solution.py:80
  19.2 7.0 %collective-permute-start.1 = (f32[19,1536]{1,0:T(8,128)S(1)}, f32[19,1536]{1,0:T(8,128)S(1)}, u32[]{:S(2)}, u32[]{:S(2)}) collective-permute-start(f32[19,1536]{1,0:T(8,128)S(1)} %pad_maximum_fusion.2), channel_id=1, source_target_pairs={{0,16},{1,17},{2,18},{3,19},{4,20},{5,21},{6,22},{7,23},{8,24},{9,... | collective-permute-start | bytes 350216 | tf_op jit(solution)/shard_map/ppermute | solution.py:80
  26.3 7.4 %collective-permute-start.2 = (f32[35,1536]{1,0:T(8,128)S(1)}, f32[35,1536]{1,0:T(8,128)S(1)}, u32[]{:S(2)}, u32[]{:S(2)}) collective-permute-start(f32[35,1536]{1,0:T(8,128)S(1)} %pad_maximum_fusion.1), channel_id=1, source_target_pairs={{0,32},{1,33},{2,34},{3,35},{4,36},{5,37},{6,38},{7,39},{8,40},{9,... | collective-permute-start | bytes 645128 | tf_op jit(solution)/shard_map/ppermute | solution.py:80
  33.9 21.1 %copy-start.2 = (s32[1024]{0:T(1024)S(1)}, s32[1024]{0:T(1024)}, u32[]{:S(2)}) copy-start(s32[1024]{0:T(1024)} %param.20) | copy-start | bytes 12292
  33.9 9.9 %collective-permute-start.3 = (f32[67,1536]{1,0:T(8,128)S(1)}, f32[67,1536]{1,0:T(8,128)S(1)}, u32[]{:S(2)}, u32[]{:S(2)}) collective-permute-start(f32[67,1536]{1,0:T(8,128)S(1)} %pad_maximum_fusion), channel_id=1, source_target_pairs={{0,64},{1,65},{2,66},{3,67},{4,68},{5,69},{6,70},{7,71},{8,72},{9,... | collective-permute-start | bytes 1234952 | tf_op jit(solution)/shard_map/ppermute | solution.py:80
  43.8 1.3 %collective-permute-start.4 = (f32[4,1536]{1,0:T(4,128)S(1)}, f32[4,1536]{1,0:T(4,128)S(1)}, u32[]{:S(2)}, u32[]{:S(2)}) collective-permute-start(f32[4,1536]{1,0:T(4,128)S(1)} %pad_maximum_fusion.4), channel_id=1, source_target_pairs={{0,1},{1,0},{2,3},{3,2},{4,5},{5,4},{6,7},{7,6},{8,9},{9,8},{10,11... | collective-permute-start | bytes 73736 | tf_op jit(solution)/shard_map/ppermute | solution.py:80
  45.1 3.9 %collective-permute-start.5 = (f32[4,1536]{1,0:T(4,128)S(1)}, f32[4,1536]{1,0:T(4,128)S(1)}, u32[]{:S(2)}, u32[]{:S(2)}) collective-permute-start(f32[4,1536]{1,0:T(4,128)S(1)} %fusion.40), channel_id=1, source_target_pairs={{0,2},{1,3},{2,0},{3,1},{4,6},{5,7},{6,4},{7,5},{8,10},{9,11},{10,... | collective-permute-start | bytes 73736 | tf_op jit(solution)/shard_map/ppermute | solution.py:80
  49.1 5.4 %collective-permute-start.6 = (f32[4,1536]{1,0:T(4,128)S(1)}, f32[4,1536]{1,0:T(4,128)S(1)}, u32[]{:S(2)}, u32[]{:S(2)}) collective-permute-start(f32[4,1536]{1,0:T(4,128)S(1)} %add.315), channel_id=1, source_target_pairs={{0,4},{1,5},{2,6},{3,7},{4,0},{5,1},{6,2},{7,3},{8,12},{9,13},{10,... | collective-permute-start | bytes 73736 | tf_op jit(solution)/shard_map/ppermute | solution.py:80
  56.3 0.8 copy-start.1
  67.2 9.2 %collective-permute-start.7 = (f32[2,1536]{1,0:T(2,128)S(1)}, f32[2,1536]{1,0:T(2,128)S(1)}, u32[]{:S(2)}, u32[]{:S(2)}) collective-permute-start(f32[2,1536]{1,0:T(2,128)S(1)} %pad_maximum_fusion.5), channel_id=1, source_target_pairs={{0,1},{1,2},{2,3},{3,4},{4,5},{5,6},{6,7},{7,8},{8,9},{9,10},{10,1... | collective-permute-start | bytes 36872 | tf_op jit(solution)/shard_map/ppermute | solution.py:182
  77.7 7.6 %collective-permute-start.8 = (f32[2,1536]{1,0:T(2,128)S(1)}, f32[2,1536]{1,0:T(2,128)S(1)}, u32[]{:S(2)}, u32[]{:S(2)}) collective-permute-start(f32[2,1536]{1,0:T(2,128)S(1)} %pad_maximum_fusion.6), channel_id=1, source_target_pairs={{1,0},{2,1},{3,2},{4,3},{5,4},{6,5},{7,6},{8,7},{9,8},{10,9},{11,1... | collective-permute-start | bytes 36872 | tf_op jit(solution)/shard_map/ppermute | solution.py:183
  81.0 12.3 %all-to-all-start.1 = ((f32[8,6,1536]{2,1,0:T(8,128)}), f32[8,6,1536]{2,1,0:T(8,128)S(1)}, u32[]{:S(2)}, u32[]{:S(2)}) async-start(f32[8,6,1536]{2,1,0:T(8,128)} %broadcast_select_fusion.2), calls=%async_computation.1 | async-start | bytes 786432 | tf_op jit(solution)/shard_map/all_to_all | solution.py:163

commit v8 on v7

--- a/solution.py
+++ b/solution.py
@@ -76,8 +76,16 @@
     )(table, *smalls, *consts)
 
 
+def _partner(i, bit):
+    if bit in (4, 16, 64):
+        low = bit // 2
+        r = (i // low) % 4
+        return i + ((3 - r) - r) * low
+    return i ^ bit
+
+
 def _xor(x, n, bit):
-    return lax.ppermute(x, AXES, [(i, i ^ bit) for i in range(n)])
+    return lax.ppermute(x, AXES, [(i, _partner(i, bit)) for i in range(n)])
 
 
 def make_body(n):

time: 105 us -> 104 us (level)
  waiting for transfers between devices: 36.3 us -> 35.1 us
    ppermute x7, waiting for transfers between devices: 23.8 us -> 22.5 us  [_xor(): return lax.ppermute(x, AXES, [(i, _partner(i, bit)) for i in range(n)])]
where the time goes in v8:
time: 104 us; the launch traced here: 103 us
  waiting for transfers between devices  35.1 us (34%)
  starting transfers between devices  19.6 us (19%)
  Pallas kernels  18.6 us (18%)
  other arithmetic  15 us (14%)
  local copies, waits for them, and re-layouts  8.97 us (9%)
  between operations  5.71 us (5%)
    ppermute x7, waiting for transfers between devices, _xor(): return lax.ppermute(x, AXES, [(i, _partner(i, bit)) for i in range(n)])  22.5 us
    pallas_call x3, Pallas kernels, _table_call(): pl.pallas_call(kernel, grid=grid, in_specs=specs, out_specs=pl.BlockSpec(...  18.6 us
    ppermute x7, starting transfers between devices, _xor(): return lax.ppermute(x, AXES, [(i, _partner(i, bit)) for i in range(n)])  12.3 us
    ppermute x1, waiting for transfers between devices, body(): from_left = lax.ppermute(to_right, AXES, right)  6.46 us
    all_to_all x1, waiting for transfers between devices, exchange(): return lax.all_to_all(sent, 'mem', 0, 0, tiled=True)  6.1 us
    all_to_all x1, starting transfers between devices, exchange(): return lax.all_to_all(sent, 'mem', 0, 0, tiled=True)  3.47 us
  transfers between devices with their start and end apart: 10, of which 9 were waited for; matrix products, arithmetic and copies ran while one was open for 4% of the time, Pallas kernels for 0%

profile of v8, /device:TPU:6, one launch (start us, length us, event | category | flops | bytes accessed | tf_op | source)
XLA Modules:
  0.0 103.0 jit_solution(15918358121386161988)
XLA Ops:
  0.0 1.3 %fusion.42 = (s32[1]{0:T(128)}, s32[1]{0:T(128)}) fusion(s32[16]{0:T(128)} %param.19), kind=kLoop, calls=%fused_computation.151 | loop fusion | bytes 16 | tf_op jit(solution)/shard_map/slice | solution.py:111
  2.0 0.9 select_reduce_fusion.2
  2.9 2.0 %compare_and_fusion.3 = (pred[16]{0:T(512)(128)(4,1)S(1)}, s32[16]{0:T(128)S(1)}, pred[16]{0:T(512)(128)(4,1)S(1)}) fusion(s32[16]{0:T(128)} %param.19, s32[]{:T(128)} %bitcast.1, s32[]{:T(128)} %bitcast.2), kind=kLoop, calls=%fused_computation.120 | loop fusion | flops 144 | bytes 168 | tf_op jit(solution)/shard_map/jit(_take)/and | solution.py:195
  6.4 4.8 %shard_map.91 = f32[16,96,32]{2,1,0:T(8,128)} custom-call(f32[16,96,1024]{2,1,0:T(8,128)} %pop_ref.5, bf16[128,32]{1,0:T(8,128)(2,1)} %constant.230.clone.g1_ref), custom_call_target="tpu_custom_call" | custom-call | tf_op jit(solution)/shard_map/pallas_call | solution.py:70
  11.2 1.5 %reduce_sum.94 = f32[16,96]{1,0:T(8,128)S(1)} reduce(f32[16,96,32]{2,1,0:T(8,128)} %shard_map.91, f32[]{:T(128)} %constant.209.clone.1), dimensions={2}, to_apply=%region_2.3 | reduce | flops 47616 | bytes 202756 | tf_op jit(solution)/shard_map/reduce_sum | solution.py:129
  12.7 1.4 %multiply_reduce_fusion.1 = f32[96,32]{1,0:T(8,128)S(1)} fusion(f32[16,96,32]{2,1,0:T(8,128)} %shard_map.91, f32[16,96]{1,0:T(8,128)S(1)} %div.53), kind=kLoop, calls=%fused_computation.30 | loop fusion | flops 95232 | bytes 215040 | tf_op jit(solution)/shard_map/reduce_sum | solution.py:131
  14.3 2.0 %collective-permute-start = (f32[11,1536]{1,0:T(8,128)S(1)}, f32[11,1536]{1,0:T(8,128)S(1)}, u32[]{:S(2)}, u32[]{:S(2)}) collective-permute-start(f32[11,1536]{1,0:T(8,128)S(1)} %pad_maximum_fusion.3), channel_id=1, source_target_pairs={{0,8},{1,9},{2,10},{3,11},{4,12},{5,13},{6,14},{7,15},{8,0},{9,1},... | collective-permute-start | bytes 202760 | tf_op jit(solution)/shard_map/ppermute | solution.py:88
  17.7 1.4 %collective-permute-done = f32[11,1536]{1,0:T(8,128)S(1)} collective-permute-done((f32[11,1536]{1,0:T(8,128)S(1)}, f32[11,1536]{1,0:T(8,128)S(1)}, u32[]{:S(2)}, u32[]{:S(2)}) %collective-permute-start) | collective-permute-done | bytes 67616 | tf_op jit(solution)/shard_map/ppermute | solution.py:88
  19.2 4.0 %collective-permute-start.1 = (f32[19,1536]{1,0:T(8,128)S(1)}, f32[19,1536]{1,0:T(8,128)S(1)}, u32[]{:S(2)}, u32[]{:S(2)}) collective-permute-start(f32[19,1536]{1,0:T(8,128)S(1)} %pad_maximum_fusion.2), channel_id=1, source_target_pairs={{0,24},{1,25},{2,26},{3,27},{4,28},{5,29},{6,30},{7,31},{8,16},{9,... | collective-permute-start | bytes 350216 | tf_op jit(solution)/shard_map/ppermute | solution.py:88
  24.6 0.7 and_reduce_fusion
  25.3 1.0 collective-permute-done.1
  26.5 0.9 collective-permute-start.2
  27.4 5.3 %collective-permute-done.2 = f32[35,1536]{1,0:T(8,128)S(1)} collective-permute-done((f32[35,1536]{1,0:T(8,128)S(1)}, f32[35,1536]{1,0:T(8,128)S(1)}, u32[]{:S(2)}, u32[]{:S(2)}) %collective-permute-start.2) | collective-permute-done | bytes 215072 | tf_op jit(solution)/shard_map/ppermute | solution.py:88
  33.5 9.4 %collective-permute-done.3 = f32[67,1536]{1,0:T(8,128)S(1)} collective-permute-done((f32[67,1536]{1,0:T(8,128)S(1)}, f32[67,1536]{1,0:T(8,128)S(1)}, u32[]{:S(2)}, u32[]{:S(2)}) %collective-permute-start.3) | collective-permute-done | bytes 411680 | tf_op jit(solution)/shard_map/ppermute | solution.py:88
  43.1 1.2 %collective-permute-done.4 = f32[4,1536]{1,0:T(4,128)S(1)} collective-permute-done((f32[4,1536]{1,0:T(4,128)S(1)}, f32[4,1536]{1,0:T(4,128)S(1)}, u32[]{:S(2)}, u32[]{:S(2)}) %collective-permute-start.4) | collective-permute-done | bytes 24608 | tf_op jit(solution)/shard_map/ppermute | solution.py:88
  44.3 1.7 %collective-permute-start.5 = (f32[4,1536]{1,0:T(4,128)S(1)}, f32[4,1536]{1,0:T(4,128)S(1)}, u32[]{:S(2)}, u32[]{:S(2)}) collective-permute-start(f32[4,1536]{1,0:T(4,128)S(1)} %fusion.40), channel_id=1, source_target_pairs={{0,2},{1,3},{2,0},{3,1},{4,6},{5,7},{6,4},{7,5},{8,10},{9,11},{10,... | collective-permute-start | bytes 73736 | tf_op jit(solution)/shard_map/ppermute | solution.py:88
  46.0 2.2 %collective-permute-done.5 = f32[4,1536]{1,0:T(4,128)S(1)} collective-permute-done((f32[4,1536]{1,0:T(4,128)S(1)}, f32[4,1536]{1,0:T(4,128)S(1)}, u32[]{:S(2)}, u32[]{:S(2)}) %collective-permute-start.5) | collective-permute-done | bytes 24608 | tf_op jit(solution)/shard_map/ppermute | solution.py:88
  48.2 3.1 %collective-permute-start.6 = (f32[4,1536]{1,0:T(4,128)S(1)}, f32[4,1536]{1,0:T(4,128)S(1)}, u32[]{:S(2)}, u32[]{:S(2)}) collective-permute-start(f32[4,1536]{1,0:T(4,128)S(1)} %add.315), channel_id=1, source_target_pairs={{0,6},{1,7},{2,4},{3,5},{4,2},{5,3},{6,0},{7,1},{8,14},{9,15},{10,... | collective-permute-start | bytes 73736 | tf_op jit(solution)/shard_map/ppermute | solution.py:88
  51.4 2.0 %collective-permute-done.6 = f32[4,1536]{1,0:T(4,128)S(1)} collective-permute-done((f32[4,1536]{1,0:T(4,128)S(1)}, f32[4,1536]{1,0:T(4,128)S(1)}, u32[]{:S(2)}, u32[]{:S(2)}) %collective-permute-start.6) | collective-permute-done | bytes 24608 | tf_op jit(solution)/shard_map/ppermute | solution.py:88
  55.2 0.7 gather_fusion.1
  56.0 0.9 copy.45.s2t_ref
  57.0 6.3 %shard_map.92 = f32[16,96,32]{2,1,0:T(8,128)} custom-call(f32[16,96,1024]{2,1,0:T(8,128)} %pop_ref.5, f32[96,1024]{1,0:T(8,128)} %copy.45.s2t_ref, bf16[1024,32]{1,0:T(8,128)(2,1)} %constant.232.clone.e2t_ref), custom_call_target="tpu_custom_call" | custom-call | tf_op jit(solution)/shard_map/pallas_call | solution.py:70
  63.3 1.4 %broadcast_multiply_fusion.1 = f32[16,96,32]{2,1,0:T(8,128)S(1)} fusion(f32[16,96,32]{2,1,0:T(8,128)} %shard_map.92, f32[16,96]{1,0:T(8,128)S(1)} %div.53), kind=kLoop, calls=%fused_computation.35 | loop fusion | flops 49152 | bytes 399360 | tf_op jit(solution)/shard_map/mul | solution.py:180
  64.7 1.0 reduce_sum.100
  66.0 1.9 %collective-permute-start.7 = (f32[2,1536]{1,0:T(2,128)S(1)}, f32[2,1536]{1,0:T(2,128)S(1)}, u32[]{:S(2)}, u32[]{:S(2)}) collective-permute-start(f32[2,1536]{1,0:T(2,128)S(1)} %pad_maximum_fusion.5), channel_id=1, source_target_pairs={{0,1},{1,2},{2,3},{3,4},{4,5},{5,6},{6,7},{7,8},{8,9},{9,10},{10,1... | collective-permute-start | bytes 36872 | tf_op jit(solution)/shard_map/ppermute | solution.py:190
  68.0 0.8 broadcast_select_fusion.2
  68.8 6.5 %collective-permute-done.7 = f32[2,1536]{1,0:T(2,128)S(1)} collective-permute-done((f32[2,1536]{1,0:T(2,128)S(1)}, f32[2,1536]{1,0:T(2,128)S(1)}, u32[]{:S(2)}, u32[]{:S(2)}) %collective-permute-start.7) | collective-permute-done | bytes 12320 | tf_op jit(solution)/shard_map/ppermute | solution.py:190
  76.5 1.9 %collective-permute-start.8 = (f32[2,1536]{1,0:T(2,128)S(1)}, f32[2,1536]{1,0:T(2,128)S(1)}, u32[]{:S(2)}, u32[]{:S(2)}) collective-permute-start(f32[2,1536]{1,0:T(2,128)S(1)} %pad_maximum_fusion.6), channel_id=1, source_target_pairs={{1,0},{2,1},{3,2},{4,3},{5,4},{6,5},{7,6},{8,7},{9,8},{10,9},{11,1... | collective-permute-start | bytes 36872 | tf_op jit(solution)/shard_map/ppermute | solution.py:191
  79.8 3.5 %all-to-all-start.1 = ((f32[8,6,1536]{2,1,0:T(8,128)}), f32[8,6,1536]{2,1,0:T(8,128)S(1)}, u32[]{:S(2)}, u32[]{:S(2)}) async-start(f32[8,6,1536]{2,1,0:T(8,128)} %broadcast_select_fusion.2), calls=%async_computation.1 | async-start | bytes 786432 | tf_op jit(solution)/shard_map/all_to_all | solution.py:171
  86.0 6.1 %all-to-all-done.1 = f32[8,6,1536]{2,1,0:T(8,128)S(1)} async-done(((f32[8,6,1536]{2,1,0:T(8,128)}), f32[8,6,1536]{2,1,0:T(8,128)S(1)}, u32[]{:S(2)}, u32[]{:S(2)}) %all-to-all-start.1) | async-done | bytes 294944 | tf_op jit(solution)/shard_map/all_to_all | solution.py:171
  94.3 1.2 %broadcast_multiply_fusion.r_ref = f32[16,96,32]{2,1,0:T(8,128)} fusion(f32[16,96,32]{2,1,0:T(8,128)S(1)} %bitcast.40, f32[16,96]{1,0:T(8,128)S(1)} %div.53), kind=kLoop, calls=%fused_computation.34 | loop fusion | flops 49152 | bytes 399360 | tf_op jit(solution)/shard_map/mul | solution.py:197
  95.5 7.5 %shard_map.93 = f32[16,96,1024]{2,1,0:T(8,128)} custom-call(f32[16,96,1024]{2,1,0:T(8,128)} %pop_ref.5, f32[16,96,32]{2,1,0:T(8,128)} %broadcast_multiply_fusion.r_ref, f32[96,1024]{1,0:T(8,128)} %copy.45.s2t_ref, bf16[32,1024]{1,0:T(8,128)(2,1)} %constant.231.clone.e2_ref), custom_call_target="tpu_custom_call" | custom-call | tf_op jit(solution)/shard_map/pallas_call | solution.py:70
  (103 shorter events, 10.8 us)
Async XLA Ops:
  6.4 6.3 %copy-start.3 = (f32[16,96]{1,0:T(8,128)S(1)}, f32[16,96]{1,0:T(8,128)}, u32[]{:S(2)}) copy-start(f32[16,96]{1,0:T(8,128)} %param.16) | copy-start | bytes 18436
  11.2 3.0 %copy-start = (f32[8,1536]{1,0:T(8,128)S(1)}, f32[8,1536]{1,0:T(8,128)}, u32[]{:S(2)}) copy-start(f32[8,1536]{1,0:T(8,128)} %param.18) | copy-start | bytes 147460
  11.2 13.3 %copy-start.4 = (s32[2]{0:T(128)S(1)}, s32[2]{0:T(128)}, u32[]{:S(2)}) copy-start(s32[2]{0:T(128)} %constant.228.clone.1) | copy-start | bytes 28
  14.3 4.8 %collective-permute-start = (f32[11,1536]{1,0:T(8,128)S(1)}, f32[11,1536]{1,0:T(8,128)S(1)}, u32[]{:S(2)}, u32[]{:S(2)}) collective-permute-start(f32[11,1536]{1,0:T(8,128)S(1)} %pad_maximum_fusion.3), channel_id=1, source_target_pairs={{0,8},{1,9},{2,10},{3,11},{4,12},{5,13},{6,14},{7,15},{8,0},{9,1},... | collective-permute-start | bytes 202760 | tf_op jit(solution)/shard_map/ppermute | solution.py:88
  19.2 7.1 %collective-permute-start.1 = (f32[19,1536]{1,0:T(8,128)S(1)}, f32[19,1536]{1,0:T(8,128)S(1)}, u32[]{:S(2)}, u32[]{:S(2)}) collective-permute-start(f32[19,1536]{1,0:T(8,128)S(1)} %pad_maximum_fusion.2), channel_id=1, source_target_pairs={{0,24},{1,25},{2,26},{3,27},{4,28},{5,29},{6,30},{7,31},{8,16},{9,... | collective-permute-start | bytes 350216 | tf_op jit(solution)/shard_map/ppermute | solution.py:88
  26.5 6.3 %collective-permute-start.2 = (f32[35,1536]{1,0:T(8,128)S(1)}, f32[35,1536]{1,0:T(8,128)S(1)}, u32[]{:S(2)}, u32[]{:S(2)}) collective-permute-start(f32[35,1536]{1,0:T(8,128)S(1)} %pad_maximum_fusion.1), channel_id=1, source_target_pairs={{0,32},{1,33},{2,34},{3,35},{4,36},{5,37},{6,38},{7,39},{8,40},{9,... | collective-permute-start | bytes 645128 | tf_op jit(solution)/shard_map/ppermute | solution.py:88
  32.9 21.0 %copy-start.2 = (s32[1024]{0:T(1024)S(1)}, s32[1024]{0:T(1024)}, u32[]{:S(2)}) copy-start(s32[1024]{0:T(1024)} %param.20) | copy-start | bytes 12292
  32.9 10.0 %collective-permute-start.3 = (f32[67,1536]{1,0:T(8,128)S(1)}, f32[67,1536]{1,0:T(8,128)S(1)}, u32[]{:S(2)}, u32[]{:S(2)}) collective-permute-start(f32[67,1536]{1,0:T(8,128)S(1)} %pad_maximum_fusion), channel_id=1, source_target_pairs={{0,96},{1,97},{2,98},{3,99},{4,100},{5,101},{6,102},{7,103},{8,104... | collective-permute-start | bytes 1234952 | tf_op jit(solution)/shard_map/ppermute | solution.py:88
  43.0 1.3 %collective-permute-start.4 = (f32[4,1536]{1,0:T(4,128)S(1)}, f32[4,1536]{1,0:T(4,128)S(1)}, u32[]{:S(2)}, u32[]{:S(2)}) collective-permute-start(f32[4,1536]{1,0:T(4,128)S(1)} %pad_maximum_fusion.4), channel_id=1, source_target_pairs={{0,1},{1,0},{2,3},{3,2},{4,5},{5,4},{6,7},{7,6},{8,9},{9,8},{10,11... | collective-permute-start | bytes 73736 | tf_op jit(solution)/shard_map/ppermute | solution.py:88
  44.3 3.9 %collective-permute-start.5 = (f32[4,1536]{1,0:T(4,128)S(1)}, f32[4,1536]{1,0:T(4,128)S(1)}, u32[]{:S(2)}, u32[]{:S(2)}) collective-permute-start(f32[4,1536]{1,0:T(4,128)S(1)} %fusion.40), channel_id=1, source_target_pairs={{0,2},{1,3},{2,0},{3,1},{4,6},{5,7},{6,4},{7,5},{8,10},{9,11},{10,... | collective-permute-start | bytes 73736 | tf_op jit(solution)/shard_map/ppermute | solution.py:88
  48.2 5.1 %collective-permute-start.6 = (f32[4,1536]{1,0:T(4,128)S(1)}, f32[4,1536]{1,0:T(4,128)S(1)}, u32[]{:S(2)}, u32[]{:S(2)}) collective-permute-start(f32[4,1536]{1,0:T(4,128)S(1)} %add.315), channel_id=1, source_target_pairs={{0,6},{1,7},{2,4},{3,5},{4,2},{5,3},{6,0},{7,1},{8,14},{9,15},{10,... | collective-permute-start | bytes 73736 | tf_op jit(solution)/shard_map/ppermute | solution.py:88
  55.2 0.8 copy-start.1
  66.0 9.2 %collective-permute-start.7 = (f32[2,1536]{1,0:T(2,128)S(1)}, f32[2,1536]{1,0:T(2,128)S(1)}, u32[]{:S(2)}, u32[]{:S(2)}) collective-permute-start(f32[2,1536]{1,0:T(2,128)S(1)} %pad_maximum_fusion.5), channel_id=1, source_target_pairs={{0,1},{1,2},{2,3},{3,4},{4,5},{5,6},{6,7},{7,8},{8,9},{9,10},{10,1... | collective-permute-start | bytes 36872 | tf_op jit(solution)/shard_map/ppermute | solution.py:190
  76.5 7.6 %collective-permute-start.8 = (f32[2,1536]{1,0:T(2,128)S(1)}, f32[2,1536]{1,0:T(2,128)S(1)}, u32[]{:S(2)}, u32[]{:S(2)}) collective-permute-start(f32[2,1536]{1,0:T(2,128)S(1)} %pad_maximum_fusion.6), channel_id=1, source_target_pairs={{1,0},{2,1},{3,2},{4,3},{5,4},{6,5},{7,6},{8,7},{9,8},{10,9},{11,1... | collective-permute-start | bytes 36872 | tf_op jit(solution)/shard_map/ppermute | solution.py:191
  79.8 12.3 %all-to-all-start.1 = ((f32[8,6,1536]{2,1,0:T(8,128)}), f32[8,6,1536]{2,1,0:T(8,128)S(1)}, u32[]{:S(2)}, u32[]{:S(2)}) async-start(f32[8,6,1536]{2,1,0:T(8,128)} %broadcast_select_fusion.2), calls=%async_computation.1 | async-start | bytes 786432 | tf_op jit(solution)/shard_map/all_to_all | solution.py:171

commit v9 on v8

--- a/solution.py
+++ b/solution.py
@@ -173,6 +173,7 @@
         fast = exchange(ROOMY, 0)
         spare = most - ROOMY
         slow = lax.cond(total_over > 0, lambda: exchange(spare, ROOMY), lambda: jnp.zeros((MEMBERS, spare, width), f32))
+        fast, s2 = lax.optimization_barrier((fast, s2))
         target = jnp.where((m_rank < ROOMY)[:, None], fast[m_mem, jnp.minimum(m_rank, ROOMY - 1)],
                            slow[m_mem, jnp.clip(m_rank - ROOMY, 0, spare - 1)])
 

time: 104 us -> 108 us (1.038)
  waiting for transfers between devices: 35.1 us -> 38.8 us
    all_to_all x1, waiting for transfers between devices: 6.1 us -> 7.88 us  [exchange(): return lax.all_to_all(sent, 'mem', 0, 0, tiled=True)]
    ppermute x7, waiting for transfers between devices: 22.5 us -> 23.6 us  [_xor(): return lax.ppermute(x, AXES, [(i, _partner(i, bit)) for i in range(n)])]
  transfers between devices with their start and end apart: 10 -> 10, of which waited for: 9 -> 9; matrix products, arithmetic and copies ran while one was open for 4% -> 3% of each run, Pallas kernels for 0% -> 0%
where the time goes in v9:
time: 108 us; the launch traced here: 107 us
  waiting for transfers between devices  38.8 us (36%)
  starting transfers between devices  20.5 us (19%)
  Pallas kernels  18.6 us (17%)
  other arithmetic  14.7 us (14%)
  local copies, waits for them, and re-layouts  8.95 us (8%)
  between operations  5.57 us (5%)
    ppermute x7, waiting for transfers between devices, _xor(): return lax.ppermute(x, AXES, [(i, _partner(i, bit)) for i in range(n)])  23.6 us
    pallas_call x3, Pallas kernels, _table_call(): pl.pallas_call(kernel, grid=grid, in_specs=specs, out_specs=pl.BlockSpec(...  18.6 us
    ppermute x7, starting transfers between devices, _xor(): return lax.ppermute(x, AXES, [(i, _partner(i, bit)) for i in range(n)])  12.3 us
    all_to_all x1, waiting for transfers between devices, exchange(): return lax.all_to_all(sent, 'mem', 0, 0, tiled=True)  7.88 us
    ppermute x1, waiting for transfers between devices, body(): from_left = lax.ppermute(to_right, AXES, right)  7.28 us
    all_to_all x1, starting transfers between devices, exchange(): return lax.all_to_all(sent, 'mem', 0, 0, tiled=True)  4.29 us
  transfers between devices with their start and end apart: 10, of which 9 were waited for; matrix products, arithmetic and copies ran while one was open for 3% of the time, Pallas kernels for 0%

profile of v9, /device:TPU:6, one launch (start us, length us, event | category | flops | bytes accessed | tf_op | source)
XLA Modules:
  0.0 107.1 jit_solution(16996921534972073635)
XLA Ops:
  0.0 1.3 %fusion.42 = (s32[1]{0:T(128)}, s32[1]{0:T(128)}) fusion(s32[16]{0:T(128)} %param.19), kind=kLoop, calls=%fused_computation.151 | loop fusion | bytes 16 | tf_op jit(solution)/shard_map/slice | solution.py:111
  1.9 0.9 select_reduce_fusion.2
  2.8 1.9 %compare_and_fusion.3 = (pred[16]{0:T(512)(128)(4,1)S(1)}, s32[16]{0:T(128)S(1)}, pred[16]{0:T(512)(128)(4,1)S(1)}) fusion(s32[16]{0:T(128)} %param.19, s32[]{:T(128)} %bitcast.1, s32[]{:T(128)} %bitcast.2), kind=kLoop, calls=%fused_computation.120 | loop fusion | flops 144 | bytes 168 | tf_op jit(solution)/shard_map/jit(_take)/and | solution.py:196
  6.2 4.8 %shard_map.91 = f32[16,96,32]{2,1,0:T(8,128)} custom-call(f32[16,96,1024]{2,1,0:T(8,128)} %pop_ref.5, bf16[128,32]{1,0:T(8,128)(2,1)} %constant.230.clone.g1_ref), custom_call_target="tpu_custom_call" | custom-call | tf_op jit(solution)/shard_map/pallas_call | solution.py:70
  11.0 1.5 %reduce_sum.94 = f32[16,96]{1,0:T(8,128)S(1)} reduce(f32[16,96,32]{2,1,0:T(8,128)} %shard_map.91, f32[]{:T(128)} %constant.209.clone.1), dimensions={2}, to_apply=%region_2.3 | reduce | flops 47616 | bytes 202756 | tf_op jit(solution)/shard_map/reduce_sum | solution.py:129
  12.5 1.4 %multiply_reduce_fusion.1 = f32[96,32]{1,0:T(8,128)S(1)} fusion(f32[16,96,32]{2,1,0:T(8,128)} %shard_map.91, f32[16,96]{1,0:T(8,128)S(1)} %div.53), kind=kLoop, calls=%fused_computation.30 | loop fusion | flops 95232 | bytes 215040 | tf_op jit(solution)/shard_map/reduce_sum | solution.py:131
  14.0 2.0 %collective-permute-start = (f32[11,1536]{1,0:T(8,128)S(1)}, f32[11,1536]{1,0:T(8,128)S(1)}, u32[]{:S(2)}, u32[]{:S(2)}) collective-permute-start(f32[11,1536]{1,0:T(8,128)S(1)} %pad_maximum_fusion.3), channel_id=1, source_target_pairs={{0,8},{1,9},{2,10},{3,11},{4,12},{5,13},{6,14},{7,15},{8,0},{9,1},... | collective-permute-start | bytes 202760 | tf_op jit(solution)/shard_map/ppermute | solution.py:88
  17.2 1.6 %collective-permute-done = f32[11,1536]{1,0:T(8,128)S(1)} collective-permute-done((f32[11,1536]{1,0:T(8,128)S(1)}, f32[11,1536]{1,0:T(8,128)S(1)}, u32[]{:S(2)}, u32[]{:S(2)}) %collective-permute-start) | collective-permute-done | bytes 67616 | tf_op jit(solution)/shard_map/ppermute | solution.py:88
  18.9 4.0 %collective-permute-start.1 = (f32[19,1536]{1,0:T(8,128)S(1)}, f32[19,1536]{1,0:T(8,128)S(1)}, u32[]{:S(2)}, u32[]{:S(2)}) collective-permute-start(f32[19,1536]{1,0:T(8,128)S(1)} %pad_maximum_fusion.2), channel_id=1, source_target_pairs={{0,24},{1,25},{2,26},{3,27},{4,28},{5,29},{6,30},{7,31},{8,16},{9,... | collective-permute-start | bytes 350216 | tf_op jit(solution)/shard_map/ppermute | solution.py:88
  23.0 3.1 %collective-permute-done.1 = f32[19,1536]{1,0:T(8,128)S(1)} collective-permute-done((f32[19,1536]{1,0:T(8,128)S(1)}, f32[19,1536]{1,0:T(8,128)S(1)}, u32[]{:S(2)}, u32[]{:S(2)}) %collective-permute-start.1) | collective-permute-done | bytes 116768 | tf_op jit(solution)/shard_map/ppermute | solution.py:88
  26.2 0.9 collective-permute-start.2
  27.1 5.4 %collective-permute-done.2 = f32[35,1536]{1,0:T(8,128)S(1)} collective-permute-done((f32[35,1536]{1,0:T(8,128)S(1)}, f32[35,1536]{1,0:T(8,128)S(1)}, u32[]{:S(2)}, u32[]{:S(2)}) %collective-permute-start.2) | collective-permute-done | bytes 215072 | tf_op jit(solution)/shard_map/ppermute | solution.py:88
  33.2 9.4 %collective-permute-done.3 = f32[67,1536]{1,0:T(8,128)S(1)} collective-permute-done((f32[67,1536]{1,0:T(8,128)S(1)}, f32[67,1536]{1,0:T(8,128)S(1)}, u32[]{:S(2)}, u32[]{:S(2)}) %collective-permute-start.3) | collective-permute-done | bytes 411680 | tf_op jit(solution)/shard_map/ppermute | solution.py:88
  42.8 1.2 %collective-permute-done.4 = f32[4,1536]{1,0:T(4,128)S(1)} collective-permute-done((f32[4,1536]{1,0:T(4,128)S(1)}, f32[4,1536]{1,0:T(4,128)S(1)}, u32[]{:S(2)}, u32[]{:S(2)}) %collective-permute-start.4) | collective-permute-done | bytes 24608 | tf_op jit(solution)/shard_map/ppermute | solution.py:88
  44.0 1.7 %collective-permute-start.5 = (f32[4,1536]{1,0:T(4,128)S(1)}, f32[4,1536]{1,0:T(4,128)S(1)}, u32[]{:S(2)}, u32[]{:S(2)}) collective-permute-start(f32[4,1536]{1,0:T(4,128)S(1)} %fusion.40), channel_id=1, source_target_pairs={{0,2},{1,3},{2,0},{3,1},{4,6},{5,7},{6,4},{7,5},{8,10},{9,11},{10,... | collective-permute-start | bytes 73736 | tf_op jit(solution)/shard_map/ppermute | solution.py:88
  46.9 1.0 collective-permute-done.5
  48.0 3.1 %collective-permute-start.6 = (f32[4,1536]{1,0:T(4,128)S(1)}, f32[4,1536]{1,0:T(4,128)S(1)}, u32[]{:S(2)}, u32[]{:S(2)}) collective-permute-start(f32[4,1536]{1,0:T(4,128)S(1)} %add.315), channel_id=1, source_target_pairs={{0,6},{1,7},{2,4},{3,5},{4,2},{5,3},{6,0},{7,1},{8,14},{9,15},{10,... | collective-permute-start | bytes 73736 | tf_op jit(solution)/shard_map/ppermute | solution.py:88
  51.1 2.0 %collective-permute-done.6 = f32[4,1536]{1,0:T(4,128)S(1)} collective-permute-done((f32[4,1536]{1,0:T(4,128)S(1)}, f32[4,1536]{1,0:T(4,128)S(1)}, u32[]{:S(2)}, u32[]{:S(2)}) %collective-permute-start.6) | collective-permute-done | bytes 24608 | tf_op jit(solution)/shard_map/ppermute | solution.py:88
  54.8 0.7 gather_fusion.1
  55.5 0.8 broadcast_select_fusion.2
  56.4 4.3 %all-to-all-start.1 = ((f32[8,6,1536]{2,1,0:T(8,128)}), f32[8,6,1536]{2,1,0:T(8,128)S(1)}, u32[]{:S(2)}, u32[]{:S(2)}) async-start(f32[8,6,1536]{2,1,0:T(8,128)} %broadcast_select_fusion.2), calls=%async_computation.1 | async-start | bytes 786432 | tf_op jit(solution)/shard_map/all_to_all | solution.py:171
  60.7 0.7 and_reduce_fusion
  61.7 7.9 %all-to-all-done.1 = f32[8,6,1536]{2,1,0:T(8,128)S(1)} async-done(((f32[8,6,1536]{2,1,0:T(8,128)}), f32[8,6,1536]{2,1,0:T(8,128)S(1)}, u32[]{:S(2)}, u32[]{:S(2)}) %all-to-all-start.1) | async-done | bytes 294944 | tf_op jit(solution)/shard_map/all_to_all | solution.py:171
  69.7 0.9 copy.36.s2t_ref
  70.6 6.3 %shard_map.92 = f32[16,96,32]{2,1,0:T(8,128)} custom-call(f32[16,96,1024]{2,1,0:T(8,128)} %pop_ref.5, f32[96,1024]{1,0:T(8,128)} %copy.36.s2t_ref, bf16[1024,32]{1,0:T(8,128)(2,1)} %constant.232.clone.e2t_ref), custom_call_target="tpu_custom_call" | custom-call | tf_op jit(solution)/shard_map/pallas_call | solution.py:70
  76.9 1.4 %broadcast_multiply_fusion.1 = f32[16,96,32]{2,1,0:T(8,128)S(1)} fusion(f32[16,96,32]{2,1,0:T(8,128)} %shard_map.92, f32[16,96]{1,0:T(8,128)S(1)} %div.53), kind=kLoop, calls=%fused_computation.35 | loop fusion | flops 49152 | bytes 399360 | tf_op jit(solution)/shard_map/mul | solution.py:181
  78.3 1.0 reduce_sum.100
  79.7 1.9 %collective-permute-start.7 = (f32[2,1536]{1,0:T(2,128)S(1)}, f32[2,1536]{1,0:T(2,128)S(1)}, u32[]{:S(2)}, u32[]{:S(2)}) collective-permute-start(f32[2,1536]{1,0:T(2,128)S(1)} %pad_maximum_fusion.5), channel_id=1, source_target_pairs={{0,1},{1,2},{2,3},{3,4},{4,5},{5,6},{6,7},{7,8},{8,9},{9,10},{10,1... | collective-permute-start | bytes 36872 | tf_op jit(solution)/shard_map/ppermute | solution.py:191
  81.7 7.3 %collective-permute-done.7 = f32[2,1536]{1,0:T(2,128)S(1)} collective-permute-done((f32[2,1536]{1,0:T(2,128)S(1)}, f32[2,1536]{1,0:T(2,128)S(1)}, u32[]{:S(2)}, u32[]{:S(2)}) %collective-permute-start.7) | collective-permute-done | bytes 12320 | tf_op jit(solution)/shard_map/ppermute | solution.py:191
  90.2 1.9 %collective-permute-start.8 = (f32[2,1536]{1,0:T(2,128)S(1)}, f32[2,1536]{1,0:T(2,128)S(1)}, u32[]{:S(2)}, u32[]{:S(2)}) collective-permute-start(f32[2,1536]{1,0:T(2,128)S(1)} %pad_maximum_fusion.6), channel_id=1, source_target_pairs={{1,0},{2,1},{3,2},{4,3},{5,4},{6,5},{7,6},{8,7},{9,8},{10,9},{11,1... | collective-permute-start | bytes 36872 | tf_op jit(solution)/shard_map/ppermute | solution.py:192
  98.4 1.2 %broadcast_multiply_fusion.r_ref = f32[16,96,32]{2,1,0:T(8,128)} fusion(f32[16,96,32]{2,1,0:T(8,128)S(1)} %bitcast.40, f32[16,96]{1,0:T(8,128)S(1)} %div.53), kind=kLoop, calls=%fused_computation.34 | loop fusion | flops 49152 | bytes 399360 | tf_op jit(solution)/shard_map/mul | solution.py:198
  99.6 7.5 %shard_map.93 = f32[16,96,1024]{2,1,0:T(8,128)} custom-call(f32[16,96,1024]{2,1,0:T(8,128)} %pop_ref.5, f32[16,96,32]{2,1,0:T(8,128)} %broadcast_multiply_fusion.r_ref, f32[96,1024]{1,0:T(8,128)} %copy.36.s2t_ref, bf16[32,1024]{1,0:T(8,128)(2,1)} %constant.231.clone.e2_ref), custom_call_target="tpu_custom_call" | custom-call | tf_op jit(solution)/shard_map/pallas_call | solution.py:70
  (104 shorter events, 10.7 us)
Async XLA Ops:
  6.2 6.3 %copy-start.3 = (f32[16,96]{1,0:T(8,128)S(1)}, f32[16,96]{1,0:T(8,128)}, u32[]{:S(2)}) copy-start(f32[16,96]{1,0:T(8,128)} %param.16) | copy-start | bytes 18436
  11.0 3.0 %copy-start = (f32[8,1536]{1,0:T(8,128)S(1)}, f32[8,1536]{1,0:T(8,128)}, u32[]{:S(2)}) copy-start(f32[8,1536]{1,0:T(8,128)} %param.18) | copy-start | bytes 147460
  14.0 4.8 %collective-permute-start = (f32[11,1536]{1,0:T(8,128)S(1)}, f32[11,1536]{1,0:T(8,128)S(1)}, u32[]{:S(2)}, u32[]{:S(2)}) collective-permute-start(f32[11,1536]{1,0:T(8,128)S(1)} %pad_maximum_fusion.3), channel_id=1, source_target_pairs={{0,8},{1,9},{2,10},{3,11},{4,12},{5,13},{6,14},{7,15},{8,0},{9,1},... | collective-permute-start | bytes 202760 | tf_op jit(solution)/shard_map/ppermute | solution.py:88
  18.9 7.1 %collective-permute-start.1 = (f32[19,1536]{1,0:T(8,128)S(1)}, f32[19,1536]{1,0:T(8,128)S(1)}, u32[]{:S(2)}, u32[]{:S(2)}) collective-permute-start(f32[19,1536]{1,0:T(8,128)S(1)} %pad_maximum_fusion.2), channel_id=1, source_target_pairs={{0,24},{1,25},{2,26},{3,27},{4,28},{5,29},{6,30},{7,31},{8,16},{9,... | collective-permute-start | bytes 350216 | tf_op jit(solution)/shard_map/ppermute | solution.py:88
  26.2 6.3 %collective-permute-start.2 = (f32[35,1536]{1,0:T(8,128)S(1)}, f32[35,1536]{1,0:T(8,128)S(1)}, u32[]{:S(2)}, u32[]{:S(2)}) collective-permute-start(f32[35,1536]{1,0:T(8,128)S(1)} %pad_maximum_fusion.1), channel_id=1, source_target_pairs={{0,32},{1,33},{2,34},{3,35},{4,36},{5,37},{6,38},{7,39},{8,40},{9,... | collective-permute-start | bytes 645128 | tf_op jit(solution)/shard_map/ppermute | solution.py:88
  32.6 21.0 %copy-start.1 = (s32[1024]{0:T(1024)S(1)}, s32[1024]{0:T(1024)}, u32[]{:S(2)}) copy-start(s32[1024]{0:T(1024)} %param.20) | copy-start | bytes 12292
  32.6 10.0 %collective-permute-start.3 = (f32[67,1536]{1,0:T(8,128)S(1)}, f32[67,1536]{1,0:T(8,128)S(1)}, u32[]{:S(2)}, u32[]{:S(2)}) collective-permute-start(f32[67,1536]{1,0:T(8,128)S(1)} %pad_maximum_fusion), channel_id=1, source_target_pairs={{0,96},{1,97},{2,98},{3,99},{4,100},{5,101},{6,102},{7,103},{8,104... | collective-permute-start | bytes 1234952 | tf_op jit(solution)/shard_map/ppermute | solution.py:88
  42.7 1.3 %collective-permute-start.4 = (f32[4,1536]{1,0:T(4,128)S(1)}, f32[4,1536]{1,0:T(4,128)S(1)}, u32[]{:S(2)}, u32[]{:S(2)}) collective-permute-start(f32[4,1536]{1,0:T(4,128)S(1)} %pad_maximum_fusion.4), channel_id=1, source_target_pairs={{0,1},{1,0},{2,3},{3,2},{4,5},{5,4},{6,7},{7,6},{8,9},{9,8},{10,11... | collective-permute-start | bytes 73736 | tf_op jit(solution)/shard_map/ppermute | solution.py:88
  44.0 3.9 %collective-permute-start.5 = (f32[4,1536]{1,0:T(4,128)S(1)}, f32[4,1536]{1,0:T(4,128)S(1)}, u32[]{:S(2)}, u32[]{:S(2)}) collective-permute-start(f32[4,1536]{1,0:T(4,128)S(1)} %fusion.40), channel_id=1, source_target_pairs={{0,2},{1,3},{2,0},{3,1},{4,6},{5,7},{6,4},{7,5},{8,10},{9,11},{10,... | collective-permute-start | bytes 73736 | tf_op jit(solution)/shard_map/ppermute | solution.py:88
  48.0 5.1 %collective-permute-start.6 = (f32[4,1536]{1,0:T(4,128)S(1)}, f32[4,1536]{1,0:T(4,128)S(1)}, u32[]{:S(2)}, u32[]{:S(2)}) collective-permute-start(f32[4,1536]{1,0:T(4,128)S(1)} %add.315), channel_id=1, source_target_pairs={{0,6},{1,7},{2,4},{3,5},{4,2},{5,3},{6,0},{7,1},{8,14},{9,15},{10,... | collective-permute-start | bytes 73736 | tf_op jit(solution)/shard_map/ppermute | solution.py:88
  55.4 5.2 %copy-start.4 = (s32[2]{0:T(128)S(1)}, s32[2]{0:T(128)}, u32[]{:S(2)}) copy-start(s32[2]{0:T(128)} %constant.228.clone.1) | copy-start | bytes 28
  55.5 5.9 %copy-start.2 = (f32[96,32]{0,1:T(8,128)S(1)}, f32[96,32]{0,1:T(8,128)}, u32[]{:S(2)}) copy-start(f32[96,32]{0,1:T(8,128)} %param.17) | copy-start | bytes 36868
  56.4 13.2 %all-to-all-start.1 = ((f32[8,6,1536]{2,1,0:T(8,128)}), f32[8,6,1536]{2,1,0:T(8,128)S(1)}, u32[]{:S(2)}, u32[]{:S(2)}) async-start(f32[8,6,1536]{2,1,0:T(8,128)} %broadcast_select_fusion.2), calls=%async_computation.1 | async-start | bytes 786432 | tf_op jit(solution)/shard_map/all_to_all | solution.py:171
  79.7 9.2 %collective-permute-start.7 = (f32[2,1536]{1,0:T(2,128)S(1)}, f32[2,1536]{1,0:T(2,128)S(1)}, u32[]{:S(2)}, u32[]{:S(2)}) collective-permute-start(f32[2,1536]{1,0:T(2,128)S(1)} %pad_maximum_fusion.5), channel_id=1, source_target_pairs={{0,1},{1,2},{2,3},{3,4},{4,5},{5,6},{6,7},{7,8},{8,9},{9,10},{10,1... | collective-permute-start | bytes 36872 | tf_op jit(solution)/shard_map/ppermute | solution.py:191
  90.2 4.9 %collective-permute-start.8 = (f32[2,1536]{1,0:T(2,128)S(1)}, f32[2,1536]{1,0:T(2,128)S(1)}, u32[]{:S(2)}, u32[]{:S(2)}) collective-permute-start(f32[2,1536]{1,0:T(2,128)S(1)} %pad_maximum_fusion.6), channel_id=1, source_target_pairs={{1,0},{2,1},{3,2},{4,3},{5,4},{6,5},{7,6},{8,7},{9,8},{10,9},{11,1... | collective-permute-start | bytes 36872 | tf_op jit(solution)/shard_map/ppermute | solution.py:192

commit v10 on v8

--- a/solution.py
+++ b/solution.py
@@ -30,9 +30,14 @@
     return x1, x2, x3
 
 
-def _dot3(x, e, dims):
+def _split2(x):
+    x1 = x.astype(jnp.bfloat16)
+    return x1, (x - x1.astype(jnp.float32)).astype(jnp.bfloat16)
+
+
+def _dot3(x, e, dims, split=_split3):
     out = None
-    for part in _split3(x):
+    for part in split(x):
         term = lax.dot_general(part, e, dims, preferred_element_type=jnp.float32)
         out = term if out is None else out + term
     return out
@@ -52,7 +57,7 @@
 
 def _margin_kernel(pop_ref, s2t_ref, e2t_ref, o_ref):
     for b in range(pop_ref.shape[0]):
-        o_ref[b] = _dot3(pop_ref[b] * s2t_ref[...], e2t_ref[...], ROWS)
+        o_ref[b] = _dot3(pop_ref[b] * s2t_ref[...], e2t_ref[...], ROWS, _split2)
 
 
 def _fit_kernel(pop_ref, r_ref, s2t_ref, e2_ref, o_ref):

time: 104 us -> 103 us (level)
  transfers between devices with their start and end apart: 10 -> 10, of which waited for: 9 -> 9; matrix products, arithmetic and copies ran while one was open for 4% -> 5% of each run, Pallas kernels for 0% -> 0%
where the time goes in v10:
time: 103 us; the launch traced here: 102 us
  waiting for transfers between devices  35.1 us (34%)
  starting transfers between devices  19.6 us (19%)
  Pallas kernels  17.9 us (17%)
  other arithmetic  15 us (15%)
  local copies, waits for them, and re-layouts  8.97 us (9%)
  between operations  5.71 us (6%)
    ppermute x7, waiting for transfers between devices, _xor(): return lax.ppermute(x, AXES, [(i, _partner(i, bit)) for i in range(n)])  22.5 us
    pallas_call x3, Pallas kernels, _table_call(): pl.pallas_call(kernel, grid=grid, in_specs=specs, out_specs=pl.BlockSpec(...  17.9 us
    ppermute x7, starting transfers between devices, _xor(): return lax.ppermute(x, AXES, [(i, _partner(i, bit)) for i in range(n)])  12.3 us
    ppermute x1, waiting for transfers between devices, body(): from_left = lax.ppermute(to_right, AXES, right)  6.46 us
    all_to_all x1, waiting for transfers between devices, exchange(): return lax.all_to_all(sent, 'mem', 0, 0, tiled=True)  6.1 us
    all_to_all x1, starting transfers between devices, exchange(): return lax.all_to_all(sent, 'mem', 0, 0, tiled=True)  3.47 us
  transfers between devices with their start and end apart: 10, of which 9 were waited for; matrix products, arithmetic and copies ran while one was open for 5% of the time, Pallas kernels for 0%

profile of v10, /device:TPU:6, one launch (start us, length us, event | category | flops | bytes accessed | tf_op | source)
XLA Modules:
  0.0 102.3 jit_solution(6384398010723867345)
XLA Ops:
  0.0 1.3 %fusion.42 = (s32[1]{0:T(128)}, s32[1]{0:T(128)}) fusion(s32[16]{0:T(128)} %param.19), kind=kLoop, calls=%fused_computation.151 | loop fusion | bytes 16 | tf_op jit(solution)/shard_map/slice | solution.py:116
  2.0 0.9 select_reduce_fusion.2
  2.9 2.0 %compare_and_fusion.3 = (pred[16]{0:T(512)(128)(4,1)S(1)}, s32[16]{0:T(128)S(1)}, pred[16]{0:T(512)(128)(4,1)S(1)}) fusion(s32[16]{0:T(128)} %param.19, s32[]{:T(128)} %bitcast.1, s32[]{:T(128)} %bitcast.2), kind=kLoop, calls=%fused_computation.120 | loop fusion | flops 144 | bytes 168 | tf_op jit(solution)/shard_map/jit(_take)/and | solution.py:200
  6.4 4.8 %shard_map.91 = f32[16,96,32]{2,1,0:T(8,128)} custom-call(f32[16,96,1024]{2,1,0:T(8,128)} %pop_ref.5, bf16[128,32]{1,0:T(8,128)(2,1)} %constant.230.clone.g1_ref), custom_call_target="tpu_custom_call" | custom-call | tf_op jit(solution)/shard_map/pallas_call | solution.py:75
  11.2 1.5 %reduce_sum.94 = f32[16,96]{1,0:T(8,128)S(1)} reduce(f32[16,96,32]{2,1,0:T(8,128)} %shard_map.91, f32[]{:T(128)} %constant.209.clone.1), dimensions={2}, to_apply=%region_2.3 | reduce | flops 47616 | bytes 202756 | tf_op jit(solution)/shard_map/reduce_sum | solution.py:134
  12.7 1.4 %multiply_reduce_fusion.1 = f32[96,32]{1,0:T(8,128)S(1)} fusion(f32[16,96,32]{2,1,0:T(8,128)} %shard_map.91, f32[16,96]{1,0:T(8,128)S(1)} %div.53), kind=kLoop, calls=%fused_computation.30 | loop fusion | flops 95232 | bytes 215040 | tf_op jit(solution)/shard_map/reduce_sum | solution.py:136
  14.3 2.0 %collective-permute-start = (f32[11,1536]{1,0:T(8,128)S(1)}, f32[11,1536]{1,0:T(8,128)S(1)}, u32[]{:S(2)}, u32[]{:S(2)}) collective-permute-start(f32[11,1536]{1,0:T(8,128)S(1)} %pad_maximum_fusion.3), channel_id=1, source_target_pairs={{0,8},{1,9},{2,10},{3,11},{4,12},{5,13},{6,14},{7,15},{8,0},{9,1},... | collective-permute-start | bytes 202760 | tf_op jit(solution)/shard_map/ppermute | solution.py:93
  17.7 1.4 %collective-permute-done = f32[11,1536]{1,0:T(8,128)S(1)} collective-permute-done((f32[11,1536]{1,0:T(8,128)S(1)}, f32[11,1536]{1,0:T(8,128)S(1)}, u32[]{:S(2)}, u32[]{:S(2)}) %collective-permute-start) | collective-permute-done | bytes 67616 | tf_op jit(solution)/shard_map/ppermute | solution.py:93
  19.2 4.0 %collective-permute-start.1 = (f32[19,1536]{1,0:T(8,128)S(1)}, f32[19,1536]{1,0:T(8,128)S(1)}, u32[]{:S(2)}, u32[]{:S(2)}) collective-permute-start(f32[19,1536]{1,0:T(8,128)S(1)} %pad_maximum_fusion.2), channel_id=1, source_target_pairs={{0,24},{1,25},{2,26},{3,27},{4,28},{5,29},{6,30},{7,31},{8,16},{9,... | collective-permute-start | bytes 350216 | tf_op jit(solution)/shard_map/ppermute | solution.py:93
  24.6 0.7 and_reduce_fusion
  25.3 1.0 collective-permute-done.1
  26.5 0.9 collective-permute-start.2
  27.4 5.3 %collective-permute-done.2 = f32[35,1536]{1,0:T(8,128)S(1)} collective-permute-done((f32[35,1536]{1,0:T(8,128)S(1)}, f32[35,1536]{1,0:T(8,128)S(1)}, u32[]{:S(2)}, u32[]{:S(2)}) %collective-permute-start.2) | collective-permute-done | bytes 215072 | tf_op jit(solution)/shard_map/ppermute | solution.py:93
  33.5 9.4 %collective-permute-done.3 = f32[67,1536]{1,0:T(8,128)S(1)} collective-permute-done((f32[67,1536]{1,0:T(8,128)S(1)}, f32[67,1536]{1,0:T(8,128)S(1)}, u32[]{:S(2)}, u32[]{:S(2)}) %collective-permute-start.3) | collective-permute-done | bytes 411680 | tf_op jit(solution)/shard_map/ppermute | solution.py:93
  43.1 1.2 %collective-permute-done.4 = f32[4,1536]{1,0:T(4,128)S(1)} collective-permute-done((f32[4,1536]{1,0:T(4,128)S(1)}, f32[4,1536]{1,0:T(4,128)S(1)}, u32[]{:S(2)}, u32[]{:S(2)}) %collective-permute-start.4) | collective-permute-done | bytes 24608 | tf_op jit(solution)/shard_map/ppermute | solution.py:93
  44.3 1.7 %collective-permute-start.5 = (f32[4,1536]{1,0:T(4,128)S(1)}, f32[4,1536]{1,0:T(4,128)S(1)}, u32[]{:S(2)}, u32[]{:S(2)}) collective-permute-start(f32[4,1536]{1,0:T(4,128)S(1)} %fusion.40), channel_id=1, source_target_pairs={{0,2},{1,3},{2,0},{3,1},{4,6},{5,7},{6,4},{7,5},{8,10},{9,11},{10,... | collective-permute-start | bytes 73736 | tf_op jit(solution)/shard_map/ppermute | solution.py:93
  46.0 2.2 %collective-permute-done.5 = f32[4,1536]{1,0:T(4,128)S(1)} collective-permute-done((f32[4,1536]{1,0:T(4,128)S(1)}, f32[4,1536]{1,0:T(4,128)S(1)}, u32[]{:S(2)}, u32[]{:S(2)}) %collective-permute-start.5) | collective-permute-done | bytes 24608 | tf_op jit(solution)/shard_map/ppermute | solution.py:93
  48.2 3.1 %collective-permute-start.6 = (f32[4,1536]{1,0:T(4,128)S(1)}, f32[4,1536]{1,0:T(4,128)S(1)}, u32[]{:S(2)}, u32[]{:S(2)}) collective-permute-start(f32[4,1536]{1,0:T(4,128)S(1)} %add.315), channel_id=1, source_target_pairs={{0,6},{1,7},{2,4},{3,5},{4,2},{5,3},{6,0},{7,1},{8,14},{9,15},{10,... | collective-permute-start | bytes 73736 | tf_op jit(solution)/shard_map/ppermute | solution.py:93
  51.4 2.0 %collective-permute-done.6 = f32[4,1536]{1,0:T(4,128)S(1)} collective-permute-done((f32[4,1536]{1,0:T(4,128)S(1)}, f32[4,1536]{1,0:T(4,128)S(1)}, u32[]{:S(2)}, u32[]{:S(2)}) %collective-permute-start.6) | collective-permute-done | bytes 24608 | tf_op jit(solution)/shard_map/ppermute | solution.py:93
  55.2 0.7 gather_fusion.1
  56.0 0.9 copy.45.s2t_ref
  57.0 5.6 %shard_map.92 = f32[16,96,32]{2,1,0:T(8,128)} custom-call(f32[16,96,1024]{2,1,0:T(8,128)} %pop_ref.5, f32[96,1024]{1,0:T(8,128)} %copy.45.s2t_ref, bf16[1024,32]{1,0:T(8,128)(2,1)} %constant.232.clone.e2t_ref), custom_call_target="tpu_custom_call" | custom-call | tf_op jit(solution)/shard_map/pallas_call | solution.py:75
  62.6 1.4 %broadcast_multiply_fusion.1 = f32[16,96,32]{2,1,0:T(8,128)S(1)} fusion(f32[16,96,32]{2,1,0:T(8,128)} %shard_map.92, f32[16,96]{1,0:T(8,128)S(1)} %div.53), kind=kLoop, calls=%fused_computation.35 | loop fusion | flops 49152 | bytes 399360 | tf_op jit(solution)/shard_map/mul | solution.py:185
  64.0 1.0 reduce_sum.100
  65.4 1.9 %collective-permute-start.7 = (f32[2,1536]{1,0:T(2,128)S(1)}, f32[2,1536]{1,0:T(2,128)S(1)}, u32[]{:S(2)}, u32[]{:S(2)}) collective-permute-start(f32[2,1536]{1,0:T(2,128)S(1)} %pad_maximum_fusion.5), channel_id=1, source_target_pairs={{0,1},{1,2},{2,3},{3,4},{4,5},{5,6},{6,7},{7,8},{8,9},{9,10},{10,1... | collective-permute-start | bytes 36872 | tf_op jit(solution)/shard_map/ppermute | solution.py:195
  67.3 0.8 broadcast_select_fusion.2
  68.1 6.5 %collective-permute-done.7 = f32[2,1536]{1,0:T(2,128)S(1)} collective-permute-done((f32[2,1536]{1,0:T(2,128)S(1)}, f32[2,1536]{1,0:T(2,128)S(1)}, u32[]{:S(2)}, u32[]{:S(2)}) %collective-permute-start.7) | collective-permute-done | bytes 12320 | tf_op jit(solution)/shard_map/ppermute | solution.py:195
  75.9 1.9 %collective-permute-start.8 = (f32[2,1536]{1,0:T(2,128)S(1)}, f32[2,1536]{1,0:T(2,128)S(1)}, u32[]{:S(2)}, u32[]{:S(2)}) collective-permute-start(f32[2,1536]{1,0:T(2,128)S(1)} %pad_maximum_fusion.6), channel_id=1, source_target_pairs={{1,0},{2,1},{3,2},{4,3},{5,4},{6,5},{7,6},{8,7},{9,8},{10,9},{11,1... | collective-permute-start | bytes 36872 | tf_op jit(solution)/shard_map/ppermute | solution.py:196
  79.2 3.5 %all-to-all-start.1 = ((f32[8,6,1536]{2,1,0:T(8,128)}), f32[8,6,1536]{2,1,0:T(8,128)S(1)}, u32[]{:S(2)}, u32[]{:S(2)}) async-start(f32[8,6,1536]{2,1,0:T(8,128)} %broadcast_select_fusion.2), calls=%async_computation.1 | async-start | bytes 786432 | tf_op jit(solution)/shard_map/all_to_all | solution.py:176
  85.4 6.1 %all-to-all-done.1 = f32[8,6,1536]{2,1,0:T(8,128)S(1)} async-done(((f32[8,6,1536]{2,1,0:T(8,128)}), f32[8,6,1536]{2,1,0:T(8,128)S(1)}, u32[]{:S(2)}, u32[]{:S(2)}) %all-to-all-start.1) | async-done | bytes 294944 | tf_op jit(solution)/shard_map/all_to_all | solution.py:176
  93.6 1.2 %broadcast_multiply_fusion.r_ref = f32[16,96,32]{2,1,0:T(8,128)} fusion(f32[16,96,32]{2,1,0:T(8,128)S(1)} %bitcast.40, f32[16,96]{1,0:T(8,128)S(1)} %div.53), kind=kLoop, calls=%fused_computation.34 | loop fusion | flops 49152 | bytes 399360 | tf_op jit(solution)/shard_map/mul | solution.py:202
  94.8 7.5 %shard_map.93 = f32[16,96,1024]{2,1,0:T(8,128)} custom-call(f32[16,96,1024]{2,1,0:T(8,128)} %pop_ref.5, f32[16,96,32]{2,1,0:T(8,128)} %broadcast_multiply_fusion.r_ref, f32[96,1024]{1,0:T(8,128)} %copy.45.s2t_ref, bf16[32,1024]{1,0:T(8,128)(2,1)} %constant.231.clone.e2_ref), custom_call_target="tpu_custom_call" | custom-call | tf_op jit(solution)/shard_map/pallas_call | solution.py:75
  (103 shorter events, 10.8 us)
Async XLA Ops:
  6.4 6.3 %copy-start.3 = (f32[16,96]{1,0:T(8,128)S(1)}, f32[16,96]{1,0:T(8,128)}, u32[]{:S(2)}) copy-start(f32[16,96]{1,0:T(8,128)} %param.16) | copy-start | bytes 18436
  11.2 3.0 %copy-start = (f32[8,1536]{1,0:T(8,128)S(1)}, f32[8,1536]{1,0:T(8,128)}, u32[]{:S(2)}) copy-start(f32[8,1536]{1,0:T(8,128)} %param.18) | copy-start | bytes 147460
  11.2 13.3 %copy-start.4 = (s32[2]{0:T(128)S(1)}, s32[2]{0:T(128)}, u32[]{:S(2)}) copy-start(s32[2]{0:T(128)} %constant.228.clone.1) | copy-start | bytes 28
  14.3 4.8 %collective-permute-start = (f32[11,1536]{1,0:T(8,128)S(1)}, f32[11,1536]{1,0:T(8,128)S(1)}, u32[]{:S(2)}, u32[]{:S(2)}) collective-permute-start(f32[11,1536]{1,0:T(8,128)S(1)} %pad_maximum_fusion.3), channel_id=1, source_target_pairs={{0,8},{1,9},{2,10},{3,11},{4,12},{5,13},{6,14},{7,15},{8,0},{9,1},... | collective-permute-start | bytes 202760 | tf_op jit(solution)/shard_map/ppermute | solution.py:93
  19.2 7.1 %collective-permute-start.1 = (f32[19,1536]{1,0:T(8,128)S(1)}, f32[19,1536]{1,0:T(8,128)S(1)}, u32[]{:S(2)}, u32[]{:S(2)}) collective-permute-start(f32[19,1536]{1,0:T(8,128)S(1)} %pad_maximum_fusion.2), channel_id=1, source_target_pairs={{0,24},{1,25},{2,26},{3,27},{4,28},{5,29},{6,30},{7,31},{8,16},{9,... | collective-permute-start | bytes 350216 | tf_op jit(solution)/shard_map/ppermute | solution.py:93
  26.5 6.3 %collective-permute-start.2 = (f32[35,1536]{1,0:T(8,128)S(1)}, f32[35,1536]{1,0:T(8,128)S(1)}, u32[]{:S(2)}, u32[]{:S(2)}) collective-permute-start(f32[35,1536]{1,0:T(8,128)S(1)} %pad_maximum_fusion.1), channel_id=1, source_target_pairs={{0,32},{1,33},{2,34},{3,35},{4,36},{5,37},{6,38},{7,39},{8,40},{9,... | collective-permute-start | bytes 645128 | tf_op jit(solution)/shard_map/ppermute | solution.py:93
  32.9 21.0 %copy-start.2 = (s32[1024]{0:T(1024)S(1)}, s32[1024]{0:T(1024)}, u32[]{:S(2)}) copy-start(s32[1024]{0:T(1024)} %param.20) | copy-start | bytes 12292
  32.9 10.0 %collective-permute-start.3 = (f32[67,1536]{1,0:T(8,128)S(1)}, f32[67,1536]{1,0:T(8,128)S(1)}, u32[]{:S(2)}, u32[]{:S(2)}) collective-permute-start(f32[67,1536]{1,0:T(8,128)S(1)} %pad_maximum_fusion), channel_id=1, source_target_pairs={{0,96},{1,97},{2,98},{3,99},{4,100},{5,101},{6,102},{7,103},{8,104... | collective-permute-start | bytes 1234952 | tf_op jit(solution)/shard_map/ppermute | solution.py:93
  43.0 1.3 %collective-permute-start.4 = (f32[4,1536]{1,0:T(4,128)S(1)}, f32[4,1536]{1,0:T(4,128)S(1)}, u32[]{:S(2)}, u32[]{:S(2)}) collective-permute-start(f32[4,1536]{1,0:T(4,128)S(1)} %pad_maximum_fusion.4), channel_id=1, source_target_pairs={{0,1},{1,0},{2,3},{3,2},{4,5},{5,4},{6,7},{7,6},{8,9},{9,8},{10,11... | collective-permute-start | bytes 73736 | tf_op jit(solution)/shard_map/ppermute | solution.py:93
  44.3 3.9 %collective-permute-start.5 = (f32[4,1536]{1,0:T(4,128)S(1)}, f32[4,1536]{1,0:T(4,128)S(1)}, u32[]{:S(2)}, u32[]{:S(2)}) collective-permute-start(f32[4,1536]{1,0:T(4,128)S(1)} %fusion.40), channel_id=1, source_target_pairs={{0,2},{1,3},{2,0},{3,1},{4,6},{5,7},{6,4},{7,5},{8,10},{9,11},{10,... | collective-permute-start | bytes 73736 | tf_op jit(solution)/shard_map/ppermute | solution.py:93
  48.2 5.1 %collective-permute-start.6 = (f32[4,1536]{1,0:T(4,128)S(1)}, f32[4,1536]{1,0:T(4,128)S(1)}, u32[]{:S(2)}, u32[]{:S(2)}) collective-permute-start(f32[4,1536]{1,0:T(4,128)S(1)} %add.315), channel_id=1, source_target_pairs={{0,6},{1,7},{2,4},{3,5},{4,2},{5,3},{6,0},{7,1},{8,14},{9,15},{10,... | collective-permute-start | bytes 73736 | tf_op jit(solution)/shard_map/ppermute | solution.py:93
  55.2 0.8 copy-start.1
  65.4 9.2 %collective-permute-start.7 = (f32[2,1536]{1,0:T(2,128)S(1)}, f32[2,1536]{1,0:T(2,128)S(1)}, u32[]{:S(2)}, u32[]{:S(2)}) collective-permute-start(f32[2,1536]{1,0:T(2,128)S(1)} %pad_maximum_fusion.5), channel_id=1, source_target_pairs={{0,1},{1,2},{2,3},{3,4},{4,5},{5,6},{6,7},{7,8},{8,9},{9,10},{10,1... | collective-permute-start | bytes 36872 | tf_op jit(solution)/shard_map/ppermute | solution.py:195
  75.9 7.6 %collective-permute-start.8 = (f32[2,1536]{1,0:T(2,128)S(1)}, f32[2,1536]{1,0:T(2,128)S(1)}, u32[]{:S(2)}, u32[]{:S(2)}) collective-permute-start(f32[2,1536]{1,0:T(2,128)S(1)} %pad_maximum_fusion.6), channel_id=1, source_target_pairs={{1,0},{2,1},{3,2},{4,3},{5,4},{6,5},{7,6},{8,7},{9,8},{10,9},{11,1... | collective-permute-start | bytes 36872 | tf_op jit(solution)/shard_map/ppermute | solution.py:196
  79.2 12.3 %all-to-all-start.1 = ((f32[8,6,1536]{2,1,0:T(8,128)}), f32[8,6,1536]{2,1,0:T(8,128)S(1)}, u32[]{:S(2)}, u32[]{:S(2)}) async-start(f32[8,6,1536]{2,1,0:T(8,128)} %broadcast_select_fusion.2), calls=%async_computation.1 | async-start | bytes 786432 | tf_op jit(solution)/shard_map/all_to_all | solution.py:176

commit v11 on v8

--- a/solution.py
+++ b/solution.py
@@ -14,6 +14,7 @@
 MEMBERS = 8
 ROOMY = 6
 AXES = ("col", "mem")
+SHIP_APART = 32
 
 
 HI = lax.Precision.HIGHEST
@@ -136,10 +137,14 @@
         pool = zone_target
         bit = MEMBERS
         while bit < n:
-            got = _xor(jnp.concatenate([nat, flag, pool], axis=0), n, bit)
+            if pool.shape[0] < SHIP_APART:
+                got = _xor(jnp.concatenate([nat, flag, pool], axis=0), n, bit)
+                theirs = got[nat_rows + 1:]
+            else:
+                got = _xor(jnp.concatenate([nat, flag], axis=0), n, bit)
+                theirs = _xor(pool, n, bit)
             nat = nat + got[:nat_rows]
             flag = flag + got[nat_rows:nat_rows + 1]
-            theirs = got[nat_rows + 1:]
             pool = jnp.where((idx & bit) == 0, jnp.concatenate([pool, theirs], 0), jnp.concatenate([theirs, pool], 0))
             bit *= 2
 

time: 104 us -> 103 us (level)
    ppermute x7 -> x9, waiting for transfers between devices: 22.5 us -> 19.9 us  [_xor(): return lax.ppermute(x, AXES, [(i, _partner(i, bit)) for i in range(n)])]
    all_to_all x1, waiting for transfers between devices: 6.1 us -> 7.36 us  [exchange(): return lax.all_to_all(sent, 'mem', 0, 0, tiled=True)]
    ppermute x7 -> x9, starting transfers between devices: 12.3 us -> 12.5 us  [_xor(): return lax.ppermute(x, AXES, [(i, _partner(i, bit)) for i in range(n)])]
  transfers between devices with their start and end apart: 10 -> 12, of which waited for: 9 -> 10; matrix products, arithmetic and copies ran while one was open for 4% -> 9% of each run, Pallas kernels for 0% -> 6%
where the time goes in v11:
time: 103 us; the launch traced here: 102 us
  waiting for transfers between devices  34.6 us (34%)
  starting transfers between devices  19.8 us (19%)
  Pallas kernels  18.6 us (18%)
  other arithmetic  14.7 us (14%)
  local copies, waits for them, and re-layouts  8.74 us (8%)
  between operations  5.55 us (5%)
    ppermute x9, waiting for transfers between devices, _xor(): return lax.ppermute(x, AXES, [(i, _partner(i, bit)) for i in range(n)])  19.9 us
    pallas_call x3, Pallas kernels, _table_call(): pl.pallas_call(kernel, grid=grid, in_specs=specs, out_specs=pl.BlockSpec(...  18.6 us
    ppermute x9, starting transfers between devices, _xor(): return lax.ppermute(x, AXES, [(i, _partner(i, bit)) for i in range(n)])  12.5 us
    all_to_all x1, waiting for transfers between devices, exchange(): return lax.all_to_all(sent, 'mem', 0, 0, tiled=True)  7.36 us
    ppermute x1, waiting for transfers between devices, body(): from_left = lax.ppermute(to_right, AXES, right)  7.29 us
    all_to_all x1, starting transfers between devices, exchange(): return lax.all_to_all(sent, 'mem', 0, 0, tiled=True)  3.47 us
  transfers between devices with their start and end apart: 12, of which 10 were waited for; matrix products, arithmetic and copies ran while one was open for 9% of the time, Pallas kernels for 6%

profile of v11, /device:TPU:6, one launch (start us, length us, event | category | flops | bytes accessed | tf_op | source)
XLA Modules:
  0.0 101.9 jit_solution(18325724011653124774)
XLA Ops:
  0.0 1.3 %fusion.42 = (s32[1]{0:T(128)}, s32[1]{0:T(128)}) fusion(s32[16]{0:T(128)} %param.19), kind=kLoop, calls=%fused_computation.151 | loop fusion | bytes 16 | tf_op jit(solution)/shard_map/slice | solution.py:112
  1.9 0.9 select_reduce_fusion.2
  2.8 1.9 %compare_and_fusion.3 = (pred[16]{0:T(512)(128)(4,1)S(1)}, s32[16]{0:T(128)S(1)}, pred[16]{0:T(512)(128)(4,1)S(1)}) fusion(s32[16]{0:T(128)} %param.19, s32[]{:T(128)} %bitcast.1, s32[]{:T(128)} %bitcast.2), kind=kLoop, calls=%fused_computation.120 | loop fusion | flops 144 | bytes 168 | tf_op jit(solution)/shard_map/jit(_take)/and | solution.py:200
  6.2 4.8 %shard_map.91 = f32[16,96,32]{2,1,0:T(8,128)} custom-call(f32[16,96,1024]{2,1,0:T(8,128)} %pop_ref.5, bf16[128,32]{1,0:T(8,128)(2,1)} %constant.230.clone.g1_ref), custom_call_target="tpu_custom_call" | custom-call | tf_op jit(solution)/shard_map/pallas_call | solution.py:71
  11.0 1.5 %reduce_sum.94 = f32[16,96]{1,0:T(8,128)S(1)} reduce(f32[16,96,32]{2,1,0:T(8,128)} %shard_map.91, f32[]{:T(128)} %constant.209.clone.1), dimensions={2}, to_apply=%region_2.3 | reduce | flops 47616 | bytes 202756 | tf_op jit(solution)/shard_map/reduce_sum | solution.py:130
  12.5 1.4 %multiply_reduce_fusion.1 = f32[96,32]{1,0:T(8,128)S(1)} fusion(f32[16,96,32]{2,1,0:T(8,128)} %shard_map.91, f32[16,96]{1,0:T(8,128)S(1)} %div.53), kind=kLoop, calls=%fused_computation.30 | loop fusion | flops 95232 | bytes 215040 | tf_op jit(solution)/shard_map/reduce_sum | solution.py:132
  14.1 2.0 %collective-permute-start = (f32[11,1536]{1,0:T(8,128)S(1)}, f32[11,1536]{1,0:T(8,128)S(1)}, u32[]{:S(2)}, u32[]{:S(2)}) collective-permute-start(f32[11,1536]{1,0:T(8,128)S(1)} %pad_maximum_fusion.1), channel_id=1, source_target_pairs={{0,8},{1,9},{2,10},{3,11},{4,12},{5,13},{6,14},{7,15},{8,0},{9,1},... | collective-permute-start | bytes 202760 | tf_op jit(solution)/shard_map/ppermute | solution.py:89
  17.4 1.5 %collective-permute-done = f32[11,1536]{1,0:T(8,128)S(1)} collective-permute-done((f32[11,1536]{1,0:T(8,128)S(1)}, f32[11,1536]{1,0:T(8,128)S(1)}, u32[]{:S(2)}, u32[]{:S(2)}) %collective-permute-start) | collective-permute-done | bytes 67616 | tf_op jit(solution)/shard_map/ppermute | solution.py:89
  19.0 4.0 %collective-permute-start.1 = (f32[19,1536]{1,0:T(8,128)S(1)}, f32[19,1536]{1,0:T(8,128)S(1)}, u32[]{:S(2)}, u32[]{:S(2)}) collective-permute-start(f32[19,1536]{1,0:T(8,128)S(1)} %pad_maximum_fusion), channel_id=1, source_target_pairs={{0,24},{1,25},{2,26},{3,27},{4,28},{5,29},{6,30},{7,31},{8,16},{9,... | collective-permute-start | bytes 350216 | tf_op jit(solution)/shard_map/ppermute | solution.py:89
  23.0 3.1 %collective-permute-done.1 = f32[19,1536]{1,0:T(8,128)S(1)} collective-permute-done((f32[19,1536]{1,0:T(8,128)S(1)}, f32[19,1536]{1,0:T(8,128)S(1)}, u32[]{:S(2)}, u32[]{:S(2)}) %collective-permute-start.1) | collective-permute-done | bytes 116768 | tf_op jit(solution)/shard_map/ppermute | solution.py:89
  26.2 0.9 collective-permute-start.2
  28.3 1.8 %collective-permute-done.2 = f32[3,1536]{1,0:T(4,128)S(1)} collective-permute-done((f32[3,1536]{1,0:T(4,128)S(1)}, f32[3,1536]{1,0:T(4,128)S(1)}, u32[]{:S(2)}, u32[]{:S(2)}) %collective-permute-start.2) | collective-permute-done | bytes 18464 | tf_op jit(solution)/shard_map/ppermute | solution.py:89
  30.7 0.7 and_reduce_fusion
  31.4 3.8 %collective-permute-done.3 = f32[3,1536]{1,0:T(4,128)S(1)} collective-permute-done((f32[3,1536]{1,0:T(4,128)S(1)}, f32[3,1536]{1,0:T(4,128)S(1)}, u32[]{:S(2)}, u32[]{:S(2)}) %collective-permute-start.3) | collective-permute-done | bytes 18464 | tf_op jit(solution)/shard_map/ppermute | solution.py:89
  35.4 1.2 %collective-permute-done.4 = f32[4,1536]{1,0:T(4,128)S(1)} collective-permute-done((f32[4,1536]{1,0:T(4,128)S(1)}, f32[4,1536]{1,0:T(4,128)S(1)}, u32[]{:S(2)}, u32[]{:S(2)}) %collective-permute-start.4) | collective-permute-done | bytes 24608 | tf_op jit(solution)/shard_map/ppermute | solution.py:89
  36.6 1.7 %collective-permute-start.5 = (f32[4,1536]{1,0:T(4,128)S(1)}, f32[4,1536]{1,0:T(4,128)S(1)}, u32[]{:S(2)}, u32[]{:S(2)}) collective-permute-start(f32[4,1536]{1,0:T(4,128)S(1)} %fusion.40), channel_id=1, source_target_pairs={{0,2},{1,3},{2,0},{3,1},{4,6},{5,7},{6,4},{7,5},{8,10},{9,11},{10,... | collective-permute-start | bytes 73736 | tf_op jit(solution)/shard_map/ppermute | solution.py:89
  38.3 2.2 %collective-permute-done.5 = f32[4,1536]{1,0:T(4,128)S(1)} collective-permute-done((f32[4,1536]{1,0:T(4,128)S(1)}, f32[4,1536]{1,0:T(4,128)S(1)}, u32[]{:S(2)}, u32[]{:S(2)}) %collective-permute-start.5) | collective-permute-done | bytes 24608 | tf_op jit(solution)/shard_map/ppermute | solution.py:89
  40.5 3.1 %collective-permute-start.6 = (f32[4,1536]{1,0:T(4,128)S(1)}, f32[4,1536]{1,0:T(4,128)S(1)}, u32[]{:S(2)}, u32[]{:S(2)}) collective-permute-start(f32[4,1536]{1,0:T(4,128)S(1)} %add.315), channel_id=1, source_target_pairs={{0,6},{1,7},{2,4},{3,5},{4,2},{5,3},{6,0},{7,1},{8,14},{9,15},{10,... | collective-permute-start | bytes 73736 | tf_op jit(solution)/shard_map/ppermute | solution.py:89
  43.7 1.9 %collective-permute-done.6 = f32[4,1536]{1,0:T(4,128)S(1)} collective-permute-done((f32[4,1536]{1,0:T(4,128)S(1)}, f32[4,1536]{1,0:T(4,128)S(1)}, u32[]{:S(2)}, u32[]{:S(2)}) %collective-permute-start.6) | collective-permute-done | bytes 24608 | tf_op jit(solution)/shard_map/ppermute | solution.py:89
  47.5 0.9 copy.45.s2t_ref
  48.4 6.3 %shard_map.92 = f32[16,96,32]{2,1,0:T(8,128)} custom-call(f32[16,96,1024]{2,1,0:T(8,128)} %pop_ref.5, f32[96,1024]{1,0:T(8,128)} %copy.45.s2t_ref, bf16[1024,32]{1,0:T(8,128)(2,1)} %constant.232.clone.e2t_ref), custom_call_target="tpu_custom_call" | custom-call | tf_op jit(solution)/shard_map/pallas_call | solution.py:71
  54.7 1.4 %broadcast_multiply_fusion.1 = f32[16,96,32]{2,1,0:T(8,128)S(1)} fusion(f32[16,96,32]{2,1,0:T(8,128)} %shard_map.92, f32[16,96]{1,0:T(8,128)S(1)} %div.53), kind=kLoop, calls=%fused_computation.34 | loop fusion | flops 49152 | bytes 399360 | tf_op jit(solution)/shard_map/mul | solution.py:185
  56.1 1.0 reduce_sum.100
  57.5 1.9 %collective-permute-start.9 = (f32[2,1536]{1,0:T(2,128)S(1)}, f32[2,1536]{1,0:T(2,128)S(1)}, u32[]{:S(2)}, u32[]{:S(2)}) collective-permute-start(f32[2,1536]{1,0:T(2,128)S(1)} %pad_maximum_fusion.5), channel_id=1, source_target_pairs={{0,1},{1,2},{2,3},{3,4},{4,5},{5,6},{6,7},{7,8},{8,9},{9,10},{10,1... | collective-permute-start | bytes 36872 | tf_op jit(solution)/shard_map/ppermute | solution.py:195
  59.4 7.3 %collective-permute-done.9 = f32[2,1536]{1,0:T(2,128)S(1)} collective-permute-done((f32[2,1536]{1,0:T(2,128)S(1)}, f32[2,1536]{1,0:T(2,128)S(1)}, u32[]{:S(2)}, u32[]{:S(2)}) %collective-permute-start.9) | collective-permute-done | bytes 12320 | tf_op jit(solution)/shard_map/ppermute | solution.py:195
  68.1 1.9 %collective-permute-start.10 = (f32[2,1536]{1,0:T(2,128)S(1)}, f32[2,1536]{1,0:T(2,128)S(1)}, u32[]{:S(2)}, u32[]{:S(2)}) collective-permute-start(f32[2,1536]{1,0:T(2,128)S(1)} %pad_maximum_fusion.6), channel_id=1, source_target_pairs={{1,0},{2,1},{3,2},{4,3},{5,4},{6,5},{7,6},{8,7},{9,8},{10,9},{11,1... | collective-permute-start | bytes 36872 | tf_op jit(solution)/shard_map/ppermute | solution.py:196
  72.6 4.4 %collective-permute-done.8 = f32[64,1536]{1,0:T(8,128)S(1)} collective-permute-done((f32[64,1536]{1,0:T(8,128)S(1)}, f32[64,1536]{1,0:T(8,128)S(1)}, u32[]{:S(2)}, u32[]{:S(2)}) %collective-permute-start.8) | collective-permute-done | bytes 393248 | tf_op jit(solution)/shard_map/ppermute | solution.py:89
  77.8 0.8 broadcast_select_fusion.2
  78.8 3.5 %all-to-all-start.1 = ((f32[8,6,1536]{2,1,0:T(8,128)}), f32[8,6,1536]{2,1,0:T(8,128)S(1)}, u32[]{:S(2)}, u32[]{:S(2)}) async-start(f32[8,6,1536]{2,1,0:T(8,128)} %broadcast_select_fusion.2), calls=%async_computation.1 | async-start | bytes 786432 | tf_op jit(solution)/shard_map/all_to_all | solution.py:176
  83.8 7.4 %all-to-all-done.1 = f32[8,6,1536]{2,1,0:T(8,128)S(1)} async-done(((f32[8,6,1536]{2,1,0:T(8,128)}), f32[8,6,1536]{2,1,0:T(8,128)S(1)}, u32[]{:S(2)}, u32[]{:S(2)}) %all-to-all-start.1) | async-done | bytes 294944 | tf_op jit(solution)/shard_map/all_to_all | solution.py:176
  93.3 1.2 %broadcast_multiply_fusion.r_ref = f32[16,96,32]{2,1,0:T(8,128)} fusion(f32[16,96,32]{2,1,0:T(8,128)S(1)} %bitcast.40, f32[16,96]{1,0:T(8,128)S(1)} %div.53), kind=kLoop, calls=%fused_computation.33 | loop fusion | flops 49152 | bytes 399360 | tf_op jit(solution)/shard_map/mul | solution.py:202
  94.4 7.5 %shard_map.93 = f32[16,96,1024]{2,1,0:T(8,128)} custom-call(f32[16,96,1024]{2,1,0:T(8,128)} %pop_ref.5, f32[16,96,32]{2,1,0:T(8,128)} %broadcast_multiply_fusion.r_ref, f32[96,1024]{1,0:T(8,128)} %copy.45.s2t_ref, bf16[32,1024]{1,0:T(8,128)(2,1)} %constant.231.clone.e2_ref), custom_call_target="tpu_custom_call" | custom-call | tf_op jit(solution)/shard_map/pallas_call | solution.py:71
  (105 shorter events, 11.3 us)
Async XLA Ops:
  6.2 6.3 %copy-start.3 = (f32[16,96]{1,0:T(8,128)S(1)}, f32[16,96]{1,0:T(8,128)}, u32[]{:S(2)}) copy-start(f32[16,96]{1,0:T(8,128)} %param.16) | copy-start | bytes 18436
  11.0 3.0 %copy-start = (f32[8,1536]{1,0:T(8,128)S(1)}, f32[8,1536]{1,0:T(8,128)}, u32[]{:S(2)}) copy-start(f32[8,1536]{1,0:T(8,128)} %param.18) | copy-start | bytes 147460
  11.0 19.7 %copy-start.4 = (s32[2]{0:T(128)S(1)}, s32[2]{0:T(128)}, u32[]{:S(2)}) copy-start(s32[2]{0:T(128)} %constant.228.clone.1) | copy-start | bytes 28
  12.5 33.6 %copy-start.2 = (s32[1024]{0:T(1024)S(1)}, s32[1024]{0:T(1024)}, u32[]{:S(2)}) copy-start(s32[1024]{0:T(1024)} %param.20) | copy-start | bytes 12292
  12.5 34.9 %copy-start.1 = (f32[96,32]{0,1:T(8,128)S(1)}, f32[96,32]{0,1:T(8,128)}, u32[]{:S(2)}) copy-start(f32[96,32]{0,1:T(8,128)} %param.17) | copy-start | bytes 36868
  14.1 4.8 %collective-permute-start = (f32[11,1536]{1,0:T(8,128)S(1)}, f32[11,1536]{1,0:T(8,128)S(1)}, u32[]{:S(2)}, u32[]{:S(2)}) collective-permute-start(f32[11,1536]{1,0:T(8,128)S(1)} %pad_maximum_fusion.1), channel_id=1, source_target_pairs={{0,8},{1,9},{2,10},{3,11},{4,12},{5,13},{6,14},{7,15},{8,0},{9,1},... | collective-permute-start | bytes 202760 | tf_op jit(solution)/shard_map/ppermute | solution.py:89
  19.0 7.1 %collective-permute-start.1 = (f32[19,1536]{1,0:T(8,128)S(1)}, f32[19,1536]{1,0:T(8,128)S(1)}, u32[]{:S(2)}, u32[]{:S(2)}) collective-permute-start(f32[19,1536]{1,0:T(8,128)S(1)} %pad_maximum_fusion), channel_id=1, source_target_pairs={{0,24},{1,25},{2,26},{3,27},{4,28},{5,29},{6,30},{7,31},{8,16},{9,... | collective-permute-start | bytes 350216 | tf_op jit(solution)/shard_map/ppermute | solution.py:89
  26.2 3.9 %collective-permute-start.2 = (f32[3,1536]{1,0:T(4,128)S(1)}, f32[3,1536]{1,0:T(4,128)S(1)}, u32[]{:S(2)}, u32[]{:S(2)}) collective-permute-start(f32[3,1536]{1,0:T(4,128)S(1)} %pad_maximum_fusion.2), channel_id=1, source_target_pairs={{0,32},{1,33},{2,34},{3,35},{4,36},{5,37},{6,38},{7,39},{8,40},{9,... | collective-permute-start | bytes 55304 | tf_op jit(solution)/shard_map/ppermute | solution.py:89
  30.1 5.1 %collective-permute-start.3 = (f32[3,1536]{1,0:T(4,128)S(1)}, f32[3,1536]{1,0:T(4,128)S(1)}, u32[]{:S(2)}, u32[]{:S(2)}) collective-permute-start(f32[3,1536]{1,0:T(4,128)S(1)} %pad_maximum_fusion.3), channel_id=1, source_target_pairs={{0,96},{1,97},{2,98},{3,99},{4,100},{5,101},{6,102},{7,103},{8,104... | collective-permute-start | bytes 55304 | tf_op jit(solution)/shard_map/ppermute | solution.py:89
  35.3 1.3 %collective-permute-start.4 = (f32[4,1536]{1,0:T(4,128)S(1)}, f32[4,1536]{1,0:T(4,128)S(1)}, u32[]{:S(2)}, u32[]{:S(2)}) collective-permute-start(f32[4,1536]{1,0:T(4,128)S(1)} %pad_maximum_fusion.4), channel_id=1, source_target_pairs={{0,1},{1,0},{2,3},{3,2},{4,5},{5,4},{6,7},{7,6},{8,9},{9,8},{10,11... | collective-permute-start | bytes 73736 | tf_op jit(solution)/shard_map/ppermute | solution.py:89
  36.6 3.9 %collective-permute-start.5 = (f32[4,1536]{1,0:T(4,128)S(1)}, f32[4,1536]{1,0:T(4,128)S(1)}, u32[]{:S(2)}, u32[]{:S(2)}) collective-permute-start(f32[4,1536]{1,0:T(4,128)S(1)} %fusion.40), channel_id=1, source_target_pairs={{0,2},{1,3},{2,0},{3,1},{4,6},{5,7},{6,4},{7,5},{8,10},{9,11},{10,... | collective-permute-start | bytes 73736 | tf_op jit(solution)/shard_map/ppermute | solution.py:89
  40.5 5.1 %collective-permute-start.6 = (f32[4,1536]{1,0:T(4,128)S(1)}, f32[4,1536]{1,0:T(4,128)S(1)}, u32[]{:S(2)}, u32[]{:S(2)}) collective-permute-start(f32[4,1536]{1,0:T(4,128)S(1)} %add.315), channel_id=1, source_target_pairs={{0,6},{1,7},{2,4},{3,5},{4,2},{5,3},{6,0},{7,1},{8,14},{9,15},{10,... | collective-permute-start | bytes 73736 | tf_op jit(solution)/shard_map/ppermute | solution.py:89
  43.6 24.3 %collective-permute-start.7 = (f32[32,1536]{1,0:T(8,128)S(1)}, f32[32,1536]{1,0:T(8,128)S(1)}, u32[]{:S(2)}, u32[]{:S(2)}) collective-permute-start(f32[32,1536]{1,0:T(8,128)S(1)} %maximum_select_fusion.2), channel_id=1, source_target_pairs={{0,32},{1,33},{2,34},{3,35},{4,36},{5,37},{6,38},{7,39},{8,40},{9,... | collective-permute-start | bytes 589832 | tf_op jit(solution)/shard_map/ppermute | solution.py:89
  57.5 9.2 %collective-permute-start.9 = (f32[2,1536]{1,0:T(2,128)S(1)}, f32[2,1536]{1,0:T(2,128)S(1)}, u32[]{:S(2)}, u32[]{:S(2)}) collective-permute-start(f32[2,1536]{1,0:T(2,128)S(1)} %pad_maximum_fusion.5), channel_id=1, source_target_pairs={{0,1},{1,2},{2,3},{3,4},{4,5},{5,6},{6,7},{7,8},{8,9},{9,10},{10,1... | collective-permute-start | bytes 36872 | tf_op jit(solution)/shard_map/ppermute | solution.py:195
  68.0 9.1 %collective-permute-start.8 = (f32[64,1536]{1,0:T(8,128)S(1)}, f32[64,1536]{1,0:T(8,128)S(1)}, u32[]{:S(2)}, u32[]{:S(2)}) collective-permute-start(f32[64,1536]{1,0:T(8,128)S(1)} %maximum_select_fusion.1), channel_id=1, source_target_pairs={{0,96},{1,97},{2,98},{3,99},{4,100},{5,101},{6,102},{7,103},{8,104... | collective-permute-start | bytes 1179656 | tf_op jit(solution)/shard_map/ppermute | solution.py:89
  68.1 3.3 %collective-permute-start.10 = (f32[2,1536]{1,0:T(2,128)S(1)}, f32[2,1536]{1,0:T(2,128)S(1)}, u32[]{:S(2)}, u32[]{:S(2)}) collective-permute-start(f32[2,1536]{1,0:T(2,128)S(1)} %pad_maximum_fusion.6), channel_id=1, source_target_pairs={{1,0},{2,1},{3,2},{4,3},{5,4},{6,5},{7,6},{8,7},{9,8},{10,9},{11,1... | collective-permute-start | bytes 36872 | tf_op jit(solution)/shard_map/ppermute | solution.py:196
  78.8 12.3 %all-to-all-start.1 = ((f32[8,6,1536]{2,1,0:T(8,128)}), f32[8,6,1536]{2,1,0:T(8,128)S(1)}, u32[]{:S(2)}, u32[]{:S(2)}) async-start(f32[8,6,1536]{2,1,0:T(8,128)} %broadcast_select_fusion.2), calls=%async_computation.1 | async-start | bytes 786432 | tf_op jit(solution)/shard_map/all_to_all | solution.py:176

commit v12 on v11

--- a/solution.py
+++ b/solution.py
@@ -89,6 +89,23 @@
     return lax.ppermute(x, AXES, [(i, _partner(i, bit)) for i in range(n)])
 
 
+def _col_partner(i, k):
+    low = MEMBERS << (2 * (k // 2))
+    flip_low = (k % 2 == 0) == (i % 2 == 0)
+    return i ^ low if flip_low else _partner(i, 2 * low)
+
+
+def _col_partner_traced(i, k):
+    low = MEMBERS << (2 * (k // 2))
+    r = (i // low) % 4
+    flip_low = (k % 2 == 0) == (i % 2 == 0)
+    return jnp.where(flip_low, i ^ low, i + ((3 - r) - r) * low)
+
+
+def _col_round(x, n, k):
+    return lax.ppermute(x, AXES, [(i, _col_partner(i, k)) for i in range(n)])
+
+
 def make_body(n):
     cols = n // MEMBERS
 
@@ -135,18 +152,26 @@
         nat = part.reshape(nat_rows, width)
         flag = jnp.where(lanes == 0, over, 0.0)[None]
         pool = zone_target
-        bit = MEMBERS
-        while bit < n:
+        rounds = (cols - 1).bit_length()
+        for k in range(rounds):
             if pool.shape[0] < SHIP_APART:
-                got = _xor(jnp.concatenate([nat, flag, pool], axis=0), n, bit)
+                got = _col_round(jnp.concatenate([nat, flag, pool], axis=0), n, k)
                 theirs = got[nat_rows + 1:]
             else:
-                got = _xor(jnp.concatenate([nat, flag], axis=0), n, bit)
-                theirs = _xor(pool, n, bit)
+                got = _col_round(jnp.concatenate([nat, flag], axis=0), n, k)
+                theirs = _col_round(pool, n, k)
             nat = nat + got[:nat_rows]
             flag = flag + got[nat_rows:nat_rows + 1]
-            pool = jnp.where((idx & bit) == 0, jnp.concatenate([pool, theirs], 0), jnp.concatenate([theirs, pool], 0))
-            bit *= 2
+            pool = jnp.concatenate([pool, theirs], 0)
+
+        def order(i, k):
+            if k == 0:
+                return [i]
+            return order(i, k - 1) + order(_col_partner_traced(i, k - 1), k - 1)
+
+        block_col = jnp.stack(order(idx, rounds)) // MEMBERS
+        col_block = jnp.sum(jnp.where(block_col[None, :] == jnp.arange(cols, dtype=jnp.int32)[:, None],
+                                      jnp.arange(cols, dtype=jnp.int32)[None, :], 0), axis=1)
 
         zrow = jnp.where(lanes == 2 * mem, zlo.astype(f32), 0.0) + jnp.where(lanes == 2 * mem + 1, zhi.astype(f32), 0.0)
         msg = jnp.concatenate([nat, flag, zrow[None]], axis=0)
@@ -166,7 +191,7 @@
         earlier = (c_mem[:, :, None] == c_mem[:, None, :]) & c_valid[:, None, :] & (ks[None, None, :] < ks[None, :, None])
         c_rank = jnp.sum(earlier.astype(jnp.int32), axis=2)
         mine = c_valid & (c_mem == mem)
-        c_at = (c_slot // (rows * MEMBERS)) * rows + c_slot % rows
+        c_at = col_block[c_slot // (rows * MEMBERS)] * rows + c_slot % rows
 
         def exchange(room, low):
             rank = c_rank - low

time: 103 us -> 104 us (level)
  local copies, waits for them, and re-layouts: 8.74 us -> 10.4 us
    ppermute x9 -> x3, waiting for transfers between devices: 19.9 us -> 5.3 us  [_xor(): return lax.ppermute(x, AXES, [(i, _partner(i, bit)) for i in range(n)])]
    ppermute x0 -> x6, waiting for transfers between devices: none -> 14.1 us  [_col_round(): return lax.ppermute(x, AXES, [(i, _col_partner(i, k)) for i in range(n)])]
    ppermute x0 -> x6, starting transfers between devices: none -> 7.75 us  [_col_round(): return lax.ppermute(x, AXES, [(i, _col_partner(i, k)) for i in range(n)])]
    ppermute x9 -> x3, starting transfers between devices: 12.5 us -> 4.83 us  [_xor(): return lax.ppermute(x, AXES, [(i, _partner(i, bit)) for i in range(n)])]
    gather x0 -> x2, local copies, waits for them, and re-layouts: none -> 1.3 us  [body(): c_at = col_block[c_slot // (rows * MEMBERS)] * rows + c_slot % rows]
  transfers between devices with their start and end apart: 12 -> 12, of which waited for: 10 -> 10; matrix products, arithmetic and copies ran while one was open for 9% -> 11% of each run, Pallas kernels for 6% -> 6%
where the time goes in v12:
time: 104 us
  waiting for transfers between devices  34 us (33%)
  starting transfers between devices  20.2 us (19%)
  Pallas kernels  18.6 us (18%)
  other arithmetic  14.7 us (14%)
  local copies, waits for them, and re-layouts  10.4 us (10%)
  between operations  5.66 us (5%)
    pallas_call x3, Pallas kernels, _table_call(): pl.pallas_call(kernel, grid=grid, in_specs=specs, out_specs=pl.BlockSpec(...  18.6 us
    ppermute x6, waiting for transfers between devices, _col_round(): return lax.ppermute(x, AXES, [(i, _col_partner(i, k)) for i in range(n)])  14.1 us
    ppermute x6, starting transfers between devices, _col_round(): return lax.ppermute(x, AXES, [(i, _col_partner(i, k)) for i in range(n)])  7.75 us
    all_to_all x1, waiting for transfers between devices, exchange(): return lax.all_to_all(sent, 'mem', 0, 0, tiled=True)  7.36 us
    ppermute x1, waiting for transfers between devices, body(): from_left = lax.ppermute(to_right, AXES, right)  7.29 us
    ppermute x3, waiting for transfers between devices, _xor(): return lax.ppermute(x, AXES, [(i, _partner(i, bit)) for i in range(n)])  5.3 us
    ppermute x3, starting transfers between devices, _xor(): return lax.ppermute(x, AXES, [(i, _partner(i, bit)) for i in range(n)])  4.83 us
    all_to_all x1, starting transfers between devices, exchange(): return lax.all_to_all(sent, 'mem', 0, 0, tiled=True)  3.47 us
  transfers between devices with their start and end apart: 12, of which 10 were waited for; matrix products, arithmetic and copies ran while one was open for 11% of the time, Pallas kernels for 6%

profile of v12, /device:TPU:6, one launch (start us, length us, event | category | flops | bytes accessed | tf_op | source)
XLA Modules:
  0.0 103.6 jit_solution(17481971515298869761)
XLA Ops:
  0.1 1.3 %fusion.40 = (s32[1]{0:T(128)}, s32[1]{0:T(128)}) fusion(s32[16]{0:T(128)} %param.19), kind=kLoop, calls=%fused_computation.159 | loop fusion | bytes 16 | tf_op jit(solution)/shard_map/slice | solution.py:129
  2.0 1.9 %compare_and_fusion.3 = (pred[16]{0:T(512)(128)(4,1)S(1)}, s32[16]{0:T(128)S(1)}, pred[16]{0:T(512)(128)(4,1)S(1)}) fusion(s32[16]{0:T(128)} %param.19, s32[]{:T(128)} %bitcast.1, s32[]{:T(128)} %bitcast.2), kind=kLoop, calls=%fused_computation.124 | loop fusion | flops 144 | bytes 168 | tf_op jit(solution)/shard_map/jit(_take)/and | solution.py:225
  3.8 0.9 select_reduce_fusion.2
  6.3 4.8 %shard_map.91 = f32[16,96,32]{2,1,0:T(8,128)} custom-call(f32[16,96,1024]{2,1,0:T(8,128)} %pop_ref.5, bf16[128,32]{1,0:T(8,128)(2,1)} %constant.426.clone.g1_ref), custom_call_target="tpu_custom_call" | custom-call | tf_op jit(solution)/shard_map/pallas_call | solution.py:71
  11.1 1.5 %reduce_sum.103 = f32[16,96]{1,0:T(8,128)S(1)} reduce(f32[16,96,32]{2,1,0:T(8,128)} %shard_map.91, f32[]{:T(128)} %constant.404.clone.1), dimensions={2}, to_apply=%region_2.3 | reduce | flops 47616 | bytes 202756 | tf_op jit(solution)/shard_map/reduce_sum | solution.py:147
  12.7 1.4 %multiply_reduce_fusion.1 = f32[96,32]{1,0:T(8,128)S(1)} fusion(f32[16,96,32]{2,1,0:T(8,128)} %shard_map.91, f32[16,96]{1,0:T(8,128)S(1)} %div.137), kind=kLoop, calls=%fused_computation.25 | loop fusion | flops 95232 | bytes 215040 | tf_op jit(solution)/shard_map/reduce_sum | solution.py:149
  14.2 2.0 %collective-permute-start = (f32[11,1536]{1,0:T(8,128)S(1)}, f32[11,1536]{1,0:T(8,128)S(1)}, u32[]{:S(2)}, u32[]{:S(2)}) collective-permute-start(f32[11,1536]{1,0:T(8,128)S(1)} %pad_maximum_fusion.3), channel_id=1, source_target_pairs={{0,8},{1,25},{2,10},{3,27},{4,12},{5,29},{6,14},{7,31},{8,0},{9,17... | collective-permute-start | bytes 202760 | tf_op jit(solution)/shard_map/ppermute | solution.py:106
  17.6 1.3 %collective-permute-done = f32[11,1536]{1,0:T(8,128)S(1)} collective-permute-done((f32[11,1536]{1,0:T(8,128)S(1)}, f32[11,1536]{1,0:T(8,128)S(1)}, u32[]{:S(2)}, u32[]{:S(2)}) %collective-permute-start) | collective-permute-done | bytes 67616 | tf_op jit(solution)/shard_map/ppermute | solution.py:106
  19.0 4.1 %collective-permute-start.1 = (f32[19,1536]{1,0:T(8,128)S(1)}, f32[19,1536]{1,0:T(8,128)S(1)}, u32[]{:S(2)}, u32[]{:S(2)}) collective-permute-start(f32[19,1536]{1,0:T(8,128)S(1)} %pad_maximum_fusion.2), channel_id=1, source_target_pairs={{0,24},{1,9},{2,26},{3,11},{4,28},{5,13},{6,30},{7,15},{8,16},{9,1... | collective-permute-start | bytes 350216 | tf_op jit(solution)/shard_map/ppermute | solution.py:106
  24.4 1.8 %collective-permute-done.1 = f32[19,1536]{1,0:T(8,128)S(1)} collective-permute-done((f32[19,1536]{1,0:T(8,128)S(1)}, f32[19,1536]{1,0:T(8,128)S(1)}, u32[]{:S(2)}, u32[]{:S(2)}) %collective-permute-start.1) | collective-permute-done | bytes 116768 | tf_op jit(solution)/shard_map/ppermute | solution.py:106
  26.3 0.9 collective-permute-start.2
  27.9 2.3 %collective-permute-done.2 = f32[3,1536]{1,0:T(4,128)S(1)} collective-permute-done((f32[3,1536]{1,0:T(4,128)S(1)}, f32[3,1536]{1,0:T(4,128)S(1)}, u32[]{:S(2)}, u32[]{:S(2)}) %collective-permute-start.2) | collective-permute-done | bytes 18464 | tf_op jit(solution)/shard_map/ppermute | solution.py:106
  30.8 4.6 %collective-permute-done.3 = f32[3,1536]{1,0:T(4,128)S(1)} collective-permute-done((f32[3,1536]{1,0:T(4,128)S(1)}, f32[3,1536]{1,0:T(4,128)S(1)}, u32[]{:S(2)}, u32[]{:S(2)}) %collective-permute-start.3) | collective-permute-done | bytes 18464 | tf_op jit(solution)/shard_map/ppermute | solution.py:106
  35.5 1.2 %collective-permute-done.4 = f32[4,1536]{1,0:T(4,128)S(1)} collective-permute-done((f32[4,1536]{1,0:T(4,128)S(1)}, f32[4,1536]{1,0:T(4,128)S(1)}, u32[]{:S(2)}, u32[]{:S(2)}) %collective-permute-start.4) | collective-permute-done | bytes 24608 | tf_op jit(solution)/shard_map/ppermute | solution.py:89
  36.7 1.7 %collective-permute-start.5 = (f32[4,1536]{1,0:T(4,128)S(1)}, f32[4,1536]{1,0:T(4,128)S(1)}, u32[]{:S(2)}, u32[]{:S(2)}) collective-permute-start(f32[4,1536]{1,0:T(4,128)S(1)} %fusion.37), channel_id=1, source_target_pairs={{0,2},{1,3},{2,0},{3,1},{4,6},{5,7},{6,4},{7,5},{8,10},{9,11},{10,... | collective-permute-start | bytes 73736 | tf_op jit(solution)/shard_map/ppermute | solution.py:89
  38.4 2.2 %collective-permute-done.5 = f32[4,1536]{1,0:T(4,128)S(1)} collective-permute-done((f32[4,1536]{1,0:T(4,128)S(1)}, f32[4,1536]{1,0:T(4,128)S(1)}, u32[]{:S(2)}, u32[]{:S(2)}) %collective-permute-start.5) | collective-permute-done | bytes 24608 | tf_op jit(solution)/shard_map/ppermute | solution.py:89
  40.7 3.1 %collective-permute-start.6 = (f32[4,1536]{1,0:T(4,128)S(1)}, f32[4,1536]{1,0:T(4,128)S(1)}, u32[]{:S(2)}, u32[]{:S(2)}) collective-permute-start(f32[4,1536]{1,0:T(4,128)S(1)} %add.446), channel_id=1, source_target_pairs={{0,6},{1,7},{2,4},{3,5},{4,2},{5,3},{6,0},{7,1},{8,14},{9,15},{10,... | collective-permute-start | bytes 73736 | tf_op jit(solution)/shard_map/ppermute | solution.py:89
  43.9 1.9 %collective-permute-done.6 = f32[4,1536]{1,0:T(4,128)S(1)} collective-permute-done((f32[4,1536]{1,0:T(4,128)S(1)}, f32[4,1536]{1,0:T(4,128)S(1)}, u32[]{:S(2)}, u32[]{:S(2)}) %collective-permute-start.6) | collective-permute-done | bytes 24608 | tf_op jit(solution)/shard_map/ppermute | solution.py:89
  46.8 1.2 %gather_fusion.1 = s32[128]{0:T(128)S(1)} fusion(s32[16]{0:T(128)S(1)} %select_reduce_fusion.4, s32[1024]{0:T(1024)S(1)} %pad_clamp_fusion.3), kind=kCustom, calls=%fused_computation.1 | custom fusion | bytes 1536 | tf_op jit(solution)/shard_map/gather | solution.py:194
  49.1 0.9 copy.45.s2t_ref
  50.1 6.3 %shard_map.92 = f32[16,96,32]{2,1,0:T(8,128)} custom-call(f32[16,96,1024]{2,1,0:T(8,128)} %pop_ref.5, f32[96,1024]{1,0:T(8,128)} %copy.45.s2t_ref, bf16[1024,32]{1,0:T(8,128)(2,1)} %constant.428.clone.e2t_ref), custom_call_target="tpu_custom_call" | custom-call | tf_op jit(solution)/shard_map/pallas_call | solution.py:71
  56.4 1.4 %broadcast_multiply_fusion.1 = f32[16,96,32]{2,1,0:T(8,128)S(1)} fusion(f32[16,96,32]{2,1,0:T(8,128)} %shard_map.92, f32[16,96]{1,0:T(8,128)S(1)} %div.137), kind=kLoop, calls=%fused_computation.29 | loop fusion | flops 49152 | bytes 399360 | tf_op jit(solution)/shard_map/mul | solution.py:210
  57.8 1.0 reduce_sum.110
  59.1 1.9 %collective-permute-start.9 = (f32[2,1536]{1,0:T(2,128)S(1)}, f32[2,1536]{1,0:T(2,128)S(1)}, u32[]{:S(2)}, u32[]{:S(2)}) collective-permute-start(f32[2,1536]{1,0:T(2,128)S(1)} %pad_maximum_fusion.7), channel_id=1, source_target_pairs={{0,1},{1,2},{2,3},{3,4},{4,5},{5,6},{6,7},{7,8},{8,9},{9,10},{10,1... | collective-permute-start | bytes 36872 | tf_op jit(solution)/shard_map/ppermute | solution.py:220
  61.1 7.3 %collective-permute-done.9 = f32[2,1536]{1,0:T(2,128)S(1)} collective-permute-done((f32[2,1536]{1,0:T(2,128)S(1)}, f32[2,1536]{1,0:T(2,128)S(1)}, u32[]{:S(2)}, u32[]{:S(2)}) %collective-permute-start.9) | collective-permute-done | bytes 12320 | tf_op jit(solution)/shard_map/ppermute | solution.py:220
  69.7 2.2 %collective-permute-start.10 = (f32[2,1536]{1,0:T(2,128)S(1)}, f32[2,1536]{1,0:T(2,128)S(1)}, u32[]{:S(2)}, u32[]{:S(2)}) collective-permute-start(f32[2,1536]{1,0:T(2,128)S(1)} %pad_maximum_fusion.8), channel_id=1, source_target_pairs={{1,0},{2,1},{3,2},{4,3},{5,4},{6,5},{7,6},{8,7},{9,8},{10,9},{11,1... | collective-permute-start | bytes 36872 | tf_op jit(solution)/shard_map/ppermute | solution.py:221
  74.6 4.1 %collective-permute-done.8 = f32[64,1536]{1,0:T(8,128)S(1)} collective-permute-done((f32[64,1536]{1,0:T(8,128)S(1)}, f32[64,1536]{1,0:T(8,128)S(1)}, u32[]{:S(2)}, u32[]{:S(2)}) %collective-permute-start.8) | collective-permute-done | bytes 393248 | tf_op jit(solution)/shard_map/ppermute | solution.py:106
  79.4 0.8 broadcast_select_fusion.2
  80.4 3.5 %all-to-all-start.1 = ((f32[8,6,1536]{2,1,0:T(8,128)}), f32[8,6,1536]{2,1,0:T(8,128)S(1)}, u32[]{:S(2)}, u32[]{:S(2)}) async-start(f32[8,6,1536]{2,1,0:T(8,128)} %broadcast_select_fusion.2), calls=%async_computation.1 | async-start | bytes 786432 | tf_op jit(solution)/shard_map/all_to_all | solution.py:201
  85.4 7.4 %all-to-all-done.1 = f32[8,6,1536]{2,1,0:T(8,128)S(1)} async-done(((f32[8,6,1536]{2,1,0:T(8,128)}), f32[8,6,1536]{2,1,0:T(8,128)S(1)}, u32[]{:S(2)}, u32[]{:S(2)}) %all-to-all-start.1) | async-done | bytes 294944 | tf_op jit(solution)/shard_map/all_to_all | solution.py:201
  94.9 1.2 %broadcast_multiply_fusion.r_ref = f32[16,96,32]{2,1,0:T(8,128)} fusion(f32[16,96,32]{2,1,0:T(8,128)S(1)} %bitcast.58, f32[16,96]{1,0:T(8,128)S(1)} %div.137), kind=kLoop, calls=%fused_computation.28 | loop fusion | flops 49152 | bytes 399360 | tf_op jit(solution)/shard_map/mul | solution.py:227
  96.0 7.5 %shard_map.93 = f32[16,96,1024]{2,1,0:T(8,128)} custom-call(f32[16,96,1024]{2,1,0:T(8,128)} %pop_ref.5, f32[16,96,32]{2,1,0:T(8,128)} %broadcast_multiply_fusion.r_ref, f32[96,1024]{1,0:T(8,128)} %copy.45.s2t_ref, bf16[32,1024]{1,0:T(8,128)(2,1)} %constant.427.clone.e2_ref), custom_call_target="tpu_custom_call" | custom-call | tf_op jit(solution)/shard_map/pallas_call | solution.py:71
  (112 shorter events, 12.4 us)
Async XLA Ops:
  6.3 6.3 %copy-start.3 = (f32[16,96]{1,0:T(8,128)S(1)}, f32[16,96]{1,0:T(8,128)}, u32[]{:S(2)}) copy-start(f32[16,96]{1,0:T(8,128)} %param.16) | copy-start | bytes 18436
  11.1 3.0 %copy-start = (f32[8,1536]{1,0:T(8,128)S(1)}, f32[8,1536]{1,0:T(8,128)}, u32[]{:S(2)}) copy-start(f32[8,1536]{1,0:T(8,128)} %param.18) | copy-start | bytes 147460
  11.1 16.1 %copy-start.4 = (s32[2]{0:T(128)S(1)}, s32[2]{0:T(128)}, u32[]{:S(2)}) copy-start(s32[2]{0:T(128)} %constant.424.clone.1) | copy-start | bytes 28
  12.6 33.6 %copy-start.2 = (s32[1024]{0:T(1024)S(1)}, s32[1024]{0:T(1024)}, u32[]{:S(2)}) copy-start(s32[1024]{0:T(1024)} %param.20) | copy-start | bytes 12292
  14.2 4.7 %collective-permute-start = (f32[11,1536]{1,0:T(8,128)S(1)}, f32[11,1536]{1,0:T(8,128)S(1)}, u32[]{:S(2)}, u32[]{:S(2)}) collective-permute-start(f32[11,1536]{1,0:T(8,128)S(1)} %pad_maximum_fusion.3), channel_id=1, source_target_pairs={{0,8},{1,25},{2,10},{3,27},{4,12},{5,29},{6,14},{7,31},{8,0},{9,17... | collective-permute-start | bytes 202760 | tf_op jit(solution)/shard_map/ppermute | solution.py:106
  19.0 7.2 %collective-permute-start.1 = (f32[19,1536]{1,0:T(8,128)S(1)}, f32[19,1536]{1,0:T(8,128)S(1)}, u32[]{:S(2)}, u32[]{:S(2)}) collective-permute-start(f32[19,1536]{1,0:T(8,128)S(1)} %pad_maximum_fusion.2), channel_id=1, source_target_pairs={{0,24},{1,9},{2,26},{3,11},{4,28},{5,13},{6,30},{7,15},{8,16},{9,1... | collective-permute-start | bytes 350216 | tf_op jit(solution)/shard_map/ppermute | solution.py:106
  26.3 3.9 %collective-permute-start.2 = (f32[3,1536]{1,0:T(4,128)S(1)}, f32[3,1536]{1,0:T(4,128)S(1)}, u32[]{:S(2)}, u32[]{:S(2)}) collective-permute-start(f32[3,1536]{1,0:T(4,128)S(1)} %pad_maximum_fusion.4), channel_id=1, source_target_pairs={{0,32},{1,97},{2,34},{3,99},{4,36},{5,101},{6,38},{7,103},{8,40},{... | collective-permute-start | bytes 55304 | tf_op jit(solution)/shard_map/ppermute | solution.py:106
  30.3 5.1 %collective-permute-start.3 = (f32[3,1536]{1,0:T(4,128)S(1)}, f32[3,1536]{1,0:T(4,128)S(1)}, u32[]{:S(2)}, u32[]{:S(2)}) collective-permute-start(f32[3,1536]{1,0:T(4,128)S(1)} %pad_maximum_fusion.5), channel_id=1, source_target_pairs={{0,96},{1,33},{2,98},{3,35},{4,100},{5,37},{6,102},{7,39},{8,104},... | collective-permute-start | bytes 55304 | tf_op jit(solution)/shard_map/ppermute | solution.py:106
  35.4 1.3 %collective-permute-start.4 = (f32[4,1536]{1,0:T(4,128)S(1)}, f32[4,1536]{1,0:T(4,128)S(1)}, u32[]{:S(2)}, u32[]{:S(2)}) collective-permute-start(f32[4,1536]{1,0:T(4,128)S(1)} %pad_maximum_fusion.6), channel_id=1, source_target_pairs={{0,1},{1,0},{2,3},{3,2},{4,5},{5,4},{6,7},{7,6},{8,9},{9,8},{10,11... | collective-permute-start | bytes 73736 | tf_op jit(solution)/shard_map/ppermute | solution.py:89
  36.7 3.9 %collective-permute-start.5 = (f32[4,1536]{1,0:T(4,128)S(1)}, f32[4,1536]{1,0:T(4,128)S(1)}, u32[]{:S(2)}, u32[]{:S(2)}) collective-permute-start(f32[4,1536]{1,0:T(4,128)S(1)} %fusion.37), channel_id=1, source_target_pairs={{0,2},{1,3},{2,0},{3,1},{4,6},{5,7},{6,4},{7,5},{8,10},{9,11},{10,... | collective-permute-start | bytes 73736 | tf_op jit(solution)/shard_map/ppermute | solution.py:89
  40.7 5.1 %collective-permute-start.6 = (f32[4,1536]{1,0:T(4,128)S(1)}, f32[4,1536]{1,0:T(4,128)S(1)}, u32[]{:S(2)}, u32[]{:S(2)}) collective-permute-start(f32[4,1536]{1,0:T(4,128)S(1)} %add.446), channel_id=1, source_target_pairs={{0,6},{1,7},{2,4},{3,5},{4,2},{5,3},{6,0},{7,1},{8,14},{9,15},{10,... | collective-permute-start | bytes 73736 | tf_op jit(solution)/shard_map/ppermute | solution.py:89
  43.8 25.8 %collective-permute-start.7 = (f32[32,1536]{1,0:T(8,128)S(1)}, f32[32,1536]{1,0:T(8,128)S(1)}, u32[]{:S(2)}, u32[]{:S(2)}) collective-permute-start(f32[32,1536]{1,0:T(8,128)S(1)} %pad_maximum_fusion.1), channel_id=1, source_target_pairs={{0,32},{1,97},{2,34},{3,99},{4,36},{5,101},{6,38},{7,103},{8,40},{... | collective-permute-start | bytes 589832 | tf_op jit(solution)/shard_map/ppermute | solution.py:106
  46.8 2.2 %copy-start.1 = (f32[96,32]{0,1:T(8,128)S(1)}, f32[96,32]{0,1:T(8,128)}, u32[]{:S(2)}) copy-start(f32[96,32]{0,1:T(8,128)} %param.17) | copy-start | bytes 36868
  59.1 9.2 %collective-permute-start.9 = (f32[2,1536]{1,0:T(2,128)S(1)}, f32[2,1536]{1,0:T(2,128)S(1)}, u32[]{:S(2)}, u32[]{:S(2)}) collective-permute-start(f32[2,1536]{1,0:T(2,128)S(1)} %pad_maximum_fusion.7), channel_id=1, source_target_pairs={{0,1},{1,2},{2,3},{3,4},{4,5},{5,6},{6,7},{7,8},{8,9},{9,10},{10,1... | collective-permute-start | bytes 36872 | tf_op jit(solution)/shard_map/ppermute | solution.py:220
  69.6 9.1 %collective-permute-start.8 = (f32[64,1536]{1,0:T(8,128)S(1)}, f32[64,1536]{1,0:T(8,128)S(1)}, u32[]{:S(2)}, u32[]{:S(2)}) collective-permute-start(f32[64,1536]{1,0:T(8,128)S(1)} %pad_maximum_fusion), channel_id=1, source_target_pairs={{0,96},{1,33},{2,98},{3,35},{4,100},{5,37},{6,102},{7,39},{8,104},... | collective-permute-start | bytes 1179656 | tf_op jit(solution)/shard_map/ppermute | solution.py:106
  69.7 3.6 %collective-permute-start.10 = (f32[2,1536]{1,0:T(2,128)S(1)}, f32[2,1536]{1,0:T(2,128)S(1)}, u32[]{:S(2)}, u32[]{:S(2)}) collective-permute-start(f32[2,1536]{1,0:T(2,128)S(1)} %pad_maximum_fusion.8), channel_id=1, source_target_pairs={{1,0},{2,1},{3,2},{4,3},{5,4},{6,5},{7,6},{8,7},{9,8},{10,9},{11,1... | collective-permute-start | bytes 36872 | tf_op jit(solution)/shard_map/ppermute | solution.py:221
  80.4 12.3 %all-to-all-start.1 = ((f32[8,6,1536]{2,1,0:T(8,128)}), f32[8,6,1536]{2,1,0:T(8,128)S(1)}, u32[]{:S(2)}, u32[]{:S(2)}) async-start(f32[8,6,1536]{2,1,0:T(8,128)} %broadcast_select_fusion.2), calls=%async_computation.1 | async-start | bytes 786432 | tf_op jit(solution)/shard_map/all_to_all | solution.py:201

commit v13 on v11

--- a/solution.py
+++ b/solution.py
@@ -14,7 +14,7 @@
 MEMBERS = 8
 ROOMY = 6
 AXES = ("col", "mem")
-SHIP_APART = 32
+SHIP_APART = 16
 
 
 HI = lax.Precision.HIGHEST

time: 103 us -> 103 us (level)
  starting transfers between devices: 19.8 us -> 23.1 us
  waiting for transfers between devices: 34.6 us -> 32.1 us
    ppermute x9 -> x10, starting transfers between devices: 12.5 us -> 15.8 us  [_xor(): return lax.ppermute(x, AXES, [(i, _partner(i, bit)) for i in range(n)])]
    ppermute x9 -> x10, waiting for transfers between devices: 19.9 us -> 17.4 us  [_xor(): return lax.ppermute(x, AXES, [(i, _partner(i, bit)) for i in range(n)])]
  transfers between devices with their start and end apart: 12 -> 13, of which waited for: 10 -> 9; matrix products, arithmetic and copies ran while one was open for 9% -> 9% of each run, Pallas kernels for 6% -> 6%
where the time goes in v13:
time: 103 us
  waiting for transfers between devices  32.1 us (31%)
  starting transfers between devices  23.1 us (22%)
  Pallas kernels  18.6 us (18%)
  other arithmetic  14.7 us (14%)
  local copies, waits for them, and re-layouts  8.73 us (8%)
  between operations  5.54 us (5%)
    pallas_call x3, Pallas kernels, _table_call(): pl.pallas_call(kernel, grid=grid, in_specs=specs, out_specs=pl.BlockSpec(...  18.6 us
    ppermute x10, waiting for transfers between devices, _xor(): return lax.ppermute(x, AXES, [(i, _partner(i, bit)) for i in range(n)])  17.4 us
    ppermute x10, starting transfers between devices, _xor(): return lax.ppermute(x, AXES, [(i, _partner(i, bit)) for i in range(n)])  15.8 us
    all_to_all x1, waiting for transfers between devices, exchange(): return lax.all_to_all(sent, 'mem', 0, 0, tiled=True)  7.36 us
    ppermute x1, waiting for transfers between devices, body(): from_left = lax.ppermute(to_right, AXES, right)  7.29 us
    all_to_all x1, starting transfers between devices, exchange(): return lax.all_to_all(sent, 'mem', 0, 0, tiled=True)  3.47 us
  transfers between devices with their start and end apart: 13, of which 9 were waited for; matrix products, arithmetic and copies ran while one was open for 9% of the time, Pallas kernels for 6%

profile of v13, /device:TPU:6, one launch (start us, length us, event | category | flops | bytes accessed | tf_op | source)
XLA Modules:
  0.0 102.7 jit_solution(9909490337463814730)
XLA Ops:
  0.0 1.3 %fusion.42 = (s32[1]{0:T(128)}, s32[1]{0:T(128)}) fusion(s32[16]{0:T(128)} %param.19), kind=kLoop, calls=%fused_computation.151 | loop fusion | bytes 16 | tf_op jit(solution)/shard_map/slice | solution.py:112
  1.9 0.9 select_reduce_fusion.2
  2.8 1.9 %compare_and_fusion.3 = (pred[16]{0:T(512)(128)(4,1)S(1)}, s32[16]{0:T(128)S(1)}, pred[16]{0:T(512)(128)(4,1)S(1)}) fusion(s32[16]{0:T(128)} %param.19, s32[]{:T(128)} %bitcast.1, s32[]{:T(128)} %bitcast.2), kind=kLoop, calls=%fused_computation.120 | loop fusion | flops 144 | bytes 168 | tf_op jit(solution)/shard_map/jit(_take)/and | solution.py:200
  6.2 4.8 %shard_map.91 = f32[16,96,32]{2,1,0:T(8,128)} custom-call(f32[16,96,1024]{2,1,0:T(8,128)} %pop_ref.5, bf16[128,32]{1,0:T(8,128)(2,1)} %constant.230.clone.g1_ref), custom_call_target="tpu_custom_call" | custom-call | tf_op jit(solution)/shard_map/pallas_call | solution.py:71
  11.0 1.5 %reduce_sum.94 = f32[16,96]{1,0:T(8,128)S(1)} reduce(f32[16,96,32]{2,1,0:T(8,128)} %shard_map.91, f32[]{:T(128)} %constant.209.clone.1), dimensions={2}, to_apply=%region_2.3 | reduce | flops 47616 | bytes 202756 | tf_op jit(solution)/shard_map/reduce_sum | solution.py:130
  12.5 1.4 %multiply_reduce_fusion.1 = f32[96,32]{1,0:T(8,128)S(1)} fusion(f32[16,96,32]{2,1,0:T(8,128)} %shard_map.91, f32[16,96]{1,0:T(8,128)S(1)} %div.53), kind=kLoop, calls=%fused_computation.30 | loop fusion | flops 95232 | bytes 215040 | tf_op jit(solution)/shard_map/reduce_sum | solution.py:132
  14.1 2.0 %collective-permute-start = (f32[11,1536]{1,0:T(8,128)S(1)}, f32[11,1536]{1,0:T(8,128)S(1)}, u32[]{:S(2)}, u32[]{:S(2)}) collective-permute-start(f32[11,1536]{1,0:T(8,128)S(1)} %pad_maximum_fusion), channel_id=1, source_target_pairs={{0,8},{1,9},{2,10},{3,11},{4,12},{5,13},{6,14},{7,15},{8,0},{9,1},... | collective-permute-start | bytes 202760 | tf_op jit(solution)/shard_map/ppermute | solution.py:89
  17.4 1.4 %collective-permute-done = f32[11,1536]{1,0:T(8,128)S(1)} collective-permute-done((f32[11,1536]{1,0:T(8,128)S(1)}, f32[11,1536]{1,0:T(8,128)S(1)}, u32[]{:S(2)}, u32[]{:S(2)}) %collective-permute-start) | collective-permute-done | bytes 67616 | tf_op jit(solution)/shard_map/ppermute | solution.py:89
  18.9 4.0 %collective-permute-start.1 = (f32[3,1536]{1,0:T(4,128)S(1)}, f32[3,1536]{1,0:T(4,128)S(1)}, u32[]{:S(2)}, u32[]{:S(2)}) collective-permute-start(f32[3,1536]{1,0:T(4,128)S(1)} %pad_maximum_fusion.1), channel_id=1, source_target_pairs={{0,24},{1,25},{2,26},{3,27},{4,28},{5,29},{6,30},{7,31},{8,16},{9,... | collective-permute-start | bytes 55304 | tf_op jit(solution)/shard_map/ppermute | solution.py:89
  24.8 0.9 collective-permute-start.2
  25.7 0.7 and_reduce_fusion
  26.5 2.3 %collective-permute-done.2 = f32[3,1536]{1,0:T(4,128)S(1)} collective-permute-done((f32[3,1536]{1,0:T(4,128)S(1)}, f32[3,1536]{1,0:T(4,128)S(1)}, u32[]{:S(2)}, u32[]{:S(2)}) %collective-permute-start.2) | collective-permute-done | bytes 18464 | tf_op jit(solution)/shard_map/ppermute | solution.py:89
  29.3 4.5 %collective-permute-done.3 = f32[3,1536]{1,0:T(4,128)S(1)} collective-permute-done((f32[3,1536]{1,0:T(4,128)S(1)}, f32[3,1536]{1,0:T(4,128)S(1)}, u32[]{:S(2)}, u32[]{:S(2)}) %collective-permute-start.3) | collective-permute-done | bytes 18464 | tf_op jit(solution)/shard_map/ppermute | solution.py:89
  34.1 3.3 %collective-permute-start.7 = (f32[16,1536]{1,0:T(8,128)S(1)}, f32[16,1536]{1,0:T(8,128)S(1)}, u32[]{:S(2)}, u32[]{:S(2)}) collective-permute-start(f32[16,1536]{1,0:T(8,128)S(1)} %maximum_select_fusion.3), channel_id=1, source_target_pairs={{0,24},{1,25},{2,26},{3,27},{4,28},{5,29},{6,30},{7,31},{8,16},{9,... | collective-permute-start | bytes 294920 | tf_op jit(solution)/shard_map/ppermute | solution.py:89
  37.4 1.7 %collective-permute-start.5 = (f32[4,1536]{1,0:T(4,128)S(1)}, f32[4,1536]{1,0:T(4,128)S(1)}, u32[]{:S(2)}, u32[]{:S(2)}) collective-permute-start(f32[4,1536]{1,0:T(4,128)S(1)} %fusion.40), channel_id=1, source_target_pairs={{0,2},{1,3},{2,0},{3,1},{4,6},{5,7},{6,4},{7,5},{8,10},{9,11},{10,... | collective-permute-start | bytes 73736 | tf_op jit(solution)/shard_map/ppermute | solution.py:89
  39.1 2.2 %collective-permute-done.5 = f32[4,1536]{1,0:T(4,128)S(1)} collective-permute-done((f32[4,1536]{1,0:T(4,128)S(1)}, f32[4,1536]{1,0:T(4,128)S(1)}, u32[]{:S(2)}, u32[]{:S(2)}) %collective-permute-start.5) | collective-permute-done | bytes 24608 | tf_op jit(solution)/shard_map/ppermute | solution.py:89
  41.3 3.1 %collective-permute-start.6 = (f32[4,1536]{1,0:T(4,128)S(1)}, f32[4,1536]{1,0:T(4,128)S(1)}, u32[]{:S(2)}, u32[]{:S(2)}) collective-permute-start(f32[4,1536]{1,0:T(4,128)S(1)} %add.315), channel_id=1, source_target_pairs={{0,6},{1,7},{2,4},{3,5},{4,2},{5,3},{6,0},{7,1},{8,14},{9,15},{10,... | collective-permute-start | bytes 73736 | tf_op jit(solution)/shard_map/ppermute | solution.py:89
  44.5 1.9 %collective-permute-done.6 = f32[4,1536]{1,0:T(4,128)S(1)} collective-permute-done((f32[4,1536]{1,0:T(4,128)S(1)}, f32[4,1536]{1,0:T(4,128)S(1)}, u32[]{:S(2)}, u32[]{:S(2)}) %collective-permute-start.6) | collective-permute-done | bytes 24608 | tf_op jit(solution)/shard_map/ppermute | solution.py:89
  48.3 0.9 copy.45.s2t_ref
  49.2 6.3 %shard_map.92 = f32[16,96,32]{2,1,0:T(8,128)} custom-call(f32[16,96,1024]{2,1,0:T(8,128)} %pop_ref.5, f32[96,1024]{1,0:T(8,128)} %copy.45.s2t_ref, bf16[1024,32]{1,0:T(8,128)(2,1)} %constant.232.clone.e2t_ref), custom_call_target="tpu_custom_call" | custom-call | tf_op jit(solution)/shard_map/pallas_call | solution.py:71
  55.5 1.4 %broadcast_multiply_fusion.1 = f32[16,96,32]{2,1,0:T(8,128)S(1)} fusion(f32[16,96,32]{2,1,0:T(8,128)} %shard_map.92, f32[16,96]{1,0:T(8,128)S(1)} %div.53), kind=kLoop, calls=%fused_computation.34 | loop fusion | flops 49152 | bytes 399360 | tf_op jit(solution)/shard_map/mul | solution.py:185
  56.9 1.0 reduce_sum.100
  58.3 1.9 %collective-permute-start.10 = (f32[2,1536]{1,0:T(2,128)S(1)}, f32[2,1536]{1,0:T(2,128)S(1)}, u32[]{:S(2)}, u32[]{:S(2)}) collective-permute-start(f32[2,1536]{1,0:T(2,128)S(1)} %pad_maximum_fusion.5), channel_id=1, source_target_pairs={{0,1},{1,2},{2,3},{3,4},{4,5},{5,6},{6,7},{7,8},{8,9},{9,10},{10,1... | collective-permute-start | bytes 36872 | tf_op jit(solution)/shard_map/ppermute | solution.py:195
  60.3 7.3 %collective-permute-done.10 = f32[2,1536]{1,0:T(2,128)S(1)} collective-permute-done((f32[2,1536]{1,0:T(2,128)S(1)}, f32[2,1536]{1,0:T(2,128)S(1)}, u32[]{:S(2)}, u32[]{:S(2)}) %collective-permute-start.10) | collective-permute-done | bytes 12320 | tf_op jit(solution)/shard_map/ppermute | solution.py:195
  68.9 1.9 %collective-permute-start.11 = (f32[2,1536]{1,0:T(2,128)S(1)}, f32[2,1536]{1,0:T(2,128)S(1)}, u32[]{:S(2)}, u32[]{:S(2)}) collective-permute-start(f32[2,1536]{1,0:T(2,128)S(1)} %pad_maximum_fusion.6), channel_id=1, source_target_pairs={{1,0},{2,1},{3,2},{4,3},{5,4},{6,5},{7,6},{8,7},{9,8},{10,9},{11,1... | collective-permute-start | bytes 36872 | tf_op jit(solution)/shard_map/ppermute | solution.py:196
  73.4 4.4 %collective-permute-done.9 = f32[64,1536]{1,0:T(8,128)S(1)} collective-permute-done((f32[64,1536]{1,0:T(8,128)S(1)}, f32[64,1536]{1,0:T(8,128)S(1)}, u32[]{:S(2)}, u32[]{:S(2)}) %collective-permute-start.9) | collective-permute-done | bytes 393248 | tf_op jit(solution)/shard_map/ppermute | solution.py:89
  77.9 0.7 gather_fusion.1
  78.6 0.8 broadcast_select_fusion.2
  79.6 3.5 %all-to-all-start.1 = ((f32[8,6,1536]{2,1,0:T(8,128)}), f32[8,6,1536]{2,1,0:T(8,128)S(1)}, u32[]{:S(2)}, u32[]{:S(2)}) async-start(f32[8,6,1536]{2,1,0:T(8,128)} %broadcast_select_fusion.2), calls=%async_computation.1 | async-start | bytes 786432 | tf_op jit(solution)/shard_map/all_to_all | solution.py:176
  84.6 7.4 %all-to-all-done.1 = f32[8,6,1536]{2,1,0:T(8,128)S(1)} async-done(((f32[8,6,1536]{2,1,0:T(8,128)}), f32[8,6,1536]{2,1,0:T(8,128)S(1)}, u32[]{:S(2)}, u32[]{:S(2)}) %all-to-all-start.1) | async-done | bytes 294944 | tf_op jit(solution)/shard_map/all_to_all | solution.py:176
  94.1 1.2 %broadcast_multiply_fusion.r_ref = f32[16,96,32]{2,1,0:T(8,128)} fusion(f32[16,96,32]{2,1,0:T(8,128)S(1)} %bitcast.40, f32[16,96]{1,0:T(8,128)S(1)} %div.53), kind=kLoop, calls=%fused_computation.33 | loop fusion | flops 49152 | bytes 399360 | tf_op jit(solution)/shard_map/mul | solution.py:202
  95.2 7.5 %shard_map.93 = f32[16,96,1024]{2,1,0:T(8,128)} custom-call(f32[16,96,1024]{2,1,0:T(8,128)} %pop_ref.5, f32[16,96,32]{2,1,0:T(8,128)} %broadcast_multiply_fusion.r_ref, f32[96,1024]{1,0:T(8,128)} %copy.45.s2t_ref, bf16[32,1024]{1,0:T(8,128)(2,1)} %constant.231.clone.e2_ref), custom_call_target="tpu_custom_call" | custom-call | tf_op jit(solution)/shard_map/pallas_call | solution.py:71
  (106 shorter events, 11.2 us)
Async XLA Ops:
  6.2 6.3 %copy-start.3 = (f32[16,96]{1,0:T(8,128)S(1)}, f32[16,96]{1,0:T(8,128)}, u32[]{:S(2)}) copy-start(f32[16,96]{1,0:T(8,128)} %param.16) | copy-start | bytes 18436
  11.0 3.1 %copy-start = (f32[8,1536]{1,0:T(8,128)S(1)}, f32[8,1536]{1,0:T(8,128)}, u32[]{:S(2)}) copy-start(f32[8,1536]{1,0:T(8,128)} %param.18) | copy-start | bytes 147460
  11.0 14.7 %copy-start.4 = (s32[2]{0:T(128)S(1)}, s32[2]{0:T(128)}, u32[]{:S(2)}) copy-start(s32[2]{0:T(128)} %constant.228.clone.1) | copy-start | bytes 28
  11.0 35.9 %copy-start.2 = (s32[1024]{0:T(1024)S(1)}, s32[1024]{0:T(1024)}, u32[]{:S(2)}) copy-start(s32[1024]{0:T(1024)} %param.20) | copy-start | bytes 12292
  12.5 35.7 %copy-start.1 = (f32[96,32]{0,1:T(8,128)S(1)}, f32[96,32]{0,1:T(8,128)}, u32[]{:S(2)}) copy-start(f32[96,32]{0,1:T(8,128)} %param.17) | copy-start | bytes 36868
  14.1 4.8 %collective-permute-start = (f32[11,1536]{1,0:T(8,128)S(1)}, f32[11,1536]{1,0:T(8,128)S(1)}, u32[]{:S(2)}, u32[]{:S(2)}) collective-permute-start(f32[11,1536]{1,0:T(8,128)S(1)} %pad_maximum_fusion), channel_id=1, source_target_pairs={{0,8},{1,9},{2,10},{3,11},{4,12},{5,13},{6,14},{7,15},{8,0},{9,1},... | collective-permute-start | bytes 202760 | tf_op jit(solution)/shard_map/ppermute | solution.py:89
  18.9 5.8 %collective-permute-start.1 = (f32[3,1536]{1,0:T(4,128)S(1)}, f32[3,1536]{1,0:T(4,128)S(1)}, u32[]{:S(2)}, u32[]{:S(2)}) collective-permute-start(f32[3,1536]{1,0:T(4,128)S(1)} %pad_maximum_fusion.1), channel_id=1, source_target_pairs={{0,24},{1,25},{2,26},{3,27},{4,28},{5,29},{6,30},{7,31},{8,16},{9,... | collective-permute-start | bytes 55304 | tf_op jit(solution)/shard_map/ppermute | solution.py:89
  24.8 3.9 %collective-permute-start.2 = (f32[3,1536]{1,0:T(4,128)S(1)}, f32[3,1536]{1,0:T(4,128)S(1)}, u32[]{:S(2)}, u32[]{:S(2)}) collective-permute-start(f32[3,1536]{1,0:T(4,128)S(1)} %pad_maximum_fusion.2), channel_id=1, source_target_pairs={{0,32},{1,33},{2,34},{3,35},{4,36},{5,37},{6,38},{7,39},{8,40},{9,... | collective-permute-start | bytes 55304 | tf_op jit(solution)/shard_map/ppermute | solution.py:89
  28.8 5.1 %collective-permute-start.3 = (f32[3,1536]{1,0:T(4,128)S(1)}, f32[3,1536]{1,0:T(4,128)S(1)}, u32[]{:S(2)}, u32[]{:S(2)}) collective-permute-start(f32[3,1536]{1,0:T(4,128)S(1)} %pad_maximum_fusion.3), channel_id=1, source_target_pairs={{0,96},{1,97},{2,98},{3,99},{4,100},{5,101},{6,102},{7,103},{8,104... | collective-permute-start | bytes 55304 | tf_op jit(solution)/shard_map/ppermute | solution.py:89
  33.9 3.4 %collective-permute-start.4 = (f32[4,1536]{1,0:T(4,128)S(1)}, f32[4,1536]{1,0:T(4,128)S(1)}, u32[]{:S(2)}, u32[]{:S(2)}) collective-permute-start(f32[4,1536]{1,0:T(4,128)S(1)} %pad_maximum_fusion.4), channel_id=1, source_target_pairs={{0,1},{1,0},{2,3},{3,2},{4,5},{5,4},{6,7},{7,6},{8,9},{9,8},{10,11... | collective-permute-start | bytes 73736 | tf_op jit(solution)/shard_map/ppermute | solution.py:89
  34.1 10.4 %collective-permute-start.7 = (f32[16,1536]{1,0:T(8,128)S(1)}, f32[16,1536]{1,0:T(8,128)S(1)}, u32[]{:S(2)}, u32[]{:S(2)}) collective-permute-start(f32[16,1536]{1,0:T(8,128)S(1)} %maximum_select_fusion.3), channel_id=1, source_target_pairs={{0,24},{1,25},{2,26},{3,27},{4,28},{5,29},{6,30},{7,31},{8,16},{9,... | collective-permute-start | bytes 294920 | tf_op jit(solution)/shard_map/ppermute | solution.py:89
  37.4 3.9 %collective-permute-start.5 = (f32[4,1536]{1,0:T(4,128)S(1)}, f32[4,1536]{1,0:T(4,128)S(1)}, u32[]{:S(2)}, u32[]{:S(2)}) collective-permute-start(f32[4,1536]{1,0:T(4,128)S(1)} %fusion.40), channel_id=1, source_target_pairs={{0,2},{1,3},{2,0},{3,1},{4,6},{5,7},{6,4},{7,5},{8,10},{9,11},{10,... | collective-permute-start | bytes 73736 | tf_op jit(solution)/shard_map/ppermute | solution.py:89
  41.3 5.1 %collective-permute-start.6 = (f32[4,1536]{1,0:T(4,128)S(1)}, f32[4,1536]{1,0:T(4,128)S(1)}, u32[]{:S(2)}, u32[]{:S(2)}) collective-permute-start(f32[4,1536]{1,0:T(4,128)S(1)} %add.315), channel_id=1, source_target_pairs={{0,6},{1,7},{2,4},{3,5},{4,2},{5,3},{6,0},{7,1},{8,14},{9,15},{10,... | collective-permute-start | bytes 73736 | tf_op jit(solution)/shard_map/ppermute | solution.py:89
  44.4 24.3 %collective-permute-start.8 = (f32[32,1536]{1,0:T(8,128)S(1)}, f32[32,1536]{1,0:T(8,128)S(1)}, u32[]{:S(2)}, u32[]{:S(2)}) collective-permute-start(f32[32,1536]{1,0:T(8,128)S(1)} %maximum_select_fusion.2), channel_id=1, source_target_pairs={{0,32},{1,33},{2,34},{3,35},{4,36},{5,37},{6,38},{7,39},{8,40},{9,... | collective-permute-start | bytes 589832 | tf_op jit(solution)/shard_map/ppermute | solution.py:89
  58.3 9.2 %collective-permute-start.10 = (f32[2,1536]{1,0:T(2,128)S(1)}, f32[2,1536]{1,0:T(2,128)S(1)}, u32[]{:S(2)}, u32[]{:S(2)}) collective-permute-start(f32[2,1536]{1,0:T(2,128)S(1)} %pad_maximum_fusion.5), channel_id=1, source_target_pairs={{0,1},{1,2},{2,3},{3,4},{4,5},{5,6},{6,7},{7,8},{8,9},{9,10},{10,1... | collective-permute-start | bytes 36872 | tf_op jit(solution)/shard_map/ppermute | solution.py:195
  68.8 9.1 %collective-permute-start.9 = (f32[64,1536]{1,0:T(8,128)S(1)}, f32[64,1536]{1,0:T(8,128)S(1)}, u32[]{:S(2)}, u32[]{:S(2)}) collective-permute-start(f32[64,1536]{1,0:T(8,128)S(1)} %maximum_select_fusion.1), channel_id=1, source_target_pairs={{0,96},{1,97},{2,98},{3,99},{4,100},{5,101},{6,102},{7,103},{8,104... | collective-permute-start | bytes 1179656 | tf_op jit(solution)/shard_map/ppermute | solution.py:89
  68.9 3.3 %collective-permute-start.11 = (f32[2,1536]{1,0:T(2,128)S(1)}, f32[2,1536]{1,0:T(2,128)S(1)}, u32[]{:S(2)}, u32[]{:S(2)}) collective-permute-start(f32[2,1536]{1,0:T(2,128)S(1)} %pad_maximum_fusion.6), channel_id=1, source_target_pairs={{1,0},{2,1},{3,2},{4,3},{5,4},{6,5},{7,6},{8,7},{9,8},{10,9},{11,1... | collective-permute-start | bytes 36872 | tf_op jit(solution)/shard_map/ppermute | solution.py:196
  79.6 12.3 %all-to-all-start.1 = ((f32[8,6,1536]{2,1,0:T(8,128)}), f32[8,6,1536]{2,1,0:T(8,128)S(1)}, u32[]{:S(2)}, u32[]{:S(2)}) async-start(f32[8,6,1536]{2,1,0:T(8,128)} %broadcast_select_fusion.2), calls=%async_computation.1 | async-start | bytes 786432 | tf_op jit(solution)/shard_map/all_to_all | solution.py:176

commit v14 on v11

--- a/solution.py
+++ b/solution.py
@@ -49,6 +49,24 @@
         for j in range(1, x.shape[1] // 128):
             folded = folded + x[:, j * 128:(j + 1) * 128]
         o_ref[b] = _dot3(folded, g1_ref[...], ROWS)
+
+
+def _scale_kernel(pop_ref, at_ref, g1_ref, s1_ref, part_ref):
+    @pl.when(pl.program_id(0) == 0)
+    def _():
+        part_ref[...] = jnp.zeros_like(part_ref)
+
+    acc = part_ref[...]
+    for b in range(pop_ref.shape[0]):
+        x = pop_ref[b]
+        folded = x[:, 0:128]
+        for j in range(1, x.shape[1] // 128):
+            folded = folded + x[:, j * 128:(j + 1) * 128]
+        t = _dot3(folded, g1_ref[...], ROWS)
+        s1 = at_ref[b] / jnp.sum(t, axis=1, keepdims=True)
+        s1_ref[b] = s1
+        acc = acc + t * s1
+    part_ref[...] = acc
 
 
 def _margin_kernel(pop_ref, s2t_ref, e2t_ref, o_ref):
@@ -126,10 +144,18 @@
         e2_np = np.arange(INC * HH * TU)[None, :] // (HH * TU) == np.arange(INC)[:, None]
         e2 = jnp.asarray(e2_np, bf)
         e2t = jnp.asarray(e2_np.T, bf)
-        t1 = _table_call(_sum_kernel, population, [], [g1], HH * TU)
-        area_sum = jnp.sum(t1, axis=2)
-        s1 = area_target / area_sum
-        part = jnp.sum(t1 * s1[:, :, None], axis=0)
+        s1c, part = pl.pallas_call(
+            _scale_kernel,
+            grid=(count // BLOCK,),
+            in_specs=[pl.BlockSpec((BLOCK, AGE * SEX, INC * HH * TU), lambda i: (i, 0, 0)),
+                      pl.BlockSpec((BLOCK, AGE * SEX, 1), lambda i: (i, 0, 0)),
+                      pl.BlockSpec(g1.shape, lambda i: (0, 0))],
+            out_specs=[pl.BlockSpec((BLOCK, AGE * SEX, 1), lambda i: (i, 0, 0)),
+                       pl.BlockSpec((AGE * SEX, HH * TU), lambda i: (0, 0))],
+            out_shape=[jax.ShapeDtypeStruct((count, AGE * SEX, 1), f32),
+                       jax.ShapeDtypeStruct((AGE * SEX, HH * TU), f32)],
+        )(population, area_target[:, :, None], g1)
+        s1 = s1c[:, :, 0]
         nat_rows = (AGE * SEX * HH * TU) // width
 
         nat = part.reshape(nat_rows, width)

time: 103 us -> 103 us (level)
  local copies, waits for them, and re-layouts: 8.74 us -> 11.5 us
  other arithmetic: 14.7 us -> 12.1 us
    pallas_call x0 -> x1, Pallas kernels: none -> 5.09 us  [body(): pl.pallas_call(_scale_kernel, grid=(count // BLOCK,), in_specs=[pl.BlockS...]
    pallas_call x3 -> x2, Pallas kernels: 18.6 us -> 13.8 us  [_table_call(): pl.pallas_call(kernel, grid=grid, in_specs=specs, out_specs=pl.BlockSpec(...]
    reduce_sum x2 -> x0, other arithmetic: 2.89 us -> none  [the longest x1 1.48 us: body(): area_sum = jnp.sum(t1, axis=2)]
    broadcast_in_dim x0 -> x1, local copies, waits for them, and re-layouts: none -> 1.89 us  [body(): area_target[:, :, None]]
  transfers between devices with their start and end apart: 12 -> 12, of which waited for: 10 -> 10; matrix products, arithmetic and copies ran while one was open for 9% -> 10% of each run, Pallas kernels for 6% -> 6%
where the time goes in v14:
time: 103 us; the launch traced here: 102 us
  waiting for transfers between devices  34.2 us (33%)
  starting transfers between devices  19.8 us (19%)
  Pallas kernels  18.9 us (18%)
  other arithmetic  12.1 us (12%)
  local copies, waits for them, and re-layouts  11.5 us (11%)
  between operations  5.53 us (5%)
    ppermute x9, waiting for transfers between devices, _xor(): return lax.ppermute(x, AXES, [(i, _partner(i, bit)) for i in range(n)])  19.6 us
    pallas_call x2, Pallas kernels, _table_call(): pl.pallas_call(kernel, grid=grid, in_specs=specs, out_specs=pl.BlockSpec(...  13.8 us
    ppermute x9, starting transfers between devices, _xor(): return lax.ppermute(x, AXES, [(i, _partner(i, bit)) for i in range(n)])  12.5 us
    all_to_all x1, waiting for transfers between devices, exchange(): return lax.all_to_all(sent, 'mem', 0, 0, tiled=True)  7.36 us
    ppermute x1, waiting for transfers between devices, body(): from_left = lax.ppermute(to_right, AXES, right)  7.29 us
    pallas_call x1, Pallas kernels, body(): pl.pallas_call(_scale_kernel, grid=(count // BLOCK,), in_specs=[pl.BlockS...  5.09 us
    all_to_all x1, starting transfers between devices, exchange(): return lax.all_to_all(sent, 'mem', 0, 0, tiled=True)  3.47 us
  transfers between devices with their start and end apart: 12, of which 10 were waited for; matrix products, arithmetic and copies ran while one was open for 10% of the time, Pallas kernels for 6%

profile of v14, /device:TPU:6, one launch (start us, length us, event | category | flops | bytes accessed | tf_op | source)
XLA Modules:
  0.0 102.0 jit_solution(12572132457908360610)
XLA Ops:
  0.0 1.3 %fusion.42 = (s32[1]{0:T(128)}, s32[1]{0:T(128)}) fusion(s32[16]{0:T(128)} %param.19), kind=kLoop, calls=%fused_computation.150 | loop fusion | bytes 16 | tf_op jit(solution)/shard_map/slice | solution.py:130
  1.9 0.9 select_reduce_fusion.2
  2.8 1.9 %compare_and_fusion.3 = (pred[16]{0:T(512)(128)(4,1)S(1)}, s32[16]{0:T(128)S(1)}, pred[16]{0:T(512)(128)(4,1)S(1)}) fusion(s32[16]{0:T(128)} %param.19, s32[]{:T(128)} %bitcast.1, s32[]{:T(128)} %bitcast.2), kind=kLoop, calls=%fused_computation.119 | loop fusion | flops 144 | bytes 168 | tf_op jit(solution)/shard_map/jit(_take)/and | solution.py:226
  6.2 1.9 %copy.43.at_ref = f32[16,96,1]{2,1,0:T(8,128)} copy(f32[16,96,1]{1,0,2:T(8,128)} %bitcast.43) | data formatting | bytes 12288 | tf_op jit(solution)/shard_map/broadcast_in_dim | solution.py:157
  8.0 5.1 %shard_map.91 = (f32[16,96,1]{2,1,0:T(8,128)}, f32[96,32]{1,0:T(8,128)}) custom-call(f32[16,96,1024]{2,1,0:T(8,128)} %pop_ref.5, f32[16,96,1]{2,1,0:T(8,128)} %copy.43.at_ref, bf16[128,32]{1,0:T(8,128)(2,1)} %constant.230.clone.g1_ref), custom_call_target="tpu_custom_call" | custom-call | tf_op jit(solution)/shard_map/pallas_call | solution.py:147
  13.2 1.0 reshape.653
  14.2 2.0 %collective-permute-start = (f32[11,1536]{1,0:T(8,128)S(1)}, f32[11,1536]{1,0:T(8,128)S(1)}, u32[]{:S(2)}, u32[]{:S(2)}) collective-permute-start(f32[11,1536]{1,0:T(8,128)S(1)} %pad_maximum_fusion.1), channel_id=1, source_target_pairs={{0,8},{1,9},{2,10},{3,11},{4,12},{5,13},{6,14},{7,15},{8,0},{9,1},... | collective-permute-start | bytes 202760 | tf_op jit(solution)/shard_map/ppermute | solution.py:107
  17.5 1.5 %collective-permute-done = f32[11,1536]{1,0:T(8,128)S(1)} collective-permute-done((f32[11,1536]{1,0:T(8,128)S(1)}, f32[11,1536]{1,0:T(8,128)S(1)}, u32[]{:S(2)}, u32[]{:S(2)}) %collective-permute-start) | collective-permute-done | bytes 67616 | tf_op jit(solution)/shard_map/ppermute | solution.py:107
  19.1 4.0 %collective-permute-start.1 = (f32[19,1536]{1,0:T(8,128)S(1)}, f32[19,1536]{1,0:T(8,128)S(1)}, u32[]{:S(2)}, u32[]{:S(2)}) collective-permute-start(f32[19,1536]{1,0:T(8,128)S(1)} %pad_maximum_fusion), channel_id=1, source_target_pairs={{0,24},{1,25},{2,26},{3,27},{4,28},{5,29},{6,30},{7,31},{8,16},{9,... | collective-permute-start | bytes 350216 | tf_op jit(solution)/shard_map/ppermute | solution.py:107
  23.1 3.1 %collective-permute-done.1 = f32[19,1536]{1,0:T(8,128)S(1)} collective-permute-done((f32[19,1536]{1,0:T(8,128)S(1)}, f32[19,1536]{1,0:T(8,128)S(1)}, u32[]{:S(2)}, u32[]{:S(2)}) %collective-permute-start.1) | collective-permute-done | bytes 116768 | tf_op jit(solution)/shard_map/ppermute | solution.py:107
  26.3 0.9 collective-permute-start.2
  28.4 1.8 %collective-permute-done.2 = f32[3,1536]{1,0:T(4,128)S(1)} collective-permute-done((f32[3,1536]{1,0:T(4,128)S(1)}, f32[3,1536]{1,0:T(4,128)S(1)}, u32[]{:S(2)}, u32[]{:S(2)}) %collective-permute-start.2) | collective-permute-done | bytes 18464 | tf_op jit(solution)/shard_map/ppermute | solution.py:107
  30.8 0.7 and_reduce_fusion
  31.5 3.8 %collective-permute-done.3 = f32[3,1536]{1,0:T(4,128)S(1)} collective-permute-done((f32[3,1536]{1,0:T(4,128)S(1)}, f32[3,1536]{1,0:T(4,128)S(1)}, u32[]{:S(2)}, u32[]{:S(2)}) %collective-permute-start.3) | collective-permute-done | bytes 18464 | tf_op jit(solution)/shard_map/ppermute | solution.py:107
  35.5 1.2 %collective-permute-done.4 = f32[4,1536]{1,0:T(4,128)S(1)} collective-permute-done((f32[4,1536]{1,0:T(4,128)S(1)}, f32[4,1536]{1,0:T(4,128)S(1)}, u32[]{:S(2)}, u32[]{:S(2)}) %collective-permute-start.4) | collective-permute-done | bytes 24608 | tf_op jit(solution)/shard_map/ppermute | solution.py:107
  36.7 1.7 %collective-permute-start.5 = (f32[4,1536]{1,0:T(4,128)S(1)}, f32[4,1536]{1,0:T(4,128)S(1)}, u32[]{:S(2)}, u32[]{:S(2)}) collective-permute-start(f32[4,1536]{1,0:T(4,128)S(1)} %fusion.40), channel_id=1, source_target_pairs={{0,2},{1,3},{2,0},{3,1},{4,6},{5,7},{6,4},{7,5},{8,10},{9,11},{10,... | collective-permute-start | bytes 73736 | tf_op jit(solution)/shard_map/ppermute | solution.py:107
  38.7 1.9 %collective-permute-done.5 = f32[4,1536]{1,0:T(4,128)S(1)} collective-permute-done((f32[4,1536]{1,0:T(4,128)S(1)}, f32[4,1536]{1,0:T(4,128)S(1)}, u32[]{:S(2)}, u32[]{:S(2)}) %collective-permute-start.5) | collective-permute-done | bytes 24608 | tf_op jit(solution)/shard_map/ppermute | solution.py:107
  40.6 3.1 %collective-permute-start.6 = (f32[4,1536]{1,0:T(4,128)S(1)}, f32[4,1536]{1,0:T(4,128)S(1)}, u32[]{:S(2)}, u32[]{:S(2)}) collective-permute-start(f32[4,1536]{1,0:T(4,128)S(1)} %add.315), channel_id=1, source_target_pairs={{0,6},{1,7},{2,4},{3,5},{4,2},{5,3},{6,0},{7,1},{8,14},{9,15},{10,... | collective-permute-start | bytes 73736 | tf_op jit(solution)/shard_map/ppermute | solution.py:107
  43.8 1.9 %collective-permute-done.6 = f32[4,1536]{1,0:T(4,128)S(1)} collective-permute-done((f32[4,1536]{1,0:T(4,128)S(1)}, f32[4,1536]{1,0:T(4,128)S(1)}, u32[]{:S(2)}, u32[]{:S(2)}) %collective-permute-start.6) | collective-permute-done | bytes 24608 | tf_op jit(solution)/shard_map/ppermute | solution.py:107
  47.6 0.9 copy.49.s2t_ref
  48.5 6.3 %shard_map.92 = f32[16,96,32]{2,1,0:T(8,128)} custom-call(f32[16,96,1024]{2,1,0:T(8,128)} %pop_ref.5, f32[96,1024]{1,0:T(8,128)} %copy.49.s2t_ref, bf16[1024,32]{1,0:T(8,128)(2,1)} %constant.232.clone.e2t_ref), custom_call_target="tpu_custom_call" | custom-call | tf_op jit(solution)/shard_map/pallas_call | solution.py:89
  54.8 1.4 %broadcast_multiply_fusion.1 = f32[16,96,32]{2,1,0:T(8,128)S(1)} fusion(f32[16,96,32]{2,1,0:T(8,128)} %shard_map.92, f32[16,96]{1,0:T(8,128)S(1)} %reduce.12), kind=kLoop, calls=%fused_computation.33 | loop fusion | flops 49152 | bytes 399360 | tf_op jit(solution)/shard_map/mul | solution.py:211
  56.2 1.0 reduce_sum.80
  57.6 1.9 %collective-permute-start.9 = (f32[2,1536]{1,0:T(2,128)S(1)}, f32[2,1536]{1,0:T(2,128)S(1)}, u32[]{:S(2)}, u32[]{:S(2)}) collective-permute-start(f32[2,1536]{1,0:T(2,128)S(1)} %pad_maximum_fusion.5), channel_id=1, source_target_pairs={{0,1},{1,2},{2,3},{3,4},{4,5},{5,6},{6,7},{7,8},{8,9},{9,10},{10,1... | collective-permute-start | bytes 36872 | tf_op jit(solution)/shard_map/ppermute | solution.py:221
  59.5 7.3 %collective-permute-done.9 = f32[2,1536]{1,0:T(2,128)S(1)} collective-permute-done((f32[2,1536]{1,0:T(2,128)S(1)}, f32[2,1536]{1,0:T(2,128)S(1)}, u32[]{:S(2)}, u32[]{:S(2)}) %collective-permute-start.9) | collective-permute-done | bytes 12320 | tf_op jit(solution)/shard_map/ppermute | solution.py:221
  68.2 1.9 %collective-permute-start.10 = (f32[2,1536]{1,0:T(2,128)S(1)}, f32[2,1536]{1,0:T(2,128)S(1)}, u32[]{:S(2)}, u32[]{:S(2)}) collective-permute-start(f32[2,1536]{1,0:T(2,128)S(1)} %pad_maximum_fusion.6), channel_id=1, source_target_pairs={{1,0},{2,1},{3,2},{4,3},{5,4},{6,5},{7,6},{8,7},{9,8},{10,9},{11,1... | collective-permute-start | bytes 36872 | tf_op jit(solution)/shard_map/ppermute | solution.py:222
  72.7 4.4 %collective-permute-done.8 = f32[64,1536]{1,0:T(8,128)S(1)} collective-permute-done((f32[64,1536]{1,0:T(8,128)S(1)}, f32[64,1536]{1,0:T(8,128)S(1)}, u32[]{:S(2)}, u32[]{:S(2)}) %collective-permute-start.8) | collective-permute-done | bytes 393248 | tf_op jit(solution)/shard_map/ppermute | solution.py:107
  77.9 0.8 broadcast_select_fusion.2
  78.9 3.5 %all-to-all-start.1 = ((f32[8,6,1536]{2,1,0:T(8,128)}), f32[8,6,1536]{2,1,0:T(8,128)S(1)}, u32[]{:S(2)}, u32[]{:S(2)}) async-start(f32[8,6,1536]{2,1,0:T(8,128)} %broadcast_select_fusion.2), calls=%async_computation.1 | async-start | bytes 786432 | tf_op jit(solution)/shard_map/all_to_all | solution.py:202
  83.8 7.4 %all-to-all-done.1 = f32[8,6,1536]{2,1,0:T(8,128)S(1)} async-done(((f32[8,6,1536]{2,1,0:T(8,128)}), f32[8,6,1536]{2,1,0:T(8,128)S(1)}, u32[]{:S(2)}, u32[]{:S(2)}) %all-to-all-start.1) | async-done | bytes 294944 | tf_op jit(solution)/shard_map/all_to_all | solution.py:202
  93.4 1.1 %broadcast_multiply_fusion.r_ref = f32[16,96,32]{2,1,0:T(8,128)} fusion(f32[16,96,32]{2,1,0:T(8,128)S(1)} %bitcast.41, f32[16,96]{1,0:T(8,128)S(1)} %reduce.12), kind=kLoop, calls=%fused_computation.32 | loop fusion | flops 49152 | bytes 399360 | tf_op jit(solution)/shard_map/mul | solution.py:228
  94.5 7.5 %shard_map.93 = f32[16,96,1024]{2,1,0:T(8,128)} custom-call(f32[16,96,1024]{2,1,0:T(8,128)} %pop_ref.5, f32[16,96,32]{2,1,0:T(8,128)} %broadcast_multiply_fusion.r_ref, f32[96,1024]{1,0:T(8,128)} %copy.49.s2t_ref, bf16[32,1024]{1,0:T(8,128)(2,1)} %constant.231.clone.e2_ref), custom_call_target="tpu_custom_call" | custom-call | tf_op jit(solution)/shard_map/pallas_call | solution.py:89
  (104 shorter events, 11.5 us)
Async XLA Ops:
  8.0 6.1 %copy-start.1 = (f32[8,1536]{1,0:T(8,128)S(1)}, f32[8,1536]{1,0:T(8,128)}, u32[]{:S(2)}) copy-start(f32[8,1536]{1,0:T(8,128)} %param.18) | copy-start | bytes 147460
  8.0 22.7 %copy-start.4 = (s32[2]{0:T(128)S(1)}, s32[2]{0:T(128)}, u32[]{:S(2)}) copy-start(s32[2]{0:T(128)} %constant.228.clone.1) | copy-start | bytes 28
  13.1 25.2 %copy-start = (f32[16,96,1]{2,1,0:T(8,128)S(1)}, f32[16,96,1]{2,1,0:T(8,128)}, u32[]{:S(2)}) copy-start(f32[16,96,1]{2,1,0:T(8,128)} %get-tuple-element.117) | copy-start | bytes 18436
  13.1 33.1 %copy-start.3 = (s32[1024]{0:T(1024)S(1)}, s32[1024]{0:T(1024)}, u32[]{:S(2)}) copy-start(s32[1024]{0:T(1024)} %param.20) | copy-start | bytes 12292
  13.1 34.3 %copy-start.2 = (f32[96,32]{0,1:T(8,128)S(1)}, f32[96,32]{0,1:T(8,128)}, u32[]{:S(2)}) copy-start(f32[96,32]{0,1:T(8,128)} %param.17) | copy-start | bytes 36868
  14.2 4.8 %collective-permute-start = (f32[11,1536]{1,0:T(8,128)S(1)}, f32[11,1536]{1,0:T(8,128)S(1)}, u32[]{:S(2)}, u32[]{:S(2)}) collective-permute-start(f32[11,1536]{1,0:T(8,128)S(1)} %pad_maximum_fusion.1), channel_id=1, source_target_pairs={{0,8},{1,9},{2,10},{3,11},{4,12},{5,13},{6,14},{7,15},{8,0},{9,1},... | collective-permute-start | bytes 202760 | tf_op jit(solution)/shard_map/ppermute | solution.py:107
  19.1 7.1 %collective-permute-start.1 = (f32[19,1536]{1,0:T(8,128)S(1)}, f32[19,1536]{1,0:T(8,128)S(1)}, u32[]{:S(2)}, u32[]{:S(2)}) collective-permute-start(f32[19,1536]{1,0:T(8,128)S(1)} %pad_maximum_fusion), channel_id=1, source_target_pairs={{0,24},{1,25},{2,26},{3,27},{4,28},{5,29},{6,30},{7,31},{8,16},{9,... | collective-permute-start | bytes 350216 | tf_op jit(solution)/shard_map/ppermute | solution.py:107
  26.3 3.9 %collective-permute-start.2 = (f32[3,1536]{1,0:T(4,128)S(1)}, f32[3,1536]{1,0:T(4,128)S(1)}, u32[]{:S(2)}, u32[]{:S(2)}) collective-permute-start(f32[3,1536]{1,0:T(4,128)S(1)} %pad_maximum_fusion.2), channel_id=1, source_target_pairs={{0,32},{1,33},{2,34},{3,35},{4,36},{5,37},{6,38},{7,39},{8,40},{9,... | collective-permute-start | bytes 55304 | tf_op jit(solution)/shard_map/ppermute | solution.py:107
  30.2 5.1 %collective-permute-start.3 = (f32[3,1536]{1,0:T(4,128)S(1)}, f32[3,1536]{1,0:T(4,128)S(1)}, u32[]{:S(2)}, u32[]{:S(2)}) collective-permute-start(f32[3,1536]{1,0:T(4,128)S(1)} %pad_maximum_fusion.3), channel_id=1, source_target_pairs={{0,96},{1,97},{2,98},{3,99},{4,100},{5,101},{6,102},{7,103},{8,104... | collective-permute-start | bytes 55304 | tf_op jit(solution)/shard_map/ppermute | solution.py:107
  35.4 1.3 %collective-permute-start.4 = (f32[4,1536]{1,0:T(4,128)S(1)}, f32[4,1536]{1,0:T(4,128)S(1)}, u32[]{:S(2)}, u32[]{:S(2)}) collective-permute-start(f32[4,1536]{1,0:T(4,128)S(1)} %pad_maximum_fusion.4), channel_id=1, source_target_pairs={{0,1},{1,0},{2,3},{3,2},{4,5},{5,4},{6,7},{7,6},{8,9},{9,8},{10,11... | collective-permute-start | bytes 73736 | tf_op jit(solution)/shard_map/ppermute | solution.py:107
  36.7 3.9 %collective-permute-start.5 = (f32[4,1536]{1,0:T(4,128)S(1)}, f32[4,1536]{1,0:T(4,128)S(1)}, u32[]{:S(2)}, u32[]{:S(2)}) collective-permute-start(f32[4,1536]{1,0:T(4,128)S(1)} %fusion.40), channel_id=1, source_target_pairs={{0,2},{1,3},{2,0},{3,1},{4,6},{5,7},{6,4},{7,5},{8,10},{9,11},{10,... | collective-permute-start | bytes 73736 | tf_op jit(solution)/shard_map/ppermute | solution.py:107
  40.6 5.1 %collective-permute-start.6 = (f32[4,1536]{1,0:T(4,128)S(1)}, f32[4,1536]{1,0:T(4,128)S(1)}, u32[]{:S(2)}, u32[]{:S(2)}) collective-permute-start(f32[4,1536]{1,0:T(4,128)S(1)} %add.315), channel_id=1, source_target_pairs={{0,6},{1,7},{2,4},{3,5},{4,2},{5,3},{6,0},{7,1},{8,14},{9,15},{10,... | collective-permute-start | bytes 73736 | tf_op jit(solution)/shard_map/ppermute | solution.py:107
  43.7 24.3 %collective-permute-start.7 = (f32[32,1536]{1,0:T(8,128)S(1)}, f32[32,1536]{1,0:T(8,128)S(1)}, u32[]{:S(2)}, u32[]{:S(2)}) collective-permute-start(f32[32,1536]{1,0:T(8,128)S(1)} %maximum_select_fusion.2), channel_id=1, source_target_pairs={{0,32},{1,33},{2,34},{3,35},{4,36},{5,37},{6,38},{7,39},{8,40},{9,... | collective-permute-start | bytes 589832 | tf_op jit(solution)/shard_map/ppermute | solution.py:107
  57.6 9.2 %collective-permute-start.9 = (f32[2,1536]{1,0:T(2,128)S(1)}, f32[2,1536]{1,0:T(2,128)S(1)}, u32[]{:S(2)}, u32[]{:S(2)}) collective-permute-start(f32[2,1536]{1,0:T(2,128)S(1)} %pad_maximum_fusion.5), channel_id=1, source_target_pairs={{0,1},{1,2},{2,3},{3,4},{4,5},{5,6},{6,7},{7,8},{8,9},{9,10},{10,1... | collective-permute-start | bytes 36872 | tf_op jit(solution)/shard_map/ppermute | solution.py:221
  68.1 9.1 %collective-permute-start.8 = (f32[64,1536]{1,0:T(8,128)S(1)}, f32[64,1536]{1,0:T(8,128)S(1)}, u32[]{:S(2)}, u32[]{:S(2)}) collective-permute-start(f32[64,1536]{1,0:T(8,128)S(1)} %maximum_select_fusion.1), channel_id=1, source_target_pairs={{0,96},{1,97},{2,98},{3,99},{4,100},{5,101},{6,102},{7,103},{8,104... | collective-permute-start | bytes 1179656 | tf_op jit(solution)/shard_map/ppermute | solution.py:107
  68.2 3.3 %collective-permute-start.10 = (f32[2,1536]{1,0:T(2,128)S(1)}, f32[2,1536]{1,0:T(2,128)S(1)}, u32[]{:S(2)}, u32[]{:S(2)}) collective-permute-start(f32[2,1536]{1,0:T(2,128)S(1)} %pad_maximum_fusion.6), channel_id=1, source_target_pairs={{1,0},{2,1},{3,2},{4,3},{5,4},{6,5},{7,6},{8,7},{9,8},{10,9},{11,1... | collective-permute-start | bytes 36872 | tf_op jit(solution)/shard_map/ppermute | solution.py:222
  78.9 12.3 %all-to-all-start.1 = ((f32[8,6,1536]{2,1,0:T(8,128)}), f32[8,6,1536]{2,1,0:T(8,128)S(1)}, u32[]{:S(2)}, u32[]{:S(2)}) async-start(f32[8,6,1536]{2,1,0:T(8,128)} %broadcast_select_fusion.2), calls=%async_computation.1 | async-start | bytes 786432 | tf_op jit(solution)/shard_map/all_to_all | solution.py:202

commit v15 on v14

--- a/solution.py
+++ b/solution.py
@@ -69,9 +69,10 @@
     part_ref[...] = acc
 
 
-def _margin_kernel(pop_ref, s2t_ref, e2t_ref, o_ref):
-    for b in range(pop_ref.shape[0]):
-        o_ref[b] = _dot3(pop_ref[b] * s2t_ref[...], e2t_ref[...], ROWS)
+def _margin_kernel(pop_ref, s1_ref, s2t_ref, e2t_ref, pair_ref, o_ref):
+    for b in range(pop_ref.shape[0]):
+        o = _dot3(pop_ref[b] * s2t_ref[...], e2t_ref[...], ROWS) * s1_ref[b]
+        o_ref[b] = jnp.dot(pair_ref[...], o, precision=HI, preferred_element_type=jnp.float32)
 
 
 def _fit_kernel(pop_ref, r_ref, s2t_ref, e2_ref, o_ref):
@@ -208,8 +209,18 @@
                            slow[m_mem, jnp.clip(m_rank - ROOMY, 0, spare - 1)])
 
         s2t = jnp.tile(s2, (1, INC))
-        am = _table_call(_margin_kernel, population, [], [s2t, e2t], INC) * s1[:, :, None]
-        am = jnp.sum(am.reshape(count, AGE, SEX, INC), axis=2).reshape(count, AGE * INC)
+        pair = jnp.asarray(np.arange(AGE * SEX)[None, :] // SEX == np.arange(AGE)[:, None], f32)
+        am = pl.pallas_call(
+            _margin_kernel,
+            grid=(count // BLOCK,),
+            in_specs=[pl.BlockSpec((BLOCK, AGE * SEX, INC * HH * TU), lambda i: (i, 0, 0)),
+                      pl.BlockSpec((BLOCK, AGE * SEX, 1), lambda i: (i, 0, 0)),
+                      pl.BlockSpec(s2t.shape, lambda i: (0, 0)),
+                      pl.BlockSpec(e2t.shape, lambda i: (0, 0)),
+                      pl.BlockSpec(pair.shape, lambda i: (0, 0))],
+            out_specs=pl.BlockSpec((BLOCK, AGE, INC), lambda i: (i, 0, 0)),
+            out_shape=jax.ShapeDtypeStruct((count, AGE, INC), f32),
+        )(population, s1c, s2t, e2t, pair).reshape(count, AGE * INC)
         k_a = area_zone - zlo
         onehot = (k_a[:, None] == ks[None, :]).astype(f32)
         zp = jnp.sum(onehot[:, :, None] * am[:, None, :], axis=0)

time: 103 us -> 103 us (level)
  other arithmetic: 12.1 us -> 9.84 us
  Pallas kernels: 18.9 us -> 20.8 us
    pallas_call x0 -> x1, Pallas kernels: none -> 8.2 us  [body(): pl.pallas_call(_margin_kernel, grid=(count // BLOCK,), in_specs=[pl.Block...]
    pallas_call x2 -> x1, Pallas kernels: 13.8 us -> 7.5 us  [_table_call(): pl.pallas_call(kernel, grid=grid, in_specs=specs, out_specs=pl.BlockSpec(...]
    mul x1 -> x0, other arithmetic: 1.4 us -> none  [body(): _table_call(_margin_kernel, population, [], [s2t, e2t], INC)]
  transfers between devices with their start and end apart: 12 -> 12, of which waited for: 10 -> 10; matrix products, arithmetic and copies ran while one was open for 10% -> 8% of each run, Pallas kernels for 6% -> 8%
where the time goes in v15:
time: 103 us
  waiting for transfers between devices  34.1 us (33%)
  Pallas kernels  20.8 us (20%)
  starting transfers between devices  19.8 us (19%)
  local copies, waits for them, and re-layouts  12.5 us (12%)
  other arithmetic  9.84 us (10%)
  between operations  5.64 us (5%)
    ppermute x9, waiting for transfers between devices, _xor(): return lax.ppermute(x, AXES, [(i, _partner(i, bit)) for i in range(n)])  19.4 us
    ppermute x9, starting transfers between devices, _xor(): return lax.ppermute(x, AXES, [(i, _partner(i, bit)) for i in range(n)])  12.5 us
    pallas_call x1, Pallas kernels, body(): pl.pallas_call(_margin_kernel, grid=(count // BLOCK,), in_specs=[pl.Block...  8.2 us
    pallas_call x1, Pallas kernels, _table_call(): pl.pallas_call(kernel, grid=grid, in_specs=specs, out_specs=pl.BlockSpec(...  7.5 us
    all_to_all x1, waiting for transfers between devices, exchange(): return lax.all_to_all(sent, 'mem', 0, 0, tiled=True)  7.39 us
    ppermute x1, waiting for transfers between devices, body(): from_left = lax.ppermute(to_right, AXES, right)  7.29 us
    pallas_call x1, Pallas kernels, body(): pl.pallas_call(_scale_kernel, grid=(count // BLOCK,), in_specs=[pl.BlockS...  5.09 us
    all_to_all x1, starting transfers between devices, exchange(): return lax.all_to_all(sent, 'mem', 0, 0, tiled=True)  3.47 us
  transfers between devices with their start and end apart: 12, of which 10 were waited for; matrix products, arithmetic and copies ran while one was open for 8% of the time, Pallas kernels for 8%

profile of v15, /device:TPU:6, one launch (start us, length us, event | category | flops | bytes accessed | tf_op | source)
XLA Modules:
  0.0 102.6 jit_solution(14014111720352234985)
XLA Ops:
  0.0 1.3 %fusion.42 = (s32[1]{0:T(128)}, s32[1]{0:T(128)}) fusion(s32[16]{0:T(128)} %param.20), kind=kLoop, calls=%fused_computation.149 | loop fusion | bytes 16 | tf_op jit(solution)/shard_map/slice | solution.py:131
  2.0 0.9 select_reduce_fusion.2
  2.9 1.9 %compare_and_fusion.3 = (pred[16]{0:T(512)(128)(4,1)S(1)}, s32[16]{0:T(128)S(1)}, pred[16]{0:T(512)(128)(4,1)S(1)}) fusion(s32[16]{0:T(128)} %param.20, s32[]{:T(128)} %bitcast.1, s32[]{:T(128)} %bitcast.2), kind=kLoop, calls=%fused_computation.118 | loop fusion | flops 144 | bytes 168 | tf_op jit(solution)/shard_map/jit(_take)/and | solution.py:237
  6.3 1.9 %copy.44.at_ref = f32[16,96,1]{2,1,0:T(8,128)} copy(f32[16,96,1]{1,0,2:T(8,128)} %bitcast.41) | data formatting | bytes 12288 | tf_op jit(solution)/shard_map/broadcast_in_dim | solution.py:158
  8.2 5.1 %shard_map.100 = (f32[16,96,1]{2,1,0:T(8,128)}, f32[96,32]{1,0:T(8,128)}) custom-call(f32[16,96,1024]{2,1,0:T(8,128)} %pop_ref.5, f32[16,96,1]{2,1,0:T(8,128)} %copy.44.at_ref, bf16[128,32]{1,0:T(8,128)(2,1)} %constant.232.clone.g1_ref), custom_call_target="tpu_custom_call" | custom-call | tf_op jit(solution)/shard_map/pallas_call | solution.py:148
  13.3 1.0 reshape.650
  14.3 2.0 %collective-permute-start = (f32[11,1536]{1,0:T(8,128)S(1)}, f32[11,1536]{1,0:T(8,128)S(1)}, u32[]{:S(2)}, u32[]{:S(2)}) collective-permute-start(f32[11,1536]{1,0:T(8,128)S(1)} %pad_maximum_fusion.1), channel_id=1, source_target_pairs={{0,8},{1,9},{2,10},{3,11},{4,12},{5,13},{6,14},{7,15},{8,0},{9,1},... | collective-permute-start | bytes 202760 | tf_op jit(solution)/shard_map/ppermute | solution.py:108
  17.7 1.4 %collective-permute-done = f32[11,1536]{1,0:T(8,128)S(1)} collective-permute-done((f32[11,1536]{1,0:T(8,128)S(1)}, f32[11,1536]{1,0:T(8,128)S(1)}, u32[]{:S(2)}, u32[]{:S(2)}) %collective-permute-start) | collective-permute-done | bytes 67616 | tf_op jit(solution)/shard_map/ppermute | solution.py:108
  19.2 4.0 %collective-permute-start.1 = (f32[19,1536]{1,0:T(8,128)S(1)}, f32[19,1536]{1,0:T(8,128)S(1)}, u32[]{:S(2)}, u32[]{:S(2)}) collective-permute-start(f32[19,1536]{1,0:T(8,128)S(1)} %pad_maximum_fusion), channel_id=1, source_target_pairs={{0,24},{1,25},{2,26},{3,27},{4,28},{5,29},{6,30},{7,31},{8,16},{9,... | collective-permute-start | bytes 350216 | tf_op jit(solution)/shard_map/ppermute | solution.py:108
  23.2 3.1 %collective-permute-done.1 = f32[19,1536]{1,0:T(8,128)S(1)} collective-permute-done((f32[19,1536]{1,0:T(8,128)S(1)}, f32[19,1536]{1,0:T(8,128)S(1)}, u32[]{:S(2)}, u32[]{:S(2)}) %collective-permute-start.1) | collective-permute-done | bytes 116768 | tf_op jit(solution)/shard_map/ppermute | solution.py:108
  26.4 0.9 collective-permute-start.2
  28.6 1.7 %collective-permute-done.2 = f32[3,1536]{1,0:T(4,128)S(1)} collective-permute-done((f32[3,1536]{1,0:T(4,128)S(1)}, f32[3,1536]{1,0:T(4,128)S(1)}, u32[]{:S(2)}, u32[]{:S(2)}) %collective-permute-start.2) | collective-permute-done | bytes 18464 | tf_op jit(solution)/shard_map/ppermute | solution.py:108
  30.9 0.7 and_reduce_fusion
  31.6 3.8 %collective-permute-done.3 = f32[3,1536]{1,0:T(4,128)S(1)} collective-permute-done((f32[3,1536]{1,0:T(4,128)S(1)}, f32[3,1536]{1,0:T(4,128)S(1)}, u32[]{:S(2)}, u32[]{:S(2)}) %collective-permute-start.3) | collective-permute-done | bytes 18464 | tf_op jit(solution)/shard_map/ppermute | solution.py:108
  35.6 1.2 %collective-permute-done.4 = f32[4,1536]{1,0:T(4,128)S(1)} collective-permute-done((f32[4,1536]{1,0:T(4,128)S(1)}, f32[4,1536]{1,0:T(4,128)S(1)}, u32[]{:S(2)}, u32[]{:S(2)}) %collective-permute-start.4) | collective-permute-done | bytes 24608 | tf_op jit(solution)/shard_map/ppermute | solution.py:108
  36.8 1.7 %collective-permute-start.5 = (f32[4,1536]{1,0:T(4,128)S(1)}, f32[4,1536]{1,0:T(4,128)S(1)}, u32[]{:S(2)}, u32[]{:S(2)}) collective-permute-start(f32[4,1536]{1,0:T(4,128)S(1)} %fusion.40), channel_id=1, source_target_pairs={{0,2},{1,3},{2,0},{3,1},{4,6},{5,7},{6,4},{7,5},{8,10},{9,11},{10,... | collective-permute-start | bytes 73736 | tf_op jit(solution)/shard_map/ppermute | solution.py:108
  38.9 1.9 %collective-permute-done.5 = f32[4,1536]{1,0:T(4,128)S(1)} collective-permute-done((f32[4,1536]{1,0:T(4,128)S(1)}, f32[4,1536]{1,0:T(4,128)S(1)}, u32[]{:S(2)}, u32[]{:S(2)}) %collective-permute-start.5) | collective-permute-done | bytes 24608 | tf_op jit(solution)/shard_map/ppermute | solution.py:108
  40.7 3.1 %collective-permute-start.6 = (f32[4,1536]{1,0:T(4,128)S(1)}, f32[4,1536]{1,0:T(4,128)S(1)}, u32[]{:S(2)}, u32[]{:S(2)}) collective-permute-start(f32[4,1536]{1,0:T(4,128)S(1)} %add.315), channel_id=1, source_target_pairs={{0,6},{1,7},{2,4},{3,5},{4,2},{5,3},{6,0},{7,1},{8,14},{9,15},{10,... | collective-permute-start | bytes 73736 | tf_op jit(solution)/shard_map/ppermute | solution.py:108
  44.0 1.9 %collective-permute-done.6 = f32[4,1536]{1,0:T(4,128)S(1)} collective-permute-done((f32[4,1536]{1,0:T(4,128)S(1)}, f32[4,1536]{1,0:T(4,128)S(1)}, u32[]{:S(2)}, u32[]{:S(2)}) %collective-permute-start.6) | collective-permute-done | bytes 24608 | tf_op jit(solution)/shard_map/ppermute | solution.py:108
  47.7 0.9 copy.50.s2t_ref
  48.6 8.2 %shard_map.101 = f32[16,48,32]{2,1,0:T(8,128)} custom-call(f32[16,96,1024]{2,1,0:T(8,128)} %pop_ref.5, f32[16,96,1]{2,1,0:T(8,128)} %get-tuple-element.117.s1_ref, f32[96,1024]{1,0:T(8,128)} %copy.50.s2t_ref, bf16[1024,32]{1,0:T(8,128)(2,1)} %constant.234.clone.e2t_ref, f32[48,96]{1,0:T(8,128)} %constant.235.clone.pair_ref), custom_call_target="tpu_custom_call" | custom-call | tf_op jit(solution)/shard_map/pallas_call | solution.py:213
  56.9 1.1 %mul.47 = f32[16,1536]{1,0:T(8,128)S(1)} reshape(f32[16,48,32]{2,1,0:T(8,128)} %shard_map.101) | data formatting | bytes 196608 | tf_op jit(solution)/shard_map/mul | solution.py:226
  58.2 1.9 %collective-permute-start.9 = (f32[2,1536]{1,0:T(2,128)S(1)}, f32[2,1536]{1,0:T(2,128)S(1)}, u32[]{:S(2)}, u32[]{:S(2)}) collective-permute-start(f32[2,1536]{1,0:T(2,128)S(1)} %pad_maximum_fusion.5), channel_id=1, source_target_pairs={{0,1},{1,2},{2,3},{3,4},{4,5},{5,6},{6,7},{7,8},{8,9},{9,10},{10,1... | collective-permute-start | bytes 36872 | tf_op jit(solution)/shard_map/ppermute | solution.py:232
  60.2 7.3 %collective-permute-done.9 = f32[2,1536]{1,0:T(2,128)S(1)} collective-permute-done((f32[2,1536]{1,0:T(2,128)S(1)}, f32[2,1536]{1,0:T(2,128)S(1)}, u32[]{:S(2)}, u32[]{:S(2)}) %collective-permute-start.9) | collective-permute-done | bytes 12320 | tf_op jit(solution)/shard_map/ppermute | solution.py:232
  68.8 1.9 %collective-permute-start.10 = (f32[2,1536]{1,0:T(2,128)S(1)}, f32[2,1536]{1,0:T(2,128)S(1)}, u32[]{:S(2)}, u32[]{:S(2)}) collective-permute-start(f32[2,1536]{1,0:T(2,128)S(1)} %pad_maximum_fusion.6), channel_id=1, source_target_pairs={{1,0},{2,1},{3,2},{4,3},{5,4},{6,5},{7,6},{8,7},{9,8},{10,9},{11,1... | collective-permute-start | bytes 36872 | tf_op jit(solution)/shard_map/ppermute | solution.py:233
  73.3 4.4 %collective-permute-done.8 = f32[64,1536]{1,0:T(8,128)S(1)} collective-permute-done((f32[64,1536]{1,0:T(8,128)S(1)}, f32[64,1536]{1,0:T(8,128)S(1)}, u32[]{:S(2)}, u32[]{:S(2)}) %collective-permute-start.8) | collective-permute-done | bytes 393248 | tf_op jit(solution)/shard_map/ppermute | solution.py:108
  77.8 0.7 gather_fusion.1
  78.5 0.8 broadcast_select_fusion.2
  79.5 3.5 %all-to-all-start.1 = ((f32[8,6,1536]{2,1,0:T(8,128)}), f32[8,6,1536]{2,1,0:T(8,128)S(1)}, u32[]{:S(2)}, u32[]{:S(2)}) async-start(f32[8,6,1536]{2,1,0:T(8,128)} %broadcast_select_fusion.2), calls=%async_computation.1 | async-start | bytes 786432 | tf_op jit(solution)/shard_map/all_to_all | solution.py:203
  84.4 7.4 %all-to-all-done.1 = f32[8,6,1536]{2,1,0:T(8,128)S(1)} async-done(((f32[8,6,1536]{2,1,0:T(8,128)}), f32[8,6,1536]{2,1,0:T(8,128)S(1)}, u32[]{:S(2)}, u32[]{:S(2)}) %all-to-all-start.1) | async-done | bytes 294944 | tf_op jit(solution)/shard_map/all_to_all | solution.py:203
  94.0 1.1 %broadcast_multiply_fusion.r_ref = f32[16,96,32]{2,1,0:T(8,128)} fusion(f32[16,96,32]{2,1,0:T(8,128)S(1)} %bitcast.39, f32[16,96]{1,0:T(8,128)S(1)} %reduce.12), kind=kLoop, calls=%fused_computation.32 | loop fusion | flops 49152 | bytes 399360 | tf_op jit(solution)/shard_map/mul | solution.py:239
  95.1 7.5 %shard_map.102 = f32[16,96,1024]{2,1,0:T(8,128)} custom-call(f32[16,96,1024]{2,1,0:T(8,128)} %pop_ref.5, f32[16,96,32]{2,1,0:T(8,128)} %broadcast_multiply_fusion.r_ref, f32[96,1024]{1,0:T(8,128)} %copy.50.s2t_ref, bf16[32,1024]{1,0:T(8,128)(2,1)} %constant.233.clone.e2_ref), custom_call_target="tpu_custom_call" | custom-call | tf_op jit(solution)/shard_map/pallas_call | solution.py:90
  (102 shorter events, 10.7 us)
Async XLA Ops:
  8.2 6.1 %copy-start.1 = (f32[8,1536]{1,0:T(8,128)S(1)}, f32[8,1536]{1,0:T(8,128)}, u32[]{:S(2)}) copy-start(f32[8,1536]{1,0:T(8,128)} %param.19) | copy-start | bytes 147460
  8.2 22.7 %copy-start.4 = (s32[2]{0:T(128)S(1)}, s32[2]{0:T(128)}, u32[]{:S(2)}) copy-start(s32[2]{0:T(128)} %constant.230.clone.1) | copy-start | bytes 28
  13.3 25.2 %copy-start = (f32[16,96,1]{2,1,0:T(8,128)S(1)}, f32[16,96,1]{2,1,0:T(8,128)}, u32[]{:S(2)}) copy-start(f32[16,96,1]{2,1,0:T(8,128)} %get-tuple-element.117.s1_ref) | copy-start | bytes 18436
  13.3 33.1 %copy-start.3 = (s32[1024]{0:T(1024)S(1)}, s32[1024]{0:T(1024)}, u32[]{:S(2)}) copy-start(s32[1024]{0:T(1024)} %param.21) | copy-start | bytes 12292
  13.3 34.3 %copy-start.2 = (f32[96,32]{0,1:T(8,128)S(1)}, f32[96,32]{0,1:T(8,128)}, u32[]{:S(2)}) copy-start(f32[96,32]{0,1:T(8,128)} %param.18) | copy-start | bytes 36868
  14.3 4.8 %collective-permute-start = (f32[11,1536]{1,0:T(8,128)S(1)}, f32[11,1536]{1,0:T(8,128)S(1)}, u32[]{:S(2)}, u32[]{:S(2)}) collective-permute-start(f32[11,1536]{1,0:T(8,128)S(1)} %pad_maximum_fusion.1), channel_id=1, source_target_pairs={{0,8},{1,9},{2,10},{3,11},{4,12},{5,13},{6,14},{7,15},{8,0},{9,1},... | collective-permute-start | bytes 202760 | tf_op jit(solution)/shard_map/ppermute | solution.py:108
  19.2 7.1 %collective-permute-start.1 = (f32[19,1536]{1,0:T(8,128)S(1)}, f32[19,1536]{1,0:T(8,128)S(1)}, u32[]{:S(2)}, u32[]{:S(2)}) collective-permute-start(f32[19,1536]{1,0:T(8,128)S(1)} %pad_maximum_fusion), channel_id=1, source_target_pairs={{0,24},{1,25},{2,26},{3,27},{4,28},{5,29},{6,30},{7,31},{8,16},{9,... | collective-permute-start | bytes 350216 | tf_op jit(solution)/shard_map/ppermute | solution.py:108
  26.4 3.9 %collective-permute-start.2 = (f32[3,1536]{1,0:T(4,128)S(1)}, f32[3,1536]{1,0:T(4,128)S(1)}, u32[]{:S(2)}, u32[]{:S(2)}) collective-permute-start(f32[3,1536]{1,0:T(4,128)S(1)} %pad_maximum_fusion.2), channel_id=1, source_target_pairs={{0,32},{1,33},{2,34},{3,35},{4,36},{5,37},{6,38},{7,39},{8,40},{9,... | collective-permute-start | bytes 55304 | tf_op jit(solution)/shard_map/ppermute | solution.py:108
  30.3 5.1 %collective-permute-start.3 = (f32[3,1536]{1,0:T(4,128)S(1)}, f32[3,1536]{1,0:T(4,128)S(1)}, u32[]{:S(2)}, u32[]{:S(2)}) collective-permute-start(f32[3,1536]{1,0:T(4,128)S(1)} %pad_maximum_fusion.3), channel_id=1, source_target_pairs={{0,96},{1,97},{2,98},{3,99},{4,100},{5,101},{6,102},{7,103},{8,104... | collective-permute-start | bytes 55304 | tf_op jit(solution)/shard_map/ppermute | solution.py:108
  35.5 1.3 %collective-permute-start.4 = (f32[4,1536]{1,0:T(4,128)S(1)}, f32[4,1536]{1,0:T(4,128)S(1)}, u32[]{:S(2)}, u32[]{:S(2)}) collective-permute-start(f32[4,1536]{1,0:T(4,128)S(1)} %pad_maximum_fusion.4), channel_id=1, source_target_pairs={{0,1},{1,0},{2,3},{3,2},{4,5},{5,4},{6,7},{7,6},{8,9},{9,8},{10,11... | collective-permute-start | bytes 73736 | tf_op jit(solution)/shard_map/ppermute | solution.py:108
  36.8 3.9 %collective-permute-start.5 = (f32[4,1536]{1,0:T(4,128)S(1)}, f32[4,1536]{1,0:T(4,128)S(1)}, u32[]{:S(2)}, u32[]{:S(2)}) collective-permute-start(f32[4,1536]{1,0:T(4,128)S(1)} %fusion.40), channel_id=1, source_target_pairs={{0,2},{1,3},{2,0},{3,1},{4,6},{5,7},{6,4},{7,5},{8,10},{9,11},{10,... | collective-permute-start | bytes 73736 | tf_op jit(solution)/shard_map/ppermute | solution.py:108
  40.7 5.1 %collective-permute-start.6 = (f32[4,1536]{1,0:T(4,128)S(1)}, f32[4,1536]{1,0:T(4,128)S(1)}, u32[]{:S(2)}, u32[]{:S(2)}) collective-permute-start(f32[4,1536]{1,0:T(4,128)S(1)} %add.315), channel_id=1, source_target_pairs={{0,6},{1,7},{2,4},{3,5},{4,2},{5,3},{6,0},{7,1},{8,14},{9,15},{10,... | collective-permute-start | bytes 73736 | tf_op jit(solution)/shard_map/ppermute | solution.py:108
  43.9 24.8 %collective-permute-start.7 = (f32[32,1536]{1,0:T(8,128)S(1)}, f32[32,1536]{1,0:T(8,128)S(1)}, u32[]{:S(2)}, u32[]{:S(2)}) collective-permute-start(f32[32,1536]{1,0:T(8,128)S(1)} %maximum_select_fusion.2), channel_id=1, source_target_pairs={{0,32},{1,33},{2,34},{3,35},{4,36},{5,37},{6,38},{7,39},{8,40},{9,... | collective-permute-start | bytes 589832 | tf_op jit(solution)/shard_map/ppermute | solution.py:108
  58.2 9.2 %collective-permute-start.9 = (f32[2,1536]{1,0:T(2,128)S(1)}, f32[2,1536]{1,0:T(2,128)S(1)}, u32[]{:S(2)}, u32[]{:S(2)}) collective-permute-start(f32[2,1536]{1,0:T(2,128)S(1)} %pad_maximum_fusion.5), channel_id=1, source_target_pairs={{0,1},{1,2},{2,3},{3,4},{4,5},{5,6},{6,7},{7,8},{8,9},{9,10},{10,1... | collective-permute-start | bytes 36872 | tf_op jit(solution)/shard_map/ppermute | solution.py:232
  68.7 9.1 %collective-permute-start.8 = (f32[64,1536]{1,0:T(8,128)S(1)}, f32[64,1536]{1,0:T(8,128)S(1)}, u32[]{:S(2)}, u32[]{:S(2)}) collective-permute-start(f32[64,1536]{1,0:T(8,128)S(1)} %maximum_select_fusion.1), channel_id=1, source_target_pairs={{0,96},{1,97},{2,98},{3,99},{4,100},{5,101},{6,102},{7,103},{8,104... | collective-permute-start | bytes 1179656 | tf_op jit(solution)/shard_map/ppermute | solution.py:108
  68.8 3.3 %collective-permute-start.10 = (f32[2,1536]{1,0:T(2,128)S(1)}, f32[2,1536]{1,0:T(2,128)S(1)}, u32[]{:S(2)}, u32[]{:S(2)}) collective-permute-start(f32[2,1536]{1,0:T(2,128)S(1)} %pad_maximum_fusion.6), channel_id=1, source_target_pairs={{1,0},{2,1},{3,2},{4,3},{5,4},{6,5},{7,6},{8,7},{9,8},{10,9},{11,1... | collective-permute-start | bytes 36872 | tf_op jit(solution)/shard_map/ppermute | solution.py:233
  79.5 12.3 %all-to-all-start.1 = ((f32[8,6,1536]{2,1,0:T(8,128)}), f32[8,6,1536]{2,1,0:T(8,128)S(1)}, u32[]{:S(2)}, u32[]{:S(2)}) async-start(f32[8,6,1536]{2,1,0:T(8,128)} %broadcast_select_fusion.2), calls=%async_computation.1 | async-start | bytes 786432 | tf_op jit(solution)/shard_map/all_to_all | solution.py:203

commit v16 on v14

--- a/solution.py
+++ b/solution.py
@@ -14,7 +14,7 @@
 MEMBERS = 8
 ROOMY = 6
 AXES = ("col", "mem")
-SHIP_APART = 32
+SHIP_APART = 64
 
 
 HI = lax.Precision.HIGHEST

time: 103 us -> 101 us (0.981)
  waiting for transfers between devices: 34.2 us -> 31.7 us
    ppermute x9 -> x8, waiting for transfers between devices: 19.6 us -> 17 us  [_xor(): return lax.ppermute(x, AXES, [(i, _partner(i, bit)) for i in range(n)])]
    ppermute x9 -> x8, starting transfers between devices: 12.5 us -> 12.9 us  [_xor(): return lax.ppermute(x, AXES, [(i, _partner(i, bit)) for i in range(n)])]
  transfers between devices with their start and end apart: 12 -> 11, of which waited for: 10 -> 9; matrix products, arithmetic and copies ran while one was open for 10% -> 10% of each run, Pallas kernels for 6% -> 6%
where the time goes in v16:
time: 101 us; the launch traced here: 99.9 us
  waiting for transfers between devices  31.7 us (31%)
  starting transfers between devices  20.2 us (20%)
  Pallas kernels  18.9 us (19%)
  other arithmetic  12.1 us (12%)
  local copies, waits for them, and re-layouts  11.5 us (11%)
  between operations  5.52 us (5%)
    ppermute x8, waiting for transfers between devices, _xor(): return lax.ppermute(x, AXES, [(i, _partner(i, bit)) for i in range(n)])  17 us
    pallas_call x2, Pallas kernels, _table_call(): pl.pallas_call(kernel, grid=grid, in_specs=specs, out_specs=pl.BlockSpec(...  13.8 us
    ppermute x8, starting transfers between devices, _xor(): return lax.ppermute(x, AXES, [(i, _partner(i, bit)) for i in range(n)])  12.9 us
    all_to_all x1, waiting for transfers between devices, exchange(): return lax.all_to_all(sent, 'mem', 0, 0, tiled=True)  7.36 us
    ppermute x1, waiting for transfers between devices, body(): from_left = lax.ppermute(to_right, AXES, right)  7.29 us
    pallas_call x1, Pallas kernels, body(): pl.pallas_call(_scale_kernel, grid=(count // BLOCK,), in_specs=[pl.BlockS...  5.07 us
    all_to_all x1, starting transfers between devices, exchange(): return lax.all_to_all(sent, 'mem', 0, 0, tiled=True)  3.47 us
  transfers between devices with their start and end apart: 11, of which 9 were waited for; matrix products, arithmetic and copies ran while one was open for 10% of the time, Pallas kernels for 6%

profile of v16, /device:TPU:6, one launch (start us, length us, event | category | flops | bytes accessed | tf_op | source)
XLA Modules:
  0.0 99.9 jit_solution(3788621866559338982)
XLA Ops:
  0.0 1.3 %fusion.42 = (s32[1]{0:T(128)}, s32[1]{0:T(128)}) fusion(s32[16]{0:T(128)} %param.19), kind=kLoop, calls=%fused_computation.150 | loop fusion | bytes 16 | tf_op jit(solution)/shard_map/slice | solution.py:130
  1.9 0.9 select_reduce_fusion.2
  2.8 1.9 %compare_and_fusion.3 = (pred[16]{0:T(512)(128)(4,1)S(1)}, s32[16]{0:T(128)S(1)}, pred[16]{0:T(512)(128)(4,1)S(1)}) fusion(s32[16]{0:T(128)} %param.19, s32[]{:T(128)} %bitcast.1, s32[]{:T(128)} %bitcast.2), kind=kLoop, calls=%fused_computation.119 | loop fusion | flops 144 | bytes 168 | tf_op jit(solution)/shard_map/jit(_take)/and | solution.py:226
  6.2 1.9 %copy.43.at_ref = f32[16,96,1]{2,1,0:T(8,128)} copy(f32[16,96,1]{1,0,2:T(8,128)} %bitcast.43) | data formatting | bytes 12288 | tf_op jit(solution)/shard_map/broadcast_in_dim | solution.py:157
  8.0 5.1 %shard_map.91 = (f32[16,96,1]{2,1,0:T(8,128)}, f32[96,32]{1,0:T(8,128)}) custom-call(f32[16,96,1024]{2,1,0:T(8,128)} %pop_ref.5, f32[16,96,1]{2,1,0:T(8,128)} %copy.43.at_ref, bf16[128,32]{1,0:T(8,128)(2,1)} %constant.230.clone.g1_ref), custom_call_target="tpu_custom_call" | custom-call | tf_op jit(solution)/shard_map/pallas_call | solution.py:147
  13.1 1.0 reshape.653
  14.1 2.0 %collective-permute-start = (f32[11,1536]{1,0:T(8,128)S(1)}, f32[11,1536]{1,0:T(8,128)S(1)}, u32[]{:S(2)}, u32[]{:S(2)}) collective-permute-start(f32[11,1536]{1,0:T(8,128)S(1)} %pad_maximum_fusion.2), channel_id=1, source_target_pairs={{0,8},{1,9},{2,10},{3,11},{4,12},{5,13},{6,14},{7,15},{8,0},{9,1},... | collective-permute-start | bytes 202760 | tf_op jit(solution)/shard_map/ppermute | solution.py:107
  19.0 4.0 %collective-permute-start.1 = (f32[19,1536]{1,0:T(8,128)S(1)}, f32[19,1536]{1,0:T(8,128)S(1)}, u32[]{:S(2)}, u32[]{:S(2)}) collective-permute-start(f32[19,1536]{1,0:T(8,128)S(1)} %pad_maximum_fusion.1), channel_id=1, source_target_pairs={{0,24},{1,25},{2,26},{3,27},{4,28},{5,29},{6,30},{7,31},{8,16},{9,... | collective-permute-start | bytes 350216 | tf_op jit(solution)/shard_map/ppermute | solution.py:107
  23.1 3.1 %collective-permute-done.1 = f32[19,1536]{1,0:T(8,128)S(1)} collective-permute-done((f32[19,1536]{1,0:T(8,128)S(1)}, f32[19,1536]{1,0:T(8,128)S(1)}, u32[]{:S(2)}, u32[]{:S(2)}) %collective-permute-start.1) | collective-permute-done | bytes 116768 | tf_op jit(solution)/shard_map/ppermute | solution.py:107
  26.3 0.9 collective-permute-start.2
  27.2 5.4 %collective-permute-done.2 = f32[35,1536]{1,0:T(8,128)S(1)} collective-permute-done((f32[35,1536]{1,0:T(8,128)S(1)}, f32[35,1536]{1,0:T(8,128)S(1)}, u32[]{:S(2)}, u32[]{:S(2)}) %collective-permute-start.2) | collective-permute-done | bytes 215072 | tf_op jit(solution)/shard_map/ppermute | solution.py:107
  33.2 0.7 and_reduce_fusion
  33.9 3.8 %collective-permute-done.3 = f32[3,1536]{1,0:T(4,128)S(1)} collective-permute-done((f32[3,1536]{1,0:T(4,128)S(1)}, f32[3,1536]{1,0:T(4,128)S(1)}, u32[]{:S(2)}, u32[]{:S(2)}) %collective-permute-start.3) | collective-permute-done | bytes 18464 | tf_op jit(solution)/shard_map/ppermute | solution.py:107
  37.9 1.2 %collective-permute-done.4 = f32[4,1536]{1,0:T(4,128)S(1)} collective-permute-done((f32[4,1536]{1,0:T(4,128)S(1)}, f32[4,1536]{1,0:T(4,128)S(1)}, u32[]{:S(2)}, u32[]{:S(2)}) %collective-permute-start.4) | collective-permute-done | bytes 24608 | tf_op jit(solution)/shard_map/ppermute | solution.py:107
  39.1 1.7 %collective-permute-start.5 = (f32[4,1536]{1,0:T(4,128)S(1)}, f32[4,1536]{1,0:T(4,128)S(1)}, u32[]{:S(2)}, u32[]{:S(2)}) collective-permute-start(f32[4,1536]{1,0:T(4,128)S(1)} %fusion.40), channel_id=1, source_target_pairs={{0,2},{1,3},{2,0},{3,1},{4,6},{5,7},{6,4},{7,5},{8,10},{9,11},{10,... | collective-permute-start | bytes 73736 | tf_op jit(solution)/shard_map/ppermute | solution.py:107
  41.2 1.9 %collective-permute-done.5 = f32[4,1536]{1,0:T(4,128)S(1)} collective-permute-done((f32[4,1536]{1,0:T(4,128)S(1)}, f32[4,1536]{1,0:T(4,128)S(1)}, u32[]{:S(2)}, u32[]{:S(2)}) %collective-permute-start.5) | collective-permute-done | bytes 24608 | tf_op jit(solution)/shard_map/ppermute | solution.py:107
  43.1 3.1 %collective-permute-start.6 = (f32[4,1536]{1,0:T(4,128)S(1)}, f32[4,1536]{1,0:T(4,128)S(1)}, u32[]{:S(2)}, u32[]{:S(2)}) collective-permute-start(f32[4,1536]{1,0:T(4,128)S(1)} %add.315), channel_id=1, source_target_pairs={{0,6},{1,7},{2,4},{3,5},{4,2},{5,3},{6,0},{7,1},{8,14},{9,15},{10,... | collective-permute-start | bytes 73736 | tf_op jit(solution)/shard_map/ppermute | solution.py:107
  46.7 1.4 %collective-permute-done.6 = f32[4,1536]{1,0:T(4,128)S(1)} collective-permute-done((f32[4,1536]{1,0:T(4,128)S(1)}, f32[4,1536]{1,0:T(4,128)S(1)}, u32[]{:S(2)}, u32[]{:S(2)}) %collective-permute-start.6) | collective-permute-done | bytes 24608 | tf_op jit(solution)/shard_map/ppermute | solution.py:107
  50.0 0.9 copy.49.s2t_ref
  51.0 6.3 %shard_map.92 = f32[16,96,32]{2,1,0:T(8,128)} custom-call(f32[16,96,1024]{2,1,0:T(8,128)} %pop_ref.5, f32[96,1024]{1,0:T(8,128)} %copy.49.s2t_ref, bf16[1024,32]{1,0:T(8,128)(2,1)} %constant.232.clone.e2t_ref), custom_call_target="tpu_custom_call" | custom-call | tf_op jit(solution)/shard_map/pallas_call | solution.py:89
  57.2 1.4 %broadcast_multiply_fusion.1 = f32[16,96,32]{2,1,0:T(8,128)S(1)} fusion(f32[16,96,32]{2,1,0:T(8,128)} %shard_map.92, f32[16,96]{1,0:T(8,128)S(1)} %reduce.12), kind=kLoop, calls=%fused_computation.33 | loop fusion | flops 49152 | bytes 399360 | tf_op jit(solution)/shard_map/mul | solution.py:211
  58.6 1.0 reduce_sum.80
  60.0 1.9 %collective-permute-start.8 = (f32[2,1536]{1,0:T(2,128)S(1)}, f32[2,1536]{1,0:T(2,128)S(1)}, u32[]{:S(2)}, u32[]{:S(2)}) collective-permute-start(f32[2,1536]{1,0:T(2,128)S(1)} %pad_maximum_fusion.5), channel_id=1, source_target_pairs={{0,1},{1,2},{2,3},{3,4},{4,5},{5,6},{6,7},{7,8},{8,9},{9,10},{10,1... | collective-permute-start | bytes 36872 | tf_op jit(solution)/shard_map/ppermute | solution.py:221
  62.0 7.3 %collective-permute-done.8 = f32[2,1536]{1,0:T(2,128)S(1)} collective-permute-done((f32[2,1536]{1,0:T(2,128)S(1)}, f32[2,1536]{1,0:T(2,128)S(1)}, u32[]{:S(2)}, u32[]{:S(2)}) %collective-permute-start.8) | collective-permute-done | bytes 12320 | tf_op jit(solution)/shard_map/ppermute | solution.py:221
  70.5 1.9 %collective-permute-start.9 = (f32[2,1536]{1,0:T(2,128)S(1)}, f32[2,1536]{1,0:T(2,128)S(1)}, u32[]{:S(2)}, u32[]{:S(2)}) collective-permute-start(f32[2,1536]{1,0:T(2,128)S(1)} %pad_maximum_fusion.6), channel_id=1, source_target_pairs={{1,0},{2,1},{3,2},{4,3},{5,4},{6,5},{7,6},{8,7},{9,8},{10,9},{11,1... | collective-permute-start | bytes 36872 | tf_op jit(solution)/shard_map/ppermute | solution.py:222
  75.1 0.7 gather_fusion.1
  75.8 0.8 broadcast_select_fusion.2
  76.8 3.5 %all-to-all-start.1 = ((f32[8,6,1536]{2,1,0:T(8,128)}), f32[8,6,1536]{2,1,0:T(8,128)S(1)}, u32[]{:S(2)}, u32[]{:S(2)}) async-start(f32[8,6,1536]{2,1,0:T(8,128)} %broadcast_select_fusion.2), calls=%async_computation.1 | async-start | bytes 786432 | tf_op jit(solution)/shard_map/all_to_all | solution.py:202
  80.3 0.7 broadcast_select_fusion.4
  81.7 7.4 %all-to-all-done.1 = f32[8,6,1536]{2,1,0:T(8,128)S(1)} async-done(((f32[8,6,1536]{2,1,0:T(8,128)}), f32[8,6,1536]{2,1,0:T(8,128)S(1)}, u32[]{:S(2)}, u32[]{:S(2)}) %all-to-all-start.1) | async-done | bytes 294944 | tf_op jit(solution)/shard_map/all_to_all | solution.py:202
  91.3 1.1 %broadcast_multiply_fusion.r_ref = f32[16,96,32]{2,1,0:T(8,128)} fusion(f32[16,96,32]{2,1,0:T(8,128)S(1)} %bitcast.41, f32[16,96]{1,0:T(8,128)S(1)} %reduce.12), kind=kLoop, calls=%fused_computation.32 | loop fusion | flops 49152 | bytes 399360 | tf_op jit(solution)/shard_map/mul | solution.py:228
  92.4 7.5 %shard_map.93 = f32[16,96,1024]{2,1,0:T(8,128)} custom-call(f32[16,96,1024]{2,1,0:T(8,128)} %pop_ref.5, f32[16,96,32]{2,1,0:T(8,128)} %broadcast_multiply_fusion.r_ref, f32[96,1024]{1,0:T(8,128)} %copy.49.s2t_ref, bf16[32,1024]{1,0:T(8,128)(2,1)} %constant.231.clone.e2_ref), custom_call_target="tpu_custom_call" | custom-call | tf_op jit(solution)/shard_map/pallas_call | solution.py:89
  (103 shorter events, 10.9 us)
Async XLA Ops:
  8.0 6.0 %copy-start.1 = (f32[8,1536]{1,0:T(8,128)S(1)}, f32[8,1536]{1,0:T(8,128)}, u32[]{:S(2)}) copy-start(f32[8,1536]{1,0:T(8,128)} %param.18) | copy-start | bytes 147460
  13.1 20.1 %copy-start.4 = (s32[2]{0:T(128)S(1)}, s32[2]{0:T(128)}, u32[]{:S(2)}) copy-start(s32[2]{0:T(128)} %constant.228.clone.1) | copy-start | bytes 28
  13.1 27.7 %copy-start = (f32[16,96,1]{2,1,0:T(8,128)S(1)}, f32[16,96,1]{2,1,0:T(8,128)}, u32[]{:S(2)}) copy-start(f32[16,96,1]{2,1,0:T(8,128)} %get-tuple-element.117) | copy-start | bytes 18436
  14.1 4.8 %collective-permute-start = (f32[11,1536]{1,0:T(8,128)S(1)}, f32[11,1536]{1,0:T(8,128)S(1)}, u32[]{:S(2)}, u32[]{:S(2)}) collective-permute-start(f32[11,1536]{1,0:T(8,128)S(1)} %pad_maximum_fusion.2), channel_id=1, source_target_pairs={{0,8},{1,9},{2,10},{3,11},{4,12},{5,13},{6,14},{7,15},{8,0},{9,1},... | collective-permute-start | bytes 202760 | tf_op jit(solution)/shard_map/ppermute | solution.py:107
  19.0 7.1 %collective-permute-start.1 = (f32[19,1536]{1,0:T(8,128)S(1)}, f32[19,1536]{1,0:T(8,128)S(1)}, u32[]{:S(2)}, u32[]{:S(2)}) collective-permute-start(f32[19,1536]{1,0:T(8,128)S(1)} %pad_maximum_fusion.1), channel_id=1, source_target_pairs={{0,24},{1,25},{2,26},{3,27},{4,28},{5,29},{6,30},{7,31},{8,16},{9,... | collective-permute-start | bytes 350216 | tf_op jit(solution)/shard_map/ppermute | solution.py:107
  26.2 22.4 %copy-start.3 = (s32[1024]{0:T(1024)S(1)}, s32[1024]{0:T(1024)}, u32[]{:S(2)}) copy-start(s32[1024]{0:T(1024)} %param.20) | copy-start | bytes 12292
  26.3 23.7 %copy-start.2 = (f32[96,32]{0,1:T(8,128)S(1)}, f32[96,32]{0,1:T(8,128)}, u32[]{:S(2)}) copy-start(f32[96,32]{0,1:T(8,128)} %param.17) | copy-start | bytes 36868
  26.3 6.3 %collective-permute-start.2 = (f32[35,1536]{1,0:T(8,128)S(1)}, f32[35,1536]{1,0:T(8,128)S(1)}, u32[]{:S(2)}, u32[]{:S(2)}) collective-permute-start(f32[35,1536]{1,0:T(8,128)S(1)} %pad_maximum_fusion), channel_id=1, source_target_pairs={{0,32},{1,33},{2,34},{3,35},{4,36},{5,37},{6,38},{7,39},{8,40},{9,... | collective-permute-start | bytes 645128 | tf_op jit(solution)/shard_map/ppermute | solution.py:107
  32.7 5.1 %collective-permute-start.3 = (f32[3,1536]{1,0:T(4,128)S(1)}, f32[3,1536]{1,0:T(4,128)S(1)}, u32[]{:S(2)}, u32[]{:S(2)}) collective-permute-start(f32[3,1536]{1,0:T(4,128)S(1)} %pad_maximum_fusion.3), channel_id=1, source_target_pairs={{0,96},{1,97},{2,98},{3,99},{4,100},{5,101},{6,102},{7,103},{8,104... | collective-permute-start | bytes 55304 | tf_op jit(solution)/shard_map/ppermute | solution.py:107
  37.8 1.3 %collective-permute-start.4 = (f32[4,1536]{1,0:T(4,128)S(1)}, f32[4,1536]{1,0:T(4,128)S(1)}, u32[]{:S(2)}, u32[]{:S(2)}) collective-permute-start(f32[4,1536]{1,0:T(4,128)S(1)} %pad_maximum_fusion.4), channel_id=1, source_target_pairs={{0,1},{1,0},{2,3},{3,2},{4,5},{5,4},{6,7},{7,6},{8,9},{9,8},{10,11... | collective-permute-start | bytes 73736 | tf_op jit(solution)/shard_map/ppermute | solution.py:107
  39.1 3.9 %collective-permute-start.5 = (f32[4,1536]{1,0:T(4,128)S(1)}, f32[4,1536]{1,0:T(4,128)S(1)}, u32[]{:S(2)}, u32[]{:S(2)}) collective-permute-start(f32[4,1536]{1,0:T(4,128)S(1)} %fusion.40), channel_id=1, source_target_pairs={{0,2},{1,3},{2,0},{3,1},{4,6},{5,7},{6,4},{7,5},{8,10},{9,11},{10,... | collective-permute-start | bytes 73736 | tf_op jit(solution)/shard_map/ppermute | solution.py:107
  43.1 5.1 %collective-permute-start.6 = (f32[4,1536]{1,0:T(4,128)S(1)}, f32[4,1536]{1,0:T(4,128)S(1)}, u32[]{:S(2)}, u32[]{:S(2)}) collective-permute-start(f32[4,1536]{1,0:T(4,128)S(1)} %add.315), channel_id=1, source_target_pairs={{0,6},{1,7},{2,4},{3,5},{4,2},{5,3},{6,0},{7,1},{8,14},{9,15},{10,... | collective-permute-start | bytes 73736 | tf_op jit(solution)/shard_map/ppermute | solution.py:107
  46.2 28.8 %collective-permute-start.7 = (f32[64,1536]{1,0:T(8,128)S(1)}, f32[64,1536]{1,0:T(8,128)S(1)}, u32[]{:S(2)}, u32[]{:S(2)}) collective-permute-start(f32[64,1536]{1,0:T(8,128)S(1)} %maximum_select_fusion.1), channel_id=1, source_target_pairs={{0,96},{1,97},{2,98},{3,99},{4,100},{5,101},{6,102},{7,103},{8,104... | collective-permute-start | bytes 1179656 | tf_op jit(solution)/shard_map/ppermute | solution.py:107
  60.0 9.2 %collective-permute-start.8 = (f32[2,1536]{1,0:T(2,128)S(1)}, f32[2,1536]{1,0:T(2,128)S(1)}, u32[]{:S(2)}, u32[]{:S(2)}) collective-permute-start(f32[2,1536]{1,0:T(2,128)S(1)} %pad_maximum_fusion.5), channel_id=1, source_target_pairs={{0,1},{1,2},{2,3},{3,4},{4,5},{5,6},{6,7},{7,8},{8,9},{9,10},{10,1... | collective-permute-start | bytes 36872 | tf_op jit(solution)/shard_map/ppermute | solution.py:221
  70.5 3.3 %collective-permute-start.9 = (f32[2,1536]{1,0:T(2,128)S(1)}, f32[2,1536]{1,0:T(2,128)S(1)}, u32[]{:S(2)}, u32[]{:S(2)}) collective-permute-start(f32[2,1536]{1,0:T(2,128)S(1)} %pad_maximum_fusion.6), channel_id=1, source_target_pairs={{1,0},{2,1},{3,2},{4,3},{5,4},{6,5},{7,6},{8,7},{9,8},{10,9},{11,1... | collective-permute-start | bytes 36872 | tf_op jit(solution)/shard_map/ppermute | solution.py:222
  76.8 12.3 %all-to-all-start.1 = ((f32[8,6,1536]{2,1,0:T(8,128)}), f32[8,6,1536]{2,1,0:T(8,128)S(1)}, u32[]{:S(2)}, u32[]{:S(2)}) async-start(f32[8,6,1536]{2,1,0:T(8,128)} %broadcast_select_fusion.2), calls=%async_computation.1 | async-start | bytes 786432 | tf_op jit(solution)/shard_map/all_to_all | solution.py:202

commit v17 on v16

--- a/solution.py
+++ b/solution.py
@@ -19,6 +19,7 @@
 
 HI = lax.Precision.HIGHEST
 BLOCK = 4
+SCALE_BLOCK = 8
 LANES = (((1,), (1,)), ((), ()))
 
 
@@ -146,11 +147,11 @@
         e2t = jnp.asarray(e2_np.T, bf)
         s1c, part = pl.pallas_call(
             _scale_kernel,
-            grid=(count // BLOCK,),
-            in_specs=[pl.BlockSpec((BLOCK, AGE * SEX, INC * HH * TU), lambda i: (i, 0, 0)),
-                      pl.BlockSpec((BLOCK, AGE * SEX, 1), lambda i: (i, 0, 0)),
+            grid=(count // SCALE_BLOCK,),
+            in_specs=[pl.BlockSpec((SCALE_BLOCK, AGE * SEX, INC * HH * TU), lambda i: (i, 0, 0)),
+                      pl.BlockSpec((SCALE_BLOCK, AGE * SEX, 1), lambda i: (i, 0, 0)),
                       pl.BlockSpec(g1.shape, lambda i: (0, 0))],
-            out_specs=[pl.BlockSpec((BLOCK, AGE * SEX, 1), lambda i: (i, 0, 0)),
+            out_specs=[pl.BlockSpec((SCALE_BLOCK, AGE * SEX, 1), lambda i: (i, 0, 0)),
                        pl.BlockSpec((AGE * SEX, HH * TU), lambda i: (0, 0))],
             out_shape=[jax.ShapeDtypeStruct((count, AGE * SEX, 1), f32),
                        jax.ShapeDtypeStruct((AGE * SEX, HH * TU), f32)],

time: 101 us -> 100 us (0.990)
  no operation moved by 1% of the time
where the time goes in v17:
time: 100 us; the launch traced here: 99.7 us
  waiting for transfers between devices  31.7 us (32%)
  starting transfers between devices  20.2 us (20%)
  Pallas kernels  18.6 us (19%)
  other arithmetic  12.1 us (12%)
  local copies, waits for them, and re-layouts  11.5 us (12%)
  between operations  5.52 us (6%)
    ppermute x8, waiting for transfers between devices, _xor(): return lax.ppermute(x, AXES, [(i, _partner(i, bit)) for i in range(n)])  17 us
    pallas_call x2, Pallas kernels, _table_call(): pl.pallas_call(kernel, grid=grid, in_specs=specs, out_specs=pl.BlockSpec(...  13.8 us
    ppermute x8, starting transfers between devices, _xor(): return lax.ppermute(x, AXES, [(i, _partner(i, bit)) for i in range(n)])  12.9 us
    all_to_all x1, waiting for transfers between devices, exchange(): return lax.all_to_all(sent, 'mem', 0, 0, tiled=True)  7.36 us
    ppermute x1, waiting for transfers between devices, body(): from_left = lax.ppermute(to_right, AXES, right)  7.29 us
    pallas_call x1, Pallas kernels, body(): pl.pallas_call(_scale_kernel, grid=(count // SCALE_BLOCK,), in_specs=[pl....  4.84 us
    all_to_all x1, starting transfers between devices, exchange(): return lax.all_to_all(sent, 'mem', 0, 0, tiled=True)  3.47 us
  transfers between devices with their start and end apart: 11, of which 9 were waited for; matrix products, arithmetic and copies ran while one was open for 10% of the time, Pallas kernels for 6%

profile of v17, /device:TPU:6, one launch (start us, length us, event | category | flops | bytes accessed | tf_op | source)
XLA Modules:
  0.0 99.7 jit_solution(2285986734963524816)
XLA Ops:
  0.0 1.3 %fusion.42 = (s32[1]{0:T(128)}, s32[1]{0:T(128)}) fusion(s32[16]{0:T(128)} %param.19), kind=kLoop, calls=%fused_computation.150 | loop fusion | bytes 16 | tf_op jit(solution)/shard_map/slice | solution.py:131
  1.9 0.9 select_reduce_fusion.2
  2.8 1.9 %compare_and_fusion.3 = (pred[16]{0:T(512)(128)(4,1)S(1)}, s32[16]{0:T(128)S(1)}, pred[16]{0:T(512)(128)(4,1)S(1)}) fusion(s32[16]{0:T(128)} %param.19, s32[]{:T(128)} %bitcast.1, s32[]{:T(128)} %bitcast.2), kind=kLoop, calls=%fused_computation.119 | loop fusion | flops 144 | bytes 168 | tf_op jit(solution)/shard_map/jit(_take)/and | solution.py:227
  6.2 1.9 %copy.43.at_ref = f32[16,96,1]{2,1,0:T(8,128)} copy(f32[16,96,1]{1,0,2:T(8,128)} %bitcast.43) | data formatting | bytes 12288 | tf_op jit(solution)/shard_map/broadcast_in_dim | solution.py:158
  8.0 4.8 %shard_map.91 = (f32[16,96,1]{2,1,0:T(8,128)}, f32[96,32]{1,0:T(8,128)}) custom-call(f32[16,96,1024]{2,1,0:T(8,128)} %pop_ref.5, f32[16,96,1]{2,1,0:T(8,128)} %copy.43.at_ref, bf16[128,32]{1,0:T(8,128)(2,1)} %constant.230.clone.g1_ref), custom_call_target="tpu_custom_call" | custom-call | tf_op jit(solution)/shard_map/pallas_call | solution.py:148
  12.9 1.0 reshape.653
  13.9 2.0 %collective-permute-start = (f32[11,1536]{1,0:T(8,128)S(1)}, f32[11,1536]{1,0:T(8,128)S(1)}, u32[]{:S(2)}, u32[]{:S(2)}) collective-permute-start(f32[11,1536]{1,0:T(8,128)S(1)} %pad_maximum_fusion.2), channel_id=1, source_target_pairs={{0,8},{1,9},{2,10},{3,11},{4,12},{5,13},{6,14},{7,15},{8,0},{9,1},... | collective-permute-start | bytes 202760 | tf_op jit(solution)/shard_map/ppermute | solution.py:108
  18.8 4.0 %collective-permute-start.1 = (f32[19,1536]{1,0:T(8,128)S(1)}, f32[19,1536]{1,0:T(8,128)S(1)}, u32[]{:S(2)}, u32[]{:S(2)}) collective-permute-start(f32[19,1536]{1,0:T(8,128)S(1)} %pad_maximum_fusion.1), channel_id=1, source_target_pairs={{0,24},{1,25},{2,26},{3,27},{4,28},{5,29},{6,30},{7,31},{8,16},{9,... | collective-permute-start | bytes 350216 | tf_op jit(solution)/shard_map/ppermute | solution.py:108
  22.8 3.1 %collective-permute-done.1 = f32[19,1536]{1,0:T(8,128)S(1)} collective-permute-done((f32[19,1536]{1,0:T(8,128)S(1)}, f32[19,1536]{1,0:T(8,128)S(1)}, u32[]{:S(2)}, u32[]{:S(2)}) %collective-permute-start.1) | collective-permute-done | bytes 116768 | tf_op jit(solution)/shard_map/ppermute | solution.py:108
  26.1 0.9 collective-permute-start.2
  27.0 5.4 %collective-permute-done.2 = f32[35,1536]{1,0:T(8,128)S(1)} collective-permute-done((f32[35,1536]{1,0:T(8,128)S(1)}, f32[35,1536]{1,0:T(8,128)S(1)}, u32[]{:S(2)}, u32[]{:S(2)}) %collective-permute-start.2) | collective-permute-done | bytes 215072 | tf_op jit(solution)/shard_map/ppermute | solution.py:108
  33.0 0.7 and_reduce_fusion
  33.7 3.8 %collective-permute-done.3 = f32[3,1536]{1,0:T(4,128)S(1)} collective-permute-done((f32[3,1536]{1,0:T(4,128)S(1)}, f32[3,1536]{1,0:T(4,128)S(1)}, u32[]{:S(2)}, u32[]{:S(2)}) %collective-permute-start.3) | collective-permute-done | bytes 18464 | tf_op jit(solution)/shard_map/ppermute | solution.py:108
  37.7 1.2 %collective-permute-done.4 = f32[4,1536]{1,0:T(4,128)S(1)} collective-permute-done((f32[4,1536]{1,0:T(4,128)S(1)}, f32[4,1536]{1,0:T(4,128)S(1)}, u32[]{:S(2)}, u32[]{:S(2)}) %collective-permute-start.4) | collective-permute-done | bytes 24608 | tf_op jit(solution)/shard_map/ppermute | solution.py:108
  38.9 1.7 %collective-permute-start.5 = (f32[4,1536]{1,0:T(4,128)S(1)}, f32[4,1536]{1,0:T(4,128)S(1)}, u32[]{:S(2)}, u32[]{:S(2)}) collective-permute-start(f32[4,1536]{1,0:T(4,128)S(1)} %fusion.40), channel_id=1, source_target_pairs={{0,2},{1,3},{2,0},{3,1},{4,6},{5,7},{6,4},{7,5},{8,10},{9,11},{10,... | collective-permute-start | bytes 73736 | tf_op jit(solution)/shard_map/ppermute | solution.py:108
  40.9 1.9 %collective-permute-done.5 = f32[4,1536]{1,0:T(4,128)S(1)} collective-permute-done((f32[4,1536]{1,0:T(4,128)S(1)}, f32[4,1536]{1,0:T(4,128)S(1)}, u32[]{:S(2)}, u32[]{:S(2)}) %collective-permute-start.5) | collective-permute-done | bytes 24608 | tf_op jit(solution)/shard_map/ppermute | solution.py:108
  42.8 3.1 %collective-permute-start.6 = (f32[4,1536]{1,0:T(4,128)S(1)}, f32[4,1536]{1,0:T(4,128)S(1)}, u32[]{:S(2)}, u32[]{:S(2)}) collective-permute-start(f32[4,1536]{1,0:T(4,128)S(1)} %add.315), channel_id=1, source_target_pairs={{0,6},{1,7},{2,4},{3,5},{4,2},{5,3},{6,0},{7,1},{8,14},{9,15},{10,... | collective-permute-start | bytes 73736 | tf_op jit(solution)/shard_map/ppermute | solution.py:108
  46.5 1.4 %collective-permute-done.6 = f32[4,1536]{1,0:T(4,128)S(1)} collective-permute-done((f32[4,1536]{1,0:T(4,128)S(1)}, f32[4,1536]{1,0:T(4,128)S(1)}, u32[]{:S(2)}, u32[]{:S(2)}) %collective-permute-start.6) | collective-permute-done | bytes 24608 | tf_op jit(solution)/shard_map/ppermute | solution.py:108
  49.8 0.9 copy.49.s2t_ref
  50.7 6.3 %shard_map.92 = f32[16,96,32]{2,1,0:T(8,128)} custom-call(f32[16,96,1024]{2,1,0:T(8,128)} %pop_ref.5, f32[96,1024]{1,0:T(8,128)} %copy.49.s2t_ref, bf16[1024,32]{1,0:T(8,128)(2,1)} %constant.232.clone.e2t_ref), custom_call_target="tpu_custom_call" | custom-call | tf_op jit(solution)/shard_map/pallas_call | solution.py:90
  57.0 1.4 %broadcast_multiply_fusion.1 = f32[16,96,32]{2,1,0:T(8,128)S(1)} fusion(f32[16,96,32]{2,1,0:T(8,128)} %shard_map.92, f32[16,96]{1,0:T(8,128)S(1)} %reduce.12), kind=kLoop, calls=%fused_computation.33 | loop fusion | flops 49152 | bytes 399360 | tf_op jit(solution)/shard_map/mul | solution.py:212
  58.4 1.0 reduce_sum.80
  59.8 1.9 %collective-permute-start.8 = (f32[2,1536]{1,0:T(2,128)S(1)}, f32[2,1536]{1,0:T(2,128)S(1)}, u32[]{:S(2)}, u32[]{:S(2)}) collective-permute-start(f32[2,1536]{1,0:T(2,128)S(1)} %pad_maximum_fusion.5), channel_id=1, source_target_pairs={{0,1},{1,2},{2,3},{3,4},{4,5},{5,6},{6,7},{7,8},{8,9},{9,10},{10,1... | collective-permute-start | bytes 36872 | tf_op jit(solution)/shard_map/ppermute | solution.py:222
  61.7 7.3 %collective-permute-done.8 = f32[2,1536]{1,0:T(2,128)S(1)} collective-permute-done((f32[2,1536]{1,0:T(2,128)S(1)}, f32[2,1536]{1,0:T(2,128)S(1)}, u32[]{:S(2)}, u32[]{:S(2)}) %collective-permute-start.8) | collective-permute-done | bytes 12320 | tf_op jit(solution)/shard_map/ppermute | solution.py:222
  70.2 1.9 %collective-permute-start.9 = (f32[2,1536]{1,0:T(2,128)S(1)}, f32[2,1536]{1,0:T(2,128)S(1)}, u32[]{:S(2)}, u32[]{:S(2)}) collective-permute-start(f32[2,1536]{1,0:T(2,128)S(1)} %pad_maximum_fusion.6), channel_id=1, source_target_pairs={{1,0},{2,1},{3,2},{4,3},{5,4},{6,5},{7,6},{8,7},{9,8},{10,9},{11,1... | collective-permute-start | bytes 36872 | tf_op jit(solution)/shard_map/ppermute | solution.py:223
  74.8 0.7 gather_fusion.1
  75.6 0.8 broadcast_select_fusion.2
  76.5 3.5 %all-to-all-start.1 = ((f32[8,6,1536]{2,1,0:T(8,128)}), f32[8,6,1536]{2,1,0:T(8,128)S(1)}, u32[]{:S(2)}, u32[]{:S(2)}) async-start(f32[8,6,1536]{2,1,0:T(8,128)} %broadcast_select_fusion.2), calls=%async_computation.1 | async-start | bytes 786432 | tf_op jit(solution)/shard_map/all_to_all | solution.py:203
  80.0 0.7 broadcast_select_fusion.4
  81.5 7.4 %all-to-all-done.1 = f32[8,6,1536]{2,1,0:T(8,128)S(1)} async-done(((f32[8,6,1536]{2,1,0:T(8,128)}), f32[8,6,1536]{2,1,0:T(8,128)S(1)}, u32[]{:S(2)}, u32[]{:S(2)}) %all-to-all-start.1) | async-done | bytes 294944 | tf_op jit(solution)/shard_map/all_to_all | solution.py:203
  91.0 1.1 %broadcast_multiply_fusion.r_ref = f32[16,96,32]{2,1,0:T(8,128)} fusion(f32[16,96,32]{2,1,0:T(8,128)S(1)} %bitcast.41, f32[16,96]{1,0:T(8,128)S(1)} %reduce.12), kind=kLoop, calls=%fused_computation.32 | loop fusion | flops 49152 | bytes 399360 | tf_op jit(solution)/shard_map/mul | solution.py:229
  92.2 7.5 %shard_map.93 = f32[16,96,1024]{2,1,0:T(8,128)} custom-call(f32[16,96,1024]{2,1,0:T(8,128)} %pop_ref.5, f32[16,96,32]{2,1,0:T(8,128)} %broadcast_multiply_fusion.r_ref, f32[96,1024]{1,0:T(8,128)} %copy.49.s2t_ref, bf16[32,1024]{1,0:T(8,128)(2,1)} %constant.231.clone.e2_ref), custom_call_target="tpu_custom_call" | custom-call | tf_op jit(solution)/shard_map/pallas_call | solution.py:90
  (103 shorter events, 10.9 us)
Async XLA Ops:
  8.0 5.8 %copy-start.1 = (f32[8,1536]{1,0:T(8,128)S(1)}, f32[8,1536]{1,0:T(8,128)}, u32[]{:S(2)}) copy-start(f32[8,1536]{1,0:T(8,128)} %param.18) | copy-start | bytes 147460
  12.9 20.1 %copy-start.4 = (s32[2]{0:T(128)S(1)}, s32[2]{0:T(128)}, u32[]{:S(2)}) copy-start(s32[2]{0:T(128)} %constant.228.clone.1) | copy-start | bytes 28
  12.9 27.7 %copy-start = (f32[16,96,1]{2,1,0:T(8,128)S(1)}, f32[16,96,1]{2,1,0:T(8,128)}, u32[]{:S(2)}) copy-start(f32[16,96,1]{2,1,0:T(8,128)} %get-tuple-element.117) | copy-start | bytes 18436
  13.9 4.8 %collective-permute-start = (f32[11,1536]{1,0:T(8,128)S(1)}, f32[11,1536]{1,0:T(8,128)S(1)}, u32[]{:S(2)}, u32[]{:S(2)}) collective-permute-start(f32[11,1536]{1,0:T(8,128)S(1)} %pad_maximum_fusion.2), channel_id=1, source_target_pairs={{0,8},{1,9},{2,10},{3,11},{4,12},{5,13},{6,14},{7,15},{8,0},{9,1},... | collective-permute-start | bytes 202760 | tf_op jit(solution)/shard_map/ppermute | solution.py:108
  18.8 7.1 %collective-permute-start.1 = (f32[19,1536]{1,0:T(8,128)S(1)}, f32[19,1536]{1,0:T(8,128)S(1)}, u32[]{:S(2)}, u32[]{:S(2)}) collective-permute-start(f32[19,1536]{1,0:T(8,128)S(1)} %pad_maximum_fusion.1), channel_id=1, source_target_pairs={{0,24},{1,25},{2,26},{3,27},{4,28},{5,29},{6,30},{7,31},{8,16},{9,... | collective-permute-start | bytes 350216 | tf_op jit(solution)/shard_map/ppermute | solution.py:108
  26.0 22.4 %copy-start.3 = (s32[1024]{0:T(1024)S(1)}, s32[1024]{0:T(1024)}, u32[]{:S(2)}) copy-start(s32[1024]{0:T(1024)} %param.20) | copy-start | bytes 12292
  26.0 23.7 %copy-start.2 = (f32[96,32]{0,1:T(8,128)S(1)}, f32[96,32]{0,1:T(8,128)}, u32[]{:S(2)}) copy-start(f32[96,32]{0,1:T(8,128)} %param.17) | copy-start | bytes 36868
  26.1 6.3 %collective-permute-start.2 = (f32[35,1536]{1,0:T(8,128)S(1)}, f32[35,1536]{1,0:T(8,128)S(1)}, u32[]{:S(2)}, u32[]{:S(2)}) collective-permute-start(f32[35,1536]{1,0:T(8,128)S(1)} %pad_maximum_fusion), channel_id=1, source_target_pairs={{0,32},{1,33},{2,34},{3,35},{4,36},{5,37},{6,38},{7,39},{8,40},{9,... | collective-permute-start | bytes 645128 | tf_op jit(solution)/shard_map/ppermute | solution.py:108
  32.4 5.1 %collective-permute-start.3 = (f32[3,1536]{1,0:T(4,128)S(1)}, f32[3,1536]{1,0:T(4,128)S(1)}, u32[]{:S(2)}, u32[]{:S(2)}) collective-permute-start(f32[3,1536]{1,0:T(4,128)S(1)} %pad_maximum_fusion.3), channel_id=1, source_target_pairs={{0,96},{1,97},{2,98},{3,99},{4,100},{5,101},{6,102},{7,103},{8,104... | collective-permute-start | bytes 55304 | tf_op jit(solution)/shard_map/ppermute | solution.py:108
  37.6 1.3 %collective-permute-start.4 = (f32[4,1536]{1,0:T(4,128)S(1)}, f32[4,1536]{1,0:T(4,128)S(1)}, u32[]{:S(2)}, u32[]{:S(2)}) collective-permute-start(f32[4,1536]{1,0:T(4,128)S(1)} %pad_maximum_fusion.4), channel_id=1, source_target_pairs={{0,1},{1,0},{2,3},{3,2},{4,5},{5,4},{6,7},{7,6},{8,9},{9,8},{10,11... | collective-permute-start | bytes 73736 | tf_op jit(solution)/shard_map/ppermute | solution.py:108
  38.9 3.9 %collective-permute-start.5 = (f32[4,1536]{1,0:T(4,128)S(1)}, f32[4,1536]{1,0:T(4,128)S(1)}, u32[]{:S(2)}, u32[]{:S(2)}) collective-permute-start(f32[4,1536]{1,0:T(4,128)S(1)} %fusion.40), channel_id=1, source_target_pairs={{0,2},{1,3},{2,0},{3,1},{4,6},{5,7},{6,4},{7,5},{8,10},{9,11},{10,... | collective-permute-start | bytes 73736 | tf_op jit(solution)/shard_map/ppermute | solution.py:108
  42.8 5.1 %collective-permute-start.6 = (f32[4,1536]{1,0:T(4,128)S(1)}, f32[4,1536]{1,0:T(4,128)S(1)}, u32[]{:S(2)}, u32[]{:S(2)}) collective-permute-start(f32[4,1536]{1,0:T(4,128)S(1)} %add.315), channel_id=1, source_target_pairs={{0,6},{1,7},{2,4},{3,5},{4,2},{5,3},{6,0},{7,1},{8,14},{9,15},{10,... | collective-permute-start | bytes 73736 | tf_op jit(solution)/shard_map/ppermute | solution.py:108
  45.9 28.8 %collective-permute-start.7 = (f32[64,1536]{1,0:T(8,128)S(1)}, f32[64,1536]{1,0:T(8,128)S(1)}, u32[]{:S(2)}, u32[]{:S(2)}) collective-permute-start(f32[64,1536]{1,0:T(8,128)S(1)} %maximum_select_fusion.1), channel_id=1, source_target_pairs={{0,96},{1,97},{2,98},{3,99},{4,100},{5,101},{6,102},{7,103},{8,104... | collective-permute-start | bytes 1179656 | tf_op jit(solution)/shard_map/ppermute | solution.py:108
  59.8 9.2 %collective-permute-start.8 = (f32[2,1536]{1,0:T(2,128)S(1)}, f32[2,1536]{1,0:T(2,128)S(1)}, u32[]{:S(2)}, u32[]{:S(2)}) collective-permute-start(f32[2,1536]{1,0:T(2,128)S(1)} %pad_maximum_fusion.5), channel_id=1, source_target_pairs={{0,1},{1,2},{2,3},{3,4},{4,5},{5,6},{6,7},{7,8},{8,9},{9,10},{10,1... | collective-permute-start | bytes 36872 | tf_op jit(solution)/shard_map/ppermute | solution.py:222
  70.2 3.3 %collective-permute-start.9 = (f32[2,1536]{1,0:T(2,128)S(1)}, f32[2,1536]{1,0:T(2,128)S(1)}, u32[]{:S(2)}, u32[]{:S(2)}) collective-permute-start(f32[2,1536]{1,0:T(2,128)S(1)} %pad_maximum_fusion.6), channel_id=1, source_target_pairs={{1,0},{2,1},{3,2},{4,3},{5,4},{6,5},{7,6},{8,7},{9,8},{10,9},{11,1... | collective-permute-start | bytes 36872 | tf_op jit(solution)/shard_map/ppermute | solution.py:223
  76.5 12.3 %all-to-all-start.1 = ((f32[8,6,1536]{2,1,0:T(8,128)}), f32[8,6,1536]{2,1,0:T(8,128)S(1)}, u32[]{:S(2)}, u32[]{:S(2)}) async-start(f32[8,6,1536]{2,1,0:T(8,128)} %broadcast_select_fusion.2), calls=%async_computation.1 | async-start | bytes 786432 | tf_op jit(solution)/shard_map/all_to_all | solution.py:203
